TPU v7x, 256 devices: a whole 4x4x8 slice. The times are simulated.
256 devices in a mesh: tm: 2 (over core), tile: 128 (over x, z, y).
Axes of the slice: x: 4, y: 4, z: 8, core: 2. Of those that a mesh axis runs over, the one named last changes fastest.
Arguments:
- features: bfloat16 [4, 128, 128, 384], P('tm', 'tile'), may hold values from -48 to 48
- query_weight: bfloat16 [384, 384], replicated, may hold values from -1 to 1
- key_weight: bfloat16 [384, 384], replicated, may hold values from -12 to 12
- value_weight: bfloat16 [384, 384], replicated, may hold values from -0.3125 to 0.3125
- out_weight: bfloat16 [384, 384], replicated, may hold values from -1.25 to 1.25
- conv_weight: bfloat16 [3, 3, 3, 384, 384], replicated, may hold values from -0.0625 to 0.0625
Outputs:
- decoded: bfloat16 [4, 128, 128, 384], P('tm', 'tile')
All inputs are finite; a program needn't handle non-finite values.
Results may differ from a plain program's by a relative error of at most 0.019.
Values may be sent and summed in bfloat16 or wider, within the bound.
No kernel may reach another device: no remote copies, remote signals or barrier semaphores. Data moves between devices by JAX's collectives and lax.ppermute only.
A program may use at most 128 MiB of HBM per device.

v0:
```python
import functools
import math

import jax
import jax.numpy as jnp
from jax import lax
from jax.experimental import pallas as pl
from jax.experimental.pallas import tpu as pltpu
from jax.sharding import Mesh
from jax.sharding import PartitionSpec as P

ROW_AXES = ("x", "z", "y")


def rms_rows(values):
    return values * lax.rsqrt(jnp.mean(values * values, axis=-1, keepdims=True) + 1e-06)


def project(flat_rows, weight):
    return jnp.dot(flat_rows, weight, preferred_element_type=jnp.float32).astype(jnp.bfloat16)


def ring_shift(block, axis, step):
    n = lax.axis_size(axis)
    return lax.ppermute(block, axis, [(i, (i + step) % n) for i in range(n)])


def ring_gather(block, axis):
    n = lax.axis_size(axis)
    rel = [None] * n
    rel[0] = block
    right = left = block
    for s in range(1, n // 2 + 1):
        right = ring_shift(right, axis, 1)
        rel[(n - s) % n] = right
    for s in range(1, n // 2):
        left = ring_shift(left, axis, -1)
        rel[s] = left
    return rel


def split3(values):
    hi = values.astype(jnp.bfloat16)
    rest = values - hi.astype(jnp.float32)
    mid = rest.astype(jnp.bfloat16)
    lo = (rest - mid.astype(jnp.float32)).astype(jnp.bfloat16)
    return [hi, mid, lo]


def join3(parts):
    hi, mid, lo = (p.astype(jnp.float32) for p in parts)
    return (hi + mid) + lo


def pack(state):
    high, total, summed = state
    frames, rows, width = summed.shape
    stats = jnp.stack(split3(high) + split3(total), axis=1).reshape(frames, -1, width)
    return jnp.concatenate([summed.astype(jnp.bfloat16), stats], axis=1)


def unpack(payload, rows):
    frames, _, width = payload.shape
    summed = payload[:, :rows].astype(jnp.float32)
    stats = payload[:, rows:].reshape(frames, 6, rows)
    high = join3([stats[:, 0], stats[:, 1], stats[:, 2]])
    total = join3([stats[:, 3], stats[:, 4], stats[:, 5]])
    return high, total, summed


def combine(first, second):
    high_a, total_a, summed_a = first
    high_b, total_b, summed_b = second
    fresh = jnp.maximum(high_a, high_b)
    weight_a = jnp.exp(high_a - fresh)
    weight_b = jnp.exp(high_b - fresh)
    total = total_a * weight_a + total_b * weight_b
    summed = summed_a * weight_a[..., None] + summed_b * weight_b[..., None]
    return fresh, total, summed


def ring_reduce(parts, axis, rows):
    n = lax.axis_size(axis)
    right_hops = n // 2
    left_hops = n - 1 - right_hops
    right = parts[right_hops]
    for s in range(1, right_hops + 1):
        right = unpack(ring_shift(pack(right), axis, 1), rows)
        if s < right_hops:
            right = combine(right, parts[right_hops - s])
    left = parts[(n - left_hops) % n]
    for s in range(1, left_hops + 1):
        left = unpack(ring_shift(pack(left), axis, -1), rows)
        if s < left_hops:
            left = combine(left, parts[(n - left_hops + s) % n])
    return combine(combine(right, left), parts[0])


def row_shift(block, forward):
    count = 1
    for name in ROW_AXES:
        count *= lax.axis_size(name)
    if forward:
        route = [(i, i + 1) for i in range(count - 1)]
    else:
        route = [(i + 1, i) for i in range(count - 1)]
    return lax.ppermute(block, ROW_AXES, route)


def attention_kernel(scale, query_ref, key_ref, value_ref, high_ref, total_ref, summed_ref):
    scores = lax.dot_general(
        query_ref[0], key_ref[0], (((1,), (1,)), ((), ())), preferred_element_type=jnp.float32
    ) * scale
    high = jnp.max(scores, axis=-1, keepdims=True)
    expo = jnp.exp(scores - high)
    high_ref[0] = high
    total_ref[0] = jnp.sum(expo, axis=-1, keepdims=True)
    summed_ref[0] = jnp.dot(expo.astype(jnp.bfloat16), value_ref[0], preferred_element_type=jnp.float32)


def attention(query_rows, key_rows, value_rows):
    frames, queries, width = query_rows.shape
    keys = key_rows.shape[1]
    tile = 256
    scale = 1.0 / math.sqrt(width)
    stat = jax.ShapeDtypeStruct((frames, queries, 1), jnp.float32)
    return pl.pallas_call(
        functools.partial(attention_kernel, scale),
        grid=(frames, queries // tile),
        in_specs=[
            pl.BlockSpec((1, tile, width), lambda f, i: (f, i, 0)),
            pl.BlockSpec((1, keys, width), lambda f, i: (f, 0, 0)),
            pl.BlockSpec((1, keys, width), lambda f, i: (f, 0, 0)),
        ],
        out_specs=[
            pl.BlockSpec((1, tile, 1), lambda f, i: (f, i, 0)),
            pl.BlockSpec((1, tile, 1), lambda f, i: (f, i, 0)),
            pl.BlockSpec((1, tile, width), lambda f, i: (f, i, 0)),
        ],
        out_shape=[stat, stat, jax.ShapeDtypeStruct((frames, queries, width), jnp.float32)],
        cost_estimate=pl.CostEstimate(
            flops=4 * frames * queries * keys * width,
            transcendentals=frames * queries * keys,
            bytes_accessed=2 * frames * (queries + 2 * keys) * width + 4 * frames * queries * width,
        ),
    )(query_rows, key_rows, value_rows)


def per_device(features, query_weight, key_weight, value_weight, out_weight, conv_weight):
    frames, rows, cols, width = features.shape
    count = rows * cols
    widened = features.astype(jnp.float32)
    normed = rms_rows(widened).astype(jnp.bfloat16)
    flat = normed.reshape(frames * count, width)
    scale = 1.0 / math.sqrt(width)

    query = project(flat, query_weight).reshape(frames, count, width)
    query_rel = ring_gather(query, "z")
    inner = jnp.stack(ring_gather(normed.reshape(frames, count, width), "y"))
    outer = jnp.stack(ring_gather(inner, "x"))
    keys_in = jnp.transpose(outer, (2, 0, 1, 3, 4)).reshape(-1, width)
    key_rows = project(keys_in, key_weight).reshape(frames, -1, width)
    value_rows = project(keys_in, value_weight).reshape(frames, -1, width)
    query_rows = jnp.stack(query_rel, axis=1).reshape(frames, -1, width)

    highest, total, summed = attention(query_rows, key_rows, value_rows)
    highest, total = highest[..., 0], total[..., 0]

    parts = []
    for k in range(len(query_rel)):
        lo, hi = k * count, (k + 1) * count
        parts.append((highest[:, lo:hi], total[:, lo:hi], summed[:, lo:hi]))
    _, total, summed = ring_reduce(parts, "z", count)
    attended = (summed / total[..., None]).astype(jnp.bfloat16)

    projected = jnp.dot(attended.reshape(-1, width), out_weight, preferred_element_type=jnp.float32)
    mixed = (widened + projected.reshape(features.shape)).astype(jnp.bfloat16)
    mixed_wide = mixed.astype(jnp.float32)
    activated = jax.nn.silu(rms_rows(mixed_wide)).astype(jnp.bfloat16)

    earlier = lax.ppermute(activated, "tm", [(0, 1)])
    stacked = jnp.concatenate([earlier, activated], axis=0)
    above = row_shift(stacked, True)
    below = row_shift(stacked, False)
    padded = jnp.concatenate([above, stacked, below], axis=1)
    padded = jnp.pad(padded, ((0, 0), (0, 0), (1, 1), (0, 0)))
    patches = []
    for tap_time in range(3):
        for tap_row in range(3):
            for tap_col in range(3):
                patches.append(
                    padded[
                        tap_time : tap_time + frames,
                        tap_row : tap_row + rows,
                        tap_col : tap_col + cols,
                    ]
                )
    columns = jnp.concatenate(patches, axis=-1).reshape(frames * count, 27 * width)
    conv = jnp.dot(
        columns, conv_weight.reshape(27 * width, width), preferred_element_type=jnp.float32
    )
    return (mixed_wide + conv.reshape(features.shape)).astype(jnp.bfloat16)


def solution(mesh):
    sizes = dict(zip(mesh.axis_names, mesh.devices.shape))
    tile = sizes["tile"]
    y = 4
    z = 8
    x = tile // (y * z)
    fine = Mesh(mesh.devices.reshape(sizes["tm"], x, z, y), ("tm", *ROW_AXES))
    spec = P("tm", ROW_AXES, None, None)
    in_specs = (spec, P(), P(), P(), P(), P())
    return jax.shard_map(
        per_device, mesh=fine, in_specs=in_specs, out_specs=spec, check_vma=False
    )
```

profile of v0, /device:TPU:2, one launch (start us, length us, event | category | flops | bytes accessed | tf_op | source)
XLA Modules:
  0.0 173.6 jit_solution(13267241392307826662)
XLA Ops:
  0.0 1.1 fusion.21
  1.1 1.0 fusion.109
  2.1 1.7 collective-permute-start.8
  3.8 1.0 fusion.22
  4.8 1.2 convolution_convert_fusion.2
  6.1 2.0 %collective-permute-start.3 = (bf16[2,128,384]{2,1,0:T(8,128)(2,1)S(1)}, bf16[2,128,384]{2,1,0:T(8,128)(2,1)S(1)}, u32[]{:S(2)}, u32[]{:S(2)}) collective-permute-start(bf16[2,128,384]{2,1,0:T(8,128)(2,1)S(1)} %bitcast.346), channel_id=1, source_target_pairs={{0,4},{4,8},{8,12},{12,16},{16,20},{20,24},{24,28},{28,0},{1,5},{5... | collective-permute-start | bytes 589832 | tf_op jit(solution)/shard_map/ppermute | solution.py:25
  8.1 4.0 %collective-permute-start = (bf16[2,128,384]{2,1,0:T(8,128)(2,1)S(1)}, bf16[2,128,384]{2,1,0:T(8,128)(2,1)S(1)}, u32[]{:S(2)}, u32[]{:S(2)}) collective-permute-start(bf16[2,128,384]{2,1,0:T(8,128)(2,1)S(1)} %bitcast.347), channel_id=1, source_target_pairs={{0,28},{4,0},{8,4},{12,8},{16,12},{20,16},{24,20},{28,24},{1,29},{... | collective-permute-start | bytes 589832 | tf_op jit(solution)/shard_map/ppermute | solution.py:25
  12.1 1.7 collective-permute-start.7
  14.1 1.0 fusion.108
  15.2 3.0 %collective-permute-done.7 = bf16[2,128,384]{2,1,0:T(8,128)(2,1)S(1)} collective-permute-done((bf16[2,128,384]{2,1,0:T(8,128)(2,1)S(1)}, bf16[2,128,384]{2,1,0:T(8,128)(2,1)S(1)}, u32[]{:S(2)}, u32[]{:S(2)}) %collective-permute-start.7) | collective-permute-done | bytes 196640 | tf_op jit(solution)/shard_map/ppermute | solution.py:25
  18.2 2.7 %collective-permute-done.9 = bf16[2,128,384]{2,1,0:T(8,128)(2,1)S(1)} collective-permute-done((bf16[2,128,384]{2,1,0:T(8,128)(2,1)S(1)}, bf16[2,128,384]{2,1,0:T(8,128)(2,1)S(1)}, u32[]{:S(2)}, u32[]{:S(2)}) %collective-permute-start.9) | collective-permute-done | bytes 196640 | tf_op jit(solution)/shard_map/ppermute | solution.py:25
  21.0 1.6 collective-permute-start.11
  22.7 3.2 %collective-permute-start.1 = (bf16[2,128,384]{2,1,0:T(8,128)(2,1)S(1)}, bf16[2,128,384]{2,1,0:T(8,128)(2,1)S(1)}, u32[]{:S(2)}, u32[]{:S(2)}) collective-permute-start(bf16[2,128,384]{2,1,0:T(8,128)(2,1)S(1)} %collective-permute-done), channel_id=1, source_target_pairs={{0,28},{4,0},{8,4},{12,8},{16,12},{20,16},{24,20},{28,24},{1,29},{... | collective-permute-start | bytes 589832 | tf_op jit(solution)/shard_map/ppermute | solution.py:25
  26.0 0.6 collective-permute-start.10
  26.6 3.0 %collective-permute-done.4 = bf16[2,128,384]{2,1,0:T(8,128)(2,1)S(1)} collective-permute-done((bf16[2,128,384]{2,1,0:T(8,128)(2,1)S(1)}, bf16[2,128,384]{2,1,0:T(8,128)(2,1)S(1)}, u32[]{:S(2)}, u32[]{:S(2)}) %collective-permute-start.4) | collective-permute-done | bytes 196640 | tf_op jit(solution)/shard_map/ppermute | solution.py:25
  29.6 3.2 %collective-permute-start.2 = (bf16[2,128,384]{2,1,0:T(8,128)(2,1)S(1)}, bf16[2,128,384]{2,1,0:T(8,128)(2,1)S(1)}, u32[]{:S(2)}, u32[]{:S(2)}) collective-permute-start(bf16[2,128,384]{2,1,0:T(8,128)(2,1)S(1)} %collective-permute-done.1), channel_id=1, source_target_pairs={{0,28},{4,0},{8,4},{12,8},{16,12},{20,16},{24,20},{28,24},{1,29},{... | collective-permute-start | bytes 589832 | tf_op jit(solution)/shard_map/ppermute | solution.py:25
  32.8 4.2 %collective-permute-done.5 = bf16[2,128,384]{2,1,0:T(8,128)(2,1)S(1)} collective-permute-done((bf16[2,128,384]{2,1,0:T(8,128)(2,1)S(1)}, bf16[2,128,384]{2,1,0:T(8,128)(2,1)S(1)}, u32[]{:S(2)}, u32[]{:S(2)}) %collective-permute-start.5) | collective-permute-done | bytes 196640 | tf_op jit(solution)/shard_map/ppermute | solution.py:25
  37.1 1.7 collective-permute-done.11
  38.8 1.5 collective-permute-start.12
  40.3 3.6 %collective-permute-done.6 = bf16[2,128,384]{2,1,0:T(8,128)(2,1)S(1)} collective-permute-done((bf16[2,128,384]{2,1,0:T(8,128)(2,1)S(1)}, bf16[2,128,384]{2,1,0:T(8,128)(2,1)S(1)}, u32[]{:S(2)}, u32[]{:S(2)}) %collective-permute-start.6) | collective-permute-done | bytes 196640 | tf_op jit(solution)/shard_map/ppermute | solution.py:25
  44.1 11.5 %collective-permute-done.12 = bf16[4,2,128,384]{3,2,1,0:T(8,128)(2,1)S(1)} collective-permute-done((bf16[4,2,128,384]{3,2,1,0:T(8,128)(2,1)S(1)}, bf16[4,2,128,384]{3,2,1,0:T(8,128)(2,1)S(1)}, u32[]{:S(2)}, u32[]{:S(2)}) %collective-permute-start.12) | collective-permute-done | bytes 786464 | tf_op jit(solution)/shard_map/ppermute | solution.py:25
  55.6 0.5 maximum_bitcast_fusion
  56.1 0.5 copy.73
  56.7 3.8 %convolution_convert_fusion = bf16[4096,384]{1,0:T(8,128)(2,1)} fusion(bf16[4096,384]{1,0:T(8,128)(2,1)S(1)} %bitcast.339, bf16[384,384]{1,0:T(8,128)(2,1)S(1)} %copy-done), kind=kOutput, calls=%fused_computation | convolution fusion | flops 1209532416 | bytes 6586368 | tf_op jit(solution)/shard_map/dot_general | solution.py:20
  60.4 3.8 %convolution_convert_fusion.1 = bf16[4096,384]{1,0:T(8,128)(2,1)} fusion(bf16[4096,384]{1,0:T(8,128)(2,1)S(1)} %bitcast.340, bf16[384,384]{1,0:T(8,128)(2,1)S(1)} %copy-done.2), kind=kOutput, calls=%fused_computation.1 | convolution fusion | flops 1209532416 | bytes 6586368 | tf_op jit(solution)/shard_map/dot_general | solution.py:20
  64.2 17.2 %shard_map.64 = (f32[2,1024,1]{2,1,0:T(8,128)}, f32[2,1024,1]{2,1,0:T(8,128)}, f32[2,1024,384]{2,1,0:T(8,128)}) custom-call(bf16[2,1024,384]{2,1,0:T(8,128)(2,1)} %bitcast.353, bf16[2,2048,384]{2,1,0:T(8,128)(2,1)} %bitcast.342, bf16[2,2048,384]{2,1,0:T(8,128)(2,1)} %bitcast.341), custom_call_target="tpu_custom_call" | custom-call | flops 6442450944 | bytes 11010048 | tf_op jit(solution)/shard_map/pallas_call | solution.py:127
  81.4 1.6 reduce.2
  83.0 1.6 reduce.3
  84.6 2.2 %convert.4 = bf16[2,1024,384]{2,1,0:T(8,128)(2,1)S(1)} convert(f32[2,1024,384]{2,1,0:T(8,128)} %get-tuple-element.8) | non-fusion elementwise | flops 786432 | bytes 4718592 | tf_op jit(solution)/shard_map/convert.1
  86.9 0.7 fusion.93
  87.7 7.0 %collective-permute-done.13 = bf16[2,130,384]{2,1,0:T(8,128)(2,1)S(1)} collective-permute-done((bf16[2,130,384]{2,1,0:T(8,128)(2,1)S(1)}, bf16[2,130,384]{2,1,0:T(8,128)(2,1)S(1)}, u32[]{:S(2)}, u32[]{:S(2)}) %collective-permute-start.13) | collective-permute-done | bytes 199712 | tf_op jit(solution)/shard_map/ppermute | solution.py:25
  94.7 0.7 copy-done.4
  95.6 1.1 add_convert_fusion.4
  96.8 7.0 %collective-permute-done.14 = bf16[2,130,384]{2,1,0:T(8,128)(2,1)S(1)} collective-permute-done((bf16[2,130,384]{2,1,0:T(8,128)(2,1)S(1)}, bf16[2,130,384]{2,1,0:T(8,128)(2,1)S(1)}, u32[]{:S(2)}, u32[]{:S(2)}) %collective-permute-start.14) | collective-permute-done | bytes 199712 | tf_op jit(solution)/shard_map/ppermute | solution.py:25
  103.8 0.7 copy-done.3
  104.6 1.6 pad_maximum_fusion.6
  106.3 6.1 %collective-permute-done.17 = bf16[2,130,384]{2,1,0:T(8,128)(2,1)} collective-permute-done((bf16[2,130,384]{2,1,0:T(8,128)(2,1)}, bf16[2,130,384]{2,1,0:T(8,128)(2,1)}, u32[]{:S(2)}, u32[]{:S(2)}) %collective-permute-start.17) | collective-permute-done | bytes 199712 | tf_op jit(solution)/shard_map/ppermute | solution.py:25
  112.4 0.7 slice.484
  113.2 1.9 %add_convert_fusion.3 = (bf16[2,128,384]{2,1,0:T(8,128)(2,1)S(1)}, bf16[2,128,384]{2,1,0:T(8,128)(2,1)}) fusion(f32[2,1024,384]{2,1,0:T(8,128)S(1)} %copy-done.1, bf16[2,130,384]{2,1,0:T(8,128)(2,1)} %copy-done.3, f32[2,128]{1,0:T(2,128)S(1)} %get-tuple-element.25, f32[2,128]{1,0:T(2,128)S(1)} %get-tuple-element.24, f32[2,128]{1,0:T(2,128)S(1)} %get-tuple-element.43, ...), kind=kLoop, calls=%fused_computation.36 | loop fusion | flops 983040 | bytes 1576960 | tf_op jit(solution)/shard_map/convert_element_type | solution.py:59
  115.1 0.7 pad_maximum_fusion.4
  115.8 1.7 pad_maximum_fusion.7
  117.5 3.2 %collective-permute-start.18 = (bf16[2,130,384]{2,1,0:T(8,128)(2,1)}, bf16[2,130,384]{2,1,0:T(8,128)(2,1)}, u32[]{:S(2)}, u32[]{:S(2)}) collective-permute-start(bf16[2,130,384]{2,1,0:T(8,128)(2,1)} %pad_maximum_fusion.7), channel_id=1, source_target_pairs={{0,28},{4,0},{8,4},{12,8},{16,12},{20,16},{24,20},{28,24},{1,29},{... | collective-permute-start | bytes 599048 | tf_op jit(solution)/shard_map/ppermute | solution.py:25
  120.7 2.4 %collective-permute-done.15 = bf16[2,130,384]{2,1,0:T(8,128)(2,1)} collective-permute-done((bf16[2,130,384]{2,1,0:T(8,128)(2,1)}, bf16[2,130,384]{2,1,0:T(8,128)(2,1)}, u32[]{:S(2)}, u32[]{:S(2)}) %collective-permute-start.15) | collective-permute-done | bytes 199712 | tf_op jit(solution)/shard_map/ppermute | solution.py:25
  123.1 0.7 slice.466
  123.9 0.5 collective-permute-done.18
  124.4 0.7 slice.494
  125.2 1.9 %add_convert_fusion.2 = (bf16[2,128,384]{2,1,0:T(8,128)(2,1)S(1)}, bf16[2,128,384]{2,1,0:T(8,128)(2,1)}) fusion(f32[2,1024,384]{2,1,0:T(8,128)S(1)} %copy-done.1, bf16[2,130,384]{2,1,0:T(8,128)(2,1)} %collective-permute-done.15, f32[2,128]{1,0:T(2,128)S(1)} %get-tuple-element.19, f32[2,128]{1,0:T(2,128)S(1)} %get-tuple-element.18, ...), kind=kLoop, calls=%fused_computation.35 | loop fusion | flops 983040 | bytes 1576960 | tf_op jit(solution)/shard_map/convert_element_type | solution.py:59
  127.1 0.7 pad_maximum_fusion.5
  127.8 0.6 collective-permute-start.16
  128.5 1.7 pad_maximum_fusion.8
  130.1 3.1 %collective-permute-start.19 = (bf16[2,130,384]{2,1,0:T(8,128)(2,1)}, bf16[2,130,384]{2,1,0:T(8,128)(2,1)}, u32[]{:S(2)}, u32[]{:S(2)}) collective-permute-start(bf16[2,130,384]{2,1,0:T(8,128)(2,1)} %pad_maximum_fusion.8), channel_id=1, source_target_pairs={{0,28},{4,0},{8,4},{12,8},{16,12},{20,16},{24,20},{28,24},{1,29},{... | collective-permute-start | bytes 599048 | tf_op jit(solution)/shard_map/ppermute | solution.py:25
  133.2 2.4 %collective-permute-done.16 = bf16[2,130,384]{2,1,0:T(8,128)(2,1)} collective-permute-done((bf16[2,130,384]{2,1,0:T(8,128)(2,1)}, bf16[2,130,384]{2,1,0:T(8,128)(2,1)}, u32[]{:S(2)}, u32[]{:S(2)}) %collective-permute-start.16) | collective-permute-done | bytes 199712 | tf_op jit(solution)/shard_map/ppermute | solution.py:25
  135.6 0.7 slice.476
  136.4 0.5 collective-permute-done.19
  136.9 0.7 slice.503
  137.7 1.9 %multiply_reduce_fusion = (f32[2,128]{1,0:T(2,128)S(1)}, f32[2,1,128,384]{3,2,0,1:T(8,128)S(1)}) fusion(bf16[384,384]{1,0:T(8,128)(2,1)} %param.10, f32[2,1024,384]{2,1,0:T(8,128)S(1)} %copy-done.1, bf16[2,130,384]{2,1,0:T(8,128)(2,1)} %collective-permute-done.19, bf16[2,130,384]{2,1,0:T(8,128)(2,1)} %collective-permute-done.16, ...), kind=kOutput, calls=%fused_computation.31 | convolution fusion | flops 77070080 | bytes 1677312 | tf_op jit(solution)/shard_map/dot_general | solution.py:176
  139.8 1.3 collective-permute-start.20
  141.1 1.0 collective-permute-done.20
  142.2 8.0 %collective-permute-start.22 = (bf16[4,1,128,384]{3,2,0,1:T(8,128)(2,1)S(1)}, bf16[4,1,128,384]{3,2,0,1:T(8,128)(2,1)S(1)}, u32[]{:S(2)}, u32[]{:S(2)}) collective-permute-start(bf16[4,1,128,384]{3,2,0,1:T(8,128)(2,1)S(1)} %pad_maximum_fusion.1), channel_id=1, source_target_pairs={{1,0},{2,1},{3,2},{4,3},{5,4},{6,5},{7,6},{8,7},{9,8},{10,9},{11,1... | collective-permute-start | bytes 1179656 | tf_op jit(solution)/shard_map/ppermute | solution.py:107
  150.2 1.9 %collective-permute-start.21 = (bf16[4,1,128,384]{3,2,0,1:T(8,128)(2,1)S(1)}, bf16[4,1,128,384]{3,2,0,1:T(8,128)(2,1)S(1)}, u32[]{:S(2)}, u32[]{:S(2)}) collective-permute-start(bf16[4,1,128,384]{3,2,0,1:T(8,128)(2,1)S(1)} %pad_maximum_fusion.1), channel_id=1, source_target_pairs={{0,1},{1,2},{2,3},{3,4},{4,5},{5,6},{6,7},{7,8},{8,9},{9,10},{10,1... | collective-permute-start | bytes 1179656 | tf_op jit(solution)/shard_map/ppermute | solution.py:107
  152.1 7.0 %collective-permute-done.22 = bf16[4,1,128,384]{3,2,0,1:T(8,128)(2,1)S(1)} collective-permute-done((bf16[4,1,128,384]{3,2,0,1:T(8,128)(2,1)S(1)}, bf16[4,1,128,384]{3,2,0,1:T(8,128)(2,1)S(1)}, u32[]{:S(2)}, u32[]{:S(2)}) %collective-permute-start.22) | collective-permute-done | bytes 393248 | tf_op jit(solution)/shard_map/ppermute | solution.py:107
  159.1 8.3 %collective-permute-done.21 = bf16[4,1,128,384]{3,2,0,1:T(8,128)(2,1)S(1)} collective-permute-done((bf16[4,1,128,384]{3,2,0,1:T(8,128)(2,1)S(1)}, bf16[4,1,128,384]{3,2,0,1:T(8,128)(2,1)S(1)}, u32[]{:S(2)}, u32[]{:S(2)}) %collective-permute-start.21) | collective-permute-done | bytes 393248 | tf_op jit(solution)/shard_map/ppermute | solution.py:107
  169.3 0.8 slice-done.1
  170.0 3.6 %fusion.18 = bf16[2,1,128,384]{3,2,1,0:T(8,128)(2,1)} fusion(f32[2,1,128,384]{3,2,0,1:T(8,128)S(1)} %get-tuple-element.101, bf16[10368,384,1]{1,0,2:T(8,128)(2,1)S(1)} %bitcast.356, bf16[2,1,128,10368]{3,2,0,1:T(8,128)(2,1)S(1)} %slice_dynamic-update-slice_fusion), kind=kOutput, calls=%fused_computation.21 | convolution fusion | flops 2038628352 | bytes 13860864 | tf_op jit(solution)/shard_map/dot_general | solution.py:199
  (140 shorter events, 4.0 us)
Async XLA Ops:
  0.0 56.6 %copy-start = (bf16[384,384]{1,0:T(8,128)(2,1)S(1)}, bf16[384,384]{1,0:T(8,128)(2,1)}, u32[]{:S(2)}) copy-start(bf16[384,384]{1,0:T(8,128)(2,1)} %param.9) | copy-start | bytes 884740
  2.1 11.6 %collective-permute-start.8 = (bf16[2,128,384]{2,1,0:T(8,128)(2,1)S(1)}, bf16[2,128,384]{2,1,0:T(8,128)(2,1)S(1)}, u32[]{:S(2)}, u32[]{:S(2)}) collective-permute-start(bf16[2,128,384]{2,1,0:T(8,128)(2,1)S(1)} %fusion.109), channel_id=1, source_target_pairs={{0,1},{1,2},{2,3},{3,0},{4,5},{5,6},{6,7},{7,4},{8,9},{9,10},{10,1... | collective-permute-start | bytes 589832 | tf_op jit(solution)/shard_map/ppermute | solution.py:25
  6.1 16.5 %collective-permute-start.3 = (bf16[2,128,384]{2,1,0:T(8,128)(2,1)S(1)}, bf16[2,128,384]{2,1,0:T(8,128)(2,1)S(1)}, u32[]{:S(2)}, u32[]{:S(2)}) collective-permute-start(bf16[2,128,384]{2,1,0:T(8,128)(2,1)S(1)} %bitcast.346), channel_id=1, source_target_pairs={{0,4},{4,8},{8,12},{12,16},{16,20},{20,24},{24,28},{28,0},{1,5},{5... | collective-permute-start | bytes 589832 | tf_op jit(solution)/shard_map/ppermute | solution.py:25
  8.1 14.6 %collective-permute-start = (bf16[2,128,384]{2,1,0:T(8,128)(2,1)S(1)}, bf16[2,128,384]{2,1,0:T(8,128)(2,1)S(1)}, u32[]{:S(2)}, u32[]{:S(2)}) collective-permute-start(bf16[2,128,384]{2,1,0:T(8,128)(2,1)S(1)} %bitcast.347), channel_id=1, source_target_pairs={{0,28},{4,0},{8,4},{12,8},{16,12},{20,16},{24,20},{28,24},{1,29},{... | collective-permute-start | bytes 589832 | tf_op jit(solution)/shard_map/ppermute | solution.py:25
  12.1 6.1 %collective-permute-start.7 = (bf16[2,128,384]{2,1,0:T(8,128)(2,1)S(1)}, bf16[2,128,384]{2,1,0:T(8,128)(2,1)S(1)}, u32[]{:S(2)}, u32[]{:S(2)}) collective-permute-start(bf16[2,128,384]{2,1,0:T(8,128)(2,1)S(1)} %fusion.109), channel_id=1, source_target_pairs={{0,3},{1,0},{2,1},{3,2},{4,7},{5,4},{6,5},{7,6},{8,11},{9,8},{10,9... | collective-permute-start | bytes 589832 | tf_op jit(solution)/shard_map/ppermute | solution.py:25
  13.8 7.1 %collective-permute-start.9 = (bf16[2,128,384]{2,1,0:T(8,128)(2,1)S(1)}, bf16[2,128,384]{2,1,0:T(8,128)(2,1)S(1)}, u32[]{:S(2)}, u32[]{:S(2)}) collective-permute-start(bf16[2,128,384]{2,1,0:T(8,128)(2,1)S(1)} %collective-permute-done.8), channel_id=1, source_target_pairs={{0,1},{1,2},{2,3},{3,0},{4,5},{5,6},{6,7},{7,4},{8,9},{9,10},{10,1... | collective-permute-start | bytes 589832 | tf_op jit(solution)/shard_map/ppermute | solution.py:25
  21.0 17.8 %collective-permute-start.11 = (bf16[4,2,128,384]{3,2,1,0:T(8,128)(2,1)S(1)}, bf16[4,2,128,384]{3,2,1,0:T(8,128)(2,1)S(1)}, u32[]{:S(2)}, u32[]{:S(2)}) collective-permute-start(bf16[4,2,128,384]{3,2,1,0:T(8,128)(2,1)S(1)} %get-tuple-element.53), channel_id=1, source_target_pairs={{0,32},{32,64},{64,96},{96,0},{1,33},{33,65},{65,97},{97,1},{2,34}... | collective-permute-start | bytes 2359304 | tf_op jit(solution)/shard_map/ppermute | solution.py:25
  22.6 7.0 %collective-permute-start.4 = (bf16[2,128,384]{2,1,0:T(8,128)(2,1)S(1)}, bf16[2,128,384]{2,1,0:T(8,128)(2,1)S(1)}, u32[]{:S(2)}, u32[]{:S(2)}) collective-permute-start(bf16[2,128,384]{2,1,0:T(8,128)(2,1)S(1)} %collective-permute-done.3), channel_id=1, source_target_pairs={{0,4},{4,8},{8,12},{12,16},{16,20},{20,24},{24,28},{28,0},{1,5},{5... | collective-permute-start | bytes 589832 | tf_op jit(solution)/shard_map/ppermute | solution.py:25
  22.7 6.9 %collective-permute-start.1 = (bf16[2,128,384]{2,1,0:T(8,128)(2,1)S(1)}, bf16[2,128,384]{2,1,0:T(8,128)(2,1)S(1)}, u32[]{:S(2)}, u32[]{:S(2)}) collective-permute-start(bf16[2,128,384]{2,1,0:T(8,128)(2,1)S(1)} %collective-permute-done), channel_id=1, source_target_pairs={{0,28},{4,0},{8,4},{12,8},{16,12},{20,16},{24,20},{28,24},{1,29},{... | collective-permute-start | bytes 589832 | tf_op jit(solution)/shard_map/ppermute | solution.py:25
  26.0 18.1 %collective-permute-start.10 = (bf16[4,2,128,384]{3,2,1,0:T(8,128)(2,1)S(1)}, bf16[4,2,128,384]{3,2,1,0:T(8,128)(2,1)S(1)}, u32[]{:S(2)}, u32[]{:S(2)}) collective-permute-start(bf16[4,2,128,384]{3,2,1,0:T(8,128)(2,1)S(1)} %get-tuple-element.53), channel_id=1, source_target_pairs={{0,96},{32,0},{64,32},{96,64},{1,97},{33,1},{65,33},{97,65},{2,98}... | collective-permute-start | bytes 2359304 | tf_op jit(solution)/shard_map/ppermute | solution.py:25
  29.6 7.4 %collective-permute-start.5 = (bf16[2,128,384]{2,1,0:T(8,128)(2,1)S(1)}, bf16[2,128,384]{2,1,0:T(8,128)(2,1)S(1)}, u32[]{:S(2)}, u32[]{:S(2)}) collective-permute-start(bf16[2,128,384]{2,1,0:T(8,128)(2,1)S(1)} %collective-permute-done.4), channel_id=1, source_target_pairs={{0,4},{4,8},{8,12},{12,16},{16,20},{20,24},{24,28},{28,0},{1,5},{5... | collective-permute-start | bytes 589832 | tf_op jit(solution)/shard_map/ppermute | solution.py:25
  29.6 7.4 %collective-permute-start.2 = (bf16[2,128,384]{2,1,0:T(8,128)(2,1)S(1)}, bf16[2,128,384]{2,1,0:T(8,128)(2,1)S(1)}, u32[]{:S(2)}, u32[]{:S(2)}) collective-permute-start(bf16[2,128,384]{2,1,0:T(8,128)(2,1)S(1)} %collective-permute-done.1), channel_id=1, source_target_pairs={{0,28},{4,0},{8,4},{12,8},{16,12},{20,16},{24,20},{28,24},{1,29},{... | collective-permute-start | bytes 589832 | tf_op jit(solution)/shard_map/ppermute | solution.py:25
  37.0 6.9 %collective-permute-start.6 = (bf16[2,128,384]{2,1,0:T(8,128)(2,1)S(1)}, bf16[2,128,384]{2,1,0:T(8,128)(2,1)S(1)}, u32[]{:S(2)}, u32[]{:S(2)}) collective-permute-start(bf16[2,128,384]{2,1,0:T(8,128)(2,1)S(1)} %collective-permute-done.5), channel_id=1, source_target_pairs={{0,4},{4,8},{8,12},{12,16},{16,20},{20,24},{24,28},{28,0},{1,5},{5... | collective-permute-start | bytes 589832 | tf_op jit(solution)/shard_map/ppermute | solution.py:25
  38.8 16.8 %collective-permute-start.12 = (bf16[4,2,128,384]{3,2,1,0:T(8,128)(2,1)S(1)}, bf16[4,2,128,384]{3,2,1,0:T(8,128)(2,1)S(1)}, u32[]{:S(2)}, u32[]{:S(2)}) collective-permute-start(bf16[4,2,128,384]{3,2,1,0:T(8,128)(2,1)S(1)} %collective-permute-done.11), channel_id=1, source_target_pairs={{0,32},{32,64},{64,96},{96,0},{1,33},{33,65},{65,97},{97,1},{2,34}... | collective-permute-start | bytes 2359304 | tf_op jit(solution)/shard_map/ppermute | solution.py:25
  44.1 12.1 %copy-start.5 = (bf16[2,8,128,384]{3,2,1,0:T(8,128)(2,1)}, bf16[2,8,128,384]{3,2,1,0:T(8,128)(2,1)S(1)}, u32[]{:S(2)}) copy-start(bf16[2,8,128,384]{3,2,1,0:T(8,128)(2,1)S(1)} %bitcast_dynamic-update-slice_fusion.6) | copy-start | bytes 4718596
  56.6 3.8 %copy-start.2 = (bf16[384,384]{1,0:T(8,128)(2,1)S(1)}, bf16[384,384]{1,0:T(8,128)(2,1)}, u32[]{:S(2)}) copy-start(bf16[384,384]{1,0:T(8,128)(2,1)} %param.8) | copy-start | bytes 884740
  84.5 11.0 %copy-start.1 = (f32[2,1024,384]{2,1,0:T(8,128)S(1)}, f32[2,1024,384]{2,1,0:T(8,128)}, u32[]{:S(2)}) copy-start(f32[2,1024,384]{2,1,0:T(8,128)} %get-tuple-element.8) | copy-start | bytes 9437188
  87.6 7.1 %collective-permute-start.13 = (bf16[2,130,384]{2,1,0:T(8,128)(2,1)S(1)}, bf16[2,130,384]{2,1,0:T(8,128)(2,1)S(1)}, u32[]{:S(2)}, u32[]{:S(2)}) collective-permute-start(bf16[2,130,384]{2,1,0:T(8,128)(2,1)S(1)} %pad_maximum_fusion.2), channel_id=1, source_target_pairs={{0,4},{4,8},{8,12},{12,16},{16,20},{20,24},{24,28},{28,0},{1,5},{5... | collective-permute-start | bytes 599048 | tf_op jit(solution)/shard_map/ppermute | solution.py:25
  94.7 0.7 copy-start.4
  96.7 7.1 %collective-permute-start.14 = (bf16[2,130,384]{2,1,0:T(8,128)(2,1)S(1)}, bf16[2,130,384]{2,1,0:T(8,128)(2,1)S(1)}, u32[]{:S(2)}, u32[]{:S(2)}) collective-permute-start(bf16[2,130,384]{2,1,0:T(8,128)(2,1)S(1)} %pad_maximum_fusion.3), channel_id=1, source_target_pairs={{0,4},{4,8},{8,12},{12,16},{16,20},{20,24},{24,28},{28,0},{1,5},{5... | collective-permute-start | bytes 599048 | tf_op jit(solution)/shard_map/ppermute | solution.py:25
  103.8 0.7 copy-start.3
  106.3 6.1 %collective-permute-start.17 = (bf16[2,130,384]{2,1,0:T(8,128)(2,1)}, bf16[2,130,384]{2,1,0:T(8,128)(2,1)}, u32[]{:S(2)}, u32[]{:S(2)}) collective-permute-start(bf16[2,130,384]{2,1,0:T(8,128)(2,1)} %pad_maximum_fusion.6), channel_id=1, source_target_pairs={{0,28},{4,0},{8,4},{12,8},{16,12},{20,16},{24,20},{28,24},{1,29},{... | collective-permute-start | bytes 599048 | tf_op jit(solution)/shard_map/ppermute | solution.py:25
  115.8 7.3 %collective-permute-start.15 = (bf16[2,130,384]{2,1,0:T(8,128)(2,1)}, bf16[2,130,384]{2,1,0:T(8,128)(2,1)}, u32[]{:S(2)}, u32[]{:S(2)}) collective-permute-start(bf16[2,130,384]{2,1,0:T(8,128)(2,1)} %pad_maximum_fusion.4), channel_id=1, source_target_pairs={{0,4},{4,8},{8,12},{12,16},{16,20},{20,24},{24,28},{28,0},{1,5},{5... | collective-permute-start | bytes 599048 | tf_op jit(solution)/shard_map/ppermute | solution.py:25
  117.5 6.9 %collective-permute-start.18 = (bf16[2,130,384]{2,1,0:T(8,128)(2,1)}, bf16[2,130,384]{2,1,0:T(8,128)(2,1)}, u32[]{:S(2)}, u32[]{:S(2)}) collective-permute-start(bf16[2,130,384]{2,1,0:T(8,128)(2,1)} %pad_maximum_fusion.7), channel_id=1, source_target_pairs={{0,28},{4,0},{8,4},{12,8},{16,12},{20,16},{24,20},{28,24},{1,29},{... | collective-permute-start | bytes 599048 | tf_op jit(solution)/shard_map/ppermute | solution.py:25
  127.8 7.8 %collective-permute-start.16 = (bf16[2,130,384]{2,1,0:T(8,128)(2,1)}, bf16[2,130,384]{2,1,0:T(8,128)(2,1)}, u32[]{:S(2)}, u32[]{:S(2)}) collective-permute-start(bf16[2,130,384]{2,1,0:T(8,128)(2,1)} %pad_maximum_fusion.5), channel_id=1, source_target_pairs={{0,4},{4,8},{8,12},{12,16},{16,20},{20,24},{24,28},{28,0},{1,5},{5... | collective-permute-start | bytes 599048 | tf_op jit(solution)/shard_map/ppermute | solution.py:25
  130.1 6.7 %collective-permute-start.19 = (bf16[2,130,384]{2,1,0:T(8,128)(2,1)}, bf16[2,130,384]{2,1,0:T(8,128)(2,1)}, u32[]{:S(2)}, u32[]{:S(2)}) collective-permute-start(bf16[2,130,384]{2,1,0:T(8,128)(2,1)} %pad_maximum_fusion.8), channel_id=1, source_target_pairs={{0,28},{4,0},{8,4},{12,8},{16,12},{20,16},{24,20},{28,24},{1,29},{... | collective-permute-start | bytes 599048 | tf_op jit(solution)/shard_map/ppermute | solution.py:25
  137.6 31.6 %slice-start = ((s8[7962624]{0:T(1024)(128)(4,1)}), s8[4194304]{0:T(1024)(128)(4,1)S(1)}, s32[]{:S(2)}) async-start(s8[7962624]{0:T(1024)(128)(4,1)} %bitcast.354), calls=%async_computation | async-start | bytes 8388608
  139.8 2.4 %collective-permute-start.20 = (bf16[2,1,128,384]{3,2,0,1:T(8,128)(2,1)S(1)}, bf16[2,1,128,384]{3,2,0,1:T(8,128)(2,1)S(1)}, u32[]{:S(2)}, u32[]{:S(2)}) collective-permute-start(bf16[2,1,128,384]{3,2,0,1:T(8,128)(2,1)S(1)} %multiply_convert_fusion), channel_id=1, source_target_pairs={{0,128},{1,129},{2,130},{3,131},{4,132},{5,133},{6,134},{7,135},{8... | collective-permute-start | bytes 589832 | tf_op jit(solution)/shard_map/ppermute | solution.py:181
  142.2 16.9 %collective-permute-start.22 = (bf16[4,1,128,384]{3,2,0,1:T(8,128)(2,1)S(1)}, bf16[4,1,128,384]{3,2,0,1:T(8,128)(2,1)S(1)}, u32[]{:S(2)}, u32[]{:S(2)}) collective-permute-start(bf16[4,1,128,384]{3,2,0,1:T(8,128)(2,1)S(1)} %pad_maximum_fusion.1), channel_id=1, source_target_pairs={{1,0},{2,1},{3,2},{4,3},{5,4},{6,5},{7,6},{8,7},{9,8},{10,9},{11,1... | collective-permute-start | bytes 1179656 | tf_op jit(solution)/shard_map/ppermute | solution.py:107
  150.2 17.2 %collective-permute-start.21 = (bf16[4,1,128,384]{3,2,0,1:T(8,128)(2,1)S(1)}, bf16[4,1,128,384]{3,2,0,1:T(8,128)(2,1)S(1)}, u32[]{:S(2)}, u32[]{:S(2)}) collective-permute-start(bf16[4,1,128,384]{3,2,0,1:T(8,128)(2,1)S(1)} %pad_maximum_fusion.1), channel_id=1, source_target_pairs={{0,1},{1,2},{2,3},{3,4},{4,5},{5,6},{6,7},{7,8},{8,9},{9,10},{10,1... | collective-permute-start | bytes 1179656 | tf_op jit(solution)/shard_map/ppermute | solution.py:107
  168.0 2.1 %slice-start.1 = ((s8[7962624]{0:T(1024)(128)(4,1)}), s8[3768320]{0:T(1024)(128)(4,1)S(1)}, s32[]{:S(2)}) async-start(s8[7962624]{0:T(1024)(128)(4,1)} %bitcast.354), calls=%async_computation.1 | async-start | bytes 7536640
where the time goes:
time: 174 us
  waiting for transfers between devices  71.9 us (41%)
  starting transfers between devices  38.2 us (22%)
  other arithmetic  22.7 us (13%)
  Pallas kernels  17.2 us (10%)
  matrix products  14.3 us (8%)
  local copies, waits for them, and re-layouts  8.74 us (5%)
    ppermute x20, waiting for transfers between devices, ring_shift(): return lax.ppermute(block, axis, [(i, (i + step) % n) for i in range(n)])  55.5 us
    ppermute x20, starting transfers between devices, ring_shift(): return lax.ppermute(block, axis, [(i, (i + step) % n) for i in range(n)])  27 us
    pallas_call x1, Pallas kernels, attention(): pl.pallas_call(functools.partial(attention_kernel, scale), grid=(frames,...  17.2 us
    ppermute x2, waiting for transfers between devices, row_shift(): return lax.ppermute(block, ROW_AXES, route)  15.3 us
    ppermute x2, starting transfers between devices, row_shift(): return lax.ppermute(block, ROW_AXES, route)  9.9 us
    dot_general x3, matrix products, project(): jnp.dot(flat_rows, weight, preferred_element_type=jnp.float32)  8.74 us
    concatenate x7, other arithmetic, pack(): return jnp.concatenate([summed.astype(jnp.bfloat16), stats], axis=1)  6.38 us
    convert_element_type x3, other arithmetic, pack(): return jnp.concatenate([summed.astype(jnp.bfloat16), stats], axis=1)  4.85 us
  transfers between devices with their start and end apart: 23, of which 17 were waited for; matrix products, arithmetic and copies ran while one was open for 5% of the time, Pallas kernels for 0%

commit v1 on v0

--- a/solution.py
+++ b/solution.py
@@ -25,17 +25,23 @@
     return lax.ppermute(block, axis, [(i, (i + step) % n) for i in range(n)])
 
 
-def ring_gather(block, axis):
+def ring_gather(block, axis, halve=False):
     n = lax.axis_size(axis)
     rel = [None] * n
     rel[0] = block
     right = left = block
-    for s in range(1, n // 2 + 1):
+    for s in range(1, n // 2):
         right = ring_shift(right, axis, 1)
-        rel[(n - s) % n] = right
-    for s in range(1, n // 2):
+        rel[n - s] = right
         left = ring_shift(left, axis, -1)
         rel[s] = left
+    if halve:
+        half = block.shape[0] // 2
+        head = ring_shift(right[:half], axis, 1)
+        tail = ring_shift(left[half:], axis, -1)
+        rel[n // 2] = jnp.concatenate([head, tail], axis=0)
+    else:
+        rel[n // 2] = ring_shift(right, axis, 1)
     return rel
 
 
@@ -107,15 +113,19 @@
     return lax.ppermute(block, ROW_AXES, route)
 
 
-def attention_kernel(scale, query_ref, key_ref, value_ref, high_ref, total_ref, summed_ref):
+def attention_kernel(scale, query_ref, key_ref, value_ref, high_ref, total_ref, summed_ref, short_ref):
     scores = lax.dot_general(
         query_ref[0], key_ref[0], (((1,), (1,)), ((), ())), preferred_element_type=jnp.float32
     ) * scale
     high = jnp.max(scores, axis=-1, keepdims=True)
     expo = jnp.exp(scores - high)
-    high_ref[0] = high
-    total_ref[0] = jnp.sum(expo, axis=-1, keepdims=True)
-    summed_ref[0] = jnp.dot(expo.astype(jnp.bfloat16), value_ref[0], preferred_element_type=jnp.float32)
+    total = jnp.sum(expo, axis=-1, keepdims=True)
+    rows = high.shape[0]
+    high_ref[0] = jnp.transpose(jnp.broadcast_to(high, (rows, 128)))[0:1, :]
+    total_ref[0] = jnp.transpose(jnp.broadcast_to(total, (rows, 128)))[0:1, :]
+    summed = jnp.dot(expo.astype(jnp.bfloat16), value_ref[0], preferred_element_type=jnp.float32)
+    summed_ref[0] = summed
+    short_ref[0] = summed.astype(jnp.bfloat16)
 
 
 def attention(query_rows, key_rows, value_rows):
@@ -123,25 +133,28 @@
     keys = key_rows.shape[1]
     tile = 256
     scale = 1.0 / math.sqrt(width)
-    stat = jax.ShapeDtypeStruct((frames, queries, 1), jnp.float32)
+    stat = jax.ShapeDtypeStruct((frames, 1, queries), jnp.float32)
+    stat_spec = pl.BlockSpec((1, 1, tile), lambda f, i: (f, 0, i))
+    row_spec = pl.BlockSpec((1, tile, width), lambda f, i: (f, i, 0))
     return pl.pallas_call(
         functools.partial(attention_kernel, scale),
         grid=(frames, queries // tile),
         in_specs=[
-            pl.BlockSpec((1, tile, width), lambda f, i: (f, i, 0)),
+            row_spec,
             pl.BlockSpec((1, keys, width), lambda f, i: (f, 0, 0)),
             pl.BlockSpec((1, keys, width), lambda f, i: (f, 0, 0)),
         ],
-        out_specs=[
-            pl.BlockSpec((1, tile, 1), lambda f, i: (f, i, 0)),
-            pl.BlockSpec((1, tile, 1), lambda f, i: (f, i, 0)),
-            pl.BlockSpec((1, tile, width), lambda f, i: (f, i, 0)),
+        out_specs=[stat_spec, stat_spec, row_spec, row_spec],
+        out_shape=[
+            stat,
+            stat,
+            jax.ShapeDtypeStruct((frames, queries, width), jnp.float32),
+            jax.ShapeDtypeStruct((frames, queries, width), jnp.bfloat16),
         ],
-        out_shape=[stat, stat, jax.ShapeDtypeStruct((frames, queries, width), jnp.float32)],
         cost_estimate=pl.CostEstimate(
             flops=4 * frames * queries * keys * width,
             transcendentals=frames * queries * keys,
-            bytes_accessed=2 * frames * (queries + 2 * keys) * width + 4 * frames * queries * width,
+            bytes_accessed=2 * frames * (queries + 2 * keys) * width + 6 * frames * queries * width,
         ),
     )(query_rows, key_rows, value_rows)
 
@@ -157,19 +170,22 @@
     query = project(flat, query_weight).reshape(frames, count, width)
     query_rel = ring_gather(query, "z")
     inner = jnp.stack(ring_gather(normed.reshape(frames, count, width), "y"))
-    outer = jnp.stack(ring_gather(inner, "x"))
+    outer = jnp.stack(ring_gather(inner, "x", halve=True))
     keys_in = jnp.transpose(outer, (2, 0, 1, 3, 4)).reshape(-1, width)
     key_rows = project(keys_in, key_weight).reshape(frames, -1, width)
     value_rows = project(keys_in, value_weight).reshape(frames, -1, width)
     query_rows = jnp.stack(query_rel, axis=1).reshape(frames, -1, width)
 
-    highest, total, summed = attention(query_rows, key_rows, value_rows)
-    highest, total = highest[..., 0], total[..., 0]
-
+    highest, total, summed, short = attention(query_rows, key_rows, value_rows)
+    highest, total = highest[:, 0], total[:, 0]
+
+    blocks = len(query_rel)
+    first_sent = (blocks // 2, (blocks + 1) // 2 + 1)
     parts = []
-    for k in range(len(query_rel)):
+    for k in range(blocks):
         lo, hi = k * count, (k + 1) * count
-        parts.append((highest[:, lo:hi], total[:, lo:hi], summed[:, lo:hi]))
+        rows_of = short if k in first_sent else summed
+        parts.append((highest[:, lo:hi], total[:, lo:hi], rows_of[:, lo:hi]))
     _, total, summed = ring_reduce(parts, "z", count)
     attended = (summed / total[..., None]).astype(jnp.bfloat16)
 
@@ -178,10 +194,16 @@
     mixed_wide = mixed.astype(jnp.float32)
     activated = jax.nn.silu(rms_rows(mixed_wide)).astype(jnp.bfloat16)
 
+    every = ("tm", *ROW_AXES)
+    count_rows = 1
+    for name in ROW_AXES:
+        count_rows *= lax.axis_size(name)
     earlier = lax.ppermute(activated, "tm", [(0, 1)])
+    earlier_above = lax.ppermute(activated, every, [(r, count_rows + r + 1) for r in range(count_rows - 1)])
+    earlier_below = lax.ppermute(activated, every, [(r + 1, count_rows + r) for r in range(count_rows - 1)])
+    above = jnp.concatenate([earlier_above, row_shift(activated, True)], axis=0)
+    below = jnp.concatenate([earlier_below, row_shift(activated, False)], axis=0)
     stacked = jnp.concatenate([earlier, activated], axis=0)
-    above = row_shift(stacked, True)
-    below = row_shift(stacked, False)
     padded = jnp.concatenate([above, stacked, below], axis=1)
     padded = jnp.pad(padded, ((0, 0), (0, 0), (1, 1), (0, 0)))
     patches = []

time: 174 us -> 156 us (0.90)
  other arithmetic: 22.7 us -> 10.2 us
  waiting for transfers between devices: 71.9 us -> 65.6 us
  starting transfers between devices: 38.2 us -> 42.4 us
  local copies, waits for them, and re-layouts: 8.74 us -> 5.24 us
    concatenate x7, other arithmetic: 6.38 us -> 0.18 us  [pack(): return jnp.concatenate([summed.astype(jnp.bfloat16), stats], axis=1)]
    ppermute x2, waiting for transfers between devices: 15.3 us -> 9.78 us  [row_shift(): return lax.ppermute(block, ROW_AXES, route)]
    slice x7, local copies, waits for them, and re-layouts: 3.57 us -> 0.04 us  [unpack(): stats = payload[:, rows:].reshape(frames, 6, rows)]
    pallas_call x2 -> x0, other arithmetic: 3.14 us -> none  [attention(): pl.pallas_call(functools.partial(attention_kernel, scale), grid=(frames,...]
    ppermute x0 -> x2, starting transfers between devices: none -> 2.87 us  [the longest x1 1.56 us: per_device(): lax.ppermute(activated, every, [(r, count_rows + r + 1) for r in range(co...]
    another operation x2, other arithmetic: 2.38 us -> 0.26 us  [per_device(): outer = jnp.stack(ring_gather(inner, 'x', halve=True))]
    ppermute x20 -> x21, starting transfers between devices: 27 us -> 28.6 us  [ring_shift(): return lax.ppermute(block, axis, [(i, (i + step) % n) for i in range(n)])]
    ppermute x20 -> x21, waiting for transfers between devices: 55.5 us -> 55.8 us  [ring_shift(): return lax.ppermute(block, axis, [(i, (i + step) % n) for i in range(n)])]
  transfers between devices with their start and end apart: 23 -> 26, of which waited for: 17 -> 14; matrix products, arithmetic and copies ran while one was open for 5% -> 2% of each run, Pallas kernels for 0% -> 0%
where the time goes in v1:
time: 156 us; the launch traced here: 155 us
  waiting for transfers between devices  65.6 us (42%)
  starting transfers between devices  42.4 us (27%)
  Pallas kernels  17.2 us (11%)
  matrix products  13.8 us (9%)
  other arithmetic  10.2 us (7%)
  local copies, waits for them, and re-layouts  5.24 us (3%)
    ppermute x21, waiting for transfers between devices, ring_shift(): return lax.ppermute(block, axis, [(i, (i + step) % n) for i in range(n)])  55.8 us
    ppermute x21, starting transfers between devices, ring_shift(): return lax.ppermute(block, axis, [(i, (i + step) % n) for i in range(n)])  28.6 us
    pallas_call x1, Pallas kernels, attention(): pl.pallas_call(functools.partial(attention_kernel, scale), grid=(frames,...  17.2 us
    ppermute x2, waiting for transfers between devices, row_shift(): return lax.ppermute(block, ROW_AXES, route)  9.78 us
    ppermute x2, starting transfers between devices, row_shift(): return lax.ppermute(block, ROW_AXES, route)  9.65 us
    dot_general x3, matrix products, project(): jnp.dot(flat_rows, weight, preferred_element_type=jnp.float32)  8.65 us
    convert_element_type x3, other arithmetic, pack(): return jnp.concatenate([summed.astype(jnp.bfloat16), stats], axis=1)  3.81 us
    dot_general x1, matrix products, per_device(): jnp.dot(columns, conv_weight.reshape(27 * width, width), preferred_elemen...  3.61 us
  transfers between devices with their start and end apart: 26, of which 14 were waited for; matrix products, arithmetic and copies ran while one was open for 2% of the time, Pallas kernels for 0%

profile of v1, /device:TPU:2, one launch (start us, length us, event | category | flops | bytes accessed | tf_op | source)
XLA Modules:
  0.0 155.2 jit_solution(1715888125240965709)
XLA Ops:
  0.0 1.1 fusion.21
  1.1 1.0 fusion.22
  2.1 1.2 convolution_convert_fusion.2
  3.4 2.0 %collective-permute-start.3 = (bf16[2,128,384]{2,1,0:T(8,128)(2,1)S(1)}, bf16[2,128,384]{2,1,0:T(8,128)(2,1)S(1)}, u32[]{:S(2)}, u32[]{:S(2)}) collective-permute-start(bf16[2,128,384]{2,1,0:T(8,128)(2,1)S(1)} %bitcast.350), channel_id=1, source_target_pairs={{0,4},{4,8},{8,12},{12,16},{16,20},{20,24},{24,28},{28,0},{1,5},{5... | collective-permute-start | bytes 589832 | tf_op jit(solution)/shard_map/ppermute | solution.py:25
  5.4 4.0 %collective-permute-start = (bf16[2,128,384]{2,1,0:T(8,128)(2,1)S(1)}, bf16[2,128,384]{2,1,0:T(8,128)(2,1)S(1)}, u32[]{:S(2)}, u32[]{:S(2)}) collective-permute-start(bf16[2,128,384]{2,1,0:T(8,128)(2,1)S(1)} %bitcast.351), channel_id=1, source_target_pairs={{0,28},{4,0},{8,4},{12,8},{16,12},{20,16},{24,20},{28,24},{1,29},{... | collective-permute-start | bytes 589832 | tf_op jit(solution)/shard_map/ppermute | solution.py:25
  9.4 1.0 fusion.108
  10.4 1.7 %collective-permute-start.8 = (bf16[2,128,384]{2,1,0:T(8,128)(2,1)S(1)}, bf16[2,128,384]{2,1,0:T(8,128)(2,1)S(1)}, u32[]{:S(2)}, u32[]{:S(2)}) collective-permute-start(bf16[2,128,384]{2,1,0:T(8,128)(2,1)S(1)} %fusion.108), channel_id=1, source_target_pairs={{0,1},{1,2},{2,3},{3,0},{4,5},{5,6},{6,7},{7,4},{8,9},{9,10},{10,1... | collective-permute-start | bytes 589832 | tf_op jit(solution)/shard_map/ppermute | solution.py:25
  12.1 1.7 %collective-permute-start.7 = (bf16[2,128,384]{2,1,0:T(8,128)(2,1)S(1)}, bf16[2,128,384]{2,1,0:T(8,128)(2,1)S(1)}, u32[]{:S(2)}, u32[]{:S(2)}) collective-permute-start(bf16[2,128,384]{2,1,0:T(8,128)(2,1)S(1)} %fusion.108), channel_id=1, source_target_pairs={{0,3},{1,0},{2,1},{3,2},{4,7},{5,4},{6,5},{7,6},{8,11},{9,8},{10,9... | collective-permute-start | bytes 589832 | tf_op jit(solution)/shard_map/ppermute | solution.py:25
  13.8 1.0 fusion.107
  14.8 0.1 collective-permute-start.4
  14.9 3.2 %collective-permute-start.1 = (bf16[2,128,384]{2,1,0:T(8,128)(2,1)S(1)}, bf16[2,128,384]{2,1,0:T(8,128)(2,1)S(1)}, u32[]{:S(2)}, u32[]{:S(2)}) collective-permute-start(bf16[2,128,384]{2,1,0:T(8,128)(2,1)S(1)} %collective-permute-done), channel_id=1, source_target_pairs={{0,28},{4,0},{8,4},{12,8},{16,12},{20,16},{24,20},{28,24},{1,29},{... | collective-permute-start | bytes 589832 | tf_op jit(solution)/shard_map/ppermute | solution.py:25
  18.1 0.9 collective-permute-start.9
  19.1 5.9 %collective-permute-done.9 = bf16[2,128,384]{2,1,0:T(8,128)(2,1)S(1)} collective-permute-done((bf16[2,128,384]{2,1,0:T(8,128)(2,1)S(1)}, bf16[2,128,384]{2,1,0:T(8,128)(2,1)S(1)}, u32[]{:S(2)}, u32[]{:S(2)}) %collective-permute-start.9) | collective-permute-done | bytes 196640 | tf_op jit(solution)/shard_map/ppermute | solution.py:25
  25.0 0.2 fusion.77
  25.2 0.6 collective-permute-start.10
  25.8 1.5 collective-permute-start.11
  27.3 3.2 %collective-permute-start.2 = (bf16[2,128,384]{2,1,0:T(8,128)(2,1)S(1)}, bf16[2,128,384]{2,1,0:T(8,128)(2,1)S(1)}, u32[]{:S(2)}, u32[]{:S(2)}) collective-permute-start(bf16[2,128,384]{2,1,0:T(8,128)(2,1)S(1)} %collective-permute-done.1), channel_id=1, source_target_pairs={{0,28},{4,0},{8,4},{12,8},{16,12},{20,16},{24,20},{28,24},{1,29},{... | collective-permute-start | bytes 589832 | tf_op jit(solution)/shard_map/ppermute | solution.py:25
  30.6 3.9 %collective-permute-done.5 = bf16[2,128,384]{2,1,0:T(8,128)(2,1)S(1)} collective-permute-done((bf16[2,128,384]{2,1,0:T(8,128)(2,1)S(1)}, bf16[2,128,384]{2,1,0:T(8,128)(2,1)S(1)}, u32[]{:S(2)}, u32[]{:S(2)}) %collective-permute-start.5) | collective-permute-done | bytes 196640 | tf_op jit(solution)/shard_map/ppermute | solution.py:25
  34.5 6.8 %collective-permute-done.6 = bf16[2,128,384]{2,1,0:T(8,128)(2,1)S(1)} collective-permute-done((bf16[2,128,384]{2,1,0:T(8,128)(2,1)S(1)}, bf16[2,128,384]{2,1,0:T(8,128)(2,1)S(1)}, u32[]{:S(2)}, u32[]{:S(2)}) %collective-permute-start.6) | collective-permute-done | bytes 196640 | tf_op jit(solution)/shard_map/ppermute | solution.py:25
  41.4 1.4 collective-permute-done.10
  42.9 0.4 collective-permute-start.13
  43.3 0.3 collective-permute-done.11
  43.7 1.7 %collective-permute-start.12 = (bf16[2,2,128,384]{3,2,1,0:T(8,128)(2,1)S(1)}, bf16[2,2,128,384]{3,2,1,0:T(8,128)(2,1)S(1)}, u32[]{:S(2)}, u32[]{:S(2)}) collective-permute-start(bf16[2,2,128,384]{3,2,1,0:T(8,128)(2,1)S(1)} %slice.436), channel_id=1, source_target_pairs={{0,32},{32,64},{64,96},{96,0},{1,33},{33,65},{65,97},{97,1},{2,34}... | collective-permute-start | bytes 1179656 | tf_op jit(solution)/shard_map/ppermute | solution.py:25
  45.4 5.4 %collective-permute-done.13 = bf16[2,2,128,384]{3,2,1,0:T(8,128)(2,1)S(1)} collective-permute-done((bf16[2,2,128,384]{3,2,1,0:T(8,128)(2,1)S(1)}, bf16[2,2,128,384]{3,2,1,0:T(8,128)(2,1)S(1)}, u32[]{:S(2)}, u32[]{:S(2)}) %collective-permute-start.13) | collective-permute-done | bytes 393248 | tf_op jit(solution)/shard_map/ppermute | solution.py:25
  50.8 2.3 %collective-permute-done.12 = bf16[2,2,128,384]{3,2,1,0:T(8,128)(2,1)S(1)} collective-permute-done((bf16[2,2,128,384]{3,2,1,0:T(8,128)(2,1)S(1)}, bf16[2,2,128,384]{3,2,1,0:T(8,128)(2,1)S(1)}, u32[]{:S(2)}, u32[]{:S(2)}) %collective-permute-start.12) | collective-permute-done | bytes 393248 | tf_op jit(solution)/shard_map/ppermute | solution.py:25
  53.0 0.1 maximum_bitcast_fusion.1
  53.1 0.5 maximum_bitcast_fusion
  53.7 0.5 copy.73
  54.2 3.7 %convolution_convert_fusion = bf16[4096,384]{1,0:T(8,128)(2,1)} fusion(bf16[4096,384]{1,0:T(8,128)(2,1)S(1)} %bitcast.344, bf16[384,384]{1,0:T(8,128)(2,1)S(1)} %copy-done), kind=kOutput, calls=%fused_computation | convolution fusion | flops 1209532416 | bytes 6586368 | tf_op jit(solution)/shard_map/dot_general | solution.py:20
  58.0 3.7 %convolution_convert_fusion.1 = bf16[4096,384]{1,0:T(8,128)(2,1)} fusion(bf16[4096,384]{1,0:T(8,128)(2,1)S(1)} %bitcast.345, bf16[384,384]{1,0:T(8,128)(2,1)S(1)} %copy-done.2), kind=kOutput, calls=%fused_computation.1 | convolution fusion | flops 1209532416 | bytes 6586368 | tf_op jit(solution)/shard_map/dot_general | solution.py:20
  61.6 17.2 %shard_map.64 = (f32[2,1,1024]{2,1,0:T(1,128)}, f32[2,1,1024]{2,1,0:T(1,128)}, f32[2,1024,384]{2,1,0:T(8,128)}, bf16[2,1024,384]{2,1,0:T(8,128)(2,1)}) custom-call(bf16[2,1024,384]{2,1,0:T(8,128)(2,1)} %bitcast.357, bf16[2,2048,384]{2,1,0:T(8,128)(2,1)} %bitcast.347, bf16[2,2048,384]{2,1,0:T(8,128)(2,1)} %bitcast.346), custom_call_target="tpu_custom_call" | custom-call | flops 6442450944 | bytes 12582912 | tf_op jit(solution)/shard_map/pallas_call | solution.py:139
  78.8 1.1 fusion.92
  79.9 0.7 copy_bitcast_fusion
  80.7 0.1 collective-permute-start.14
  80.8 7.0 %collective-permute-done.14 = bf16[2,130,384]{2,1,0:T(8,128)(2,1)S(1)} collective-permute-done((bf16[2,130,384]{2,1,0:T(8,128)(2,1)S(1)}, bf16[2,130,384]{2,1,0:T(8,128)(2,1)S(1)}, u32[]{:S(2)}, u32[]{:S(2)}) %collective-permute-start.14) | collective-permute-done | bytes 199712 | tf_op jit(solution)/shard_map/ppermute | solution.py:25
  88.0 1.1 add_convert_fusion.4
  89.2 0.1 collective-permute-start.15
  89.3 7.0 %collective-permute-done.15 = bf16[2,130,384]{2,1,0:T(8,128)(2,1)S(1)} collective-permute-done((bf16[2,130,384]{2,1,0:T(8,128)(2,1)S(1)}, bf16[2,130,384]{2,1,0:T(8,128)(2,1)S(1)}, u32[]{:S(2)}, u32[]{:S(2)}) %collective-permute-start.15) | collective-permute-done | bytes 199712 | tf_op jit(solution)/shard_map/ppermute | solution.py:25
  96.5 0.5 collective-permute-start.18
  97.1 6.9 %collective-permute-done.18 = bf16[2,130,384]{2,1,0:T(8,128)(2,1)S(1)} collective-permute-done((bf16[2,130,384]{2,1,0:T(8,128)(2,1)S(1)}, bf16[2,130,384]{2,1,0:T(8,128)(2,1)S(1)}, u32[]{:S(2)}, u32[]{:S(2)}) %collective-permute-start.18) | collective-permute-done | bytes 199712 | tf_op jit(solution)/shard_map/ppermute | solution.py:25
  104.0 1.3 add_convert_fusion.3
  105.4 0.1 collective-permute-start.16
  105.6 3.3 %collective-permute-start.19 = (bf16[2,130,384]{2,1,0:T(8,128)(2,1)S(1)}, bf16[2,130,384]{2,1,0:T(8,128)(2,1)S(1)}, u32[]{:S(2)}, u32[]{:S(2)}) collective-permute-start(bf16[2,130,384]{2,1,0:T(8,128)(2,1)S(1)} %pad_maximum_fusion.6), channel_id=1, source_target_pairs={{0,28},{4,0},{8,4},{12,8},{16,12},{20,16},{24,20},{28,24},{1,29},{... | collective-permute-start | bytes 599048 | tf_op jit(solution)/shard_map/ppermute | solution.py:25
  108.9 4.6 %collective-permute-done.16 = bf16[2,130,384]{2,1,0:T(8,128)(2,1)S(1)} collective-permute-done((bf16[2,130,384]{2,1,0:T(8,128)(2,1)S(1)}, bf16[2,130,384]{2,1,0:T(8,128)(2,1)S(1)}, u32[]{:S(2)}, u32[]{:S(2)}) %collective-permute-start.16) | collective-permute-done | bytes 199712 | tf_op jit(solution)/shard_map/ppermute | solution.py:25
  113.8 1.3 add_convert_fusion.2
  115.1 0.5 collective-permute-start.17
  115.7 3.1 %collective-permute-start.20 = (bf16[2,130,384]{2,1,0:T(8,128)(2,1)S(1)}, bf16[2,130,384]{2,1,0:T(8,128)(2,1)S(1)}, u32[]{:S(2)}, u32[]{:S(2)}) collective-permute-start(bf16[2,130,384]{2,1,0:T(8,128)(2,1)S(1)} %pad_maximum_fusion.7), channel_id=1, source_target_pairs={{0,28},{4,0},{8,4},{12,8},{16,12},{20,16},{24,20},{28,24},{1,29},{... | collective-permute-start | bytes 599048 | tf_op jit(solution)/shard_map/ppermute | solution.py:25
  118.8 3.6 %collective-permute-done.17 = bf16[2,130,384]{2,1,0:T(8,128)(2,1)S(1)} collective-permute-done((bf16[2,130,384]{2,1,0:T(8,128)(2,1)S(1)}, bf16[2,130,384]{2,1,0:T(8,128)(2,1)S(1)}, u32[]{:S(2)}, u32[]{:S(2)}) %collective-permute-start.17) | collective-permute-done | bytes 199712 | tf_op jit(solution)/shard_map/ppermute | solution.py:25
  122.5 0.7 collective-permute-done.20
  123.2 1.5 multiply_reduce_fusion
  124.8 0.2 multiply_convert_fusion
  125.0 1.6 %collective-permute-start.21 = (bf16[2,1,128,384]{3,2,0,1:T(8,128)(2,1)S(1)}, bf16[2,1,128,384]{3,2,0,1:T(8,128)(2,1)S(1)}, u32[]{:S(2)}, u32[]{:S(2)}) collective-permute-start(bf16[2,1,128,384]{3,2,0,1:T(8,128)(2,1)S(1)} %multiply_convert_fusion), channel_id=1, source_target_pairs={{0,129},{1,130},{2,131},{3,132},{4,133},{5,134},{6,135},{7,136},{8... | collective-permute-start | bytes 589832 | tf_op jit(solution)/shard_map/ppermute | solution.py:202
  126.6 1.3 collective-permute-start.24
  127.9 7.7 %collective-permute-start.25 = (bf16[2,1,128,384]{3,2,0,1:T(8,128)(2,1)S(1)}, bf16[2,1,128,384]{3,2,0,1:T(8,128)(2,1)S(1)}, u32[]{:S(2)}, u32[]{:S(2)}) collective-permute-start(bf16[2,1,128,384]{3,2,0,1:T(8,128)(2,1)S(1)} %multiply_convert_fusion), channel_id=1, source_target_pairs={{1,0},{2,1},{3,2},{4,3},{5,4},{6,5},{7,6},{8,7},{9,8},{10,9},{11,1... | collective-permute-start | bytes 589832 | tf_op jit(solution)/shard_map/ppermute | solution.py:113
  135.6 1.3 collective-permute-start.23
  136.9 1.9 %collective-permute-start.22 = (bf16[2,1,128,384]{3,2,0,1:T(8,128)(2,1)S(1)}, bf16[2,1,128,384]{3,2,0,1:T(8,128)(2,1)S(1)}, u32[]{:S(2)}, u32[]{:S(2)}) collective-permute-start(bf16[2,1,128,384]{3,2,0,1:T(8,128)(2,1)S(1)} %multiply_convert_fusion), channel_id=1, source_target_pairs={{0,1},{1,2},{2,3},{3,4},{4,5},{5,6},{6,7},{7,8},{8,9},{9,10},{10,1... | collective-permute-start | bytes 589832 | tf_op jit(solution)/shard_map/ppermute | solution.py:113
  138.9 9.8 %collective-permute-done.22 = bf16[2,1,128,384]{3,2,0,1:T(8,128)(2,1)S(1)} collective-permute-done((bf16[2,1,128,384]{3,2,0,1:T(8,128)(2,1)S(1)}, bf16[2,1,128,384]{3,2,0,1:T(8,128)(2,1)S(1)}, u32[]{:S(2)}, u32[]{:S(2)}) %collective-permute-start.22) | collective-permute-done | bytes 196640 | tf_op jit(solution)/shard_map/ppermute | solution.py:113
  148.8 0.3 select_maximum_fusion
  149.4 0.1 slice_dynamic-update-slice_fusion.16
  149.5 0.1 slice_dynamic-update-slice_fusion.14
  150.0 0.1 slice_dynamic-update-slice_fusion.6
  150.3 0.2 constant_dynamic-update-slice_fusion.48
  150.7 0.9 slice-done.1
  151.6 3.6 %fusion.18 = bf16[2,1,128,384]{3,2,1,0:T(8,128)(2,1)} fusion(f32[2,1,128,384]{3,2,0,1:T(8,128)S(1)} %get-tuple-element.103, bf16[10368,384,1]{1,0,2:T(8,128)(2,1)S(1)} %bitcast.360, bf16[2,1,128,10368]{3,2,0,1:T(8,128)(2,1)S(1)} %slice_dynamic-update-slice_fusion), kind=kOutput, calls=%fused_computation.21 | convolution fusion | flops 2038628352 | bytes 13860864 | tf_op jit(solution)/shard_map/dot_general | solution.py:221
  (149 shorter events, 2.6 us)
Async XLA Ops:
  0.0 54.2 %copy-start = (bf16[384,384]{1,0:T(8,128)(2,1)S(1)}, bf16[384,384]{1,0:T(8,128)(2,1)}, u32[]{:S(2)}) copy-start(bf16[384,384]{1,0:T(8,128)(2,1)} %param.9) | copy-start | bytes 884740
  3.4 11.4 %collective-permute-start.3 = (bf16[2,128,384]{2,1,0:T(8,128)(2,1)S(1)}, bf16[2,128,384]{2,1,0:T(8,128)(2,1)S(1)}, u32[]{:S(2)}, u32[]{:S(2)}) collective-permute-start(bf16[2,128,384]{2,1,0:T(8,128)(2,1)S(1)} %bitcast.350), channel_id=1, source_target_pairs={{0,4},{4,8},{8,12},{12,16},{16,20},{20,24},{24,28},{28,0},{1,5},{5... | collective-permute-start | bytes 589832 | tf_op jit(solution)/shard_map/ppermute | solution.py:25
  5.4 9.5 %collective-permute-start = (bf16[2,128,384]{2,1,0:T(8,128)(2,1)S(1)}, bf16[2,128,384]{2,1,0:T(8,128)(2,1)S(1)}, u32[]{:S(2)}, u32[]{:S(2)}) collective-permute-start(bf16[2,128,384]{2,1,0:T(8,128)(2,1)S(1)} %bitcast.351), channel_id=1, source_target_pairs={{0,28},{4,0},{8,4},{12,8},{16,12},{20,16},{24,20},{28,24},{1,29},{... | collective-permute-start | bytes 589832 | tf_op jit(solution)/shard_map/ppermute | solution.py:25
  10.4 7.7 %collective-permute-start.8 = (bf16[2,128,384]{2,1,0:T(8,128)(2,1)S(1)}, bf16[2,128,384]{2,1,0:T(8,128)(2,1)S(1)}, u32[]{:S(2)}, u32[]{:S(2)}) collective-permute-start(bf16[2,128,384]{2,1,0:T(8,128)(2,1)S(1)} %fusion.108), channel_id=1, source_target_pairs={{0,1},{1,2},{2,3},{3,0},{4,5},{5,6},{6,7},{7,4},{8,9},{9,10},{10,1... | collective-permute-start | bytes 589832 | tf_op jit(solution)/shard_map/ppermute | solution.py:25
  12.1 7.0 %collective-permute-start.7 = (bf16[2,128,384]{2,1,0:T(8,128)(2,1)S(1)}, bf16[2,128,384]{2,1,0:T(8,128)(2,1)S(1)}, u32[]{:S(2)}, u32[]{:S(2)}) collective-permute-start(bf16[2,128,384]{2,1,0:T(8,128)(2,1)S(1)} %fusion.108), channel_id=1, source_target_pairs={{0,3},{1,0},{2,1},{3,2},{4,7},{5,4},{6,5},{7,6},{8,11},{9,8},{10,9... | collective-permute-start | bytes 589832 | tf_op jit(solution)/shard_map/ppermute | solution.py:25
  14.8 12.5 %collective-permute-start.4 = (bf16[2,128,384]{2,1,0:T(8,128)(2,1)S(1)}, bf16[2,128,384]{2,1,0:T(8,128)(2,1)S(1)}, u32[]{:S(2)}, u32[]{:S(2)}) collective-permute-start(bf16[2,128,384]{2,1,0:T(8,128)(2,1)S(1)} %collective-permute-done.3), channel_id=1, source_target_pairs={{0,4},{4,8},{8,12},{12,16},{16,20},{20,24},{24,28},{28,0},{1,5},{5... | collective-permute-start | bytes 589832 | tf_op jit(solution)/shard_map/ppermute | solution.py:25
  14.9 12.4 %collective-permute-start.1 = (bf16[2,128,384]{2,1,0:T(8,128)(2,1)S(1)}, bf16[2,128,384]{2,1,0:T(8,128)(2,1)S(1)}, u32[]{:S(2)}, u32[]{:S(2)}) collective-permute-start(bf16[2,128,384]{2,1,0:T(8,128)(2,1)S(1)} %collective-permute-done), channel_id=1, source_target_pairs={{0,28},{4,0},{8,4},{12,8},{16,12},{20,16},{24,20},{28,24},{1,29},{... | collective-permute-start | bytes 589832 | tf_op jit(solution)/shard_map/ppermute | solution.py:25
  18.1 6.9 %collective-permute-start.9 = (bf16[2,128,384]{2,1,0:T(8,128)(2,1)S(1)}, bf16[2,128,384]{2,1,0:T(8,128)(2,1)S(1)}, u32[]{:S(2)}, u32[]{:S(2)}) collective-permute-start(bf16[2,128,384]{2,1,0:T(8,128)(2,1)S(1)} %collective-permute-done.8), channel_id=1, source_target_pairs={{0,1},{1,2},{2,3},{3,0},{4,5},{5,6},{6,7},{7,4},{8,9},{9,10},{10,1... | collective-permute-start | bytes 589832 | tf_op jit(solution)/shard_map/ppermute | solution.py:25
  25.2 17.7 %collective-permute-start.10 = (bf16[4,2,128,384]{3,2,1,0:T(8,128)(2,1)S(1)}, bf16[4,2,128,384]{3,2,1,0:T(8,128)(2,1)S(1)}, u32[]{:S(2)}, u32[]{:S(2)}) collective-permute-start(bf16[4,2,128,384]{3,2,1,0:T(8,128)(2,1)S(1)} %get-tuple-element.55), channel_id=1, source_target_pairs={{0,96},{32,0},{64,32},{96,64},{1,97},{33,1},{65,33},{97,65},{2,98}... | collective-permute-start | bytes 2359304 | tf_op jit(solution)/shard_map/ppermute | solution.py:25
  25.8 17.8 %collective-permute-start.11 = (bf16[4,2,128,384]{3,2,1,0:T(8,128)(2,1)S(1)}, bf16[4,2,128,384]{3,2,1,0:T(8,128)(2,1)S(1)}, u32[]{:S(2)}, u32[]{:S(2)}) collective-permute-start(bf16[4,2,128,384]{3,2,1,0:T(8,128)(2,1)S(1)} %get-tuple-element.55), channel_id=1, source_target_pairs={{0,32},{32,64},{64,96},{96,0},{1,33},{33,65},{65,97},{97,1},{2,34}... | collective-permute-start | bytes 2359304 | tf_op jit(solution)/shard_map/ppermute | solution.py:25
  27.3 7.2 %collective-permute-start.5 = (bf16[2,128,384]{2,1,0:T(8,128)(2,1)S(1)}, bf16[2,128,384]{2,1,0:T(8,128)(2,1)S(1)}, u32[]{:S(2)}, u32[]{:S(2)}) collective-permute-start(bf16[2,128,384]{2,1,0:T(8,128)(2,1)S(1)} %collective-permute-done.4), channel_id=1, source_target_pairs={{0,4},{4,8},{8,12},{12,16},{16,20},{20,24},{24,28},{28,0},{1,5},{5... | collective-permute-start | bytes 589832 | tf_op jit(solution)/shard_map/ppermute | solution.py:25
  27.3 7.2 %collective-permute-start.2 = (bf16[2,128,384]{2,1,0:T(8,128)(2,1)S(1)}, bf16[2,128,384]{2,1,0:T(8,128)(2,1)S(1)}, u32[]{:S(2)}, u32[]{:S(2)}) collective-permute-start(bf16[2,128,384]{2,1,0:T(8,128)(2,1)S(1)} %collective-permute-done.1), channel_id=1, source_target_pairs={{0,28},{4,0},{8,4},{12,8},{16,12},{20,16},{24,20},{28,24},{1,29},{... | collective-permute-start | bytes 589832 | tf_op jit(solution)/shard_map/ppermute | solution.py:25
  34.5 6.9 %collective-permute-start.6 = (bf16[2,128,384]{2,1,0:T(8,128)(2,1)S(1)}, bf16[2,128,384]{2,1,0:T(8,128)(2,1)S(1)}, u32[]{:S(2)}, u32[]{:S(2)}) collective-permute-start(bf16[2,128,384]{2,1,0:T(8,128)(2,1)S(1)} %collective-permute-done.5), channel_id=1, source_target_pairs={{0,4},{4,8},{8,12},{12,16},{16,20},{20,24},{24,28},{28,0},{1,5},{5... | collective-permute-start | bytes 589832 | tf_op jit(solution)/shard_map/ppermute | solution.py:25
  42.9 7.9 %collective-permute-start.13 = (bf16[2,2,128,384]{3,2,1,0:T(8,128)(2,1)S(1)}, bf16[2,2,128,384]{3,2,1,0:T(8,128)(2,1)S(1)}, u32[]{:S(2)}, u32[]{:S(2)}) collective-permute-start(bf16[2,2,128,384]{3,2,1,0:T(8,128)(2,1)S(1)} %slice.437), channel_id=1, source_target_pairs={{0,96},{32,0},{64,32},{96,64},{1,97},{33,1},{65,33},{97,65},{2,98}... | collective-permute-start | bytes 1179656 | tf_op jit(solution)/shard_map/ppermute | solution.py:25
  43.7 9.4 %collective-permute-start.12 = (bf16[2,2,128,384]{3,2,1,0:T(8,128)(2,1)S(1)}, bf16[2,2,128,384]{3,2,1,0:T(8,128)(2,1)S(1)}, u32[]{:S(2)}, u32[]{:S(2)}) collective-permute-start(bf16[2,2,128,384]{3,2,1,0:T(8,128)(2,1)S(1)} %slice.436), channel_id=1, source_target_pairs={{0,32},{32,64},{64,96},{96,0},{1,33},{33,65},{65,97},{97,1},{2,34}... | collective-permute-start | bytes 1179656 | tf_op jit(solution)/shard_map/ppermute | solution.py:25
  45.4 8.3 %copy-start.3 = (bf16[2,8,128,384]{3,2,1,0:T(8,128)(2,1)}, bf16[2,8,128,384]{3,2,1,0:T(8,128)(2,1)S(1)}, u32[]{:S(2)}) copy-start(bf16[2,8,128,384]{3,2,1,0:T(8,128)(2,1)S(1)} %bitcast_dynamic-update-slice_fusion.6) | copy-start | bytes 4718596
  54.2 3.7 %copy-start.2 = (bf16[384,384]{1,0:T(8,128)(2,1)S(1)}, bf16[384,384]{1,0:T(8,128)(2,1)}, u32[]{:S(2)}) copy-start(bf16[384,384]{1,0:T(8,128)(2,1)} %param.8) | copy-start | bytes 884740
  80.7 7.1 %collective-permute-start.14 = (bf16[2,130,384]{2,1,0:T(8,128)(2,1)S(1)}, bf16[2,130,384]{2,1,0:T(8,128)(2,1)S(1)}, u32[]{:S(2)}, u32[]{:S(2)}) collective-permute-start(bf16[2,130,384]{2,1,0:T(8,128)(2,1)S(1)} %pad_maximum_fusion.1), channel_id=1, source_target_pairs={{0,4},{4,8},{8,12},{12,16},{16,20},{20,24},{24,28},{28,0},{1,5},{5... | collective-permute-start | bytes 599048 | tf_op jit(solution)/shard_map/ppermute | solution.py:25
  89.1 34.1 %copy-start.1 = (bf16[2,1,128,384]{3,2,1,0:T(8,128)(2,1)S(1)}, bf16[2,1,128,384]{3,2,1,0:T(8,128)(2,1)}, u32[]{:S(2)}) copy-start(bf16[2,1,128,384]{3,2,1,0:T(8,128)(2,1)} %param.6) | copy-start | bytes 589828
  89.1 34.1 %copy-start.4 = (bf16[384,384]{1,0:T(8,128)(2,1)S(1)}, bf16[384,384]{1,0:T(8,128)(2,1)}, u32[]{:S(2)}) copy-start(bf16[384,384]{1,0:T(8,128)(2,1)} %param.10) | copy-start | bytes 884740
  89.2 7.1 %collective-permute-start.15 = (bf16[2,130,384]{2,1,0:T(8,128)(2,1)S(1)}, bf16[2,130,384]{2,1,0:T(8,128)(2,1)S(1)}, u32[]{:S(2)}, u32[]{:S(2)}) collective-permute-start(bf16[2,130,384]{2,1,0:T(8,128)(2,1)S(1)} %pad_maximum_fusion.2), channel_id=1, source_target_pairs={{0,4},{4,8},{8,12},{12,16},{16,20},{20,24},{24,28},{28,0},{1,5},{5... | collective-permute-start | bytes 599048 | tf_op jit(solution)/shard_map/ppermute | solution.py:25
  96.5 7.4 %collective-permute-start.18 = (bf16[2,130,384]{2,1,0:T(8,128)(2,1)S(1)}, bf16[2,130,384]{2,1,0:T(8,128)(2,1)S(1)}, u32[]{:S(2)}, u32[]{:S(2)}) collective-permute-start(bf16[2,130,384]{2,1,0:T(8,128)(2,1)S(1)} %pad_maximum_fusion.5), channel_id=1, source_target_pairs={{0,28},{4,0},{8,4},{12,8},{16,12},{20,16},{24,20},{28,24},{1,29},{... | collective-permute-start | bytes 599048 | tf_op jit(solution)/shard_map/ppermute | solution.py:25
  105.4 8.1 %collective-permute-start.16 = (bf16[2,130,384]{2,1,0:T(8,128)(2,1)S(1)}, bf16[2,130,384]{2,1,0:T(8,128)(2,1)S(1)}, u32[]{:S(2)}, u32[]{:S(2)}) collective-permute-start(bf16[2,130,384]{2,1,0:T(8,128)(2,1)S(1)} %pad_maximum_fusion.3), channel_id=1, source_target_pairs={{0,4},{4,8},{8,12},{12,16},{16,20},{20,24},{24,28},{28,0},{1,5},{5... | collective-permute-start | bytes 599048 | tf_op jit(solution)/shard_map/ppermute | solution.py:25
  105.6 8.0 %collective-permute-start.19 = (bf16[2,130,384]{2,1,0:T(8,128)(2,1)S(1)}, bf16[2,130,384]{2,1,0:T(8,128)(2,1)S(1)}, u32[]{:S(2)}, u32[]{:S(2)}) collective-permute-start(bf16[2,130,384]{2,1,0:T(8,128)(2,1)S(1)} %pad_maximum_fusion.6), channel_id=1, source_target_pairs={{0,28},{4,0},{8,4},{12,8},{16,12},{20,16},{24,20},{28,24},{1,29},{... | collective-permute-start | bytes 599048 | tf_op jit(solution)/shard_map/ppermute | solution.py:25
  115.1 7.3 %collective-permute-start.17 = (bf16[2,130,384]{2,1,0:T(8,128)(2,1)S(1)}, bf16[2,130,384]{2,1,0:T(8,128)(2,1)S(1)}, u32[]{:S(2)}, u32[]{:S(2)}) collective-permute-start(bf16[2,130,384]{2,1,0:T(8,128)(2,1)S(1)} %pad_maximum_fusion.4), channel_id=1, source_target_pairs={{0,4},{4,8},{8,12},{12,16},{16,20},{20,24},{24,28},{28,0},{1,5},{5... | collective-permute-start | bytes 599048 | tf_op jit(solution)/shard_map/ppermute | solution.py:25
  115.7 7.5 %collective-permute-start.20 = (bf16[2,130,384]{2,1,0:T(8,128)(2,1)S(1)}, bf16[2,130,384]{2,1,0:T(8,128)(2,1)S(1)}, u32[]{:S(2)}, u32[]{:S(2)}) collective-permute-start(bf16[2,130,384]{2,1,0:T(8,128)(2,1)S(1)} %pad_maximum_fusion.7), channel_id=1, source_target_pairs={{0,28},{4,0},{8,4},{12,8},{16,12},{20,16},{24,20},{28,24},{1,29},{... | collective-permute-start | bytes 599048 | tf_op jit(solution)/shard_map/ppermute | solution.py:25
  124.8 25.9 %slice-start = ((s8[7962624]{0:T(1024)(128)(4,1)}), s8[4194304]{0:T(1024)(128)(4,1)S(1)}, s32[]{:S(2)}) async-start(s8[7962624]{0:T(1024)(128)(4,1)} %bitcast.358), calls=%async_computation | async-start | bytes 8388608
  125.0 13.9 %collective-permute-start.21 = (bf16[2,1,128,384]{3,2,0,1:T(8,128)(2,1)S(1)}, bf16[2,1,128,384]{3,2,0,1:T(8,128)(2,1)S(1)}, u32[]{:S(2)}, u32[]{:S(2)}) collective-permute-start(bf16[2,1,128,384]{3,2,0,1:T(8,128)(2,1)S(1)} %multiply_convert_fusion), channel_id=1, source_target_pairs={{0,129},{1,130},{2,131},{3,132},{4,133},{5,134},{6,135},{7,136},{8... | collective-permute-start | bytes 589832 | tf_op jit(solution)/shard_map/ppermute | solution.py:202
  126.6 12.3 %collective-permute-start.24 = (bf16[2,1,128,384]{3,2,0,1:T(8,128)(2,1)S(1)}, bf16[2,1,128,384]{3,2,0,1:T(8,128)(2,1)S(1)}, u32[]{:S(2)}, u32[]{:S(2)}) collective-permute-start(bf16[2,1,128,384]{3,2,0,1:T(8,128)(2,1)S(1)} %multiply_convert_fusion), channel_id=1, source_target_pairs={{1,128},{2,129},{3,130},{4,131},{5,132},{6,133},{7,134},{8,135},{9... | collective-permute-start | bytes 589832 | tf_op jit(solution)/shard_map/ppermute | solution.py:203
  127.9 20.9 %collective-permute-start.25 = (bf16[2,1,128,384]{3,2,0,1:T(8,128)(2,1)S(1)}, bf16[2,1,128,384]{3,2,0,1:T(8,128)(2,1)S(1)}, u32[]{:S(2)}, u32[]{:S(2)}) collective-permute-start(bf16[2,1,128,384]{3,2,0,1:T(8,128)(2,1)S(1)} %multiply_convert_fusion), channel_id=1, source_target_pairs={{1,0},{2,1},{3,2},{4,3},{5,4},{6,5},{7,6},{8,7},{9,8},{10,9},{11,1... | collective-permute-start | bytes 589832 | tf_op jit(solution)/shard_map/ppermute | solution.py:113
  135.6 13.2 %collective-permute-start.23 = (bf16[2,1,128,384]{3,2,0,1:T(8,128)(2,1)S(1)}, bf16[2,1,128,384]{3,2,0,1:T(8,128)(2,1)S(1)}, u32[]{:S(2)}, u32[]{:S(2)}) collective-permute-start(bf16[2,1,128,384]{3,2,0,1:T(8,128)(2,1)S(1)} %multiply_convert_fusion), channel_id=1, source_target_pairs={{0,128},{1,129},{2,130},{3,131},{4,132},{5,133},{6,134},{7,135},{8... | collective-permute-start | bytes 589832 | tf_op jit(solution)/shard_map/ppermute | solution.py:201
  136.9 11.8 %collective-permute-start.22 = (bf16[2,1,128,384]{3,2,0,1:T(8,128)(2,1)S(1)}, bf16[2,1,128,384]{3,2,0,1:T(8,128)(2,1)S(1)}, u32[]{:S(2)}, u32[]{:S(2)}) collective-permute-start(bf16[2,1,128,384]{3,2,0,1:T(8,128)(2,1)S(1)} %multiply_convert_fusion), channel_id=1, source_target_pairs={{0,1},{1,2},{2,3},{3,4},{4,5},{5,6},{6,7},{7,8},{8,9},{9,10},{10,1... | collective-permute-start | bytes 589832 | tf_op jit(solution)/shard_map/ppermute | solution.py:113
  149.5 2.1 %slice-start.1 = ((s8[7962624]{0:T(1024)(128)(4,1)}), s8[3768320]{0:T(1024)(128)(4,1)S(1)}, s32[]{:S(2)}) async-start(s8[7962624]{0:T(1024)(128)(4,1)} %bitcast.358), calls=%async_computation.1 | async-start | bytes 7536640

commit v2 on v1

--- a/solution.py
+++ b/solution.py
@@ -113,9 +113,21 @@
     return lax.ppermute(block, ROW_AXES, route)
 
 
-def attention_kernel(scale, query_ref, key_ref, value_ref, high_ref, total_ref, summed_ref, short_ref):
+def attention_kernel(
+    scale, query_ref, token_ref, key_w_ref, value_w_ref,
+    high_ref, total_ref, summed_ref, short_ref, key_scr, value_scr,
+):
+    width = key_scr.shape[-1]
+
+    @pl.when(pl.program_id(1) == 0)
+    def _():
+        tokens = token_ref[...].reshape(-1, width)
+        key_scr[...] = jnp.dot(tokens, key_w_ref[...], preferred_element_type=jnp.float32).astype(jnp.bfloat16)
+        value_scr[...] = jnp.dot(tokens, value_w_ref[...], preferred_element_type=jnp.float32).astype(jnp.bfloat16)
+
+    query = query_ref[...].reshape(-1, width)
     scores = lax.dot_general(
-        query_ref[0], key_ref[0], (((1,), (1,)), ((), ())), preferred_element_type=jnp.float32
+        query, key_scr[...], (((1,), (1,)), ((), ())), preferred_element_type=jnp.float32
     ) * scale
     high = jnp.max(scores, axis=-1, keepdims=True)
     expo = jnp.exp(scores - high)
@@ -123,26 +135,31 @@
     rows = high.shape[0]
     high_ref[0] = jnp.transpose(jnp.broadcast_to(high, (rows, 128)))[0:1, :]
     total_ref[0] = jnp.transpose(jnp.broadcast_to(total, (rows, 128)))[0:1, :]
-    summed = jnp.dot(expo.astype(jnp.bfloat16), value_ref[0], preferred_element_type=jnp.float32)
+    summed = jnp.dot(expo.astype(jnp.bfloat16), value_scr[...], preferred_element_type=jnp.float32)
     summed_ref[0] = summed
     short_ref[0] = summed.astype(jnp.bfloat16)
 
 
-def attention(query_rows, key_rows, value_rows):
-    frames, queries, width = query_rows.shape
-    keys = key_rows.shape[1]
-    tile = 256
+def attention(query_blocks, token_blocks, key_weight, value_weight):
+    query_count, frames, rows, width = query_blocks.shape
+    key_count = token_blocks.shape[0]
+    per_tile = 2
+    tile = per_tile * rows
+    queries = query_count * rows
     scale = 1.0 / math.sqrt(width)
     stat = jax.ShapeDtypeStruct((frames, 1, queries), jnp.float32)
     stat_spec = pl.BlockSpec((1, 1, tile), lambda f, i: (f, 0, i))
     row_spec = pl.BlockSpec((1, tile, width), lambda f, i: (f, i, 0))
+    weight_spec = pl.BlockSpec((width, width), lambda f, i: (0, 0))
+    keys = key_count * rows
     return pl.pallas_call(
         functools.partial(attention_kernel, scale),
-        grid=(frames, queries // tile),
+        grid=(frames, query_count // per_tile),
         in_specs=[
-            row_spec,
-            pl.BlockSpec((1, keys, width), lambda f, i: (f, 0, 0)),
-            pl.BlockSpec((1, keys, width), lambda f, i: (f, 0, 0)),
+            pl.BlockSpec((per_tile, None, rows, width), lambda f, i: (i, f, 0, 0)),
+            pl.BlockSpec((key_count, None, rows, width), lambda f, i: (0, f, 0, 0)),
+            weight_spec,
+            weight_spec,
         ],
         out_specs=[stat_spec, stat_spec, row_spec, row_spec],
         out_shape=[
@@ -151,12 +168,16 @@
             jax.ShapeDtypeStruct((frames, queries, width), jnp.float32),
             jax.ShapeDtypeStruct((frames, queries, width), jnp.bfloat16),
         ],
+        scratch_shapes=[
+            pltpu.VMEM((keys, width), jnp.bfloat16),
+            pltpu.VMEM((keys, width), jnp.bfloat16),
+        ],
         cost_estimate=pl.CostEstimate(
-            flops=4 * frames * queries * keys * width,
+            flops=4 * frames * queries * keys * width + 4 * frames * keys * width * width,
             transcendentals=frames * queries * keys,
-            bytes_accessed=2 * frames * (queries + 2 * keys) * width + 6 * frames * queries * width,
+            bytes_accessed=2 * frames * (queries + keys) * width + 6 * frames * queries * width,
         ),
-    )(query_rows, key_rows, value_rows)
+    )(query_blocks, token_blocks, key_weight, value_weight)
 
 
 def per_device(features, query_weight, key_weight, value_weight, out_weight, conv_weight):
@@ -171,12 +192,9 @@
     query_rel = ring_gather(query, "z")
     inner = jnp.stack(ring_gather(normed.reshape(frames, count, width), "y"))
     outer = jnp.stack(ring_gather(inner, "x", halve=True))
-    keys_in = jnp.transpose(outer, (2, 0, 1, 3, 4)).reshape(-1, width)
-    key_rows = project(keys_in, key_weight).reshape(frames, -1, width)
-    value_rows = project(keys_in, value_weight).reshape(frames, -1, width)
-    query_rows = jnp.stack(query_rel, axis=1).reshape(frames, -1, width)
-
-    highest, total, summed, short = attention(query_rows, key_rows, value_rows)
+    token_blocks = outer.reshape(-1, *outer.shape[2:])
+    query_blocks = jnp.stack(query_rel)
+    highest, total, summed, short = attention(query_blocks, token_blocks, key_weight, value_weight)
     highest, total = highest[:, 0], total[:, 0]
 
     blocks = len(query_rel)

time: 156 us -> 152 us (0.974)
  matrix products: 13.8 us -> 6.39 us
  Pallas kernels: 17.2 us -> 20.7 us
    dot_general x3 -> x1, matrix products: 8.65 us -> 1.24 us  [project(): jnp.dot(flat_rows, weight, preferred_element_type=jnp.float32)]
    pallas_call x1, Pallas kernels: 17.2 us -> 20.7 us  [attention(): pl.pallas_call(functools.partial(attention_kernel, scale), grid=(frames,...]
    another operation x2 -> x3, other arithmetic: 0.26 us -> 2.13 us  [per_device(): outer = jnp.stack(ring_gather(inner, 'x', halve=True))]
where the time goes in v2:
time: 152 us; the launch traced here: 151 us
  waiting for transfers between devices  65.3 us (43%)
  starting transfers between devices  42 us (28%)
  Pallas kernels  20.7 us (14%)
  other arithmetic  11.6 us (8%)
  matrix products  6.39 us (4%)
  local copies, waits for them, and re-layouts  4.76 us (3%)
    ppermute x21, waiting for transfers between devices, ring_shift(): return lax.ppermute(block, axis, [(i, (i + step) % n) for i in range(n)])  55.7 us
    ppermute x21, starting transfers between devices, ring_shift(): return lax.ppermute(block, axis, [(i, (i + step) % n) for i in range(n)])  28.4 us
    pallas_call x1, Pallas kernels, attention(): pl.pallas_call(functools.partial(attention_kernel, scale), grid=(frames,...  20.7 us
    ppermute x2, starting transfers between devices, row_shift(): return lax.ppermute(block, ROW_AXES, route)  9.75 us
    ppermute x2, waiting for transfers between devices, row_shift(): return lax.ppermute(block, ROW_AXES, route)  9.54 us
    convert_element_type x3, other arithmetic, pack(): return jnp.concatenate([summed.astype(jnp.bfloat16), stats], axis=1)  3.81 us
    dot_general x1, matrix products, per_device(): jnp.dot(columns, conv_weight.reshape(27 * width, width), preferred_elemen...  3.61 us
  transfers between devices with their start and end apart: 26, of which 14 were waited for; matrix products, arithmetic and copies ran while one was open for 2% of the time, Pallas kernels for 0%

profile of v2, /device:TPU:2, one launch (start us, length us, event | category | flops | bytes accessed | tf_op | source)
XLA Modules:
  0.0 151.4 jit_solution(2491000749454758101)
XLA Ops:
  0.0 1.1 fusion.21
  1.1 1.0 fusion.22
  2.1 1.2 convolution_convert_fusion
  3.4 2.0 %collective-permute-start.3 = (bf16[2,128,384]{2,1,0:T(8,128)(2,1)S(1)}, bf16[2,128,384]{2,1,0:T(8,128)(2,1)S(1)}, u32[]{:S(2)}, u32[]{:S(2)}) collective-permute-start(bf16[2,128,384]{2,1,0:T(8,128)(2,1)S(1)} %bitcast.324), channel_id=1, source_target_pairs={{0,4},{4,8},{8,12},{12,16},{16,20},{20,24},{24,28},{28,0},{1,5},{5... | collective-permute-start | bytes 589832 | tf_op jit(solution)/shard_map/ppermute | solution.py:25
  5.4 4.0 %collective-permute-start = (bf16[2,128,384]{2,1,0:T(8,128)(2,1)S(1)}, bf16[2,128,384]{2,1,0:T(8,128)(2,1)S(1)}, u32[]{:S(2)}, u32[]{:S(2)}) collective-permute-start(bf16[2,128,384]{2,1,0:T(8,128)(2,1)S(1)} %bitcast.325), channel_id=1, source_target_pairs={{0,28},{4,0},{8,4},{12,8},{16,12},{20,16},{24,20},{28,24},{1,29},{... | collective-permute-start | bytes 589832 | tf_op jit(solution)/shard_map/ppermute | solution.py:25
  9.4 1.0 fusion.104
  10.4 1.7 %collective-permute-start.8 = (bf16[2,128,384]{2,1,0:T(8,128)(2,1)S(1)}, bf16[2,128,384]{2,1,0:T(8,128)(2,1)S(1)}, u32[]{:S(2)}, u32[]{:S(2)}) collective-permute-start(bf16[2,128,384]{2,1,0:T(8,128)(2,1)S(1)} %fusion.104), channel_id=1, source_target_pairs={{0,1},{1,2},{2,3},{3,0},{4,5},{5,6},{6,7},{7,4},{8,9},{9,10},{10,1... | collective-permute-start | bytes 589832 | tf_op jit(solution)/shard_map/ppermute | solution.py:25
  12.1 1.7 %collective-permute-start.7 = (bf16[2,128,384]{2,1,0:T(8,128)(2,1)S(1)}, bf16[2,128,384]{2,1,0:T(8,128)(2,1)S(1)}, u32[]{:S(2)}, u32[]{:S(2)}) collective-permute-start(bf16[2,128,384]{2,1,0:T(8,128)(2,1)S(1)} %fusion.104), channel_id=1, source_target_pairs={{0,3},{1,0},{2,1},{3,2},{4,7},{5,4},{6,5},{7,6},{8,11},{9,8},{10,9... | collective-permute-start | bytes 589832 | tf_op jit(solution)/shard_map/ppermute | solution.py:25
  13.8 1.0 fusion.103
  14.8 0.1 collective-permute-start.4
  14.9 3.2 %collective-permute-start.1 = (bf16[2,128,384]{2,1,0:T(8,128)(2,1)S(1)}, bf16[2,128,384]{2,1,0:T(8,128)(2,1)S(1)}, u32[]{:S(2)}, u32[]{:S(2)}) collective-permute-start(bf16[2,128,384]{2,1,0:T(8,128)(2,1)S(1)} %collective-permute-done), channel_id=1, source_target_pairs={{0,28},{4,0},{8,4},{12,8},{16,12},{20,16},{24,20},{28,24},{1,29},{... | collective-permute-start | bytes 589832 | tf_op jit(solution)/shard_map/ppermute | solution.py:25
  18.1 0.9 collective-permute-start.9
  19.1 5.9 %collective-permute-done.9 = bf16[2,128,384]{2,1,0:T(8,128)(2,1)S(1)} collective-permute-done((bf16[2,128,384]{2,1,0:T(8,128)(2,1)S(1)}, bf16[2,128,384]{2,1,0:T(8,128)(2,1)S(1)}, u32[]{:S(2)}, u32[]{:S(2)}) %collective-permute-start.9) | collective-permute-done | bytes 196640 | tf_op jit(solution)/shard_map/ppermute | solution.py:25
  25.0 0.2 fusion.77
  25.2 0.6 collective-permute-start.10
  25.8 1.5 collective-permute-start.11
  27.3 3.2 %collective-permute-start.2 = (bf16[2,128,384]{2,1,0:T(8,128)(2,1)S(1)}, bf16[2,128,384]{2,1,0:T(8,128)(2,1)S(1)}, u32[]{:S(2)}, u32[]{:S(2)}) collective-permute-start(bf16[2,128,384]{2,1,0:T(8,128)(2,1)S(1)} %collective-permute-done.1), channel_id=1, source_target_pairs={{0,28},{4,0},{8,4},{12,8},{16,12},{20,16},{24,20},{28,24},{1,29},{... | collective-permute-start | bytes 589832 | tf_op jit(solution)/shard_map/ppermute | solution.py:25
  30.6 3.9 %collective-permute-done.5 = bf16[2,128,384]{2,1,0:T(8,128)(2,1)S(1)} collective-permute-done((bf16[2,128,384]{2,1,0:T(8,128)(2,1)S(1)}, bf16[2,128,384]{2,1,0:T(8,128)(2,1)S(1)}, u32[]{:S(2)}, u32[]{:S(2)}) %collective-permute-start.5) | collective-permute-done | bytes 196640 | tf_op jit(solution)/shard_map/ppermute | solution.py:25
  34.5 6.8 %collective-permute-done.6 = bf16[2,128,384]{2,1,0:T(8,128)(2,1)S(1)} collective-permute-done((bf16[2,128,384]{2,1,0:T(8,128)(2,1)S(1)}, bf16[2,128,384]{2,1,0:T(8,128)(2,1)S(1)}, u32[]{:S(2)}, u32[]{:S(2)}) %collective-permute-start.6) | collective-permute-done | bytes 196640 | tf_op jit(solution)/shard_map/ppermute | solution.py:25
  41.4 1.4 collective-permute-done.10
  42.9 0.4 collective-permute-start.13
  43.3 0.3 collective-permute-done.11
  43.7 1.7 %collective-permute-start.12 = (bf16[2,2,128,384]{3,2,1,0:T(8,128)(2,1)S(1)}, bf16[2,2,128,384]{3,2,1,0:T(8,128)(2,1)S(1)}, u32[]{:S(2)}, u32[]{:S(2)}) collective-permute-start(bf16[2,2,128,384]{3,2,1,0:T(8,128)(2,1)S(1)} %slice.436), channel_id=1, source_target_pairs={{0,32},{32,64},{64,96},{96,0},{1,33},{33,65},{65,97},{97,1},{2,34}... | collective-permute-start | bytes 1179656 | tf_op jit(solution)/shard_map/ppermute | solution.py:25
  45.4 5.4 %collective-permute-done.13 = bf16[2,2,128,384]{3,2,1,0:T(8,128)(2,1)S(1)} collective-permute-done((bf16[2,2,128,384]{3,2,1,0:T(8,128)(2,1)S(1)}, bf16[2,2,128,384]{3,2,1,0:T(8,128)(2,1)S(1)}, u32[]{:S(2)}, u32[]{:S(2)}) %collective-permute-start.13) | collective-permute-done | bytes 393248 | tf_op jit(solution)/shard_map/ppermute | solution.py:25
  50.8 2.3 %collective-permute-done.12 = bf16[2,2,128,384]{3,2,1,0:T(8,128)(2,1)S(1)} collective-permute-done((bf16[2,2,128,384]{3,2,1,0:T(8,128)(2,1)S(1)}, bf16[2,2,128,384]{3,2,1,0:T(8,128)(2,1)S(1)}, u32[]{:S(2)}, u32[]{:S(2)}) %collective-permute-start.12) | collective-permute-done | bytes 393248 | tf_op jit(solution)/shard_map/ppermute | solution.py:25
  53.0 0.1 maximum_bitcast_fusion
  53.1 1.9 %pad_maximum_fusion = bf16[4,4,2,128,384]{4,3,2,1,0:T(8,128)(2,1)} fusion(bf16[1,4,2,128,384]{4,3,2,1,0:T(8,128)(2,1)S(1)} %bitcast.323, bf16[1,4,2,128,384]{4,3,2,1,0:T(8,128)(2,1)S(1)} %maximum_bitcast_fusion, bf16[1,4,2,128,384]{4,3,2,1,0:T(8,128)(2,1)S(1)} %bitcast.322, bf16[1,4,2,128,384]{4,3,2,1,0:T(8,128)(2,1)S(1)} %get-tuple-element.54), kind=kLoop, calls=%fused_computation.4 | loop fusion | flops 4718592 | bytes 6291456 | tf_op jit(solution)/shard_map/stack | solution.py:194
  55.0 20.7 %shard_map.64 = (f32[2,1,1024]{2,1,0:T(1,128)}, f32[2,1,1024]{2,1,0:T(1,128)}, f32[2,1024,384]{2,1,0:T(8,128)}, bf16[2,1024,384]{2,1,0:T(8,128)(2,1)}) custom-call(bf16[8,2,128,384]{3,2,1,0:T(8,128)(2,1)} %copy-done.2, bf16[16,2,128,384]{3,2,1,0:T(8,128)(2,1)} %bitcast.321, bf16[384,384]{1,0:T(8,128)(2,1)} %key_w_ref.1, bf16[384,384]{1,0:T(8,128)(2,1)} %value_w_ref.1), custom_call_target="tpu_custom_call" | custom-call | flops 8858370048 | bytes 9437184 | tf_op jit(solution)/shard_map/pallas_call | solution.py:155
  75.7 1.1 fusion.92
  76.8 0.7 copy_bitcast_fusion
  77.6 0.1 collective-permute-start.14
  77.7 7.0 %collective-permute-done.14 = bf16[2,130,384]{2,1,0:T(8,128)(2,1)S(1)} collective-permute-done((bf16[2,130,384]{2,1,0:T(8,128)(2,1)S(1)}, bf16[2,130,384]{2,1,0:T(8,128)(2,1)S(1)}, u32[]{:S(2)}, u32[]{:S(2)}) %collective-permute-start.14) | collective-permute-done | bytes 199712 | tf_op jit(solution)/shard_map/ppermute | solution.py:25
  84.9 1.1 add_convert_fusion.4
  86.1 0.1 collective-permute-start.15
  86.2 7.0 %collective-permute-done.15 = bf16[2,130,384]{2,1,0:T(8,128)(2,1)S(1)} collective-permute-done((bf16[2,130,384]{2,1,0:T(8,128)(2,1)S(1)}, bf16[2,130,384]{2,1,0:T(8,128)(2,1)S(1)}, u32[]{:S(2)}, u32[]{:S(2)}) %collective-permute-start.15) | collective-permute-done | bytes 199712 | tf_op jit(solution)/shard_map/ppermute | solution.py:25
  93.4 0.5 collective-permute-start.18
  94.0 6.8 %collective-permute-done.18 = bf16[2,130,384]{2,1,0:T(8,128)(2,1)S(1)} collective-permute-done((bf16[2,130,384]{2,1,0:T(8,128)(2,1)S(1)}, bf16[2,130,384]{2,1,0:T(8,128)(2,1)S(1)}, u32[]{:S(2)}, u32[]{:S(2)}) %collective-permute-start.18) | collective-permute-done | bytes 199712 | tf_op jit(solution)/shard_map/ppermute | solution.py:25
  100.9 1.3 add_convert_fusion.3
  102.3 0.1 collective-permute-start.16
  102.5 3.3 %collective-permute-start.19 = (bf16[2,130,384]{2,1,0:T(8,128)(2,1)S(1)}, bf16[2,130,384]{2,1,0:T(8,128)(2,1)S(1)}, u32[]{:S(2)}, u32[]{:S(2)}) collective-permute-start(bf16[2,130,384]{2,1,0:T(8,128)(2,1)S(1)} %pad_maximum_fusion.7), channel_id=1, source_target_pairs={{0,28},{4,0},{8,4},{12,8},{16,12},{20,16},{24,20},{28,24},{1,29},{... | collective-permute-start | bytes 599048 | tf_op jit(solution)/shard_map/ppermute | solution.py:25
  105.8 4.4 %collective-permute-done.16 = bf16[2,130,384]{2,1,0:T(8,128)(2,1)S(1)} collective-permute-done((bf16[2,130,384]{2,1,0:T(8,128)(2,1)S(1)}, bf16[2,130,384]{2,1,0:T(8,128)(2,1)S(1)}, u32[]{:S(2)}, u32[]{:S(2)}) %collective-permute-start.16) | collective-permute-done | bytes 199712 | tf_op jit(solution)/shard_map/ppermute | solution.py:25
  110.4 1.3 add_convert_fusion.2
  111.8 0.7 collective-permute-start.17
  112.6 2.7 %collective-permute-start.20 = (bf16[2,130,384]{2,1,0:T(8,128)(2,1)S(1)}, bf16[2,130,384]{2,1,0:T(8,128)(2,1)S(1)}, u32[]{:S(2)}, u32[]{:S(2)}) collective-permute-start(bf16[2,130,384]{2,1,0:T(8,128)(2,1)S(1)} %pad_maximum_fusion.8), channel_id=1, source_target_pairs={{0,28},{4,0},{8,4},{12,8},{16,12},{20,16},{24,20},{28,24},{1,29},{... | collective-permute-start | bytes 599048 | tf_op jit(solution)/shard_map/ppermute | solution.py:25
  115.3 3.6 %collective-permute-done.17 = bf16[2,130,384]{2,1,0:T(8,128)(2,1)S(1)} collective-permute-done((bf16[2,130,384]{2,1,0:T(8,128)(2,1)S(1)}, bf16[2,130,384]{2,1,0:T(8,128)(2,1)S(1)}, u32[]{:S(2)}, u32[]{:S(2)}) %collective-permute-start.17) | collective-permute-done | bytes 199712 | tf_op jit(solution)/shard_map/ppermute | solution.py:25
  118.9 0.8 collective-permute-done.20
  119.8 1.5 %multiply_reduce_fusion = (f32[2,128]{1,0:T(2,128)S(1)}, f32[2,1,128,384]{3,2,0,1:T(8,128)S(1)}) fusion(bf16[384,384]{1,0:T(8,128)(2,1)S(1)} %copy-done, f32[2,1024,384]{2,1,0:T(8,128)} %get-tuple-element.12, bf16[2,130,384]{2,1,0:T(8,128)(2,1)S(1)} %collective-permute-done.20, bf16[2,130,384]{2,1,0:T(8,128)(2,1)S(1)} %collective-permute-done.17, ...), kind=kOutput, calls=%fused_computation.27 | convolution fusion | flops 77070080 | bytes 1677312 | tf_op jit(solution)/shard_map/dot_general | solution.py:210
  121.4 0.2 multiply_convert_fusion
  121.6 1.3 collective-permute-start.21
  122.9 1.3 collective-permute-start.24
  124.2 7.6 %collective-permute-start.25 = (bf16[2,1,128,384]{3,2,0,1:T(8,128)(2,1)S(1)}, bf16[2,1,128,384]{3,2,0,1:T(8,128)(2,1)S(1)}, u32[]{:S(2)}, u32[]{:S(2)}) collective-permute-start(bf16[2,1,128,384]{3,2,0,1:T(8,128)(2,1)S(1)} %multiply_convert_fusion), channel_id=1, source_target_pairs={{1,0},{2,1},{3,2},{4,3},{5,4},{6,5},{7,6},{8,7},{9,8},{10,9},{11,1... | collective-permute-start | bytes 589832 | tf_op jit(solution)/shard_map/ppermute | solution.py:113
  131.8 1.3 collective-permute-start.23
  133.1 2.1 %collective-permute-start.22 = (bf16[2,1,128,384]{3,2,0,1:T(8,128)(2,1)S(1)}, bf16[2,1,128,384]{3,2,0,1:T(8,128)(2,1)S(1)}, u32[]{:S(2)}, u32[]{:S(2)}) collective-permute-start(bf16[2,1,128,384]{3,2,0,1:T(8,128)(2,1)S(1)} %multiply_convert_fusion), channel_id=1, source_target_pairs={{0,1},{1,2},{2,3},{3,4},{4,5},{5,6},{6,7},{7,8},{8,9},{9,10},{10,1... | collective-permute-start | bytes 589832 | tf_op jit(solution)/shard_map/ppermute | solution.py:113
  135.4 9.5 %collective-permute-done.22 = bf16[2,1,128,384]{3,2,0,1:T(8,128)(2,1)S(1)} collective-permute-done((bf16[2,1,128,384]{3,2,0,1:T(8,128)(2,1)S(1)}, bf16[2,1,128,384]{3,2,0,1:T(8,128)(2,1)S(1)}, u32[]{:S(2)}, u32[]{:S(2)}) %collective-permute-start.22) | collective-permute-done | bytes 196640 | tf_op jit(solution)/shard_map/ppermute | solution.py:113
  145.0 0.3 select_maximum_fusion
  145.4 0.1 slice_dynamic-update-slice_fusion.18
  145.6 0.1 slice_dynamic-update-slice_fusion.16
  145.7 0.1 slice_dynamic-update-slice_fusion.14
  145.9 0.1 slice_dynamic-update-slice_fusion.11
  146.0 0.1 slice_dynamic-update-slice_fusion.9
  146.2 0.1 slice_dynamic-update-slice_fusion.6
  146.4 0.2 constant_dynamic-update-slice_fusion.48
  146.9 0.9 slice-done.1
  147.8 3.6 %fusion.18 = bf16[2,1,128,384]{3,2,1,0:T(8,128)(2,1)} fusion(f32[2,1,128,384]{3,2,0,1:T(8,128)S(1)} %get-tuple-element.103, bf16[10368,384,1]{1,0,2:T(8,128)(2,1)S(1)} %bitcast.333, bf16[2,1,128,10368]{3,2,0,1:T(8,128)(2,1)S(1)} %slice_dynamic-update-slice_fusion), kind=kOutput, calls=%fused_computation.19 | convolution fusion | flops 2038628352 | bytes 13860864 | tf_op jit(solution)/shard_map/dot_general | solution.py:239
  (142 shorter events, 2.4 us)
Async XLA Ops:
  0.0 119.8 %copy-start = (bf16[384,384]{1,0:T(8,128)(2,1)S(1)}, bf16[384,384]{1,0:T(8,128)(2,1)}, u32[]{:S(2)}) copy-start(bf16[384,384]{1,0:T(8,128)(2,1)} %param.10) | copy-start | bytes 884740
  3.4 11.4 %collective-permute-start.3 = (bf16[2,128,384]{2,1,0:T(8,128)(2,1)S(1)}, bf16[2,128,384]{2,1,0:T(8,128)(2,1)S(1)}, u32[]{:S(2)}, u32[]{:S(2)}) collective-permute-start(bf16[2,128,384]{2,1,0:T(8,128)(2,1)S(1)} %bitcast.324), channel_id=1, source_target_pairs={{0,4},{4,8},{8,12},{12,16},{16,20},{20,24},{24,28},{28,0},{1,5},{5... | collective-permute-start | bytes 589832 | tf_op jit(solution)/shard_map/ppermute | solution.py:25
  5.4 9.5 %collective-permute-start = (bf16[2,128,384]{2,1,0:T(8,128)(2,1)S(1)}, bf16[2,128,384]{2,1,0:T(8,128)(2,1)S(1)}, u32[]{:S(2)}, u32[]{:S(2)}) collective-permute-start(bf16[2,128,384]{2,1,0:T(8,128)(2,1)S(1)} %bitcast.325), channel_id=1, source_target_pairs={{0,28},{4,0},{8,4},{12,8},{16,12},{20,16},{24,20},{28,24},{1,29},{... | collective-permute-start | bytes 589832 | tf_op jit(solution)/shard_map/ppermute | solution.py:25
  10.4 7.7 %collective-permute-start.8 = (bf16[2,128,384]{2,1,0:T(8,128)(2,1)S(1)}, bf16[2,128,384]{2,1,0:T(8,128)(2,1)S(1)}, u32[]{:S(2)}, u32[]{:S(2)}) collective-permute-start(bf16[2,128,384]{2,1,0:T(8,128)(2,1)S(1)} %fusion.104), channel_id=1, source_target_pairs={{0,1},{1,2},{2,3},{3,0},{4,5},{5,6},{6,7},{7,4},{8,9},{9,10},{10,1... | collective-permute-start | bytes 589832 | tf_op jit(solution)/shard_map/ppermute | solution.py:25
  12.1 7.0 %collective-permute-start.7 = (bf16[2,128,384]{2,1,0:T(8,128)(2,1)S(1)}, bf16[2,128,384]{2,1,0:T(8,128)(2,1)S(1)}, u32[]{:S(2)}, u32[]{:S(2)}) collective-permute-start(bf16[2,128,384]{2,1,0:T(8,128)(2,1)S(1)} %fusion.104), channel_id=1, source_target_pairs={{0,3},{1,0},{2,1},{3,2},{4,7},{5,4},{6,5},{7,6},{8,11},{9,8},{10,9... | collective-permute-start | bytes 589832 | tf_op jit(solution)/shard_map/ppermute | solution.py:25
  14.8 12.5 %collective-permute-start.4 = (bf16[2,128,384]{2,1,0:T(8,128)(2,1)S(1)}, bf16[2,128,384]{2,1,0:T(8,128)(2,1)S(1)}, u32[]{:S(2)}, u32[]{:S(2)}) collective-permute-start(bf16[2,128,384]{2,1,0:T(8,128)(2,1)S(1)} %collective-permute-done.3), channel_id=1, source_target_pairs={{0,4},{4,8},{8,12},{12,16},{16,20},{20,24},{24,28},{28,0},{1,5},{5... | collective-permute-start | bytes 589832 | tf_op jit(solution)/shard_map/ppermute | solution.py:25
  14.9 12.4 %collective-permute-start.1 = (bf16[2,128,384]{2,1,0:T(8,128)(2,1)S(1)}, bf16[2,128,384]{2,1,0:T(8,128)(2,1)S(1)}, u32[]{:S(2)}, u32[]{:S(2)}) collective-permute-start(bf16[2,128,384]{2,1,0:T(8,128)(2,1)S(1)} %collective-permute-done), channel_id=1, source_target_pairs={{0,28},{4,0},{8,4},{12,8},{16,12},{20,16},{24,20},{28,24},{1,29},{... | collective-permute-start | bytes 589832 | tf_op jit(solution)/shard_map/ppermute | solution.py:25
  18.1 6.9 %collective-permute-start.9 = (bf16[2,128,384]{2,1,0:T(8,128)(2,1)S(1)}, bf16[2,128,384]{2,1,0:T(8,128)(2,1)S(1)}, u32[]{:S(2)}, u32[]{:S(2)}) collective-permute-start(bf16[2,128,384]{2,1,0:T(8,128)(2,1)S(1)} %collective-permute-done.8), channel_id=1, source_target_pairs={{0,1},{1,2},{2,3},{3,0},{4,5},{5,6},{6,7},{7,4},{8,9},{9,10},{10,1... | collective-permute-start | bytes 589832 | tf_op jit(solution)/shard_map/ppermute | solution.py:25
  25.2 17.7 %collective-permute-start.10 = (bf16[4,2,128,384]{3,2,1,0:T(8,128)(2,1)S(1)}, bf16[4,2,128,384]{3,2,1,0:T(8,128)(2,1)S(1)}, u32[]{:S(2)}, u32[]{:S(2)}) collective-permute-start(bf16[4,2,128,384]{3,2,1,0:T(8,128)(2,1)S(1)} %get-tuple-element.55), channel_id=1, source_target_pairs={{0,96},{32,0},{64,32},{96,64},{1,97},{33,1},{65,33},{97,65},{2,98}... | collective-permute-start | bytes 2359304 | tf_op jit(solution)/shard_map/ppermute | solution.py:25
  25.8 17.8 %collective-permute-start.11 = (bf16[4,2,128,384]{3,2,1,0:T(8,128)(2,1)S(1)}, bf16[4,2,128,384]{3,2,1,0:T(8,128)(2,1)S(1)}, u32[]{:S(2)}, u32[]{:S(2)}) collective-permute-start(bf16[4,2,128,384]{3,2,1,0:T(8,128)(2,1)S(1)} %get-tuple-element.55), channel_id=1, source_target_pairs={{0,32},{32,64},{64,96},{96,0},{1,33},{33,65},{65,97},{97,1},{2,34}... | collective-permute-start | bytes 2359304 | tf_op jit(solution)/shard_map/ppermute | solution.py:25
  27.3 7.2 %collective-permute-start.5 = (bf16[2,128,384]{2,1,0:T(8,128)(2,1)S(1)}, bf16[2,128,384]{2,1,0:T(8,128)(2,1)S(1)}, u32[]{:S(2)}, u32[]{:S(2)}) collective-permute-start(bf16[2,128,384]{2,1,0:T(8,128)(2,1)S(1)} %collective-permute-done.4), channel_id=1, source_target_pairs={{0,4},{4,8},{8,12},{12,16},{16,20},{20,24},{24,28},{28,0},{1,5},{5... | collective-permute-start | bytes 589832 | tf_op jit(solution)/shard_map/ppermute | solution.py:25
  27.3 7.2 %collective-permute-start.2 = (bf16[2,128,384]{2,1,0:T(8,128)(2,1)S(1)}, bf16[2,128,384]{2,1,0:T(8,128)(2,1)S(1)}, u32[]{:S(2)}, u32[]{:S(2)}) collective-permute-start(bf16[2,128,384]{2,1,0:T(8,128)(2,1)S(1)} %collective-permute-done.1), channel_id=1, source_target_pairs={{0,28},{4,0},{8,4},{12,8},{16,12},{20,16},{24,20},{28,24},{1,29},{... | collective-permute-start | bytes 589832 | tf_op jit(solution)/shard_map/ppermute | solution.py:25
  34.5 6.9 %collective-permute-start.6 = (bf16[2,128,384]{2,1,0:T(8,128)(2,1)S(1)}, bf16[2,128,384]{2,1,0:T(8,128)(2,1)S(1)}, u32[]{:S(2)}, u32[]{:S(2)}) collective-permute-start(bf16[2,128,384]{2,1,0:T(8,128)(2,1)S(1)} %collective-permute-done.5), channel_id=1, source_target_pairs={{0,4},{4,8},{8,12},{12,16},{16,20},{20,24},{24,28},{28,0},{1,5},{5... | collective-permute-start | bytes 589832 | tf_op jit(solution)/shard_map/ppermute | solution.py:25
  42.9 7.9 %collective-permute-start.13 = (bf16[2,2,128,384]{3,2,1,0:T(8,128)(2,1)S(1)}, bf16[2,2,128,384]{3,2,1,0:T(8,128)(2,1)S(1)}, u32[]{:S(2)}, u32[]{:S(2)}) collective-permute-start(bf16[2,2,128,384]{3,2,1,0:T(8,128)(2,1)S(1)} %slice.437), channel_id=1, source_target_pairs={{0,96},{32,0},{64,32},{96,64},{1,97},{33,1},{65,33},{97,65},{2,98}... | collective-permute-start | bytes 1179656 | tf_op jit(solution)/shard_map/ppermute | solution.py:25
  43.7 9.4 %collective-permute-start.12 = (bf16[2,2,128,384]{3,2,1,0:T(8,128)(2,1)S(1)}, bf16[2,2,128,384]{3,2,1,0:T(8,128)(2,1)S(1)}, u32[]{:S(2)}, u32[]{:S(2)}) collective-permute-start(bf16[2,2,128,384]{3,2,1,0:T(8,128)(2,1)S(1)} %slice.436), channel_id=1, source_target_pairs={{0,32},{32,64},{64,96},{96,0},{1,33},{33,65},{65,97},{97,1},{2,34}... | collective-permute-start | bytes 1179656 | tf_op jit(solution)/shard_map/ppermute | solution.py:25
  45.4 9.6 %copy-start.2 = (bf16[8,2,128,384]{3,2,1,0:T(8,128)(2,1)}, bf16[8,2,128,384]{3,2,1,0:T(8,128)(2,1)S(1)}, u32[]{:S(2)}) copy-start(bf16[8,2,128,384]{3,2,1,0:T(8,128)(2,1)S(1)} %bitcast_dynamic-update-slice_fusion.query_ref) | copy-start | bytes 4718596
  75.7 44.1 %copy-start.1 = (bf16[2,1,128,384]{3,2,1,0:T(8,128)(2,1)S(1)}, bf16[2,1,128,384]{3,2,1,0:T(8,128)(2,1)}, u32[]{:S(2)}) copy-start(bf16[2,1,128,384]{3,2,1,0:T(8,128)(2,1)} %param.6) | copy-start | bytes 589828
  77.6 7.1 %collective-permute-start.14 = (bf16[2,130,384]{2,1,0:T(8,128)(2,1)S(1)}, bf16[2,130,384]{2,1,0:T(8,128)(2,1)S(1)}, u32[]{:S(2)}, u32[]{:S(2)}) collective-permute-start(bf16[2,130,384]{2,1,0:T(8,128)(2,1)S(1)} %pad_maximum_fusion.2), channel_id=1, source_target_pairs={{0,4},{4,8},{8,12},{12,16},{16,20},{20,24},{24,28},{28,0},{1,5},{5... | collective-permute-start | bytes 599048 | tf_op jit(solution)/shard_map/ppermute | solution.py:25
  86.1 7.1 %collective-permute-start.15 = (bf16[2,130,384]{2,1,0:T(8,128)(2,1)S(1)}, bf16[2,130,384]{2,1,0:T(8,128)(2,1)S(1)}, u32[]{:S(2)}, u32[]{:S(2)}) collective-permute-start(bf16[2,130,384]{2,1,0:T(8,128)(2,1)S(1)} %pad_maximum_fusion.3), channel_id=1, source_target_pairs={{0,4},{4,8},{8,12},{12,16},{16,20},{20,24},{24,28},{28,0},{1,5},{5... | collective-permute-start | bytes 599048 | tf_op jit(solution)/shard_map/ppermute | solution.py:25
  93.4 7.4 %collective-permute-start.18 = (bf16[2,130,384]{2,1,0:T(8,128)(2,1)S(1)}, bf16[2,130,384]{2,1,0:T(8,128)(2,1)S(1)}, u32[]{:S(2)}, u32[]{:S(2)}) collective-permute-start(bf16[2,130,384]{2,1,0:T(8,128)(2,1)S(1)} %pad_maximum_fusion.6), channel_id=1, source_target_pairs={{0,28},{4,0},{8,4},{12,8},{16,12},{20,16},{24,20},{28,24},{1,29},{... | collective-permute-start | bytes 599048 | tf_op jit(solution)/shard_map/ppermute | solution.py:25
  102.3 7.9 %collective-permute-start.16 = (bf16[2,130,384]{2,1,0:T(8,128)(2,1)S(1)}, bf16[2,130,384]{2,1,0:T(8,128)(2,1)S(1)}, u32[]{:S(2)}, u32[]{:S(2)}) collective-permute-start(bf16[2,130,384]{2,1,0:T(8,128)(2,1)S(1)} %pad_maximum_fusion.4), channel_id=1, source_target_pairs={{0,4},{4,8},{8,12},{12,16},{16,20},{20,24},{24,28},{28,0},{1,5},{5... | collective-permute-start | bytes 599048 | tf_op jit(solution)/shard_map/ppermute | solution.py:25
  102.5 7.8 %collective-permute-start.19 = (bf16[2,130,384]{2,1,0:T(8,128)(2,1)S(1)}, bf16[2,130,384]{2,1,0:T(8,128)(2,1)S(1)}, u32[]{:S(2)}, u32[]{:S(2)}) collective-permute-start(bf16[2,130,384]{2,1,0:T(8,128)(2,1)S(1)} %pad_maximum_fusion.7), channel_id=1, source_target_pairs={{0,28},{4,0},{8,4},{12,8},{16,12},{20,16},{24,20},{28,24},{1,29},{... | collective-permute-start | bytes 599048 | tf_op jit(solution)/shard_map/ppermute | solution.py:25
  111.8 7.1 %collective-permute-start.17 = (bf16[2,130,384]{2,1,0:T(8,128)(2,1)S(1)}, bf16[2,130,384]{2,1,0:T(8,128)(2,1)S(1)}, u32[]{:S(2)}, u32[]{:S(2)}) collective-permute-start(bf16[2,130,384]{2,1,0:T(8,128)(2,1)S(1)} %pad_maximum_fusion.5), channel_id=1, source_target_pairs={{0,4},{4,8},{8,12},{12,16},{16,20},{20,24},{24,28},{28,0},{1,5},{5... | collective-permute-start | bytes 599048 | tf_op jit(solution)/shard_map/ppermute | solution.py:25
  112.6 7.2 %collective-permute-start.20 = (bf16[2,130,384]{2,1,0:T(8,128)(2,1)S(1)}, bf16[2,130,384]{2,1,0:T(8,128)(2,1)S(1)}, u32[]{:S(2)}, u32[]{:S(2)}) collective-permute-start(bf16[2,130,384]{2,1,0:T(8,128)(2,1)S(1)} %pad_maximum_fusion.8), channel_id=1, source_target_pairs={{0,28},{4,0},{8,4},{12,8},{16,12},{20,16},{24,20},{28,24},{1,29},{... | collective-permute-start | bytes 599048 | tf_op jit(solution)/shard_map/ppermute | solution.py:25
  121.6 13.7 %collective-permute-start.21 = (bf16[2,1,128,384]{3,2,0,1:T(8,128)(2,1)S(1)}, bf16[2,1,128,384]{3,2,0,1:T(8,128)(2,1)S(1)}, u32[]{:S(2)}, u32[]{:S(2)}) collective-permute-start(bf16[2,1,128,384]{3,2,0,1:T(8,128)(2,1)S(1)} %multiply_convert_fusion), channel_id=1, source_target_pairs={{0,129},{1,130},{2,131},{3,132},{4,133},{5,134},{6,135},{7,136},{8... | collective-permute-start | bytes 589832 | tf_op jit(solution)/shard_map/ppermute | solution.py:220
  122.9 12.4 %collective-permute-start.24 = (bf16[2,1,128,384]{3,2,0,1:T(8,128)(2,1)S(1)}, bf16[2,1,128,384]{3,2,0,1:T(8,128)(2,1)S(1)}, u32[]{:S(2)}, u32[]{:S(2)}) collective-permute-start(bf16[2,1,128,384]{3,2,0,1:T(8,128)(2,1)S(1)} %multiply_convert_fusion), channel_id=1, source_target_pairs={{1,128},{2,129},{3,130},{4,131},{5,132},{6,133},{7,134},{8,135},{9... | collective-permute-start | bytes 589832 | tf_op jit(solution)/shard_map/ppermute | solution.py:221
  124.2 20.8 %collective-permute-start.25 = (bf16[2,1,128,384]{3,2,0,1:T(8,128)(2,1)S(1)}, bf16[2,1,128,384]{3,2,0,1:T(8,128)(2,1)S(1)}, u32[]{:S(2)}, u32[]{:S(2)}) collective-permute-start(bf16[2,1,128,384]{3,2,0,1:T(8,128)(2,1)S(1)} %multiply_convert_fusion), channel_id=1, source_target_pairs={{1,0},{2,1},{3,2},{4,3},{5,4},{6,5},{7,6},{8,7},{9,8},{10,9},{11,1... | collective-permute-start | bytes 589832 | tf_op jit(solution)/shard_map/ppermute | solution.py:113
  131.8 13.2 %collective-permute-start.23 = (bf16[2,1,128,384]{3,2,0,1:T(8,128)(2,1)S(1)}, bf16[2,1,128,384]{3,2,0,1:T(8,128)(2,1)S(1)}, u32[]{:S(2)}, u32[]{:S(2)}) collective-permute-start(bf16[2,1,128,384]{3,2,0,1:T(8,128)(2,1)S(1)} %multiply_convert_fusion), channel_id=1, source_target_pairs={{0,128},{1,129},{2,130},{3,131},{4,132},{5,133},{6,134},{7,135},{8... | collective-permute-start | bytes 589832 | tf_op jit(solution)/shard_map/ppermute | solution.py:219
  133.1 11.8 %collective-permute-start.22 = (bf16[2,1,128,384]{3,2,0,1:T(8,128)(2,1)S(1)}, bf16[2,1,128,384]{3,2,0,1:T(8,128)(2,1)S(1)}, u32[]{:S(2)}, u32[]{:S(2)}) collective-permute-start(bf16[2,1,128,384]{3,2,0,1:T(8,128)(2,1)S(1)} %multiply_convert_fusion), channel_id=1, source_target_pairs={{0,1},{1,2},{2,3},{3,4},{4,5},{5,6},{6,7},{7,8},{8,9},{9,10},{10,1... | collective-permute-start | bytes 589832 | tf_op jit(solution)/shard_map/ppermute | solution.py:113
  135.3 11.6 %slice-start = ((s8[7962624]{0:T(1024)(128)(4,1)}), s8[4194304]{0:T(1024)(128)(4,1)S(1)}, s32[]{:S(2)}) async-start(s8[7962624]{0:T(1024)(128)(4,1)} %bitcast.331), calls=%async_computation | async-start | bytes 8388608
  145.7 2.1 %slice-start.1 = ((s8[7962624]{0:T(1024)(128)(4,1)}), s8[3768320]{0:T(1024)(128)(4,1)S(1)}, s32[]{:S(2)}) async-start(s8[7962624]{0:T(1024)(128)(4,1)} %bitcast.331), calls=%async_computation.1 | async-start | bytes 7536640

commit v3 on v1

--- a/solution.py
+++ b/solution.py
@@ -113,9 +113,40 @@
     return lax.ppermute(block, ROW_AXES, route)
 
 
+def projection_kernel(token_ref, key_w_ref, value_w_ref, key_ref, value_ref):
+    width = key_ref.shape[-1]
+    tokens = token_ref[...].reshape(-1, width)
+    key_ref[0] = jnp.dot(tokens, key_w_ref[...], preferred_element_type=jnp.float32).astype(jnp.bfloat16)
+    value_ref[0] = jnp.dot(tokens, value_w_ref[...], preferred_element_type=jnp.float32).astype(jnp.bfloat16)
+
+
+def project_keys(token_blocks, key_weight, value_weight):
+    key_count, frames, rows, width = token_blocks.shape
+    keys = key_count * rows
+    weight_spec = pl.BlockSpec((width, width), lambda f: (0, 0))
+    out_spec = pl.BlockSpec((1, keys, width), lambda f: (f, 0, 0))
+    shape = jax.ShapeDtypeStruct((frames, keys, width), jnp.bfloat16)
+    return pl.pallas_call(
+        projection_kernel,
+        grid=(frames,),
+        in_specs=[
+            pl.BlockSpec((key_count, None, rows, width), lambda f: (0, f, 0, 0)),
+            weight_spec,
+            weight_spec,
+        ],
+        out_specs=[out_spec, out_spec],
+        out_shape=[shape, shape],
+        cost_estimate=pl.CostEstimate(
+            flops=4 * frames * keys * width * width,
+            transcendentals=0,
+            bytes_accessed=6 * frames * keys * width,
+        ),
+    )(token_blocks, key_weight, value_weight)
+
+
 def attention_kernel(scale, query_ref, key_ref, value_ref, high_ref, total_ref, summed_ref, short_ref):
     scores = lax.dot_general(
-        query_ref[0], key_ref[0], (((1,), (1,)), ((), ())), preferred_element_type=jnp.float32
+        query_ref[...], key_ref[0], (((1,), (1,)), ((), ())), preferred_element_type=jnp.float32
     ) * scale
     high = jnp.max(scores, axis=-1, keepdims=True)
     expo = jnp.exp(scores - high)
@@ -128,35 +159,36 @@
     short_ref[0] = summed.astype(jnp.bfloat16)
 
 
-def attention(query_rows, key_rows, value_rows):
-    frames, queries, width = query_rows.shape
+def attention(query_blocks, key_rows, value_rows, first, stride):
+    _, frames, rows, width = query_blocks.shape
     keys = key_rows.shape[1]
-    tile = 256
+    picked = 2
     scale = 1.0 / math.sqrt(width)
-    stat = jax.ShapeDtypeStruct((frames, 1, queries), jnp.float32)
-    stat_spec = pl.BlockSpec((1, 1, tile), lambda f, i: (f, 0, i))
-    row_spec = pl.BlockSpec((1, tile, width), lambda f, i: (f, i, 0))
+    stat = jax.ShapeDtypeStruct((frames, 1, picked * rows), jnp.float32)
+    stat_spec = pl.BlockSpec((1, 1, rows), lambda f, i: (f, 0, i))
+    row_spec = pl.BlockSpec((1, rows, width), lambda f, i: (f, i, 0))
+    key_spec = pl.BlockSpec((1, keys, width), lambda f, i: (f, 0, 0))
     return pl.pallas_call(
         functools.partial(attention_kernel, scale),
-        grid=(frames, queries // tile),
+        grid=(frames, picked),
         in_specs=[
-            row_spec,
-            pl.BlockSpec((1, keys, width), lambda f, i: (f, 0, 0)),
-            pl.BlockSpec((1, keys, width), lambda f, i: (f, 0, 0)),
+            pl.BlockSpec((None, None, rows, width), lambda f, i: (first + stride * i, f, 0, 0)),
+            key_spec,
+            key_spec,
         ],
         out_specs=[stat_spec, stat_spec, row_spec, row_spec],
         out_shape=[
             stat,
             stat,
-            jax.ShapeDtypeStruct((frames, queries, width), jnp.float32),
-            jax.ShapeDtypeStruct((frames, queries, width), jnp.bfloat16),
+            jax.ShapeDtypeStruct((frames, picked * rows, width), jnp.float32),
+            jax.ShapeDtypeStruct((frames, picked * rows, width), jnp.bfloat16),
         ],
         cost_estimate=pl.CostEstimate(
-            flops=4 * frames * queries * keys * width,
-            transcendentals=frames * queries * keys,
-            bytes_accessed=2 * frames * (queries + 2 * keys) * width + 6 * frames * queries * width,
+            flops=4 * frames * picked * rows * keys * width,
+            transcendentals=frames * picked * rows * keys,
+            bytes_accessed=4 * frames * keys * width + 8 * frames * picked * rows * width,
         ),
-    )(query_rows, key_rows, value_rows)
+    )(query_blocks, key_rows, value_rows)
 
 
 def per_device(features, query_weight, key_weight, value_weight, out_weight, conv_weight):
@@ -171,21 +203,23 @@
     query_rel = ring_gather(query, "z")
     inner = jnp.stack(ring_gather(normed.reshape(frames, count, width), "y"))
     outer = jnp.stack(ring_gather(inner, "x", halve=True))
-    keys_in = jnp.transpose(outer, (2, 0, 1, 3, 4)).reshape(-1, width)
-    key_rows = project(keys_in, key_weight).reshape(frames, -1, width)
-    value_rows = project(keys_in, value_weight).reshape(frames, -1, width)
-    query_rows = jnp.stack(query_rel, axis=1).reshape(frames, -1, width)
-
-    highest, total, summed, short = attention(query_rows, key_rows, value_rows)
-    highest, total = highest[:, 0], total[:, 0]
+    token_blocks = outer.reshape(-1, *outer.shape[2:])
+    query_blocks = jnp.stack(query_rel)
+    key_rows, value_rows = project_keys(token_blocks, key_weight, value_weight)
 
     blocks = len(query_rel)
-    first_sent = (blocks // 2, (blocks + 1) // 2 + 1)
-    parts = []
-    for k in range(blocks):
-        lo, hi = k * count, (k + 1) * count
-        rows_of = short if k in first_sent else summed
-        parts.append((highest[:, lo:hi], total[:, lo:hi], rows_of[:, lo:hi]))
+    right_first = blocks // 2
+    left_first = (blocks + 1) // 2 + 1
+    parts = [None] * blocks
+    for step in range(blocks // 2):
+        first, second = (right_first - step) % blocks, (left_first + step) % blocks
+        if step == blocks // 2 - 1:
+            second = 0
+        high, total, summed, short = attention(query_blocks, key_rows, value_rows, first, second - first)
+        for j, k in enumerate((first, second)):
+            rows_of = short if step == 0 else summed
+            piece = slice(j * count, (j + 1) * count)
+            parts[k] = (high[:, 0, piece], total[:, 0, piece], rows_of[:, piece])
     _, total, summed = ring_reduce(parts, "z", count)
     attended = (summed / total[..., None]).astype(jnp.bfloat16)
 

time: 156 us -> 158 us (1.013)
  Pallas kernels: 17.2 us -> 40.6 us
  waiting for transfers between devices: 65.6 us -> 48 us
  matrix products: 13.8 us -> 5.39 us
  other arithmetic: 10.2 us -> 15.1 us
    ppermute x21, waiting for transfers between devices: 55.8 us -> 38.2 us  [ring_shift(): return lax.ppermute(block, axis, [(i, (i + step) % n) for i in range(n)])]
    pallas_call x1 -> x4, Pallas kernels: 17.2 us -> 33.7 us  [attention(): pl.pallas_call(functools.partial(attention_kernel, scale), grid=(frames,...]
    dot_general x3 -> x1, matrix products: 8.65 us -> 1.24 us  [project(): jnp.dot(flat_rows, weight, preferred_element_type=jnp.float32)]
    pallas_call x0 -> x1, Pallas kernels: none -> 6.89 us  [project_keys(): pl.pallas_call(projection_kernel, grid=(frames,), in_specs=[pl.BlockSpec(...]
    convert_element_type x0 -> x15, other arithmetic: none -> 4.87 us  [the longest x7 3.51 us: split3(): lo = (rest - mid.astype(jnp.float32)).astype(jnp.bfloat16)]
    another operation x2 -> x3, other arithmetic: 0.26 us -> 2.2 us  [per_device(): outer = jnp.stack(ring_gather(inner, 'x', halve=True))]
    ppermute x2, starting transfers between devices: 9.65 us -> 7.74 us  [row_shift(): return lax.ppermute(block, ROW_AXES, route)]
  transfers between devices with their start and end apart: 26 -> 26, of which waited for: 14 -> 10; matrix products, arithmetic and copies ran while one was open for 2% -> 2% of each run, Pallas kernels for 0% -> 16%
where the time goes in v3:
time: 158 us; the launch traced here: 157 us
  waiting for transfers between devices  48 us (30%)
  starting transfers between devices  41.8 us (26%)
  Pallas kernels  40.6 us (26%)
  other arithmetic  15.1 us (10%)
  local copies, waits for them, and re-layouts  5.6 us (4%)
  matrix products  5.39 us (3%)
    ppermute x21, waiting for transfers between devices, ring_shift(): return lax.ppermute(block, axis, [(i, (i + step) % n) for i in range(n)])  38.2 us
    pallas_call x4, Pallas kernels, attention(): pl.pallas_call(functools.partial(attention_kernel, scale), grid=(frames,...  33.7 us
    ppermute x21, starting transfers between devices, ring_shift(): return lax.ppermute(block, axis, [(i, (i + step) % n) for i in range(n)])  30.1 us
    ppermute x2, waiting for transfers between devices, row_shift(): return lax.ppermute(block, ROW_AXES, route)  9.76 us
    ppermute x2, starting transfers between devices, row_shift(): return lax.ppermute(block, ROW_AXES, route)  7.74 us
    pallas_call x1, Pallas kernels, project_keys(): pl.pallas_call(projection_kernel, grid=(frames,), in_specs=[pl.BlockSpec(...  6.89 us
    dot_general x1, matrix products, per_device(): jnp.dot(columns, conv_weight.reshape(27 * width, width), preferred_elemen...  3.61 us
    convert_element_type x7, other arithmetic, split3(): lo = (rest - mid.astype(jnp.float32)).astype(jnp.bfloat16)  3.51 us
  transfers between devices with their start and end apart: 26, of which 10 were waited for; matrix products, arithmetic and copies ran while one was open for 2% of the time, Pallas kernels for 16%

profile of v3, /device:TPU:2, one launch (start us, length us, event | category | flops | bytes accessed | tf_op | source)
XLA Modules:
  0.0 157.2 jit_solution(12038555011316178137)
XLA Ops:
  0.0 1.1 fusion.21
  1.1 1.0 fusion.22
  2.1 1.2 convolution_convert_fusion
  3.4 2.0 %collective-permute-start.3 = (bf16[2,128,384]{2,1,0:T(8,128)(2,1)S(1)}, bf16[2,128,384]{2,1,0:T(8,128)(2,1)S(1)}, u32[]{:S(2)}, u32[]{:S(2)}) collective-permute-start(bf16[2,128,384]{2,1,0:T(8,128)(2,1)S(1)} %bitcast.147), channel_id=1, source_target_pairs={{0,4},{4,8},{8,12},{12,16},{16,20},{20,24},{24,28},{28,0},{1,5},{5... | collective-permute-start | bytes 589832 | tf_op jit(solution)/shard_map/ppermute | solution.py:25
  5.4 4.0 %collective-permute-start = (bf16[2,128,384]{2,1,0:T(8,128)(2,1)S(1)}, bf16[2,128,384]{2,1,0:T(8,128)(2,1)S(1)}, u32[]{:S(2)}, u32[]{:S(2)}) collective-permute-start(bf16[2,128,384]{2,1,0:T(8,128)(2,1)S(1)} %bitcast.148), channel_id=1, source_target_pairs={{0,28},{4,0},{8,4},{12,8},{16,12},{20,16},{24,20},{28,24},{1,29},{... | collective-permute-start | bytes 589832 | tf_op jit(solution)/shard_map/ppermute | solution.py:25
  9.4 1.0 fusion.117
  10.4 1.7 %collective-permute-start.8 = (bf16[2,128,384]{2,1,0:T(8,128)(2,1)S(1)}, bf16[2,128,384]{2,1,0:T(8,128)(2,1)S(1)}, u32[]{:S(2)}, u32[]{:S(2)}) collective-permute-start(bf16[2,128,384]{2,1,0:T(8,128)(2,1)S(1)} %fusion.117), channel_id=1, source_target_pairs={{0,1},{1,2},{2,3},{3,0},{4,5},{5,6},{6,7},{7,4},{8,9},{9,10},{10,1... | collective-permute-start | bytes 589832 | tf_op jit(solution)/shard_map/ppermute | solution.py:25
  12.1 1.7 %collective-permute-start.7 = (bf16[2,128,384]{2,1,0:T(8,128)(2,1)S(1)}, bf16[2,128,384]{2,1,0:T(8,128)(2,1)S(1)}, u32[]{:S(2)}, u32[]{:S(2)}) collective-permute-start(bf16[2,128,384]{2,1,0:T(8,128)(2,1)S(1)} %fusion.117), channel_id=1, source_target_pairs={{0,3},{1,0},{2,1},{3,2},{4,7},{5,4},{6,5},{7,6},{8,11},{9,8},{10,9... | collective-permute-start | bytes 589832 | tf_op jit(solution)/shard_map/ppermute | solution.py:25
  13.8 1.0 fusion.116
  14.9 3.2 %collective-permute-start.1 = (bf16[2,128,384]{2,1,0:T(8,128)(2,1)S(1)}, bf16[2,128,384]{2,1,0:T(8,128)(2,1)S(1)}, u32[]{:S(2)}, u32[]{:S(2)}) collective-permute-start(bf16[2,128,384]{2,1,0:T(8,128)(2,1)S(1)} %collective-permute-done), channel_id=1, source_target_pairs={{0,28},{4,0},{8,4},{12,8},{16,12},{20,16},{24,20},{28,24},{1,29},{... | collective-permute-start | bytes 589832 | tf_op jit(solution)/shard_map/ppermute | solution.py:25
  18.1 0.9 collective-permute-start.9
  19.1 5.9 %collective-permute-done.9 = bf16[2,128,384]{2,1,0:T(8,128)(2,1)S(1)} collective-permute-done((bf16[2,128,384]{2,1,0:T(8,128)(2,1)S(1)}, bf16[2,128,384]{2,1,0:T(8,128)(2,1)S(1)}, u32[]{:S(2)}, u32[]{:S(2)}) %collective-permute-start.9) | collective-permute-done | bytes 196640 | tf_op jit(solution)/shard_map/ppermute | solution.py:25
  25.0 0.2 fusion.93
  25.2 0.6 collective-permute-start.10
  25.8 1.5 collective-permute-start.11
  27.3 3.2 %collective-permute-start.2 = (bf16[2,128,384]{2,1,0:T(8,128)(2,1)S(1)}, bf16[2,128,384]{2,1,0:T(8,128)(2,1)S(1)}, u32[]{:S(2)}, u32[]{:S(2)}) collective-permute-start(bf16[2,128,384]{2,1,0:T(8,128)(2,1)S(1)} %collective-permute-done.1), channel_id=1, source_target_pairs={{0,28},{4,0},{8,4},{12,8},{16,12},{20,16},{24,20},{28,24},{1,29},{... | collective-permute-start | bytes 589832 | tf_op jit(solution)/shard_map/ppermute | solution.py:25
  30.6 3.9 %collective-permute-done.5 = bf16[2,128,384]{2,1,0:T(8,128)(2,1)S(1)} collective-permute-done((bf16[2,128,384]{2,1,0:T(8,128)(2,1)S(1)}, bf16[2,128,384]{2,1,0:T(8,128)(2,1)S(1)}, u32[]{:S(2)}, u32[]{:S(2)}) %collective-permute-start.5) | collective-permute-done | bytes 196640 | tf_op jit(solution)/shard_map/ppermute | solution.py:25
  34.5 6.8 %collective-permute-done.6 = bf16[2,128,384]{2,1,0:T(8,128)(2,1)S(1)} collective-permute-done((bf16[2,128,384]{2,1,0:T(8,128)(2,1)S(1)}, bf16[2,128,384]{2,1,0:T(8,128)(2,1)S(1)}, u32[]{:S(2)}, u32[]{:S(2)}) %collective-permute-start.6) | collective-permute-done | bytes 196640 | tf_op jit(solution)/shard_map/ppermute | solution.py:25
  41.4 1.4 collective-permute-done.10
  42.9 0.4 collective-permute-start.13
  43.3 0.3 collective-permute-done.11
  43.7 1.7 %collective-permute-start.12 = (bf16[2,2,128,384]{3,2,1,0:T(8,128)(2,1)S(1)}, bf16[2,2,128,384]{3,2,1,0:T(8,128)(2,1)S(1)}, u32[]{:S(2)}, u32[]{:S(2)}) collective-permute-start(bf16[2,2,128,384]{3,2,1,0:T(8,128)(2,1)S(1)} %slice.436), channel_id=1, source_target_pairs={{0,32},{32,64},{64,96},{96,0},{1,33},{33,65},{65,97},{97,1},{2,34}... | collective-permute-start | bytes 1179656 | tf_op jit(solution)/shard_map/ppermute | solution.py:25
  45.4 5.4 %collective-permute-done.13 = bf16[2,2,128,384]{3,2,1,0:T(8,128)(2,1)S(1)} collective-permute-done((bf16[2,2,128,384]{3,2,1,0:T(8,128)(2,1)S(1)}, bf16[2,2,128,384]{3,2,1,0:T(8,128)(2,1)S(1)}, u32[]{:S(2)}, u32[]{:S(2)}) %collective-permute-start.13) | collective-permute-done | bytes 393248 | tf_op jit(solution)/shard_map/ppermute | solution.py:25
  50.8 2.3 %collective-permute-done.12 = bf16[2,2,128,384]{3,2,1,0:T(8,128)(2,1)S(1)} collective-permute-done((bf16[2,2,128,384]{3,2,1,0:T(8,128)(2,1)S(1)}, bf16[2,2,128,384]{3,2,1,0:T(8,128)(2,1)S(1)}, u32[]{:S(2)}, u32[]{:S(2)}) %collective-permute-start.12) | collective-permute-done | bytes 393248 | tf_op jit(solution)/shard_map/ppermute | solution.py:25
  53.0 0.1 maximum_bitcast_fusion
  53.1 1.9 %pad_maximum_fusion = bf16[4,4,2,128,384]{4,3,2,1,0:T(8,128)(2,1)} fusion(bf16[1,4,2,128,384]{4,3,2,1,0:T(8,128)(2,1)S(1)} %bitcast.146, bf16[1,4,2,128,384]{4,3,2,1,0:T(8,128)(2,1)S(1)} %maximum_bitcast_fusion, bf16[1,4,2,128,384]{4,3,2,1,0:T(8,128)(2,1)S(1)} %bitcast.145, bf16[1,4,2,128,384]{4,3,2,1,0:T(8,128)(2,1)S(1)} %get-tuple-element.57), kind=kLoop, calls=%fused_computation.4 | loop fusion | flops 4718592 | bytes 6291456 | tf_op jit(solution)/shard_map/stack | solution.py:205
  55.1 6.9 %shard_map.64 = (bf16[2,2048,384]{2,1,0:T(8,128)(2,1)}, bf16[2,2048,384]{2,1,0:T(8,128)(2,1)}) custom-call(bf16[16,2,128,384]{3,2,1,0:T(8,128)(2,1)} %bitcast.144, bf16[384,384]{1,0:T(8,128)(2,1)} %key_w_ref.1, bf16[384,384]{1,0:T(8,128)(2,1)} %value_w_ref.1), custom_call_target="tpu_custom_call" | custom-call | flops 2415919104 | bytes 9437184 | tf_op jit(solution)/shard_map/pallas_call | solution.py:129
  62.0 8.4 %shard_map.65 = (f32[2,1,256]{2,1,0:T(1,128)}, f32[2,1,256]{2,1,0:T(1,128)}, f32[2,256,384]{2,1,0:T(8,128)}, bf16[2,256,384]{2,1,0:T(8,128)(2,1)}) custom-call(bf16[8,2,128,384]{3,2,1,0:T(8,128)(2,1)} %copy-done.1, bf16[2,2048,384]{2,1,0:T(8,128)(2,1)} %get-tuple-element.19.key_ref, bf16[2,2048,384]{2,1,0:T(8,128)(2,1)} %get-tuple-element.20.value_ref), custom_call_target="tpu_custom_call" | custom-call | flops 1610612736 | bytes 7864320 | tf_op jit(solution)/shard_map/pallas_call | solution.py:171
  70.4 0.7 fusion.111
  71.1 0.7 subtract_convert_fusion.12
  71.8 1.1 fusion.108
  73.1 3.3 %collective-permute-start.18 = (bf16[2,130,384]{2,1,0:T(8,128)(2,1)S(1)}, bf16[2,130,384]{2,1,0:T(8,128)(2,1)S(1)}, u32[]{:S(2)}, u32[]{:S(2)}) collective-permute-start(bf16[2,130,384]{2,1,0:T(8,128)(2,1)S(1)} %pad_maximum_fusion.6), channel_id=1, source_target_pairs={{0,28},{4,0},{8,4},{12,8},{16,12},{20,16},{24,20},{28,24},{1,29},{... | collective-permute-start | bytes 599048 | tf_op jit(solution)/shard_map/ppermute | solution.py:25
  76.4 8.4 %shard_map.66 = (f32[2,1,256]{2,1,0:T(1,128)}, f32[2,1,256]{2,1,0:T(1,128)}, f32[2,256,384]{2,1,0:T(8,128)}, bf16[2,256,384]{2,1,0:T(8,128)(2,1)}) custom-call(bf16[8,2,128,384]{3,2,1,0:T(8,128)(2,1)} %copy-done.1, bf16[2,2048,384]{2,1,0:T(8,128)(2,1)} %get-tuple-element.19.key_ref, bf16[2,2048,384]{2,1,0:T(8,128)(2,1)} %get-tuple-element.20.value_ref), custom_call_target="tpu_custom_call" | custom-call | flops 1610612736 | bytes 7864320 | tf_op jit(solution)/shard_map/pallas_call | solution.py:171
  84.9 0.7 subtract_convert_fusion.10
  85.6 0.7 maximum_convert_fusion.4
  86.3 0.7 subtract_convert_fusion.11
  87.2 1.3 add_convert_fusion.4
  88.6 0.6 collective-permute-start.19
  89.2 1.6 %collective-permute-start.15 = (bf16[2,130,384]{2,1,0:T(8,128)(2,1)S(1)}, bf16[2,130,384]{2,1,0:T(8,128)(2,1)S(1)}, u32[]{:S(2)}, u32[]{:S(2)}) collective-permute-start(bf16[2,130,384]{2,1,0:T(8,128)(2,1)S(1)} %pad_maximum_fusion.3), channel_id=1, source_target_pairs={{0,4},{4,8},{8,12},{12,16},{16,20},{20,24},{24,28},{28,0},{1,5},{5... | collective-permute-start | bytes 599048 | tf_op jit(solution)/shard_map/ppermute | solution.py:25
  90.8 8.4 %shard_map.68 = (f32[2,1,256]{2,1,0:T(1,128)}, f32[2,1,256]{2,1,0:T(1,128)}, f32[2,256,384]{2,1,0:T(8,128)}, bf16[2,256,384]{2,1,0:T(8,128)(2,1)}) custom-call(bf16[8,2,128,384]{3,2,1,0:T(8,128)(2,1)} %copy-done.1, bf16[2,2048,384]{2,1,0:T(8,128)(2,1)} %get-tuple-element.19.key_ref, bf16[2,2048,384]{2,1,0:T(8,128)(2,1)} %get-tuple-element.20.value_ref), custom_call_target="tpu_custom_call" | custom-call | flops 1610612736 | bytes 7864320 | tf_op jit(solution)/shard_map/pallas_call | solution.py:171
  99.2 0.8 copy.134
  100.0 8.5 %shard_map.67 = (f32[2,1,256]{2,1,0:T(1,128)}, f32[2,1,256]{2,1,0:T(1,128)}, f32[2,256,384]{2,1,0:T(8,128)}, bf16[2,256,384]{2,1,0:T(8,128)(2,1)}) custom-call(bf16[8,2,128,384]{3,2,1,0:T(8,128)(2,1)} %copy-done.1, bf16[2,2048,384]{2,1,0:T(8,128)(2,1)} %get-tuple-element.19.key_ref, bf16[2,2048,384]{2,1,0:T(8,128)(2,1)} %get-tuple-element.20.value_ref), custom_call_target="tpu_custom_call" | custom-call | flops 1610612736 | bytes 7864320 | tf_op jit(solution)/shard_map/pallas_call | solution.py:171
  108.5 0.7 subtract_convert_fusion.8
  109.2 0.6 maximum_convert_fusion.3
  109.9 0.6 subtract_convert_fusion.9
  110.6 1.3 add_convert_fusion.3
  112.0 0.1 collective-permute-start.16
  112.2 3.5 %collective-permute-start.20 = (bf16[2,130,384]{2,1,0:T(8,128)(2,1)S(1)}, bf16[2,130,384]{2,1,0:T(8,128)(2,1)S(1)}, u32[]{:S(2)}, u32[]{:S(2)}) collective-permute-start(bf16[2,130,384]{2,1,0:T(8,128)(2,1)S(1)} %pad_maximum_fusion.8), channel_id=1, source_target_pairs={{0,28},{4,0},{8,4},{12,8},{16,12},{20,16},{24,20},{28,24},{1,29},{... | collective-permute-start | bytes 599048 | tf_op jit(solution)/shard_map/ppermute | solution.py:25
  115.7 5.1 %collective-permute-done.16 = bf16[2,130,384]{2,1,0:T(8,128)(2,1)S(1)} collective-permute-done((bf16[2,130,384]{2,1,0:T(8,128)(2,1)S(1)}, bf16[2,130,384]{2,1,0:T(8,128)(2,1)S(1)}, u32[]{:S(2)}, u32[]{:S(2)}) %collective-permute-start.16) | collective-permute-done | bytes 199712 | tf_op jit(solution)/shard_map/ppermute | solution.py:25
  121.1 0.1 add_convert_fusion.2
  121.2 0.1 collective-permute-start.17
  121.3 7.0 %collective-permute-done.17 = bf16[2,130,384]{2,1,0:T(8,128)(2,1)S(1)} collective-permute-done((bf16[2,130,384]{2,1,0:T(8,128)(2,1)S(1)}, bf16[2,130,384]{2,1,0:T(8,128)(2,1)S(1)}, u32[]{:S(2)}, u32[]{:S(2)}) %collective-permute-start.17) | collective-permute-done | bytes 199712 | tf_op jit(solution)/shard_map/ppermute | solution.py:25
  128.4 0.5 multiply_reduce_fusion
  129.0 0.2 multiply_convert_fusion
  129.2 1.3 collective-permute-start.21
  130.5 1.3 collective-permute-start.24
  131.8 5.8 %collective-permute-start.25 = (bf16[2,1,128,384]{3,2,0,1:T(8,128)(2,1)S(1)}, bf16[2,1,128,384]{3,2,0,1:T(8,128)(2,1)S(1)}, u32[]{:S(2)}, u32[]{:S(2)}) collective-permute-start(bf16[2,1,128,384]{3,2,0,1:T(8,128)(2,1)S(1)} %multiply_convert_fusion), channel_id=1, source_target_pairs={{1,0},{2,1},{3,2},{4,3},{5,4},{6,5},{7,6},{8,7},{9,8},{10,9},{11,1... | collective-permute-start | bytes 589832 | tf_op jit(solution)/shard_map/ppermute | solution.py:113
  137.6 1.3 collective-permute-start.23
  138.9 1.9 %collective-permute-start.22 = (bf16[2,1,128,384]{3,2,0,1:T(8,128)(2,1)S(1)}, bf16[2,1,128,384]{3,2,0,1:T(8,128)(2,1)S(1)}, u32[]{:S(2)}, u32[]{:S(2)}) collective-permute-start(bf16[2,1,128,384]{3,2,0,1:T(8,128)(2,1)S(1)} %multiply_convert_fusion), channel_id=1, source_target_pairs={{0,1},{1,2},{2,3},{3,4},{4,5},{5,6},{6,7},{7,8},{8,9},{9,10},{10,1... | collective-permute-start | bytes 589832 | tf_op jit(solution)/shard_map/ppermute | solution.py:113
  140.9 9.8 %collective-permute-done.22 = bf16[2,1,128,384]{3,2,0,1:T(8,128)(2,1)S(1)} collective-permute-done((bf16[2,1,128,384]{3,2,0,1:T(8,128)(2,1)S(1)}, bf16[2,1,128,384]{3,2,0,1:T(8,128)(2,1)S(1)}, u32[]{:S(2)}, u32[]{:S(2)}) %collective-permute-start.22) | collective-permute-done | bytes 196640 | tf_op jit(solution)/shard_map/ppermute | solution.py:113
  150.8 0.3 select_maximum_fusion
  152.2 0.2 constant_dynamic-update-slice_fusion.6
  152.7 0.9 slice-done.1
  153.6 3.6 %fusion.18 = bf16[2,1,128,384]{3,2,1,0:T(8,128)(2,1)} fusion(f32[2,1,128,384]{3,2,0,1:T(8,128)S(1)} %get-tuple-element.136, bf16[10368,384,1]{1,0,2:T(8,128)(2,1)S(1)} %bitcast.167, bf16[2,1,128,10368]{3,2,0,1:T(8,128)(2,1)S(1)} %slice_dynamic-update-slice_fusion), kind=kOutput, calls=%fused_computation.19 | convolution fusion | flops 2038628352 | bytes 13860864 | tf_op jit(solution)/shard_map/dot_general | solution.py:255
  (129 shorter events, 2.7 us)
Async XLA Ops:
  0.0 128.4 %copy-start = (bf16[384,384]{1,0:T(8,128)(2,1)S(1)}, bf16[384,384]{1,0:T(8,128)(2,1)}, u32[]{:S(2)}) copy-start(bf16[384,384]{1,0:T(8,128)(2,1)} %param.10) | copy-start | bytes 884740
  3.4 11.4 %collective-permute-start.3 = (bf16[2,128,384]{2,1,0:T(8,128)(2,1)S(1)}, bf16[2,128,384]{2,1,0:T(8,128)(2,1)S(1)}, u32[]{:S(2)}, u32[]{:S(2)}) collective-permute-start(bf16[2,128,384]{2,1,0:T(8,128)(2,1)S(1)} %bitcast.147), channel_id=1, source_target_pairs={{0,4},{4,8},{8,12},{12,16},{16,20},{20,24},{24,28},{28,0},{1,5},{5... | collective-permute-start | bytes 589832 | tf_op jit(solution)/shard_map/ppermute | solution.py:25
  5.4 9.5 %collective-permute-start = (bf16[2,128,384]{2,1,0:T(8,128)(2,1)S(1)}, bf16[2,128,384]{2,1,0:T(8,128)(2,1)S(1)}, u32[]{:S(2)}, u32[]{:S(2)}) collective-permute-start(bf16[2,128,384]{2,1,0:T(8,128)(2,1)S(1)} %bitcast.148), channel_id=1, source_target_pairs={{0,28},{4,0},{8,4},{12,8},{16,12},{20,16},{24,20},{28,24},{1,29},{... | collective-permute-start | bytes 589832 | tf_op jit(solution)/shard_map/ppermute | solution.py:25
  10.4 7.7 %collective-permute-start.8 = (bf16[2,128,384]{2,1,0:T(8,128)(2,1)S(1)}, bf16[2,128,384]{2,1,0:T(8,128)(2,1)S(1)}, u32[]{:S(2)}, u32[]{:S(2)}) collective-permute-start(bf16[2,128,384]{2,1,0:T(8,128)(2,1)S(1)} %fusion.117), channel_id=1, source_target_pairs={{0,1},{1,2},{2,3},{3,0},{4,5},{5,6},{6,7},{7,4},{8,9},{9,10},{10,1... | collective-permute-start | bytes 589832 | tf_op jit(solution)/shard_map/ppermute | solution.py:25
  12.1 7.0 %collective-permute-start.7 = (bf16[2,128,384]{2,1,0:T(8,128)(2,1)S(1)}, bf16[2,128,384]{2,1,0:T(8,128)(2,1)S(1)}, u32[]{:S(2)}, u32[]{:S(2)}) collective-permute-start(bf16[2,128,384]{2,1,0:T(8,128)(2,1)S(1)} %fusion.117), channel_id=1, source_target_pairs={{0,3},{1,0},{2,1},{3,2},{4,7},{5,4},{6,5},{7,6},{8,11},{9,8},{10,9... | collective-permute-start | bytes 589832 | tf_op jit(solution)/shard_map/ppermute | solution.py:25
  14.8 12.5 %collective-permute-start.4 = (bf16[2,128,384]{2,1,0:T(8,128)(2,1)S(1)}, bf16[2,128,384]{2,1,0:T(8,128)(2,1)S(1)}, u32[]{:S(2)}, u32[]{:S(2)}) collective-permute-start(bf16[2,128,384]{2,1,0:T(8,128)(2,1)S(1)} %collective-permute-done.3), channel_id=1, source_target_pairs={{0,4},{4,8},{8,12},{12,16},{16,20},{20,24},{24,28},{28,0},{1,5},{5... | collective-permute-start | bytes 589832 | tf_op jit(solution)/shard_map/ppermute | solution.py:25
  14.9 12.4 %collective-permute-start.1 = (bf16[2,128,384]{2,1,0:T(8,128)(2,1)S(1)}, bf16[2,128,384]{2,1,0:T(8,128)(2,1)S(1)}, u32[]{:S(2)}, u32[]{:S(2)}) collective-permute-start(bf16[2,128,384]{2,1,0:T(8,128)(2,1)S(1)} %collective-permute-done), channel_id=1, source_target_pairs={{0,28},{4,0},{8,4},{12,8},{16,12},{20,16},{24,20},{28,24},{1,29},{... | collective-permute-start | bytes 589832 | tf_op jit(solution)/shard_map/ppermute | solution.py:25
  18.1 6.9 %collective-permute-start.9 = (bf16[2,128,384]{2,1,0:T(8,128)(2,1)S(1)}, bf16[2,128,384]{2,1,0:T(8,128)(2,1)S(1)}, u32[]{:S(2)}, u32[]{:S(2)}) collective-permute-start(bf16[2,128,384]{2,1,0:T(8,128)(2,1)S(1)} %collective-permute-done.8), channel_id=1, source_target_pairs={{0,1},{1,2},{2,3},{3,0},{4,5},{5,6},{6,7},{7,4},{8,9},{9,10},{10,1... | collective-permute-start | bytes 589832 | tf_op jit(solution)/shard_map/ppermute | solution.py:25
  25.2 17.7 %collective-permute-start.10 = (bf16[4,2,128,384]{3,2,1,0:T(8,128)(2,1)S(1)}, bf16[4,2,128,384]{3,2,1,0:T(8,128)(2,1)S(1)}, u32[]{:S(2)}, u32[]{:S(2)}) collective-permute-start(bf16[4,2,128,384]{3,2,1,0:T(8,128)(2,1)S(1)} %get-tuple-element.58), channel_id=1, source_target_pairs={{0,96},{32,0},{64,32},{96,64},{1,97},{33,1},{65,33},{97,65},{2,98}... | collective-permute-start | bytes 2359304 | tf_op jit(solution)/shard_map/ppermute | solution.py:25
  25.8 17.8 %collective-permute-start.11 = (bf16[4,2,128,384]{3,2,1,0:T(8,128)(2,1)S(1)}, bf16[4,2,128,384]{3,2,1,0:T(8,128)(2,1)S(1)}, u32[]{:S(2)}, u32[]{:S(2)}) collective-permute-start(bf16[4,2,128,384]{3,2,1,0:T(8,128)(2,1)S(1)} %get-tuple-element.58), channel_id=1, source_target_pairs={{0,32},{32,64},{64,96},{96,0},{1,33},{33,65},{65,97},{97,1},{2,34}... | collective-permute-start | bytes 2359304 | tf_op jit(solution)/shard_map/ppermute | solution.py:25
  27.3 7.2 %collective-permute-start.5 = (bf16[2,128,384]{2,1,0:T(8,128)(2,1)S(1)}, bf16[2,128,384]{2,1,0:T(8,128)(2,1)S(1)}, u32[]{:S(2)}, u32[]{:S(2)}) collective-permute-start(bf16[2,128,384]{2,1,0:T(8,128)(2,1)S(1)} %collective-permute-done.4), channel_id=1, source_target_pairs={{0,4},{4,8},{8,12},{12,16},{16,20},{20,24},{24,28},{28,0},{1,5},{5... | collective-permute-start | bytes 589832 | tf_op jit(solution)/shard_map/ppermute | solution.py:25
  27.3 7.2 %collective-permute-start.2 = (bf16[2,128,384]{2,1,0:T(8,128)(2,1)S(1)}, bf16[2,128,384]{2,1,0:T(8,128)(2,1)S(1)}, u32[]{:S(2)}, u32[]{:S(2)}) collective-permute-start(bf16[2,128,384]{2,1,0:T(8,128)(2,1)S(1)} %collective-permute-done.1), channel_id=1, source_target_pairs={{0,28},{4,0},{8,4},{12,8},{16,12},{20,16},{24,20},{28,24},{1,29},{... | collective-permute-start | bytes 589832 | tf_op jit(solution)/shard_map/ppermute | solution.py:25
  34.5 6.9 %collective-permute-start.6 = (bf16[2,128,384]{2,1,0:T(8,128)(2,1)S(1)}, bf16[2,128,384]{2,1,0:T(8,128)(2,1)S(1)}, u32[]{:S(2)}, u32[]{:S(2)}) collective-permute-start(bf16[2,128,384]{2,1,0:T(8,128)(2,1)S(1)} %collective-permute-done.5), channel_id=1, source_target_pairs={{0,4},{4,8},{8,12},{12,16},{16,20},{20,24},{24,28},{28,0},{1,5},{5... | collective-permute-start | bytes 589832 | tf_op jit(solution)/shard_map/ppermute | solution.py:25
  42.9 7.9 %collective-permute-start.13 = (bf16[2,2,128,384]{3,2,1,0:T(8,128)(2,1)S(1)}, bf16[2,2,128,384]{3,2,1,0:T(8,128)(2,1)S(1)}, u32[]{:S(2)}, u32[]{:S(2)}) collective-permute-start(bf16[2,2,128,384]{3,2,1,0:T(8,128)(2,1)S(1)} %slice.437), channel_id=1, source_target_pairs={{0,96},{32,0},{64,32},{96,64},{1,97},{33,1},{65,33},{97,65},{2,98}... | collective-permute-start | bytes 1179656 | tf_op jit(solution)/shard_map/ppermute | solution.py:25
  43.7 9.4 %collective-permute-start.12 = (bf16[2,2,128,384]{3,2,1,0:T(8,128)(2,1)S(1)}, bf16[2,2,128,384]{3,2,1,0:T(8,128)(2,1)S(1)}, u32[]{:S(2)}, u32[]{:S(2)}) collective-permute-start(bf16[2,2,128,384]{3,2,1,0:T(8,128)(2,1)S(1)} %slice.436), channel_id=1, source_target_pairs={{0,32},{32,64},{64,96},{96,0},{1,33},{33,65},{65,97},{97,1},{2,34}... | collective-permute-start | bytes 1179656 | tf_op jit(solution)/shard_map/ppermute | solution.py:25
  45.4 16.6 %copy-start.1 = (bf16[8,2,128,384]{3,2,1,0:T(8,128)(2,1)}, bf16[8,2,128,384]{3,2,1,0:T(8,128)(2,1)S(1)}, u32[]{:S(2)}) copy-start(bf16[8,2,128,384]{3,2,1,0:T(8,128)(2,1)S(1)} %bitcast_dynamic-update-slice_fusion.query_ref) | copy-start | bytes 4718596
  73.0 11.8 %collective-permute-start.14 = (bf16[2,130,384]{2,1,0:T(8,128)(2,1)S(1)}, bf16[2,130,384]{2,1,0:T(8,128)(2,1)S(1)}, u32[]{:S(2)}, u32[]{:S(2)}) collective-permute-start(bf16[2,130,384]{2,1,0:T(8,128)(2,1)S(1)} %pad_maximum_fusion.2), channel_id=1, source_target_pairs={{0,4},{4,8},{8,12},{12,16},{16,20},{20,24},{24,28},{28,0},{1,5},{5... | collective-permute-start | bytes 599048 | tf_op jit(solution)/shard_map/ppermute | solution.py:25
  73.1 11.7 %collective-permute-start.18 = (bf16[2,130,384]{2,1,0:T(8,128)(2,1)S(1)}, bf16[2,130,384]{2,1,0:T(8,128)(2,1)S(1)}, u32[]{:S(2)}, u32[]{:S(2)}) collective-permute-start(bf16[2,130,384]{2,1,0:T(8,128)(2,1)S(1)} %pad_maximum_fusion.6), channel_id=1, source_target_pairs={{0,28},{4,0},{8,4},{12,8},{16,12},{20,16},{24,20},{28,24},{1,29},{... | collective-permute-start | bytes 599048 | tf_op jit(solution)/shard_map/ppermute | solution.py:25
  88.6 19.9 %collective-permute-start.19 = (bf16[2,130,384]{2,1,0:T(8,128)(2,1)S(1)}, bf16[2,130,384]{2,1,0:T(8,128)(2,1)S(1)}, u32[]{:S(2)}, u32[]{:S(2)}) collective-permute-start(bf16[2,130,384]{2,1,0:T(8,128)(2,1)S(1)} %pad_maximum_fusion.7), channel_id=1, source_target_pairs={{0,28},{4,0},{8,4},{12,8},{16,12},{20,16},{24,20},{28,24},{1,29},{... | collective-permute-start | bytes 599048 | tf_op jit(solution)/shard_map/ppermute | solution.py:25
  89.2 19.3 %collective-permute-start.15 = (bf16[2,130,384]{2,1,0:T(8,128)(2,1)S(1)}, bf16[2,130,384]{2,1,0:T(8,128)(2,1)S(1)}, u32[]{:S(2)}, u32[]{:S(2)}) collective-permute-start(bf16[2,130,384]{2,1,0:T(8,128)(2,1)S(1)} %pad_maximum_fusion.3), channel_id=1, source_target_pairs={{0,4},{4,8},{8,12},{12,16},{16,20},{20,24},{24,28},{28,0},{1,5},{5... | collective-permute-start | bytes 599048 | tf_op jit(solution)/shard_map/ppermute | solution.py:25
  99.2 21.7 %copy-start.4 = (f32[2,1,256]{2,1,0:T(1,128)S(1)}, f32[2,1,256]{2,1,0:T(1,128)}, u32[]{:S(2)}) copy-start(f32[2,1,256]{2,1,0:T(1,128)} %get-tuple-element.30) | copy-start | bytes 6148
  99.2 21.7 %copy-start.5 = (f32[2,1,256]{2,1,0:T(1,128)S(1)}, f32[2,1,256]{2,1,0:T(1,128)}, u32[]{:S(2)}) copy-start(f32[2,1,256]{2,1,0:T(1,128)} %get-tuple-element.32) | copy-start | bytes 6148
  99.2 21.8 %copy-start.3 = (f32[2,256,384]{2,1,0:T(8,128)S(1)}, f32[2,256,384]{2,1,0:T(8,128)}, u32[]{:S(2)}) copy-start(f32[2,256,384]{2,1,0:T(8,128)} %get-tuple-element.31) | copy-start | bytes 2359300
  100.0 28.4 %copy-start.2 = (bf16[2,1,128,384]{3,2,1,0:T(8,128)(2,1)S(1)}, bf16[2,1,128,384]{3,2,1,0:T(8,128)(2,1)}, u32[]{:S(2)}) copy-start(bf16[2,1,128,384]{3,2,1,0:T(8,128)(2,1)} %param.6) | copy-start | bytes 589828
  112.0 8.9 %collective-permute-start.16 = (bf16[2,130,384]{2,1,0:T(8,128)(2,1)S(1)}, bf16[2,130,384]{2,1,0:T(8,128)(2,1)S(1)}, u32[]{:S(2)}, u32[]{:S(2)}) collective-permute-start(bf16[2,130,384]{2,1,0:T(8,128)(2,1)S(1)} %pad_maximum_fusion.4), channel_id=1, source_target_pairs={{0,4},{4,8},{8,12},{12,16},{16,20},{20,24},{24,28},{28,0},{1,5},{5... | collective-permute-start | bytes 599048 | tf_op jit(solution)/shard_map/ppermute | solution.py:25
  112.2 8.7 %collective-permute-start.20 = (bf16[2,130,384]{2,1,0:T(8,128)(2,1)S(1)}, bf16[2,130,384]{2,1,0:T(8,128)(2,1)S(1)}, u32[]{:S(2)}, u32[]{:S(2)}) collective-permute-start(bf16[2,130,384]{2,1,0:T(8,128)(2,1)S(1)} %pad_maximum_fusion.8), channel_id=1, source_target_pairs={{0,28},{4,0},{8,4},{12,8},{16,12},{20,16},{24,20},{28,24},{1,29},{... | collective-permute-start | bytes 599048 | tf_op jit(solution)/shard_map/ppermute | solution.py:25
  121.2 7.1 %collective-permute-start.17 = (bf16[2,130,384]{2,1,0:T(8,128)(2,1)S(1)}, bf16[2,130,384]{2,1,0:T(8,128)(2,1)S(1)}, u32[]{:S(2)}, u32[]{:S(2)}) collective-permute-start(bf16[2,130,384]{2,1,0:T(8,128)(2,1)S(1)} %pad_maximum_fusion.5), channel_id=1, source_target_pairs={{0,4},{4,8},{8,12},{12,16},{16,20},{20,24},{24,28},{28,0},{1,5},{5... | collective-permute-start | bytes 599048 | tf_op jit(solution)/shard_map/ppermute | solution.py:25
  129.2 11.7 %collective-permute-start.21 = (bf16[2,1,128,384]{3,2,0,1:T(8,128)(2,1)S(1)}, bf16[2,1,128,384]{3,2,0,1:T(8,128)(2,1)S(1)}, u32[]{:S(2)}, u32[]{:S(2)}) collective-permute-start(bf16[2,1,128,384]{3,2,0,1:T(8,128)(2,1)S(1)} %multiply_convert_fusion), channel_id=1, source_target_pairs={{0,129},{1,130},{2,131},{3,132},{4,133},{5,134},{6,135},{7,136},{8... | collective-permute-start | bytes 589832 | tf_op jit(solution)/shard_map/ppermute | solution.py:236
  130.5 10.4 %collective-permute-start.24 = (bf16[2,1,128,384]{3,2,0,1:T(8,128)(2,1)S(1)}, bf16[2,1,128,384]{3,2,0,1:T(8,128)(2,1)S(1)}, u32[]{:S(2)}, u32[]{:S(2)}) collective-permute-start(bf16[2,1,128,384]{3,2,0,1:T(8,128)(2,1)S(1)} %multiply_convert_fusion), channel_id=1, source_target_pairs={{1,128},{2,129},{3,130},{4,131},{5,132},{6,133},{7,134},{8,135},{9... | collective-permute-start | bytes 589832 | tf_op jit(solution)/shard_map/ppermute | solution.py:237
  131.8 19.0 %collective-permute-start.25 = (bf16[2,1,128,384]{3,2,0,1:T(8,128)(2,1)S(1)}, bf16[2,1,128,384]{3,2,0,1:T(8,128)(2,1)S(1)}, u32[]{:S(2)}, u32[]{:S(2)}) collective-permute-start(bf16[2,1,128,384]{3,2,0,1:T(8,128)(2,1)S(1)} %multiply_convert_fusion), channel_id=1, source_target_pairs={{1,0},{2,1},{3,2},{4,3},{5,4},{6,5},{7,6},{8,7},{9,8},{10,9},{11,1... | collective-permute-start | bytes 589832 | tf_op jit(solution)/shard_map/ppermute | solution.py:113
  137.6 13.2 %collective-permute-start.23 = (bf16[2,1,128,384]{3,2,0,1:T(8,128)(2,1)S(1)}, bf16[2,1,128,384]{3,2,0,1:T(8,128)(2,1)S(1)}, u32[]{:S(2)}, u32[]{:S(2)}) collective-permute-start(bf16[2,1,128,384]{3,2,0,1:T(8,128)(2,1)S(1)} %multiply_convert_fusion), channel_id=1, source_target_pairs={{0,128},{1,129},{2,130},{3,131},{4,132},{5,133},{6,134},{7,135},{8... | collective-permute-start | bytes 589832 | tf_op jit(solution)/shard_map/ppermute | solution.py:235
  138.9 11.8 %collective-permute-start.22 = (bf16[2,1,128,384]{3,2,0,1:T(8,128)(2,1)S(1)}, bf16[2,1,128,384]{3,2,0,1:T(8,128)(2,1)S(1)}, u32[]{:S(2)}, u32[]{:S(2)}) collective-permute-start(bf16[2,1,128,384]{3,2,0,1:T(8,128)(2,1)S(1)} %multiply_convert_fusion), channel_id=1, source_target_pairs={{0,1},{1,2},{2,3},{3,4},{4,5},{5,6},{6,7},{7,8},{8,9},{9,10},{10,1... | collective-permute-start | bytes 589832 | tf_op jit(solution)/shard_map/ppermute | solution.py:113
  140.9 11.8 %slice-start = ((s8[7962624]{0:T(1024)(128)(4,1)}), s8[4194304]{0:T(1024)(128)(4,1)S(1)}, s32[]{:S(2)}) async-start(s8[7962624]{0:T(1024)(128)(4,1)} %bitcast.165), calls=%async_computation | async-start | bytes 8388608
  151.5 2.1 %slice-start.1 = ((s8[7962624]{0:T(1024)(128)(4,1)}), s8[3768320]{0:T(1024)(128)(4,1)S(1)}, s32[]{:S(2)}) async-start(s8[7962624]{0:T(1024)(128)(4,1)} %bitcast.165), calls=%async_computation.1 | async-start | bytes 7536640

commit v4 on v2

--- a/solution.py
+++ b/solution.py
@@ -143,7 +143,7 @@
 def attention(query_blocks, token_blocks, key_weight, value_weight):
     query_count, frames, rows, width = query_blocks.shape
     key_count = token_blocks.shape[0]
-    per_tile = 2
+    per_tile = 4
     tile = per_tile * rows
     queries = query_count * rows
     scale = 1.0 / math.sqrt(width)

time: 152 us -> 151 us (level)
  no operation moved by 1% of the time
where the time goes in v4:
time: 151 us; the launch traced here: 150 us
  waiting for transfers between devices  66.2 us (44%)
  starting transfers between devices  41.4 us (27%)
  Pallas kernels  19.4 us (13%)
  other arithmetic  11.6 us (8%)
  matrix products  6.39 us (4%)
  local copies, waits for them, and re-layouts  4.76 us (3%)
    ppermute x21, waiting for transfers between devices, ring_shift(): return lax.ppermute(block, axis, [(i, (i + step) % n) for i in range(n)])  56.4 us
    ppermute x21, starting transfers between devices, ring_shift(): return lax.ppermute(block, axis, [(i, (i + step) % n) for i in range(n)])  28.6 us
    pallas_call x1, Pallas kernels, attention(): pl.pallas_call(functools.partial(attention_kernel, scale), grid=(frames,...  19.4 us
    ppermute x2, waiting for transfers between devices, row_shift(): return lax.ppermute(block, ROW_AXES, route)  9.76 us
    ppermute x2, starting transfers between devices, row_shift(): return lax.ppermute(block, ROW_AXES, route)  8.93 us
    convert_element_type x3, other arithmetic, pack(): return jnp.concatenate([summed.astype(jnp.bfloat16), stats], axis=1)  3.81 us
    dot_general x1, matrix products, per_device(): jnp.dot(columns, conv_weight.reshape(27 * width, width), preferred_elemen...  3.61 us
  transfers between devices with their start and end apart: 26, of which 14 were waited for; matrix products, arithmetic and copies ran while one was open for 2% of the time, Pallas kernels for 0%

profile of v4, /device:TPU:2, one launch (start us, length us, event | category | flops | bytes accessed | tf_op | source)
XLA Modules:
  0.0 150.4 jit_solution(10361932835155323735)
XLA Ops:
  0.0 1.1 fusion.21
  1.1 1.0 fusion.22
  2.1 1.2 convolution_convert_fusion
  3.4 2.0 %collective-permute-start.3 = (bf16[2,128,384]{2,1,0:T(8,128)(2,1)S(1)}, bf16[2,128,384]{2,1,0:T(8,128)(2,1)S(1)}, u32[]{:S(2)}, u32[]{:S(2)}) collective-permute-start(bf16[2,128,384]{2,1,0:T(8,128)(2,1)S(1)} %bitcast.324), channel_id=1, source_target_pairs={{0,4},{4,8},{8,12},{12,16},{16,20},{20,24},{24,28},{28,0},{1,5},{5... | collective-permute-start | bytes 589832 | tf_op jit(solution)/shard_map/ppermute | solution.py:25
  5.4 4.0 %collective-permute-start = (bf16[2,128,384]{2,1,0:T(8,128)(2,1)S(1)}, bf16[2,128,384]{2,1,0:T(8,128)(2,1)S(1)}, u32[]{:S(2)}, u32[]{:S(2)}) collective-permute-start(bf16[2,128,384]{2,1,0:T(8,128)(2,1)S(1)} %bitcast.325), channel_id=1, source_target_pairs={{0,28},{4,0},{8,4},{12,8},{16,12},{20,16},{24,20},{28,24},{1,29},{... | collective-permute-start | bytes 589832 | tf_op jit(solution)/shard_map/ppermute | solution.py:25
  9.4 1.0 fusion.104
  10.4 1.7 %collective-permute-start.8 = (bf16[2,128,384]{2,1,0:T(8,128)(2,1)S(1)}, bf16[2,128,384]{2,1,0:T(8,128)(2,1)S(1)}, u32[]{:S(2)}, u32[]{:S(2)}) collective-permute-start(bf16[2,128,384]{2,1,0:T(8,128)(2,1)S(1)} %fusion.104), channel_id=1, source_target_pairs={{0,1},{1,2},{2,3},{3,0},{4,5},{5,6},{6,7},{7,4},{8,9},{9,10},{10,1... | collective-permute-start | bytes 589832 | tf_op jit(solution)/shard_map/ppermute | solution.py:25
  12.1 1.7 %collective-permute-start.7 = (bf16[2,128,384]{2,1,0:T(8,128)(2,1)S(1)}, bf16[2,128,384]{2,1,0:T(8,128)(2,1)S(1)}, u32[]{:S(2)}, u32[]{:S(2)}) collective-permute-start(bf16[2,128,384]{2,1,0:T(8,128)(2,1)S(1)} %fusion.104), channel_id=1, source_target_pairs={{0,3},{1,0},{2,1},{3,2},{4,7},{5,4},{6,5},{7,6},{8,11},{9,8},{10,9... | collective-permute-start | bytes 589832 | tf_op jit(solution)/shard_map/ppermute | solution.py:25
  13.8 1.0 fusion.103
  14.8 0.1 collective-permute-start.4
  14.9 3.2 %collective-permute-start.1 = (bf16[2,128,384]{2,1,0:T(8,128)(2,1)S(1)}, bf16[2,128,384]{2,1,0:T(8,128)(2,1)S(1)}, u32[]{:S(2)}, u32[]{:S(2)}) collective-permute-start(bf16[2,128,384]{2,1,0:T(8,128)(2,1)S(1)} %collective-permute-done), channel_id=1, source_target_pairs={{0,28},{4,0},{8,4},{12,8},{16,12},{20,16},{24,20},{28,24},{1,29},{... | collective-permute-start | bytes 589832 | tf_op jit(solution)/shard_map/ppermute | solution.py:25
  18.1 0.9 collective-permute-start.9
  19.1 5.9 %collective-permute-done.9 = bf16[2,128,384]{2,1,0:T(8,128)(2,1)S(1)} collective-permute-done((bf16[2,128,384]{2,1,0:T(8,128)(2,1)S(1)}, bf16[2,128,384]{2,1,0:T(8,128)(2,1)S(1)}, u32[]{:S(2)}, u32[]{:S(2)}) %collective-permute-start.9) | collective-permute-done | bytes 196640 | tf_op jit(solution)/shard_map/ppermute | solution.py:25
  25.0 0.2 fusion.77
  25.2 0.6 collective-permute-start.10
  25.8 1.5 collective-permute-start.11
  27.3 3.2 %collective-permute-start.2 = (bf16[2,128,384]{2,1,0:T(8,128)(2,1)S(1)}, bf16[2,128,384]{2,1,0:T(8,128)(2,1)S(1)}, u32[]{:S(2)}, u32[]{:S(2)}) collective-permute-start(bf16[2,128,384]{2,1,0:T(8,128)(2,1)S(1)} %collective-permute-done.1), channel_id=1, source_target_pairs={{0,28},{4,0},{8,4},{12,8},{16,12},{20,16},{24,20},{28,24},{1,29},{... | collective-permute-start | bytes 589832 | tf_op jit(solution)/shard_map/ppermute | solution.py:25
  30.6 3.9 %collective-permute-done.5 = bf16[2,128,384]{2,1,0:T(8,128)(2,1)S(1)} collective-permute-done((bf16[2,128,384]{2,1,0:T(8,128)(2,1)S(1)}, bf16[2,128,384]{2,1,0:T(8,128)(2,1)S(1)}, u32[]{:S(2)}, u32[]{:S(2)}) %collective-permute-start.5) | collective-permute-done | bytes 196640 | tf_op jit(solution)/shard_map/ppermute | solution.py:25
  34.5 6.8 %collective-permute-done.6 = bf16[2,128,384]{2,1,0:T(8,128)(2,1)S(1)} collective-permute-done((bf16[2,128,384]{2,1,0:T(8,128)(2,1)S(1)}, bf16[2,128,384]{2,1,0:T(8,128)(2,1)S(1)}, u32[]{:S(2)}, u32[]{:S(2)}) %collective-permute-start.6) | collective-permute-done | bytes 196640 | tf_op jit(solution)/shard_map/ppermute | solution.py:25
  41.4 1.4 collective-permute-done.10
  42.9 0.4 collective-permute-start.13
  43.3 0.3 collective-permute-done.11
  43.7 1.7 %collective-permute-start.12 = (bf16[2,2,128,384]{3,2,1,0:T(8,128)(2,1)S(1)}, bf16[2,2,128,384]{3,2,1,0:T(8,128)(2,1)S(1)}, u32[]{:S(2)}, u32[]{:S(2)}) collective-permute-start(bf16[2,2,128,384]{3,2,1,0:T(8,128)(2,1)S(1)} %slice.436), channel_id=1, source_target_pairs={{0,32},{32,64},{64,96},{96,0},{1,33},{33,65},{65,97},{97,1},{2,34}... | collective-permute-start | bytes 1179656 | tf_op jit(solution)/shard_map/ppermute | solution.py:25
  45.4 5.4 %collective-permute-done.13 = bf16[2,2,128,384]{3,2,1,0:T(8,128)(2,1)S(1)} collective-permute-done((bf16[2,2,128,384]{3,2,1,0:T(8,128)(2,1)S(1)}, bf16[2,2,128,384]{3,2,1,0:T(8,128)(2,1)S(1)}, u32[]{:S(2)}, u32[]{:S(2)}) %collective-permute-start.13) | collective-permute-done | bytes 393248 | tf_op jit(solution)/shard_map/ppermute | solution.py:25
  50.8 2.3 %collective-permute-done.12 = bf16[2,2,128,384]{3,2,1,0:T(8,128)(2,1)S(1)} collective-permute-done((bf16[2,2,128,384]{3,2,1,0:T(8,128)(2,1)S(1)}, bf16[2,2,128,384]{3,2,1,0:T(8,128)(2,1)S(1)}, u32[]{:S(2)}, u32[]{:S(2)}) %collective-permute-start.12) | collective-permute-done | bytes 393248 | tf_op jit(solution)/shard_map/ppermute | solution.py:25
  53.0 0.1 maximum_bitcast_fusion
  53.1 1.9 %pad_maximum_fusion = bf16[4,4,2,128,384]{4,3,2,1,0:T(8,128)(2,1)} fusion(bf16[1,4,2,128,384]{4,3,2,1,0:T(8,128)(2,1)S(1)} %bitcast.323, bf16[1,4,2,128,384]{4,3,2,1,0:T(8,128)(2,1)S(1)} %maximum_bitcast_fusion, bf16[1,4,2,128,384]{4,3,2,1,0:T(8,128)(2,1)S(1)} %bitcast.322, bf16[1,4,2,128,384]{4,3,2,1,0:T(8,128)(2,1)S(1)} %get-tuple-element.54), kind=kLoop, calls=%fused_computation.4 | loop fusion | flops 4718592 | bytes 6291456 | tf_op jit(solution)/shard_map/stack | solution.py:194
  55.0 19.4 %shard_map.64 = (f32[2,1,1024]{2,1,0:T(1,128)}, f32[2,1,1024]{2,1,0:T(1,128)}, f32[2,1024,384]{2,1,0:T(8,128)}, bf16[2,1024,384]{2,1,0:T(8,128)(2,1)}) custom-call(bf16[8,2,128,384]{3,2,1,0:T(8,128)(2,1)} %copy-done.2, bf16[16,2,128,384]{3,2,1,0:T(8,128)(2,1)} %bitcast.321, bf16[384,384]{1,0:T(8,128)(2,1)} %key_w_ref.1, bf16[384,384]{1,0:T(8,128)(2,1)} %value_w_ref.1), custom_call_target="tpu_custom_call" | custom-call | flops 8858370048 | bytes 9437184 | tf_op jit(solution)/shard_map/pallas_call | solution.py:155
  74.4 1.1 fusion.92
  75.5 0.7 copy_bitcast_fusion
  76.4 0.1 collective-permute-start.14
  76.5 7.0 %collective-permute-done.14 = bf16[2,130,384]{2,1,0:T(8,128)(2,1)S(1)} collective-permute-done((bf16[2,130,384]{2,1,0:T(8,128)(2,1)S(1)}, bf16[2,130,384]{2,1,0:T(8,128)(2,1)S(1)}, u32[]{:S(2)}, u32[]{:S(2)}) %collective-permute-start.14) | collective-permute-done | bytes 199712 | tf_op jit(solution)/shard_map/ppermute | solution.py:25
  83.7 1.1 add_convert_fusion.4
  84.8 0.1 collective-permute-start.15
  84.9 7.0 %collective-permute-done.15 = bf16[2,130,384]{2,1,0:T(8,128)(2,1)S(1)} collective-permute-done((bf16[2,130,384]{2,1,0:T(8,128)(2,1)S(1)}, bf16[2,130,384]{2,1,0:T(8,128)(2,1)S(1)}, u32[]{:S(2)}, u32[]{:S(2)}) %collective-permute-start.15) | collective-permute-done | bytes 199712 | tf_op jit(solution)/shard_map/ppermute | solution.py:25
  92.1 0.5 collective-permute-start.18
  92.7 6.9 %collective-permute-done.18 = bf16[2,130,384]{2,1,0:T(8,128)(2,1)S(1)} collective-permute-done((bf16[2,130,384]{2,1,0:T(8,128)(2,1)S(1)}, bf16[2,130,384]{2,1,0:T(8,128)(2,1)S(1)}, u32[]{:S(2)}, u32[]{:S(2)}) %collective-permute-start.18) | collective-permute-done | bytes 199712 | tf_op jit(solution)/shard_map/ppermute | solution.py:25
  99.7 1.3 add_convert_fusion.3
  101.1 0.1 collective-permute-start.16
  101.2 3.3 %collective-permute-start.19 = (bf16[2,130,384]{2,1,0:T(8,128)(2,1)S(1)}, bf16[2,130,384]{2,1,0:T(8,128)(2,1)S(1)}, u32[]{:S(2)}, u32[]{:S(2)}) collective-permute-start(bf16[2,130,384]{2,1,0:T(8,128)(2,1)S(1)} %pad_maximum_fusion.7), channel_id=1, source_target_pairs={{0,28},{4,0},{8,4},{12,8},{16,12},{20,16},{24,20},{28,24},{1,29},{... | collective-permute-start | bytes 599048 | tf_op jit(solution)/shard_map/ppermute | solution.py:25
  104.5 4.4 %collective-permute-done.16 = bf16[2,130,384]{2,1,0:T(8,128)(2,1)S(1)} collective-permute-done((bf16[2,130,384]{2,1,0:T(8,128)(2,1)S(1)}, bf16[2,130,384]{2,1,0:T(8,128)(2,1)S(1)}, u32[]{:S(2)}, u32[]{:S(2)}) %collective-permute-start.16) | collective-permute-done | bytes 199712 | tf_op jit(solution)/shard_map/ppermute | solution.py:25
  109.2 1.3 add_convert_fusion.2
  110.6 0.6 collective-permute-start.17
  111.2 3.1 %collective-permute-start.20 = (bf16[2,130,384]{2,1,0:T(8,128)(2,1)S(1)}, bf16[2,130,384]{2,1,0:T(8,128)(2,1)S(1)}, u32[]{:S(2)}, u32[]{:S(2)}) collective-permute-start(bf16[2,130,384]{2,1,0:T(8,128)(2,1)S(1)} %pad_maximum_fusion.8), channel_id=1, source_target_pairs={{0,28},{4,0},{8,4},{12,8},{16,12},{20,16},{24,20},{28,24},{1,29},{... | collective-permute-start | bytes 599048 | tf_op jit(solution)/shard_map/ppermute | solution.py:25
  114.3 3.4 %collective-permute-done.17 = bf16[2,130,384]{2,1,0:T(8,128)(2,1)S(1)} collective-permute-done((bf16[2,130,384]{2,1,0:T(8,128)(2,1)S(1)}, bf16[2,130,384]{2,1,0:T(8,128)(2,1)S(1)}, u32[]{:S(2)}, u32[]{:S(2)}) %collective-permute-start.17) | collective-permute-done | bytes 199712 | tf_op jit(solution)/shard_map/ppermute | solution.py:25
  117.7 1.6 %collective-permute-done.20 = bf16[2,130,384]{2,1,0:T(8,128)(2,1)S(1)} collective-permute-done((bf16[2,130,384]{2,1,0:T(8,128)(2,1)S(1)}, bf16[2,130,384]{2,1,0:T(8,128)(2,1)S(1)}, u32[]{:S(2)}, u32[]{:S(2)}) %collective-permute-start.20) | collective-permute-done | bytes 199712 | tf_op jit(solution)/shard_map/ppermute | solution.py:25
  119.4 1.5 %multiply_reduce_fusion = (f32[2,128]{1,0:T(2,128)S(1)}, f32[2,1,128,384]{3,2,0,1:T(8,128)S(1)}) fusion(bf16[384,384]{1,0:T(8,128)(2,1)S(1)} %copy-done, f32[2,1024,384]{2,1,0:T(8,128)} %get-tuple-element.12, bf16[2,130,384]{2,1,0:T(8,128)(2,1)S(1)} %collective-permute-done.20, bf16[2,130,384]{2,1,0:T(8,128)(2,1)S(1)} %collective-permute-done.17, ...), kind=kOutput, calls=%fused_computation.27 | convolution fusion | flops 77070080 | bytes 1677312 | tf_op jit(solution)/shard_map/dot_general | solution.py:210
  121.0 0.2 multiply_convert_fusion
  121.2 1.3 collective-permute-start.21
  122.5 1.3 collective-permute-start.24
  123.8 7.0 %collective-permute-start.25 = (bf16[2,1,128,384]{3,2,0,1:T(8,128)(2,1)S(1)}, bf16[2,1,128,384]{3,2,0,1:T(8,128)(2,1)S(1)}, u32[]{:S(2)}, u32[]{:S(2)}) collective-permute-start(bf16[2,1,128,384]{3,2,0,1:T(8,128)(2,1)S(1)} %multiply_convert_fusion), channel_id=1, source_target_pairs={{1,0},{2,1},{3,2},{4,3},{5,4},{6,5},{7,6},{8,7},{9,8},{10,9},{11,1... | collective-permute-start | bytes 589832 | tf_op jit(solution)/shard_map/ppermute | solution.py:113
  130.8 1.3 collective-permute-start.23
  132.1 1.9 %collective-permute-start.22 = (bf16[2,1,128,384]{3,2,0,1:T(8,128)(2,1)S(1)}, bf16[2,1,128,384]{3,2,0,1:T(8,128)(2,1)S(1)}, u32[]{:S(2)}, u32[]{:S(2)}) collective-permute-start(bf16[2,1,128,384]{3,2,0,1:T(8,128)(2,1)S(1)} %multiply_convert_fusion), channel_id=1, source_target_pairs={{0,1},{1,2},{2,3},{3,4},{4,5},{5,6},{6,7},{7,8},{8,9},{9,10},{10,1... | collective-permute-start | bytes 589832 | tf_op jit(solution)/shard_map/ppermute | solution.py:113
  134.1 9.8 %collective-permute-done.22 = bf16[2,1,128,384]{3,2,0,1:T(8,128)(2,1)S(1)} collective-permute-done((bf16[2,1,128,384]{3,2,0,1:T(8,128)(2,1)S(1)}, bf16[2,1,128,384]{3,2,0,1:T(8,128)(2,1)S(1)}, u32[]{:S(2)}, u32[]{:S(2)}) %collective-permute-start.22) | collective-permute-done | bytes 196640 | tf_op jit(solution)/shard_map/ppermute | solution.py:113
  144.0 0.3 select_maximum_fusion
  144.4 0.1 slice_dynamic-update-slice_fusion.18
  144.6 0.1 slice_dynamic-update-slice_fusion.16
  144.7 0.1 slice_dynamic-update-slice_fusion.14
  144.9 0.1 slice_dynamic-update-slice_fusion.11
  145.0 0.1 slice_dynamic-update-slice_fusion.9
  145.4 0.2 constant_dynamic-update-slice_fusion.48
  145.8 0.1 slice_dynamic-update-slice_fusion
  145.9 0.9 slice-done.1
  146.8 3.6 %fusion.18 = bf16[2,1,128,384]{3,2,1,0:T(8,128)(2,1)} fusion(f32[2,1,128,384]{3,2,0,1:T(8,128)S(1)} %get-tuple-element.103, bf16[10368,384,1]{1,0,2:T(8,128)(2,1)S(1)} %bitcast.333, bf16[2,1,128,10368]{3,2,0,1:T(8,128)(2,1)S(1)} %slice_dynamic-update-slice_fusion), kind=kOutput, calls=%fused_computation.19 | convolution fusion | flops 2038628352 | bytes 13860864 | tf_op jit(solution)/shard_map/dot_general | solution.py:239
  (142 shorter events, 2.4 us)
Async XLA Ops:
  0.0 119.4 %copy-start = (bf16[384,384]{1,0:T(8,128)(2,1)S(1)}, bf16[384,384]{1,0:T(8,128)(2,1)}, u32[]{:S(2)}) copy-start(bf16[384,384]{1,0:T(8,128)(2,1)} %param.10) | copy-start | bytes 884740
  3.4 11.4 %collective-permute-start.3 = (bf16[2,128,384]{2,1,0:T(8,128)(2,1)S(1)}, bf16[2,128,384]{2,1,0:T(8,128)(2,1)S(1)}, u32[]{:S(2)}, u32[]{:S(2)}) collective-permute-start(bf16[2,128,384]{2,1,0:T(8,128)(2,1)S(1)} %bitcast.324), channel_id=1, source_target_pairs={{0,4},{4,8},{8,12},{12,16},{16,20},{20,24},{24,28},{28,0},{1,5},{5... | collective-permute-start | bytes 589832 | tf_op jit(solution)/shard_map/ppermute | solution.py:25
  5.4 9.5 %collective-permute-start = (bf16[2,128,384]{2,1,0:T(8,128)(2,1)S(1)}, bf16[2,128,384]{2,1,0:T(8,128)(2,1)S(1)}, u32[]{:S(2)}, u32[]{:S(2)}) collective-permute-start(bf16[2,128,384]{2,1,0:T(8,128)(2,1)S(1)} %bitcast.325), channel_id=1, source_target_pairs={{0,28},{4,0},{8,4},{12,8},{16,12},{20,16},{24,20},{28,24},{1,29},{... | collective-permute-start | bytes 589832 | tf_op jit(solution)/shard_map/ppermute | solution.py:25
  10.4 7.7 %collective-permute-start.8 = (bf16[2,128,384]{2,1,0:T(8,128)(2,1)S(1)}, bf16[2,128,384]{2,1,0:T(8,128)(2,1)S(1)}, u32[]{:S(2)}, u32[]{:S(2)}) collective-permute-start(bf16[2,128,384]{2,1,0:T(8,128)(2,1)S(1)} %fusion.104), channel_id=1, source_target_pairs={{0,1},{1,2},{2,3},{3,0},{4,5},{5,6},{6,7},{7,4},{8,9},{9,10},{10,1... | collective-permute-start | bytes 589832 | tf_op jit(solution)/shard_map/ppermute | solution.py:25
  12.1 7.0 %collective-permute-start.7 = (bf16[2,128,384]{2,1,0:T(8,128)(2,1)S(1)}, bf16[2,128,384]{2,1,0:T(8,128)(2,1)S(1)}, u32[]{:S(2)}, u32[]{:S(2)}) collective-permute-start(bf16[2,128,384]{2,1,0:T(8,128)(2,1)S(1)} %fusion.104), channel_id=1, source_target_pairs={{0,3},{1,0},{2,1},{3,2},{4,7},{5,4},{6,5},{7,6},{8,11},{9,8},{10,9... | collective-permute-start | bytes 589832 | tf_op jit(solution)/shard_map/ppermute | solution.py:25
  14.8 12.5 %collective-permute-start.4 = (bf16[2,128,384]{2,1,0:T(8,128)(2,1)S(1)}, bf16[2,128,384]{2,1,0:T(8,128)(2,1)S(1)}, u32[]{:S(2)}, u32[]{:S(2)}) collective-permute-start(bf16[2,128,384]{2,1,0:T(8,128)(2,1)S(1)} %collective-permute-done.3), channel_id=1, source_target_pairs={{0,4},{4,8},{8,12},{12,16},{16,20},{20,24},{24,28},{28,0},{1,5},{5... | collective-permute-start | bytes 589832 | tf_op jit(solution)/shard_map/ppermute | solution.py:25
  14.9 12.4 %collective-permute-start.1 = (bf16[2,128,384]{2,1,0:T(8,128)(2,1)S(1)}, bf16[2,128,384]{2,1,0:T(8,128)(2,1)S(1)}, u32[]{:S(2)}, u32[]{:S(2)}) collective-permute-start(bf16[2,128,384]{2,1,0:T(8,128)(2,1)S(1)} %collective-permute-done), channel_id=1, source_target_pairs={{0,28},{4,0},{8,4},{12,8},{16,12},{20,16},{24,20},{28,24},{1,29},{... | collective-permute-start | bytes 589832 | tf_op jit(solution)/shard_map/ppermute | solution.py:25
  18.1 6.9 %collective-permute-start.9 = (bf16[2,128,384]{2,1,0:T(8,128)(2,1)S(1)}, bf16[2,128,384]{2,1,0:T(8,128)(2,1)S(1)}, u32[]{:S(2)}, u32[]{:S(2)}) collective-permute-start(bf16[2,128,384]{2,1,0:T(8,128)(2,1)S(1)} %collective-permute-done.8), channel_id=1, source_target_pairs={{0,1},{1,2},{2,3},{3,0},{4,5},{5,6},{6,7},{7,4},{8,9},{9,10},{10,1... | collective-permute-start | bytes 589832 | tf_op jit(solution)/shard_map/ppermute | solution.py:25
  25.2 17.7 %collective-permute-start.10 = (bf16[4,2,128,384]{3,2,1,0:T(8,128)(2,1)S(1)}, bf16[4,2,128,384]{3,2,1,0:T(8,128)(2,1)S(1)}, u32[]{:S(2)}, u32[]{:S(2)}) collective-permute-start(bf16[4,2,128,384]{3,2,1,0:T(8,128)(2,1)S(1)} %get-tuple-element.55), channel_id=1, source_target_pairs={{0,96},{32,0},{64,32},{96,64},{1,97},{33,1},{65,33},{97,65},{2,98}... | collective-permute-start | bytes 2359304 | tf_op jit(solution)/shard_map/ppermute | solution.py:25
  25.8 17.8 %collective-permute-start.11 = (bf16[4,2,128,384]{3,2,1,0:T(8,128)(2,1)S(1)}, bf16[4,2,128,384]{3,2,1,0:T(8,128)(2,1)S(1)}, u32[]{:S(2)}, u32[]{:S(2)}) collective-permute-start(bf16[4,2,128,384]{3,2,1,0:T(8,128)(2,1)S(1)} %get-tuple-element.55), channel_id=1, source_target_pairs={{0,32},{32,64},{64,96},{96,0},{1,33},{33,65},{65,97},{97,1},{2,34}... | collective-permute-start | bytes 2359304 | tf_op jit(solution)/shard_map/ppermute | solution.py:25
  27.3 7.2 %collective-permute-start.5 = (bf16[2,128,384]{2,1,0:T(8,128)(2,1)S(1)}, bf16[2,128,384]{2,1,0:T(8,128)(2,1)S(1)}, u32[]{:S(2)}, u32[]{:S(2)}) collective-permute-start(bf16[2,128,384]{2,1,0:T(8,128)(2,1)S(1)} %collective-permute-done.4), channel_id=1, source_target_pairs={{0,4},{4,8},{8,12},{12,16},{16,20},{20,24},{24,28},{28,0},{1,5},{5... | collective-permute-start | bytes 589832 | tf_op jit(solution)/shard_map/ppermute | solution.py:25
  27.3 7.2 %collective-permute-start.2 = (bf16[2,128,384]{2,1,0:T(8,128)(2,1)S(1)}, bf16[2,128,384]{2,1,0:T(8,128)(2,1)S(1)}, u32[]{:S(2)}, u32[]{:S(2)}) collective-permute-start(bf16[2,128,384]{2,1,0:T(8,128)(2,1)S(1)} %collective-permute-done.1), channel_id=1, source_target_pairs={{0,28},{4,0},{8,4},{12,8},{16,12},{20,16},{24,20},{28,24},{1,29},{... | collective-permute-start | bytes 589832 | tf_op jit(solution)/shard_map/ppermute | solution.py:25
  34.5 6.9 %collective-permute-start.6 = (bf16[2,128,384]{2,1,0:T(8,128)(2,1)S(1)}, bf16[2,128,384]{2,1,0:T(8,128)(2,1)S(1)}, u32[]{:S(2)}, u32[]{:S(2)}) collective-permute-start(bf16[2,128,384]{2,1,0:T(8,128)(2,1)S(1)} %collective-permute-done.5), channel_id=1, source_target_pairs={{0,4},{4,8},{8,12},{12,16},{16,20},{20,24},{24,28},{28,0},{1,5},{5... | collective-permute-start | bytes 589832 | tf_op jit(solution)/shard_map/ppermute | solution.py:25
  42.9 7.9 %collective-permute-start.13 = (bf16[2,2,128,384]{3,2,1,0:T(8,128)(2,1)S(1)}, bf16[2,2,128,384]{3,2,1,0:T(8,128)(2,1)S(1)}, u32[]{:S(2)}, u32[]{:S(2)}) collective-permute-start(bf16[2,2,128,384]{3,2,1,0:T(8,128)(2,1)S(1)} %slice.437), channel_id=1, source_target_pairs={{0,96},{32,0},{64,32},{96,64},{1,97},{33,1},{65,33},{97,65},{2,98}... | collective-permute-start | bytes 1179656 | tf_op jit(solution)/shard_map/ppermute | solution.py:25
  43.7 9.4 %collective-permute-start.12 = (bf16[2,2,128,384]{3,2,1,0:T(8,128)(2,1)S(1)}, bf16[2,2,128,384]{3,2,1,0:T(8,128)(2,1)S(1)}, u32[]{:S(2)}, u32[]{:S(2)}) collective-permute-start(bf16[2,2,128,384]{3,2,1,0:T(8,128)(2,1)S(1)} %slice.436), channel_id=1, source_target_pairs={{0,32},{32,64},{64,96},{96,0},{1,33},{33,65},{65,97},{97,1},{2,34}... | collective-permute-start | bytes 1179656 | tf_op jit(solution)/shard_map/ppermute | solution.py:25
  45.4 9.6 %copy-start.2 = (bf16[8,2,128,384]{3,2,1,0:T(8,128)(2,1)}, bf16[8,2,128,384]{3,2,1,0:T(8,128)(2,1)S(1)}, u32[]{:S(2)}) copy-start(bf16[8,2,128,384]{3,2,1,0:T(8,128)(2,1)S(1)} %bitcast_dynamic-update-slice_fusion.query_ref) | copy-start | bytes 4718596
  74.4 45.0 %copy-start.1 = (bf16[2,1,128,384]{3,2,1,0:T(8,128)(2,1)S(1)}, bf16[2,1,128,384]{3,2,1,0:T(8,128)(2,1)}, u32[]{:S(2)}) copy-start(bf16[2,1,128,384]{3,2,1,0:T(8,128)(2,1)} %param.6) | copy-start | bytes 589828
  76.4 7.1 %collective-permute-start.14 = (bf16[2,130,384]{2,1,0:T(8,128)(2,1)S(1)}, bf16[2,130,384]{2,1,0:T(8,128)(2,1)S(1)}, u32[]{:S(2)}, u32[]{:S(2)}) collective-permute-start(bf16[2,130,384]{2,1,0:T(8,128)(2,1)S(1)} %pad_maximum_fusion.2), channel_id=1, source_target_pairs={{0,4},{4,8},{8,12},{12,16},{16,20},{20,24},{24,28},{28,0},{1,5},{5... | collective-permute-start | bytes 599048 | tf_op jit(solution)/shard_map/ppermute | solution.py:25
  84.8 7.1 %collective-permute-start.15 = (bf16[2,130,384]{2,1,0:T(8,128)(2,1)S(1)}, bf16[2,130,384]{2,1,0:T(8,128)(2,1)S(1)}, u32[]{:S(2)}, u32[]{:S(2)}) collective-permute-start(bf16[2,130,384]{2,1,0:T(8,128)(2,1)S(1)} %pad_maximum_fusion.3), channel_id=1, source_target_pairs={{0,4},{4,8},{8,12},{12,16},{16,20},{20,24},{24,28},{28,0},{1,5},{5... | collective-permute-start | bytes 599048 | tf_op jit(solution)/shard_map/ppermute | solution.py:25
  92.1 7.4 %collective-permute-start.18 = (bf16[2,130,384]{2,1,0:T(8,128)(2,1)S(1)}, bf16[2,130,384]{2,1,0:T(8,128)(2,1)S(1)}, u32[]{:S(2)}, u32[]{:S(2)}) collective-permute-start(bf16[2,130,384]{2,1,0:T(8,128)(2,1)S(1)} %pad_maximum_fusion.6), channel_id=1, source_target_pairs={{0,28},{4,0},{8,4},{12,8},{16,12},{20,16},{24,20},{28,24},{1,29},{... | collective-permute-start | bytes 599048 | tf_op jit(solution)/shard_map/ppermute | solution.py:25
  101.1 7.9 %collective-permute-start.16 = (bf16[2,130,384]{2,1,0:T(8,128)(2,1)S(1)}, bf16[2,130,384]{2,1,0:T(8,128)(2,1)S(1)}, u32[]{:S(2)}, u32[]{:S(2)}) collective-permute-start(bf16[2,130,384]{2,1,0:T(8,128)(2,1)S(1)} %pad_maximum_fusion.4), channel_id=1, source_target_pairs={{0,4},{4,8},{8,12},{12,16},{16,20},{20,24},{24,28},{28,0},{1,5},{5... | collective-permute-start | bytes 599048 | tf_op jit(solution)/shard_map/ppermute | solution.py:25
  101.2 7.8 %collective-permute-start.19 = (bf16[2,130,384]{2,1,0:T(8,128)(2,1)S(1)}, bf16[2,130,384]{2,1,0:T(8,128)(2,1)S(1)}, u32[]{:S(2)}, u32[]{:S(2)}) collective-permute-start(bf16[2,130,384]{2,1,0:T(8,128)(2,1)S(1)} %pad_maximum_fusion.7), channel_id=1, source_target_pairs={{0,28},{4,0},{8,4},{12,8},{16,12},{20,16},{24,20},{28,24},{1,29},{... | collective-permute-start | bytes 599048 | tf_op jit(solution)/shard_map/ppermute | solution.py:25
  110.6 7.1 %collective-permute-start.17 = (bf16[2,130,384]{2,1,0:T(8,128)(2,1)S(1)}, bf16[2,130,384]{2,1,0:T(8,128)(2,1)S(1)}, u32[]{:S(2)}, u32[]{:S(2)}) collective-permute-start(bf16[2,130,384]{2,1,0:T(8,128)(2,1)S(1)} %pad_maximum_fusion.5), channel_id=1, source_target_pairs={{0,4},{4,8},{8,12},{12,16},{16,20},{20,24},{24,28},{28,0},{1,5},{5... | collective-permute-start | bytes 599048 | tf_op jit(solution)/shard_map/ppermute | solution.py:25
  111.2 8.1 %collective-permute-start.20 = (bf16[2,130,384]{2,1,0:T(8,128)(2,1)S(1)}, bf16[2,130,384]{2,1,0:T(8,128)(2,1)S(1)}, u32[]{:S(2)}, u32[]{:S(2)}) collective-permute-start(bf16[2,130,384]{2,1,0:T(8,128)(2,1)S(1)} %pad_maximum_fusion.8), channel_id=1, source_target_pairs={{0,28},{4,0},{8,4},{12,8},{16,12},{20,16},{24,20},{28,24},{1,29},{... | collective-permute-start | bytes 599048 | tf_op jit(solution)/shard_map/ppermute | solution.py:25
  121.2 12.9 %collective-permute-start.21 = (bf16[2,1,128,384]{3,2,0,1:T(8,128)(2,1)S(1)}, bf16[2,1,128,384]{3,2,0,1:T(8,128)(2,1)S(1)}, u32[]{:S(2)}, u32[]{:S(2)}) collective-permute-start(bf16[2,1,128,384]{3,2,0,1:T(8,128)(2,1)S(1)} %multiply_convert_fusion), channel_id=1, source_target_pairs={{0,129},{1,130},{2,131},{3,132},{4,133},{5,134},{6,135},{7,136},{8... | collective-permute-start | bytes 589832 | tf_op jit(solution)/shard_map/ppermute | solution.py:220
  122.5 11.6 %collective-permute-start.24 = (bf16[2,1,128,384]{3,2,0,1:T(8,128)(2,1)S(1)}, bf16[2,1,128,384]{3,2,0,1:T(8,128)(2,1)S(1)}, u32[]{:S(2)}, u32[]{:S(2)}) collective-permute-start(bf16[2,1,128,384]{3,2,0,1:T(8,128)(2,1)S(1)} %multiply_convert_fusion), channel_id=1, source_target_pairs={{1,128},{2,129},{3,130},{4,131},{5,132},{6,133},{7,134},{8,135},{9... | collective-permute-start | bytes 589832 | tf_op jit(solution)/shard_map/ppermute | solution.py:221
  123.8 20.1 %collective-permute-start.25 = (bf16[2,1,128,384]{3,2,0,1:T(8,128)(2,1)S(1)}, bf16[2,1,128,384]{3,2,0,1:T(8,128)(2,1)S(1)}, u32[]{:S(2)}, u32[]{:S(2)}) collective-permute-start(bf16[2,1,128,384]{3,2,0,1:T(8,128)(2,1)S(1)} %multiply_convert_fusion), channel_id=1, source_target_pairs={{1,0},{2,1},{3,2},{4,3},{5,4},{6,5},{7,6},{8,7},{9,8},{10,9},{11,1... | collective-permute-start | bytes 589832 | tf_op jit(solution)/shard_map/ppermute | solution.py:113
  130.8 13.2 %collective-permute-start.23 = (bf16[2,1,128,384]{3,2,0,1:T(8,128)(2,1)S(1)}, bf16[2,1,128,384]{3,2,0,1:T(8,128)(2,1)S(1)}, u32[]{:S(2)}, u32[]{:S(2)}) collective-permute-start(bf16[2,1,128,384]{3,2,0,1:T(8,128)(2,1)S(1)} %multiply_convert_fusion), channel_id=1, source_target_pairs={{0,128},{1,129},{2,130},{3,131},{4,132},{5,133},{6,134},{7,135},{8... | collective-permute-start | bytes 589832 | tf_op jit(solution)/shard_map/ppermute | solution.py:219
  132.1 11.8 %collective-permute-start.22 = (bf16[2,1,128,384]{3,2,0,1:T(8,128)(2,1)S(1)}, bf16[2,1,128,384]{3,2,0,1:T(8,128)(2,1)S(1)}, u32[]{:S(2)}, u32[]{:S(2)}) collective-permute-start(bf16[2,1,128,384]{3,2,0,1:T(8,128)(2,1)S(1)} %multiply_convert_fusion), channel_id=1, source_target_pairs={{0,1},{1,2},{2,3},{3,4},{4,5},{5,6},{6,7},{7,8},{8,9},{9,10},{10,1... | collective-permute-start | bytes 589832 | tf_op jit(solution)/shard_map/ppermute | solution.py:113
  134.1 11.8 %slice-start = ((s8[7962624]{0:T(1024)(128)(4,1)}), s8[4194304]{0:T(1024)(128)(4,1)S(1)}, s32[]{:S(2)}) async-start(s8[7962624]{0:T(1024)(128)(4,1)} %bitcast.331), calls=%async_computation | async-start | bytes 8388608
  144.7 2.1 %slice-start.1 = ((s8[7962624]{0:T(1024)(128)(4,1)}), s8[3768320]{0:T(1024)(128)(4,1)S(1)}, s32[]{:S(2)}) async-start(s8[7962624]{0:T(1024)(128)(4,1)} %bitcast.331), calls=%async_computation.1 | async-start | bytes 7536640

commit v5 on v4

--- a/solution.py
+++ b/solution.py
@@ -114,16 +114,22 @@
 
 
 def attention_kernel(
-    scale, query_ref, token_ref, key_w_ref, value_w_ref,
+    scale, query_ref, first_ref, second_ref, key_w_ref, value_w_ref,
     high_ref, total_ref, summed_ref, short_ref, key_scr, value_scr,
 ):
     width = key_scr.shape[-1]
+    half = key_scr.shape[0] // 2
 
     @pl.when(pl.program_id(1) == 0)
     def _():
-        tokens = token_ref[...].reshape(-1, width)
-        key_scr[...] = jnp.dot(tokens, key_w_ref[...], preferred_element_type=jnp.float32).astype(jnp.bfloat16)
-        value_scr[...] = jnp.dot(tokens, value_w_ref[...], preferred_element_type=jnp.float32).astype(jnp.bfloat16)
+        for lo, token_ref in ((0, first_ref), (half, second_ref)):
+            tokens = token_ref[...].reshape(-1, width)
+            key_scr[lo : lo + half] = jnp.dot(
+                tokens, key_w_ref[...], preferred_element_type=jnp.float32
+            ).astype(jnp.bfloat16)
+            value_scr[lo : lo + half] = jnp.dot(
+                tokens, value_w_ref[...], preferred_element_type=jnp.float32
+            ).astype(jnp.bfloat16)
 
     query = query_ref[...].reshape(-1, width)
     scores = lax.dot_general(
@@ -140,9 +146,9 @@
     short_ref[0] = summed.astype(jnp.bfloat16)
 
 
-def attention(query_blocks, token_blocks, key_weight, value_weight):
+def attention(query_blocks, first_blocks, second_blocks, key_weight, value_weight):
     query_count, frames, rows, width = query_blocks.shape
-    key_count = token_blocks.shape[0]
+    key_count = first_blocks.shape[0]
     per_tile = 4
     tile = per_tile * rows
     queries = query_count * rows
@@ -157,7 +163,8 @@
         grid=(frames, query_count // per_tile),
         in_specs=[
             pl.BlockSpec((per_tile, None, rows, width), lambda f, i: (i, f, 0, 0)),
-            pl.BlockSpec((key_count, None, rows, width), lambda f, i: (0, f, 0, 0)),
+            pl.BlockSpec((key_count, None, rows // 2, width), lambda f, i: (0, f, 0, 0)),
+            pl.BlockSpec((key_count, None, rows // 2, width), lambda f, i: (0, f, 0, 0)),
             weight_spec,
             weight_spec,
         ],
@@ -177,7 +184,7 @@
             transcendentals=frames * queries * keys,
             bytes_accessed=2 * frames * (queries + keys) * width + 6 * frames * queries * width,
         ),
-    )(query_blocks, token_blocks, key_weight, value_weight)
+    )(query_blocks, first_blocks, second_blocks, key_weight, value_weight)
 
 
 def per_device(features, query_weight, key_weight, value_weight, out_weight, conv_weight):
@@ -190,11 +197,15 @@
 
     query = project(flat, query_weight).reshape(frames, count, width)
     query_rel = ring_gather(query, "z")
-    inner = jnp.stack(ring_gather(normed.reshape(frames, count, width), "y"))
-    outer = jnp.stack(ring_gather(inner, "x", halve=True))
-    token_blocks = outer.reshape(-1, *outer.shape[2:])
+    tokens = normed.reshape(frames, count, width)
+    half = count // 2
+    chains = []
+    for part, (first, second) in ((tokens[:, :half], ("y", "x")), (tokens[:, half:], ("x", "y"))):
+        inner = jnp.stack(ring_gather(part, first))
+        outer = jnp.stack(ring_gather(inner, second, halve=True))
+        chains.append(outer.reshape(-1, *outer.shape[2:]))
     query_blocks = jnp.stack(query_rel)
-    highest, total, summed, short = attention(query_blocks, token_blocks, key_weight, value_weight)
+    highest, total, summed, short = attention(query_blocks, chains[0], chains[1], key_weight, value_weight)
     highest, total = highest[:, 0], total[:, 0]
 
     blocks = len(query_rel)

time: 151 us -> 150 us (level)
  waiting for transfers between devices: 66.2 us -> 56.5 us
  starting transfers between devices: 41.4 us -> 48.4 us
    ppermute x21 -> x28, waiting for transfers between devices: 56.4 us -> 46.8 us  [ring_shift(): return lax.ppermute(block, axis, [(i, (i + step) % n) for i in range(n)])]
    ppermute x21 -> x28, starting transfers between devices: 28.6 us -> 36 us  [ring_shift(): return lax.ppermute(block, axis, [(i, (i + step) % n) for i in range(n)])]
    another operation x4 -> x6, other arithmetic: 3.16 us -> 3.2 us  [per_device(): outer = jnp.stack(ring_gather(inner, second, halve=True))]
  transfers between devices with their start and end apart: 26 -> 33, of which waited for: 14 -> 15; matrix products, arithmetic and copies ran while one was open for 2% -> 4% of each run, Pallas kernels for 0% -> 0%
where the time goes in v5:
time: 150 us; the launch traced here: 149 us
  waiting for transfers between devices  56.5 us (38%)
  starting transfers between devices  48.4 us (32%)
  Pallas kernels  19.4 us (13%)
  other arithmetic  11.6 us (8%)
  matrix products  6.39 us (4%)
  local copies, waits for them, and re-layouts  5.96 us (4%)
    ppermute x28, waiting for transfers between devices, ring_shift(): return lax.ppermute(block, axis, [(i, (i + step) % n) for i in range(n)])  46.8 us
    ppermute x28, starting transfers between devices, ring_shift(): return lax.ppermute(block, axis, [(i, (i + step) % n) for i in range(n)])  36 us
    pallas_call x1, Pallas kernels, attention(): pl.pallas_call(functools.partial(attention_kernel, scale), grid=(frames,...  19.4 us
    ppermute x2, waiting for transfers between devices, row_shift(): return lax.ppermute(block, ROW_AXES, route)  9.76 us
    ppermute x2, starting transfers between devices, row_shift(): return lax.ppermute(block, ROW_AXES, route)  8.5 us
    unnamed x47, local copies, waits for them, and re-layouts  4.14 us
    convert_element_type x3, other arithmetic, pack(): return jnp.concatenate([summed.astype(jnp.bfloat16), stats], axis=1)  3.81 us
    dot_general x1, matrix products, per_device(): jnp.dot(columns, conv_weight.reshape(27 * width, width), preferred_elemen...  3.61 us
  transfers between devices with their start and end apart: 33, of which 15 were waited for; matrix products, arithmetic and copies ran while one was open for 4% of the time, Pallas kernels for 0%

profile of v5, /device:TPU:2, one launch (start us, length us, event | category | flops | bytes accessed | tf_op | source)
XLA Modules:
  0.0 149.0 jit_solution(14092687387140559258)
XLA Ops:
  0.0 1.1 fusion.21
  1.1 1.0 fusion.104
  2.2 2.3 %collective-permute-start.14 = (bf16[2,64,384]{2,1,0:T(8,128)(2,1)S(1)}, bf16[2,64,384]{2,1,0:T(8,128)(2,1)S(1)}, u32[]{:S(2)}, u32[]{:S(2)}) collective-permute-start(bf16[2,64,384]{2,1,0:T(8,128)(2,1)S(1)} %get-tuple-element.60), channel_id=1, source_target_pairs={{0,96},{32,0},{64,32},{96,64},{1,97},{33,1},{65,33},{97,65},{2,98}... | collective-permute-start | bytes 294920 | tf_op jit(solution)/shard_map/ppermute | solution.py:25
  4.5 1.4 collective-permute-start.8
  5.9 1.0 fusion.22
  6.9 2.2 %collective-permute-done.15 = bf16[2,64,384]{2,1,0:T(8,128)(2,1)S(1)} collective-permute-done((bf16[2,64,384]{2,1,0:T(8,128)(2,1)S(1)}, bf16[2,64,384]{2,1,0:T(8,128)(2,1)S(1)}, u32[]{:S(2)}, u32[]{:S(2)}) %collective-permute-start.15) | collective-permute-done | bytes 98336 | tf_op jit(solution)/shard_map/ppermute | solution.py:25
  9.1 1.2 convolution_convert_fusion
  10.4 1.8 %collective-permute-start.3 = (bf16[2,128,384]{2,1,0:T(8,128)(2,1)S(1)}, bf16[2,128,384]{2,1,0:T(8,128)(2,1)S(1)}, u32[]{:S(2)}, u32[]{:S(2)}) collective-permute-start(bf16[2,128,384]{2,1,0:T(8,128)(2,1)S(1)} %bitcast.337), channel_id=1, source_target_pairs={{0,4},{4,8},{8,12},{12,16},{16,20},{20,24},{24,28},{28,0},{1,5},{5... | collective-permute-start | bytes 589832 | tf_op jit(solution)/shard_map/ppermute | solution.py:25
  12.1 3.0 %collective-permute-start.7 = (bf16[2,64,384]{2,1,0:T(8,128)(2,1)S(1)}, bf16[2,64,384]{2,1,0:T(8,128)(2,1)S(1)}, u32[]{:S(2)}, u32[]{:S(2)}) collective-permute-start(bf16[2,64,384]{2,1,0:T(8,128)(2,1)S(1)} %get-tuple-element.61), channel_id=1, source_target_pairs={{0,3},{1,0},{2,1},{3,2},{4,7},{5,4},{6,5},{7,6},{8,11},{9,8},{10,9... | collective-permute-start | bytes 294920 | tf_op jit(solution)/shard_map/ppermute | solution.py:25
  15.2 4.0 %collective-permute-start = (bf16[2,128,384]{2,1,0:T(8,128)(2,1)S(1)}, bf16[2,128,384]{2,1,0:T(8,128)(2,1)S(1)}, u32[]{:S(2)}, u32[]{:S(2)}) collective-permute-start(bf16[2,128,384]{2,1,0:T(8,128)(2,1)S(1)} %bitcast.338), channel_id=1, source_target_pairs={{0,28},{4,0},{8,4},{12,8},{16,12},{20,16},{24,20},{28,24},{1,29},{... | collective-permute-start | bytes 589832 | tf_op jit(solution)/shard_map/ppermute | solution.py:25
  19.2 0.1 fusion.77
  19.3 3.3 %collective-permute-start.17 = (bf16[4,2,64,384]{3,2,1,0:T(8,128)(2,1)S(1)}, bf16[4,2,64,384]{3,2,1,0:T(8,128)(2,1)S(1)}, u32[]{:S(2)}, u32[]{:S(2)}) collective-permute-start(bf16[4,2,64,384]{3,2,1,0:T(8,128)(2,1)S(1)} %get-tuple-element.55), channel_id=1, source_target_pairs={{0,3},{1,0},{2,1},{3,2},{4,7},{5,4},{6,5},{7,6},{8,11},{9,8},{10,9... | collective-permute-start | bytes 1179656 | tf_op jit(solution)/shard_map/ppermute | solution.py:25
  22.6 0.1 collective-permute-start.18
  22.7 3.3 %collective-permute-done.9 = bf16[2,64,384]{2,1,0:T(8,128)(2,1)S(1)} collective-permute-done((bf16[2,64,384]{2,1,0:T(8,128)(2,1)S(1)}, bf16[2,64,384]{2,1,0:T(8,128)(2,1)S(1)}, u32[]{:S(2)}, u32[]{:S(2)}) %collective-permute-start.9) | collective-permute-done | bytes 98336 | tf_op jit(solution)/shard_map/ppermute | solution.py:25
  26.1 0.1 fusion.78
  26.2 2.6 %collective-permute-start.10 = (bf16[4,2,64,384]{3,2,1,0:T(8,128)(2,1)S(1)}, bf16[4,2,64,384]{3,2,1,0:T(8,128)(2,1)S(1)}, u32[]{:S(2)}, u32[]{:S(2)}) collective-permute-start(bf16[4,2,64,384]{3,2,1,0:T(8,128)(2,1)S(1)} %get-tuple-element.57), channel_id=1, source_target_pairs={{0,96},{32,0},{64,32},{96,64},{1,97},{33,1},{65,33},{97,65},{2,98}... | collective-permute-start | bytes 1179656 | tf_op jit(solution)/shard_map/ppermute | solution.py:25
  28.7 0.8 collective-permute-done.4
  29.5 0.7 collective-permute-start.1
  30.2 6.7 %collective-permute-done.1 = bf16[2,128,384]{2,1,0:T(8,128)(2,1)S(1)} collective-permute-done((bf16[2,128,384]{2,1,0:T(8,128)(2,1)S(1)}, bf16[2,128,384]{2,1,0:T(8,128)(2,1)S(1)}, u32[]{:S(2)}, u32[]{:S(2)}) %collective-permute-start.1) | collective-permute-done | bytes 196640 | tf_op jit(solution)/shard_map/ppermute | solution.py:25
  37.0 3.2 %collective-permute-start.2 = (bf16[2,128,384]{2,1,0:T(8,128)(2,1)S(1)}, bf16[2,128,384]{2,1,0:T(8,128)(2,1)S(1)}, u32[]{:S(2)}, u32[]{:S(2)}) collective-permute-start(bf16[2,128,384]{2,1,0:T(8,128)(2,1)S(1)} %collective-permute-done.1), channel_id=1, source_target_pairs={{0,28},{4,0},{8,4},{12,8},{16,12},{20,16},{24,20},{28,24},{1,29},{... | collective-permute-start | bytes 589832 | tf_op jit(solution)/shard_map/ppermute | solution.py:25
  40.3 0.1 collective-permute-start.20
  40.4 2.1 %collective-permute-start.19 = (bf16[2,2,64,384]{3,2,1,0:T(8,128)(2,1)S(1)}, bf16[2,2,64,384]{3,2,1,0:T(8,128)(2,1)S(1)}, u32[]{:S(2)}, u32[]{:S(2)}) collective-permute-start(bf16[2,2,64,384]{3,2,1,0:T(8,128)(2,1)S(1)} %slice.456), channel_id=1, source_target_pairs={{0,1},{1,2},{2,3},{3,0},{4,5},{5,6},{6,7},{7,4},{8,9},{9,10},{10,1... | collective-permute-start | bytes 589832 | tf_op jit(solution)/shard_map/ppermute | solution.py:25
  42.5 2.7 %collective-permute-start.13 = (bf16[2,2,64,384]{3,2,1,0:T(8,128)(2,1)S(1)}, bf16[2,2,64,384]{3,2,1,0:T(8,128)(2,1)S(1)}, u32[]{:S(2)}, u32[]{:S(2)}) collective-permute-start(bf16[2,2,64,384]{3,2,1,0:T(8,128)(2,1)S(1)} %slice.454), channel_id=1, source_target_pairs={{0,96},{32,0},{64,32},{96,64},{1,97},{33,1},{65,33},{97,65},{2,98}... | collective-permute-start | bytes 589832 | tf_op jit(solution)/shard_map/ppermute | solution.py:25
  45.3 0.4 collective-permute-done.5
  45.7 1.3 collective-permute-start.12
  47.1 0.3 collective-permute-done.19
  47.4 1.5 %pad_maximum_fusion.1 = bf16[4,4,2,64,384]{4,3,2,1,0:T(8,128)(2,1)} fusion(bf16[1,4,2,64,384]{4,3,2,1,0:T(8,128)(2,1)S(1)} %bitcast.335, bf16[1,4,2,64,384]{4,3,2,1,0:T(8,128)(2,1)S(1)} %maximum_bitcast_fusion.1, bf16[1,4,2,64,384]{4,3,2,1,0:T(8,128)(2,1)S(1)} %bitcast.333, bf16[1,4,2,64,384]{4,3,2,1,0:T(8,128)(2,1)S(1)} %get-tuple-element.54), kind=kLoop, calls=%fused_computation.6 | loop fusion | flops 2359296 | bytes 3145728 | tf_op jit(solution)/shard_map/stack | solution.py:205
  48.9 3.5 %collective-permute-done.12 = bf16[2,2,64,384]{3,2,1,0:T(8,128)(2,1)S(1)} collective-permute-done((bf16[2,2,64,384]{3,2,1,0:T(8,128)(2,1)S(1)}, bf16[2,2,64,384]{3,2,1,0:T(8,128)(2,1)S(1)}, u32[]{:S(2)}, u32[]{:S(2)}) %collective-permute-start.12) | collective-permute-done | bytes 196640 | tf_op jit(solution)/shard_map/ppermute | solution.py:25
  52.4 1.4 pad_maximum_fusion
  53.9 0.1 collective-permute-done.6
  54.1 1.2 copy-done.2
  55.3 19.4 %shard_map.64 = (f32[2,1,1024]{2,1,0:T(1,128)}, f32[2,1,1024]{2,1,0:T(1,128)}, f32[2,1024,384]{2,1,0:T(8,128)}, bf16[2,1024,384]{2,1,0:T(8,128)(2,1)}) custom-call(bf16[8,2,128,384]{3,2,1,0:T(8,128)(2,1)} %copy-done.2, bf16[16,2,64,384]{3,2,1,0:T(8,128)(2,1)} %bitcast.332, bf16[16,2,64,384]{3,2,1,0:T(8,128)(2,1)} %bitcast.331, bf16[384,384]{1,0:T(8,128)(2,1)} %key_w_ref.1, ...), custom_call_target="tpu_custom_call" | custom-call | flops 8858370048 | bytes 9437184 | tf_op jit(solution)/shard_map/pallas_call | solution.py:161
  74.6 1.1 fusion.93
  75.7 0.7 copy_bitcast_fusion
  76.6 0.1 collective-permute-start.21
  76.7 7.2 %collective-permute-done.21 = bf16[2,130,384]{2,1,0:T(8,128)(2,1)S(1)} collective-permute-done((bf16[2,130,384]{2,1,0:T(8,128)(2,1)S(1)}, bf16[2,130,384]{2,1,0:T(8,128)(2,1)S(1)}, u32[]{:S(2)}, u32[]{:S(2)}) %collective-permute-start.21) | collective-permute-done | bytes 199712 | tf_op jit(solution)/shard_map/ppermute | solution.py:25
  84.0 1.1 add_convert_fusion.4
  85.2 0.1 collective-permute-start.22
  85.3 7.0 %collective-permute-done.22 = bf16[2,130,384]{2,1,0:T(8,128)(2,1)S(1)} collective-permute-done((bf16[2,130,384]{2,1,0:T(8,128)(2,1)S(1)}, bf16[2,130,384]{2,1,0:T(8,128)(2,1)S(1)}, u32[]{:S(2)}, u32[]{:S(2)}) %collective-permute-start.22) | collective-permute-done | bytes 199712 | tf_op jit(solution)/shard_map/ppermute | solution.py:25
  92.5 0.3 collective-permute-start.25
  92.9 5.7 %collective-permute-done.25 = bf16[2,130,384]{2,1,0:T(8,128)(2,1)S(1)} collective-permute-done((bf16[2,130,384]{2,1,0:T(8,128)(2,1)S(1)}, bf16[2,130,384]{2,1,0:T(8,128)(2,1)S(1)}, u32[]{:S(2)}, u32[]{:S(2)}) %collective-permute-start.25) | collective-permute-done | bytes 199712 | tf_op jit(solution)/shard_map/ppermute | solution.py:25
  98.7 1.3 add_convert_fusion.3
  100.1 0.1 collective-permute-start.23
  100.3 3.3 %collective-permute-start.26 = (bf16[2,130,384]{2,1,0:T(8,128)(2,1)S(1)}, bf16[2,130,384]{2,1,0:T(8,128)(2,1)S(1)}, u32[]{:S(2)}, u32[]{:S(2)}) collective-permute-start(bf16[2,130,384]{2,1,0:T(8,128)(2,1)S(1)} %pad_maximum_fusion.9), channel_id=1, source_target_pairs={{0,28},{4,0},{8,4},{12,8},{16,12},{20,16},{24,20},{28,24},{1,29},{... | collective-permute-start | bytes 599048 | tf_op jit(solution)/shard_map/ppermute | solution.py:25
  103.6 3.6 %collective-permute-done.23 = bf16[2,130,384]{2,1,0:T(8,128)(2,1)S(1)} collective-permute-done((bf16[2,130,384]{2,1,0:T(8,128)(2,1)S(1)}, bf16[2,130,384]{2,1,0:T(8,128)(2,1)S(1)}, u32[]{:S(2)}, u32[]{:S(2)}) %collective-permute-start.23) | collective-permute-done | bytes 199712 | tf_op jit(solution)/shard_map/ppermute | solution.py:25
  107.5 1.3 add_convert_fusion.2
  108.9 1.2 collective-permute-start.24
  110.1 2.3 %collective-permute-start.27 = (bf16[2,130,384]{2,1,0:T(8,128)(2,1)S(1)}, bf16[2,130,384]{2,1,0:T(8,128)(2,1)S(1)}, u32[]{:S(2)}, u32[]{:S(2)}) collective-permute-start(bf16[2,130,384]{2,1,0:T(8,128)(2,1)S(1)} %pad_maximum_fusion.10), channel_id=1, source_target_pairs={{0,28},{4,0},{8,4},{12,8},{16,12},{20,16},{24,20},{28,24},{1,29},{... | collective-permute-start | bytes 599048 | tf_op jit(solution)/shard_map/ppermute | solution.py:25
  112.4 3.6 %collective-permute-done.24 = bf16[2,130,384]{2,1,0:T(8,128)(2,1)S(1)} collective-permute-done((bf16[2,130,384]{2,1,0:T(8,128)(2,1)S(1)}, bf16[2,130,384]{2,1,0:T(8,128)(2,1)S(1)}, u32[]{:S(2)}, u32[]{:S(2)}) %collective-permute-start.24) | collective-permute-done | bytes 199712 | tf_op jit(solution)/shard_map/ppermute | solution.py:25
  116.0 2.3 %collective-permute-done.27 = bf16[2,130,384]{2,1,0:T(8,128)(2,1)S(1)} collective-permute-done((bf16[2,130,384]{2,1,0:T(8,128)(2,1)S(1)}, bf16[2,130,384]{2,1,0:T(8,128)(2,1)S(1)}, u32[]{:S(2)}, u32[]{:S(2)}) %collective-permute-start.27) | collective-permute-done | bytes 199712 | tf_op jit(solution)/shard_map/ppermute | solution.py:25
  118.5 1.5 %multiply_reduce_fusion = (f32[2,128]{1,0:T(2,128)S(1)}, f32[2,1,128,384]{3,2,0,1:T(8,128)S(1)}) fusion(bf16[384,384]{1,0:T(8,128)(2,1)S(1)} %copy-done, f32[2,1024,384]{2,1,0:T(8,128)} %get-tuple-element.12, bf16[2,130,384]{2,1,0:T(8,128)(2,1)S(1)} %collective-permute-done.27, bf16[2,130,384]{2,1,0:T(8,128)(2,1)S(1)} %collective-permute-done.24, ...), kind=kOutput, calls=%fused_computation.30 | convolution fusion | flops 77070080 | bytes 1677312 | tf_op jit(solution)/shard_map/dot_general | solution.py:221
  120.0 0.2 multiply_convert_fusion
  120.2 1.3 collective-permute-start.28
  121.5 1.3 collective-permute-start.31
  122.8 6.6 %collective-permute-start.32 = (bf16[2,1,128,384]{3,2,0,1:T(8,128)(2,1)S(1)}, bf16[2,1,128,384]{3,2,0,1:T(8,128)(2,1)S(1)}, u32[]{:S(2)}, u32[]{:S(2)}) collective-permute-start(bf16[2,1,128,384]{3,2,0,1:T(8,128)(2,1)S(1)} %multiply_convert_fusion), channel_id=1, source_target_pairs={{1,0},{2,1},{3,2},{4,3},{5,4},{6,5},{7,6},{8,7},{9,8},{10,9},{11,1... | collective-permute-start | bytes 589832 | tf_op jit(solution)/shard_map/ppermute | solution.py:113
  129.4 1.3 collective-permute-start.30
  130.7 1.9 %collective-permute-start.29 = (bf16[2,1,128,384]{3,2,0,1:T(8,128)(2,1)S(1)}, bf16[2,1,128,384]{3,2,0,1:T(8,128)(2,1)S(1)}, u32[]{:S(2)}, u32[]{:S(2)}) collective-permute-start(bf16[2,1,128,384]{3,2,0,1:T(8,128)(2,1)S(1)} %multiply_convert_fusion), channel_id=1, source_target_pairs={{0,1},{1,2},{2,3},{3,4},{4,5},{5,6},{6,7},{7,8},{8,9},{9,10},{10,1... | collective-permute-start | bytes 589832 | tf_op jit(solution)/shard_map/ppermute | solution.py:113
  132.8 9.8 %collective-permute-done.29 = bf16[2,1,128,384]{3,2,0,1:T(8,128)(2,1)S(1)} collective-permute-done((bf16[2,1,128,384]{3,2,0,1:T(8,128)(2,1)S(1)}, bf16[2,1,128,384]{3,2,0,1:T(8,128)(2,1)S(1)}, u32[]{:S(2)}, u32[]{:S(2)}) %collective-permute-start.29) | collective-permute-done | bytes 196640 | tf_op jit(solution)/shard_map/ppermute | solution.py:113
  142.6 0.3 select_maximum_fusion
  143.0 0.1 slice_dynamic-update-slice_fusion.18
  143.2 0.1 slice_dynamic-update-slice_fusion.16
  144.0 0.2 constant_dynamic-update-slice_fusion.48
  144.5 0.9 slice-done.1
  145.4 3.6 %fusion.18 = bf16[2,1,128,384]{3,2,1,0:T(8,128)(2,1)} fusion(f32[2,1,128,384]{3,2,0,1:T(8,128)S(1)} %get-tuple-element.109, bf16[10368,384,1]{1,0,2:T(8,128)(2,1)S(1)} %bitcast.349, bf16[2,1,128,10368]{3,2,0,1:T(8,128)(2,1)S(1)} %slice_dynamic-update-slice_fusion), kind=kOutput, calls=%fused_computation.20 | convolution fusion | flops 2038628352 | bytes 13860864 | tf_op jit(solution)/shard_map/dot_general | solution.py:250
  (161 shorter events, 2.8 us)
Async XLA Ops:
  0.0 118.4 %copy-start = (bf16[384,384]{1,0:T(8,128)(2,1)S(1)}, bf16[384,384]{1,0:T(8,128)(2,1)}, u32[]{:S(2)}) copy-start(bf16[384,384]{1,0:T(8,128)(2,1)} %param.10) | copy-start | bytes 884740
  2.2 13.0 %collective-permute-start.14 = (bf16[2,64,384]{2,1,0:T(8,128)(2,1)S(1)}, bf16[2,64,384]{2,1,0:T(8,128)(2,1)S(1)}, u32[]{:S(2)}, u32[]{:S(2)}) collective-permute-start(bf16[2,64,384]{2,1,0:T(8,128)(2,1)S(1)} %get-tuple-element.60), channel_id=1, source_target_pairs={{0,96},{32,0},{64,32},{96,64},{1,97},{33,1},{65,33},{97,65},{2,98}... | collective-permute-start | bytes 294920 | tf_op jit(solution)/shard_map/ppermute | solution.py:25
  4.5 4.6 %collective-permute-start.15 = (bf16[2,64,384]{2,1,0:T(8,128)(2,1)S(1)}, bf16[2,64,384]{2,1,0:T(8,128)(2,1)S(1)}, u32[]{:S(2)}, u32[]{:S(2)}) collective-permute-start(bf16[2,64,384]{2,1,0:T(8,128)(2,1)S(1)} %get-tuple-element.60), channel_id=1, source_target_pairs={{0,32},{32,64},{64,96},{96,0},{1,33},{33,65},{65,97},{97,1},{2,34}... | collective-permute-start | bytes 294920 | tf_op jit(solution)/shard_map/ppermute | solution.py:25
  4.5 14.7 %collective-permute-start.8 = (bf16[2,64,384]{2,1,0:T(8,128)(2,1)S(1)}, bf16[2,64,384]{2,1,0:T(8,128)(2,1)S(1)}, u32[]{:S(2)}, u32[]{:S(2)}) collective-permute-start(bf16[2,64,384]{2,1,0:T(8,128)(2,1)S(1)} %get-tuple-element.61), channel_id=1, source_target_pairs={{0,1},{1,2},{2,3},{3,0},{4,5},{5,6},{6,7},{7,4},{8,9},{9,10},{10,1... | collective-permute-start | bytes 294920 | tf_op jit(solution)/shard_map/ppermute | solution.py:25
  9.1 10.1 %collective-permute-start.16 = (bf16[2,64,384]{2,1,0:T(8,128)(2,1)S(1)}, bf16[2,64,384]{2,1,0:T(8,128)(2,1)S(1)}, u32[]{:S(2)}, u32[]{:S(2)}) collective-permute-start(bf16[2,64,384]{2,1,0:T(8,128)(2,1)S(1)} %collective-permute-done.15), channel_id=1, source_target_pairs={{0,32},{32,64},{64,96},{96,0},{1,33},{33,65},{65,97},{97,1},{2,34}... | collective-permute-start | bytes 294920 | tf_op jit(solution)/shard_map/ppermute | solution.py:25
  10.4 12.2 %collective-permute-start.3 = (bf16[2,128,384]{2,1,0:T(8,128)(2,1)S(1)}, bf16[2,128,384]{2,1,0:T(8,128)(2,1)S(1)}, u32[]{:S(2)}, u32[]{:S(2)}) collective-permute-start(bf16[2,128,384]{2,1,0:T(8,128)(2,1)S(1)} %bitcast.337), channel_id=1, source_target_pairs={{0,4},{4,8},{8,12},{12,16},{16,20},{20,24},{24,28},{28,0},{1,5},{5... | collective-permute-start | bytes 589832 | tf_op jit(solution)/shard_map/ppermute | solution.py:25
  12.1 10.5 %collective-permute-start.7 = (bf16[2,64,384]{2,1,0:T(8,128)(2,1)S(1)}, bf16[2,64,384]{2,1,0:T(8,128)(2,1)S(1)}, u32[]{:S(2)}, u32[]{:S(2)}) collective-permute-start(bf16[2,64,384]{2,1,0:T(8,128)(2,1)S(1)} %get-tuple-element.61), channel_id=1, source_target_pairs={{0,3},{1,0},{2,1},{3,2},{4,7},{5,4},{6,5},{7,6},{8,11},{9,8},{10,9... | collective-permute-start | bytes 294920 | tf_op jit(solution)/shard_map/ppermute | solution.py:25
  15.2 13.6 %collective-permute-start = (bf16[2,128,384]{2,1,0:T(8,128)(2,1)S(1)}, bf16[2,128,384]{2,1,0:T(8,128)(2,1)S(1)}, u32[]{:S(2)}, u32[]{:S(2)}) collective-permute-start(bf16[2,128,384]{2,1,0:T(8,128)(2,1)S(1)} %bitcast.338), channel_id=1, source_target_pairs={{0,28},{4,0},{8,4},{12,8},{16,12},{20,16},{24,20},{28,24},{1,29},{... | collective-permute-start | bytes 589832 | tf_op jit(solution)/shard_map/ppermute | solution.py:25
  19.2 6.9 %collective-permute-start.9 = (bf16[2,64,384]{2,1,0:T(8,128)(2,1)S(1)}, bf16[2,64,384]{2,1,0:T(8,128)(2,1)S(1)}, u32[]{:S(2)}, u32[]{:S(2)}) collective-permute-start(bf16[2,64,384]{2,1,0:T(8,128)(2,1)S(1)} %collective-permute-done.8), channel_id=1, source_target_pairs={{0,1},{1,2},{2,3},{3,0},{4,5},{5,6},{6,7},{7,4},{8,9},{9,10},{10,1... | collective-permute-start | bytes 294920 | tf_op jit(solution)/shard_map/ppermute | solution.py:25
  19.3 17.7 %collective-permute-start.17 = (bf16[4,2,64,384]{3,2,1,0:T(8,128)(2,1)S(1)}, bf16[4,2,64,384]{3,2,1,0:T(8,128)(2,1)S(1)}, u32[]{:S(2)}, u32[]{:S(2)}) collective-permute-start(bf16[4,2,64,384]{3,2,1,0:T(8,128)(2,1)S(1)} %get-tuple-element.55), channel_id=1, source_target_pairs={{0,3},{1,0},{2,1},{3,2},{4,7},{5,4},{6,5},{7,6},{8,11},{9,8},{10,9... | collective-permute-start | bytes 1179656 | tf_op jit(solution)/shard_map/ppermute | solution.py:25
  22.6 6.9 %collective-permute-start.4 = (bf16[2,128,384]{2,1,0:T(8,128)(2,1)S(1)}, bf16[2,128,384]{2,1,0:T(8,128)(2,1)S(1)}, u32[]{:S(2)}, u32[]{:S(2)}) collective-permute-start(bf16[2,128,384]{2,1,0:T(8,128)(2,1)S(1)} %collective-permute-done.3), channel_id=1, source_target_pairs={{0,4},{4,8},{8,12},{12,16},{16,20},{20,24},{24,28},{28,0},{1,5},{5... | collective-permute-start | bytes 589832 | tf_op jit(solution)/shard_map/ppermute | solution.py:25
  22.6 17.6 %collective-permute-start.18 = (bf16[4,2,64,384]{3,2,1,0:T(8,128)(2,1)S(1)}, bf16[4,2,64,384]{3,2,1,0:T(8,128)(2,1)S(1)}, u32[]{:S(2)}, u32[]{:S(2)}) collective-permute-start(bf16[4,2,64,384]{3,2,1,0:T(8,128)(2,1)S(1)} %get-tuple-element.55), channel_id=1, source_target_pairs={{0,1},{1,2},{2,3},{3,0},{4,5},{5,6},{6,7},{7,4},{8,9},{9,10},{10,1... | collective-permute-start | bytes 1179656 | tf_op jit(solution)/shard_map/ppermute | solution.py:25
  26.2 14.2 %collective-permute-start.10 = (bf16[4,2,64,384]{3,2,1,0:T(8,128)(2,1)S(1)}, bf16[4,2,64,384]{3,2,1,0:T(8,128)(2,1)S(1)}, u32[]{:S(2)}, u32[]{:S(2)}) collective-permute-start(bf16[4,2,64,384]{3,2,1,0:T(8,128)(2,1)S(1)} %get-tuple-element.57), channel_id=1, source_target_pairs={{0,96},{32,0},{64,32},{96,64},{1,97},{33,1},{65,33},{97,65},{2,98}... | collective-permute-start | bytes 1179656 | tf_op jit(solution)/shard_map/ppermute | solution.py:25
  28.7 13.8 %collective-permute-start.11 = (bf16[4,2,64,384]{3,2,1,0:T(8,128)(2,1)S(1)}, bf16[4,2,64,384]{3,2,1,0:T(8,128)(2,1)S(1)}, u32[]{:S(2)}, u32[]{:S(2)}) collective-permute-start(bf16[4,2,64,384]{3,2,1,0:T(8,128)(2,1)S(1)} %get-tuple-element.57), channel_id=1, source_target_pairs={{0,32},{32,64},{64,96},{96,0},{1,33},{33,65},{65,97},{97,1},{2,34}... | collective-permute-start | bytes 1179656 | tf_op jit(solution)/shard_map/ppermute | solution.py:25
  29.5 7.5 %collective-permute-start.1 = (bf16[2,128,384]{2,1,0:T(8,128)(2,1)S(1)}, bf16[2,128,384]{2,1,0:T(8,128)(2,1)S(1)}, u32[]{:S(2)}, u32[]{:S(2)}) collective-permute-start(bf16[2,128,384]{2,1,0:T(8,128)(2,1)S(1)} %collective-permute-done), channel_id=1, source_target_pairs={{0,28},{4,0},{8,4},{12,8},{16,12},{20,16},{24,20},{28,24},{1,29},{... | collective-permute-start | bytes 589832 | tf_op jit(solution)/shard_map/ppermute | solution.py:25
  37.0 8.8 %collective-permute-start.5 = (bf16[2,128,384]{2,1,0:T(8,128)(2,1)S(1)}, bf16[2,128,384]{2,1,0:T(8,128)(2,1)S(1)}, u32[]{:S(2)}, u32[]{:S(2)}) collective-permute-start(bf16[2,128,384]{2,1,0:T(8,128)(2,1)S(1)} %collective-permute-done.4), channel_id=1, source_target_pairs={{0,4},{4,8},{8,12},{12,16},{16,20},{20,24},{24,28},{28,0},{1,5},{5... | collective-permute-start | bytes 589832 | tf_op jit(solution)/shard_map/ppermute | solution.py:25
  37.0 10.1 %collective-permute-start.2 = (bf16[2,128,384]{2,1,0:T(8,128)(2,1)S(1)}, bf16[2,128,384]{2,1,0:T(8,128)(2,1)S(1)}, u32[]{:S(2)}, u32[]{:S(2)}) collective-permute-start(bf16[2,128,384]{2,1,0:T(8,128)(2,1)S(1)} %collective-permute-done.1), channel_id=1, source_target_pairs={{0,28},{4,0},{8,4},{12,8},{16,12},{20,16},{24,20},{28,24},{1,29},{... | collective-permute-start | bytes 589832 | tf_op jit(solution)/shard_map/ppermute | solution.py:25
  40.3 6.8 %collective-permute-start.20 = (bf16[2,2,64,384]{3,2,1,0:T(8,128)(2,1)S(1)}, bf16[2,2,64,384]{3,2,1,0:T(8,128)(2,1)S(1)}, u32[]{:S(2)}, u32[]{:S(2)}) collective-permute-start(bf16[2,2,64,384]{3,2,1,0:T(8,128)(2,1)S(1)} %slice.457), channel_id=1, source_target_pairs={{0,3},{1,0},{2,1},{3,2},{4,7},{5,4},{6,5},{7,6},{8,11},{9,8},{10,9... | collective-permute-start | bytes 589832 | tf_op jit(solution)/shard_map/ppermute | solution.py:25
  40.4 7.0 %collective-permute-start.19 = (bf16[2,2,64,384]{3,2,1,0:T(8,128)(2,1)S(1)}, bf16[2,2,64,384]{3,2,1,0:T(8,128)(2,1)S(1)}, u32[]{:S(2)}, u32[]{:S(2)}) collective-permute-start(bf16[2,2,64,384]{3,2,1,0:T(8,128)(2,1)S(1)} %slice.456), channel_id=1, source_target_pairs={{0,1},{1,2},{2,3},{3,0},{4,5},{5,6},{6,7},{7,4},{8,9},{9,10},{10,1... | collective-permute-start | bytes 589832 | tf_op jit(solution)/shard_map/ppermute | solution.py:25
  42.5 6.4 %collective-permute-start.13 = (bf16[2,2,64,384]{3,2,1,0:T(8,128)(2,1)S(1)}, bf16[2,2,64,384]{3,2,1,0:T(8,128)(2,1)S(1)}, u32[]{:S(2)}, u32[]{:S(2)}) collective-permute-start(bf16[2,2,64,384]{3,2,1,0:T(8,128)(2,1)S(1)} %slice.454), channel_id=1, source_target_pairs={{0,96},{32,0},{64,32},{96,64},{1,97},{33,1},{65,33},{97,65},{2,98}... | collective-permute-start | bytes 589832 | tf_op jit(solution)/shard_map/ppermute | solution.py:25
  45.7 6.7 %collective-permute-start.12 = (bf16[2,2,64,384]{3,2,1,0:T(8,128)(2,1)S(1)}, bf16[2,2,64,384]{3,2,1,0:T(8,128)(2,1)S(1)}, u32[]{:S(2)}, u32[]{:S(2)}) collective-permute-start(bf16[2,2,64,384]{3,2,1,0:T(8,128)(2,1)S(1)} %slice.453), channel_id=1, source_target_pairs={{0,32},{32,64},{64,96},{96,0},{1,33},{33,65},{65,97},{97,1},{2,34}... | collective-permute-start | bytes 589832 | tf_op jit(solution)/shard_map/ppermute | solution.py:25
  47.1 6.9 %collective-permute-start.6 = (bf16[2,128,384]{2,1,0:T(8,128)(2,1)S(1)}, bf16[2,128,384]{2,1,0:T(8,128)(2,1)S(1)}, u32[]{:S(2)}, u32[]{:S(2)}) collective-permute-start(bf16[2,128,384]{2,1,0:T(8,128)(2,1)S(1)} %collective-permute-done.5), channel_id=1, source_target_pairs={{0,4},{4,8},{8,12},{12,16},{16,20},{20,24},{24,28},{28,0},{1,5},{5... | collective-permute-start | bytes 589832 | tf_op jit(solution)/shard_map/ppermute | solution.py:25
  54.1 1.2 copy-start.2
  74.6 43.8 %copy-start.1 = (bf16[2,1,128,384]{3,2,1,0:T(8,128)(2,1)S(1)}, bf16[2,1,128,384]{3,2,1,0:T(8,128)(2,1)}, u32[]{:S(2)}) copy-start(bf16[2,1,128,384]{3,2,1,0:T(8,128)(2,1)} %param.6) | copy-start | bytes 589828
  76.6 7.3 %collective-permute-start.21 = (bf16[2,130,384]{2,1,0:T(8,128)(2,1)S(1)}, bf16[2,130,384]{2,1,0:T(8,128)(2,1)S(1)}, u32[]{:S(2)}, u32[]{:S(2)}) collective-permute-start(bf16[2,130,384]{2,1,0:T(8,128)(2,1)S(1)} %pad_maximum_fusion.4), channel_id=1, source_target_pairs={{0,4},{4,8},{8,12},{12,16},{16,20},{20,24},{24,28},{28,0},{1,5},{5... | collective-permute-start | bytes 599048 | tf_op jit(solution)/shard_map/ppermute | solution.py:25
  85.2 7.1 %collective-permute-start.22 = (bf16[2,130,384]{2,1,0:T(8,128)(2,1)S(1)}, bf16[2,130,384]{2,1,0:T(8,128)(2,1)S(1)}, u32[]{:S(2)}, u32[]{:S(2)}) collective-permute-start(bf16[2,130,384]{2,1,0:T(8,128)(2,1)S(1)} %pad_maximum_fusion.5), channel_id=1, source_target_pairs={{0,4},{4,8},{8,12},{12,16},{16,20},{20,24},{24,28},{28,0},{1,5},{5... | collective-permute-start | bytes 599048 | tf_op jit(solution)/shard_map/ppermute | solution.py:25
  92.5 6.1 %collective-permute-start.25 = (bf16[2,130,384]{2,1,0:T(8,128)(2,1)S(1)}, bf16[2,130,384]{2,1,0:T(8,128)(2,1)S(1)}, u32[]{:S(2)}, u32[]{:S(2)}) collective-permute-start(bf16[2,130,384]{2,1,0:T(8,128)(2,1)S(1)} %pad_maximum_fusion.8), channel_id=1, source_target_pairs={{0,28},{4,0},{8,4},{12,8},{16,12},{20,16},{24,20},{28,24},{1,29},{... | collective-permute-start | bytes 599048 | tf_op jit(solution)/shard_map/ppermute | solution.py:25
  100.1 7.1 %collective-permute-start.23 = (bf16[2,130,384]{2,1,0:T(8,128)(2,1)S(1)}, bf16[2,130,384]{2,1,0:T(8,128)(2,1)S(1)}, u32[]{:S(2)}, u32[]{:S(2)}) collective-permute-start(bf16[2,130,384]{2,1,0:T(8,128)(2,1)S(1)} %pad_maximum_fusion.6), channel_id=1, source_target_pairs={{0,4},{4,8},{8,12},{12,16},{16,20},{20,24},{24,28},{28,0},{1,5},{5... | collective-permute-start | bytes 599048 | tf_op jit(solution)/shard_map/ppermute | solution.py:25
  100.3 7.0 %collective-permute-start.26 = (bf16[2,130,384]{2,1,0:T(8,128)(2,1)S(1)}, bf16[2,130,384]{2,1,0:T(8,128)(2,1)S(1)}, u32[]{:S(2)}, u32[]{:S(2)}) collective-permute-start(bf16[2,130,384]{2,1,0:T(8,128)(2,1)S(1)} %pad_maximum_fusion.9), channel_id=1, source_target_pairs={{0,28},{4,0},{8,4},{12,8},{16,12},{20,16},{24,20},{28,24},{1,29},{... | collective-permute-start | bytes 599048 | tf_op jit(solution)/shard_map/ppermute | solution.py:25
  108.9 7.1 %collective-permute-start.24 = (bf16[2,130,384]{2,1,0:T(8,128)(2,1)S(1)}, bf16[2,130,384]{2,1,0:T(8,128)(2,1)S(1)}, u32[]{:S(2)}, u32[]{:S(2)}) collective-permute-start(bf16[2,130,384]{2,1,0:T(8,128)(2,1)S(1)} %pad_maximum_fusion.7), channel_id=1, source_target_pairs={{0,4},{4,8},{8,12},{12,16},{16,20},{20,24},{24,28},{28,0},{1,5},{5... | collective-permute-start | bytes 599048 | tf_op jit(solution)/shard_map/ppermute | solution.py:25
  110.1 8.2 %collective-permute-start.27 = (bf16[2,130,384]{2,1,0:T(8,128)(2,1)S(1)}, bf16[2,130,384]{2,1,0:T(8,128)(2,1)S(1)}, u32[]{:S(2)}, u32[]{:S(2)}) collective-permute-start(bf16[2,130,384]{2,1,0:T(8,128)(2,1)S(1)} %pad_maximum_fusion.10), channel_id=1, source_target_pairs={{0,28},{4,0},{8,4},{12,8},{16,12},{20,16},{24,20},{28,24},{1,29},{... | collective-permute-start | bytes 599048 | tf_op jit(solution)/shard_map/ppermute | solution.py:25
  120.2 12.4 %collective-permute-start.28 = (bf16[2,1,128,384]{3,2,0,1:T(8,128)(2,1)S(1)}, bf16[2,1,128,384]{3,2,0,1:T(8,128)(2,1)S(1)}, u32[]{:S(2)}, u32[]{:S(2)}) collective-permute-start(bf16[2,1,128,384]{3,2,0,1:T(8,128)(2,1)S(1)} %multiply_convert_fusion), channel_id=1, source_target_pairs={{0,129},{1,130},{2,131},{3,132},{4,133},{5,134},{6,135},{7,136},{8... | collective-permute-start | bytes 589832 | tf_op jit(solution)/shard_map/ppermute | solution.py:231
  121.5 11.2 %collective-permute-start.31 = (bf16[2,1,128,384]{3,2,0,1:T(8,128)(2,1)S(1)}, bf16[2,1,128,384]{3,2,0,1:T(8,128)(2,1)S(1)}, u32[]{:S(2)}, u32[]{:S(2)}) collective-permute-start(bf16[2,1,128,384]{3,2,0,1:T(8,128)(2,1)S(1)} %multiply_convert_fusion), channel_id=1, source_target_pairs={{1,128},{2,129},{3,130},{4,131},{5,132},{6,133},{7,134},{8,135},{9... | collective-permute-start | bytes 589832 | tf_op jit(solution)/shard_map/ppermute | solution.py:232
  122.8 19.7 %collective-permute-start.32 = (bf16[2,1,128,384]{3,2,0,1:T(8,128)(2,1)S(1)}, bf16[2,1,128,384]{3,2,0,1:T(8,128)(2,1)S(1)}, u32[]{:S(2)}, u32[]{:S(2)}) collective-permute-start(bf16[2,1,128,384]{3,2,0,1:T(8,128)(2,1)S(1)} %multiply_convert_fusion), channel_id=1, source_target_pairs={{1,0},{2,1},{3,2},{4,3},{5,4},{6,5},{7,6},{8,7},{9,8},{10,9},{11,1... | collective-permute-start | bytes 589832 | tf_op jit(solution)/shard_map/ppermute | solution.py:113
  129.4 13.2 %collective-permute-start.30 = (bf16[2,1,128,384]{3,2,0,1:T(8,128)(2,1)S(1)}, bf16[2,1,128,384]{3,2,0,1:T(8,128)(2,1)S(1)}, u32[]{:S(2)}, u32[]{:S(2)}) collective-permute-start(bf16[2,1,128,384]{3,2,0,1:T(8,128)(2,1)S(1)} %multiply_convert_fusion), channel_id=1, source_target_pairs={{0,128},{1,129},{2,130},{3,131},{4,132},{5,133},{6,134},{7,135},{8... | collective-permute-start | bytes 589832 | tf_op jit(solution)/shard_map/ppermute | solution.py:230
  130.7 11.8 %collective-permute-start.29 = (bf16[2,1,128,384]{3,2,0,1:T(8,128)(2,1)S(1)}, bf16[2,1,128,384]{3,2,0,1:T(8,128)(2,1)S(1)}, u32[]{:S(2)}, u32[]{:S(2)}) collective-permute-start(bf16[2,1,128,384]{3,2,0,1:T(8,128)(2,1)S(1)} %multiply_convert_fusion), channel_id=1, source_target_pairs={{0,1},{1,2},{2,3},{3,4},{4,5},{5,6},{6,7},{7,8},{8,9},{9,10},{10,1... | collective-permute-start | bytes 589832 | tf_op jit(solution)/shard_map/ppermute | solution.py:113
  132.7 11.8 %slice-start = ((s8[7962624]{0:T(1024)(128)(4,1)}), s8[4194304]{0:T(1024)(128)(4,1)S(1)}, s32[]{:S(2)}) async-start(s8[7962624]{0:T(1024)(128)(4,1)} %bitcast.347), calls=%async_computation | async-start | bytes 8388608
  143.3 2.1 %slice-start.1 = ((s8[7962624]{0:T(1024)(128)(4,1)}), s8[3768320]{0:T(1024)(128)(4,1)S(1)}, s32[]{:S(2)}) async-start(s8[7962624]{0:T(1024)(128)(4,1)} %bitcast.347), calls=%async_computation.1 | async-start | bytes 7536640

commit v6 on v5

--- a/solution.py
+++ b/solution.py
@@ -235,20 +235,13 @@
     stacked = jnp.concatenate([earlier, activated], axis=0)
     padded = jnp.concatenate([above, stacked, below], axis=1)
     padded = jnp.pad(padded, ((0, 0), (0, 0), (1, 1), (0, 0)))
-    patches = []
-    for tap_time in range(3):
-        for tap_row in range(3):
-            for tap_col in range(3):
-                patches.append(
-                    padded[
-                        tap_time : tap_time + frames,
-                        tap_row : tap_row + rows,
-                        tap_col : tap_col + cols,
-                    ]
-                )
-    columns = jnp.concatenate(patches, axis=-1).reshape(frames * count, 27 * width)
-    conv = jnp.dot(
-        columns, conv_weight.reshape(27 * width, width), preferred_element_type=jnp.float32
+    conv = lax.conv_general_dilated(
+        padded[None],
+        conv_weight,
+        window_strides=(1, 1, 1),
+        padding="VALID",
+        dimension_numbers=("NDHWC", "DHWIO", "NDHWC"),
+        preferred_element_type=jnp.float32,
     )
     return (mixed_wide + conv.reshape(features.shape)).astype(jnp.bfloat16)
 

time: 150 us -> 152 us (1.013)
  waiting for transfers between devices: 56.5 us -> 54.6 us
  matrix products: 6.39 us -> 8.18 us
    conv_general_dilated x0 -> x1, matrix products: none -> 6.37 us  [per_device(): lax.conv_general_dilated(padded[None], conv_weight, window_strides=(1, 1,...]
    dot_general x1 -> x0, matrix products: 3.61 us -> none  [per_device(): jnp.dot(columns, conv_weight.reshape(27 * width, width), preferred_elemen...]
    unnamed x47 -> x22, local copies, waits for them, and re-layouts: 4.14 us -> 3.07 us
  transfers between devices with their start and end apart: 33 -> 33, of which waited for: 15 -> 15; matrix products, arithmetic and copies ran while one was open for 4% -> 3% of each run, Pallas kernels for 0% -> 0%
where the time goes in v6:
time: 152 us; the launch traced here: 150 us
  waiting for transfers between devices  54.6 us (36%)
  starting transfers between devices  49.1 us (32%)
  Pallas kernels  19.4 us (13%)
  other arithmetic  12.1 us (8%)
  matrix products  8.18 us (5%)
  local copies, waits for them, and re-layouts  5.69 us (4%)
    ppermute x28, waiting for transfers between devices, ring_shift(): return lax.ppermute(block, axis, [(i, (i + step) % n) for i in range(n)])  46 us
    ppermute x28, starting transfers between devices, ring_shift(): return lax.ppermute(block, axis, [(i, (i + step) % n) for i in range(n)])  36 us
    pallas_call x1, Pallas kernels, attention(): pl.pallas_call(functools.partial(attention_kernel, scale), grid=(frames,...  19.4 us
    ppermute x2, starting transfers between devices, row_shift(): return lax.ppermute(block, ROW_AXES, route)  9.25 us
    ppermute x2, waiting for transfers between devices, row_shift(): return lax.ppermute(block, ROW_AXES, route)  8.52 us
    conv_general_dilated x1, matrix products, per_device(): lax.conv_general_dilated(padded[None], conv_weight, window_strides=(1, 1,...  6.37 us
    convert_element_type x3, other arithmetic, pack(): return jnp.concatenate([summed.astype(jnp.bfloat16), stats], axis=1)  3.8 us
    another operation x6, other arithmetic, per_device(): outer = jnp.stack(ring_gather(inner, second, halve=True))  3.16 us
  transfers between devices with their start and end apart: 33, of which 15 were waited for; matrix products, arithmetic and copies ran while one was open for 3% of the time, Pallas kernels for 0%

profile of v6, /device:TPU:2, one launch (start us, length us, event | category | flops | bytes accessed | tf_op | source)
XLA Modules:
  0.0 149.6 jit_solution(13514496847328023281)
XLA Ops:
  0.0 1.1 fusion.22
  1.1 1.0 fusion.110
  2.2 2.3 %collective-permute-start.14 = (bf16[2,64,384]{2,1,0:T(8,128)(2,1)S(1)}, bf16[2,64,384]{2,1,0:T(8,128)(2,1)S(1)}, u32[]{:S(2)}, u32[]{:S(2)}) collective-permute-start(bf16[2,64,384]{2,1,0:T(8,128)(2,1)S(1)} %get-tuple-element.60), channel_id=1, source_target_pairs={{0,96},{32,0},{64,32},{96,64},{1,97},{33,1},{65,33},{97,65},{2,98}... | collective-permute-start | bytes 294920 | tf_op jit(solution)/shard_map/ppermute | solution.py:25
  4.5 1.4 collective-permute-start.8
  5.9 1.0 fusion.23
  6.9 2.2 %collective-permute-done.15 = bf16[2,64,384]{2,1,0:T(8,128)(2,1)S(1)} collective-permute-done((bf16[2,64,384]{2,1,0:T(8,128)(2,1)S(1)}, bf16[2,64,384]{2,1,0:T(8,128)(2,1)S(1)}, u32[]{:S(2)}, u32[]{:S(2)}) %collective-permute-start.15) | collective-permute-done | bytes 98336 | tf_op jit(solution)/shard_map/ppermute | solution.py:25
  9.1 0.3 convolution_convert_fusion
  9.4 1.8 %collective-permute-start.3 = (bf16[2,128,384]{2,1,0:T(8,128)(2,1)S(1)}, bf16[2,128,384]{2,1,0:T(8,128)(2,1)S(1)}, u32[]{:S(2)}, u32[]{:S(2)}) collective-permute-start(bf16[2,128,384]{2,1,0:T(8,128)(2,1)S(1)} %bitcast.334), channel_id=1, source_target_pairs={{0,4},{4,8},{8,12},{12,16},{16,20},{20,24},{24,28},{28,0},{1,5},{5... | collective-permute-start | bytes 589832 | tf_op jit(solution)/shard_map/ppermute | solution.py:25
  11.2 3.0 %collective-permute-start.7 = (bf16[2,64,384]{2,1,0:T(8,128)(2,1)S(1)}, bf16[2,64,384]{2,1,0:T(8,128)(2,1)S(1)}, u32[]{:S(2)}, u32[]{:S(2)}) collective-permute-start(bf16[2,64,384]{2,1,0:T(8,128)(2,1)S(1)} %get-tuple-element.61), channel_id=1, source_target_pairs={{0,3},{1,0},{2,1},{3,2},{4,7},{5,4},{6,5},{7,6},{8,11},{9,8},{10,9... | collective-permute-start | bytes 294920 | tf_op jit(solution)/shard_map/ppermute | solution.py:25
  14.2 4.0 %collective-permute-start = (bf16[2,128,384]{2,1,0:T(8,128)(2,1)S(1)}, bf16[2,128,384]{2,1,0:T(8,128)(2,1)S(1)}, u32[]{:S(2)}, u32[]{:S(2)}) collective-permute-start(bf16[2,128,384]{2,1,0:T(8,128)(2,1)S(1)} %bitcast.335), channel_id=1, source_target_pairs={{0,28},{4,0},{8,4},{12,8},{16,12},{20,16},{24,20},{28,24},{1,29},{... | collective-permute-start | bytes 589832 | tf_op jit(solution)/shard_map/ppermute | solution.py:25
  18.3 0.1 fusion.83
  18.4 3.3 %collective-permute-start.17 = (bf16[4,2,64,384]{3,2,1,0:T(8,128)(2,1)S(1)}, bf16[4,2,64,384]{3,2,1,0:T(8,128)(2,1)S(1)}, u32[]{:S(2)}, u32[]{:S(2)}) collective-permute-start(bf16[4,2,64,384]{3,2,1,0:T(8,128)(2,1)S(1)} %get-tuple-element.55), channel_id=1, source_target_pairs={{0,3},{1,0},{2,1},{3,2},{4,7},{5,4},{6,5},{7,6},{8,11},{9,8},{10,9... | collective-permute-start | bytes 1179656 | tf_op jit(solution)/shard_map/ppermute | solution.py:25
  21.8 3.3 %collective-permute-done.9 = bf16[2,64,384]{2,1,0:T(8,128)(2,1)S(1)} collective-permute-done((bf16[2,64,384]{2,1,0:T(8,128)(2,1)S(1)}, bf16[2,64,384]{2,1,0:T(8,128)(2,1)S(1)}, u32[]{:S(2)}, u32[]{:S(2)}) %collective-permute-start.9) | collective-permute-done | bytes 98336 | tf_op jit(solution)/shard_map/ppermute | solution.py:25
  25.1 0.1 fusion.84
  25.2 2.6 %collective-permute-start.10 = (bf16[4,2,64,384]{3,2,1,0:T(8,128)(2,1)S(1)}, bf16[4,2,64,384]{3,2,1,0:T(8,128)(2,1)S(1)}, u32[]{:S(2)}, u32[]{:S(2)}) collective-permute-start(bf16[4,2,64,384]{3,2,1,0:T(8,128)(2,1)S(1)} %get-tuple-element.57), channel_id=1, source_target_pairs={{0,96},{32,0},{64,32},{96,64},{1,97},{33,1},{65,33},{97,65},{2,98}... | collective-permute-start | bytes 1179656 | tf_op jit(solution)/shard_map/ppermute | solution.py:25
  27.8 0.8 collective-permute-done.4
  28.5 0.7 collective-permute-start.1
  29.3 6.7 %collective-permute-done.1 = bf16[2,128,384]{2,1,0:T(8,128)(2,1)S(1)} collective-permute-done((bf16[2,128,384]{2,1,0:T(8,128)(2,1)S(1)}, bf16[2,128,384]{2,1,0:T(8,128)(2,1)S(1)}, u32[]{:S(2)}, u32[]{:S(2)}) %collective-permute-start.1) | collective-permute-done | bytes 196640 | tf_op jit(solution)/shard_map/ppermute | solution.py:25
  36.0 3.2 %collective-permute-start.2 = (bf16[2,128,384]{2,1,0:T(8,128)(2,1)S(1)}, bf16[2,128,384]{2,1,0:T(8,128)(2,1)S(1)}, u32[]{:S(2)}, u32[]{:S(2)}) collective-permute-start(bf16[2,128,384]{2,1,0:T(8,128)(2,1)S(1)} %collective-permute-done.1), channel_id=1, source_target_pairs={{0,28},{4,0},{8,4},{12,8},{16,12},{20,16},{24,20},{28,24},{1,29},{... | collective-permute-start | bytes 589832 | tf_op jit(solution)/shard_map/ppermute | solution.py:25
  39.5 2.1 %collective-permute-start.19 = (bf16[2,2,64,384]{3,2,1,0:T(8,128)(2,1)S(1)}, bf16[2,2,64,384]{3,2,1,0:T(8,128)(2,1)S(1)}, u32[]{:S(2)}, u32[]{:S(2)}) collective-permute-start(bf16[2,2,64,384]{3,2,1,0:T(8,128)(2,1)S(1)} %slice.350), channel_id=1, source_target_pairs={{0,1},{1,2},{2,3},{3,0},{4,5},{5,6},{6,7},{7,4},{8,9},{9,10},{10,1... | collective-permute-start | bytes 589832 | tf_op jit(solution)/shard_map/ppermute | solution.py:25
  41.6 2.7 %collective-permute-start.13 = (bf16[2,2,64,384]{3,2,1,0:T(8,128)(2,1)S(1)}, bf16[2,2,64,384]{3,2,1,0:T(8,128)(2,1)S(1)}, u32[]{:S(2)}, u32[]{:S(2)}) collective-permute-start(bf16[2,2,64,384]{3,2,1,0:T(8,128)(2,1)S(1)} %slice.348), channel_id=1, source_target_pairs={{0,96},{32,0},{64,32},{96,64},{1,97},{33,1},{65,33},{97,65},{2,98}... | collective-permute-start | bytes 589832 | tf_op jit(solution)/shard_map/ppermute | solution.py:25
  44.3 0.4 collective-permute-done.5
  44.8 1.3 collective-permute-start.12
  46.2 0.3 collective-permute-done.19
  46.5 1.5 pad_maximum_fusion.1
  48.0 3.5 %collective-permute-done.12 = bf16[2,2,64,384]{3,2,1,0:T(8,128)(2,1)S(1)} collective-permute-done((bf16[2,2,64,384]{3,2,1,0:T(8,128)(2,1)S(1)}, bf16[2,2,64,384]{3,2,1,0:T(8,128)(2,1)S(1)}, u32[]{:S(2)}, u32[]{:S(2)}) %collective-permute-start.12) | collective-permute-done | bytes 196640 | tf_op jit(solution)/shard_map/ppermute | solution.py:25
  51.5 1.4 pad_maximum_fusion
  52.9 0.1 collective-permute-done.6
  53.2 1.2 copy-done.3
  54.3 19.4 %shard_map.64 = (f32[2,1,1024]{2,1,0:T(1,128)}, f32[2,1,1024]{2,1,0:T(1,128)}, f32[2,1024,384]{2,1,0:T(8,128)}, bf16[2,1024,384]{2,1,0:T(8,128)(2,1)}) custom-call(bf16[8,2,128,384]{3,2,1,0:T(8,128)(2,1)} %copy-done.3, bf16[16,2,64,384]{3,2,1,0:T(8,128)(2,1)} %bitcast.329, bf16[16,2,64,384]{3,2,1,0:T(8,128)(2,1)} %bitcast.328, bf16[384,384]{1,0:T(8,128)(2,1)} %key_w_ref.1, ...), custom_call_target="tpu_custom_call" | custom-call | flops 8858370048 | bytes 9437184 | tf_op jit(solution)/shard_map/pallas_call | solution.py:161
  73.7 1.1 fusion.99
  74.8 0.7 copy_bitcast_fusion.1
  75.6 0.1 collective-permute-start.21
  75.7 7.2 %collective-permute-done.21 = bf16[2,130,384]{2,1,0:T(8,128)(2,1)S(1)} collective-permute-done((bf16[2,130,384]{2,1,0:T(8,128)(2,1)S(1)}, bf16[2,130,384]{2,1,0:T(8,128)(2,1)S(1)}, u32[]{:S(2)}, u32[]{:S(2)}) %collective-permute-start.21) | collective-permute-done | bytes 199712 | tf_op jit(solution)/shard_map/ppermute | solution.py:25
  83.1 1.1 add_convert_fusion.4
  84.2 0.1 collective-permute-start.22
  84.3 7.0 %collective-permute-done.22 = bf16[2,130,384]{2,1,0:T(8,128)(2,1)S(1)} collective-permute-done((bf16[2,130,384]{2,1,0:T(8,128)(2,1)S(1)}, bf16[2,130,384]{2,1,0:T(8,128)(2,1)S(1)}, u32[]{:S(2)}, u32[]{:S(2)}) %collective-permute-start.22) | collective-permute-done | bytes 199712 | tf_op jit(solution)/shard_map/ppermute | solution.py:25
  91.5 0.3 collective-permute-start.25
  91.9 5.7 %collective-permute-done.25 = bf16[2,130,384]{2,1,0:T(8,128)(2,1)S(1)} collective-permute-done((bf16[2,130,384]{2,1,0:T(8,128)(2,1)S(1)}, bf16[2,130,384]{2,1,0:T(8,128)(2,1)S(1)}, u32[]{:S(2)}, u32[]{:S(2)}) %collective-permute-start.25) | collective-permute-done | bytes 199712 | tf_op jit(solution)/shard_map/ppermute | solution.py:25
  97.7 1.3 add_convert_fusion.3
  99.3 3.3 %collective-permute-start.26 = (bf16[2,130,384]{2,1,0:T(8,128)(2,1)S(1)}, bf16[2,130,384]{2,1,0:T(8,128)(2,1)S(1)}, u32[]{:S(2)}, u32[]{:S(2)}) collective-permute-start(bf16[2,130,384]{2,1,0:T(8,128)(2,1)S(1)} %pad_maximum_fusion.9), channel_id=1, source_target_pairs={{0,28},{4,0},{8,4},{12,8},{16,12},{20,16},{24,20},{28,24},{1,29},{... | collective-permute-start | bytes 599048 | tf_op jit(solution)/shard_map/ppermute | solution.py:25
  102.6 3.6 %collective-permute-done.23 = bf16[2,130,384]{2,1,0:T(8,128)(2,1)S(1)} collective-permute-done((bf16[2,130,384]{2,1,0:T(8,128)(2,1)S(1)}, bf16[2,130,384]{2,1,0:T(8,128)(2,1)S(1)}, u32[]{:S(2)}, u32[]{:S(2)}) %collective-permute-start.23) | collective-permute-done | bytes 199712 | tf_op jit(solution)/shard_map/ppermute | solution.py:25
  106.5 1.3 add_convert_fusion.2
  107.9 1.2 collective-permute-start.24
  109.2 2.2 %collective-permute-start.27 = (bf16[2,130,384]{2,1,0:T(8,128)(2,1)S(1)}, bf16[2,130,384]{2,1,0:T(8,128)(2,1)S(1)}, u32[]{:S(2)}, u32[]{:S(2)}) collective-permute-start(bf16[2,130,384]{2,1,0:T(8,128)(2,1)S(1)} %pad_maximum_fusion.10), channel_id=1, source_target_pairs={{0,28},{4,0},{8,4},{12,8},{16,12},{20,16},{24,20},{28,24},{1,29},{... | collective-permute-start | bytes 599048 | tf_op jit(solution)/shard_map/ppermute | solution.py:25
  111.4 3.6 %collective-permute-done.24 = bf16[2,130,384]{2,1,0:T(8,128)(2,1)S(1)} collective-permute-done((bf16[2,130,384]{2,1,0:T(8,128)(2,1)S(1)}, bf16[2,130,384]{2,1,0:T(8,128)(2,1)S(1)}, u32[]{:S(2)}, u32[]{:S(2)}) %collective-permute-start.24) | collective-permute-done | bytes 199712 | tf_op jit(solution)/shard_map/ppermute | solution.py:25
  115.1 1.6 %collective-permute-done.27 = bf16[2,130,384]{2,1,0:T(8,128)(2,1)S(1)} collective-permute-done((bf16[2,130,384]{2,1,0:T(8,128)(2,1)S(1)}, bf16[2,130,384]{2,1,0:T(8,128)(2,1)S(1)}, u32[]{:S(2)}, u32[]{:S(2)}) %collective-permute-start.27) | collective-permute-done | bytes 199712 | tf_op jit(solution)/shard_map/ppermute | solution.py:25
  116.7 1.5 %multiply_reduce_fusion = (f32[2,128]{1,0:T(2,128)S(1)}, f32[2,1,128,384]{3,2,0,1:T(8,128)S(1)}) fusion(bf16[384,384]{1,0:T(8,128)(2,1)S(1)} %copy-done, f32[2,1024,384]{2,1,0:T(8,128)} %get-tuple-element.12, bf16[2,130,384]{2,1,0:T(8,128)(2,1)S(1)} %collective-permute-done.27, bf16[2,130,384]{2,1,0:T(8,128)(2,1)S(1)} %collective-permute-done.24, ...), kind=kOutput, calls=%fused_computation.40 | convolution fusion | flops 77070080 | bytes 1677312 | tf_op jit(solution)/shard_map/dot_general | solution.py:221
  118.3 0.2 multiply_convert_fusion
  118.5 7.3 %collective-permute-start.32 = (bf16[2,1,128,384]{3,2,0,1:T(8,128)(2,1)S(1)}, bf16[2,1,128,384]{3,2,0,1:T(8,128)(2,1)S(1)}, u32[]{:S(2)}, u32[]{:S(2)}) collective-permute-start(bf16[2,1,128,384]{3,2,0,1:T(8,128)(2,1)S(1)} %multiply_convert_fusion), channel_id=1, source_target_pairs={{1,0},{2,1},{3,2},{4,3},{5,4},{6,5},{7,6},{8,7},{9,8},{10,9},{11,1... | collective-permute-start | bytes 589832 | tf_op jit(solution)/shard_map/ppermute | solution.py:113
  125.8 1.3 collective-permute-start.31
  127.1 1.3 collective-permute-start.30
  128.4 1.9 %collective-permute-start.29 = (bf16[2,1,128,384]{3,2,0,1:T(8,128)(2,1)S(1)}, bf16[2,1,128,384]{3,2,0,1:T(8,128)(2,1)S(1)}, u32[]{:S(2)}, u32[]{:S(2)}) collective-permute-start(bf16[2,1,128,384]{3,2,0,1:T(8,128)(2,1)S(1)} %multiply_convert_fusion), channel_id=1, source_target_pairs={{0,1},{1,2},{2,3},{3,4},{4,5},{5,6},{6,7},{7,8},{8,9},{9,10},{10,1... | collective-permute-start | bytes 589832 | tf_op jit(solution)/shard_map/ppermute | solution.py:113
  130.4 1.3 collective-permute-start.28
  131.7 8.5 %collective-permute-done.29 = bf16[2,1,128,384]{3,2,0,1:T(8,128)(2,1)S(1)} collective-permute-done((bf16[2,1,128,384]{3,2,0,1:T(8,128)(2,1)S(1)}, bf16[2,1,128,384]{3,2,0,1:T(8,128)(2,1)S(1)}, u32[]{:S(2)}, u32[]{:S(2)}) %collective-permute-start.29) | collective-permute-done | bytes 196640 | tf_op jit(solution)/shard_map/ppermute | solution.py:113
  140.2 0.3 fusion.10
  140.6 0.5 copy.162
  141.0 0.5 pad.5.clone
  141.5 0.2 copy.113
  141.7 0.5 copy-done.4
  142.2 6.4 %fusion.15 = f32[2,1,8,17,384]{4,2,3,1,0:T(8,128)S(1)} fusion(bf16[3,3,3,384,384]{4,3,2,1,0:T(8,128)(2,1)} %param.11, bf16[4,3,1,7,2,384]{5,3,4,1,0,2:T(8,128)(2,1)S(1)} %slice.424, bf16[4,3,1,8,17,384]{5,3,4,1,0,2:T(8,128)(2,1)S(1)} %copy.113, pred[8,17]{0,1:T(8,128)(4,1)S(1)} %copy-done.4), kind=kOutput, calls=%fused_computation.22 | convolution fusion | flops 2170140672 | bytes 9762952 | tf_op jit(solution)/shard_map/conv_general_dilated | solution.py:238
  148.6 0.2 copy.114
  148.8 0.1 slice.425
  148.9 0.7 fusion.27
  (136 shorter events, 2.0 us)
Async XLA Ops:
  0.0 116.7 %copy-start = (bf16[384,384]{1,0:T(8,128)(2,1)S(1)}, bf16[384,384]{1,0:T(8,128)(2,1)}, u32[]{:S(2)}) copy-start(bf16[384,384]{1,0:T(8,128)(2,1)} %param.10) | copy-start | bytes 884740
  0.0 9.1 %copy-start.2 = (bf16[384,384]{1,0:T(8,128)(2,1)S(1)}, bf16[384,384]{1,0:T(8,128)(2,1)}, u32[]{:S(2)}) copy-start(bf16[384,384]{1,0:T(8,128)(2,1)} %param.7) | copy-start | bytes 884740
  2.2 12.0 %collective-permute-start.14 = (bf16[2,64,384]{2,1,0:T(8,128)(2,1)S(1)}, bf16[2,64,384]{2,1,0:T(8,128)(2,1)S(1)}, u32[]{:S(2)}, u32[]{:S(2)}) collective-permute-start(bf16[2,64,384]{2,1,0:T(8,128)(2,1)S(1)} %get-tuple-element.60), channel_id=1, source_target_pairs={{0,96},{32,0},{64,32},{96,64},{1,97},{33,1},{65,33},{97,65},{2,98}... | collective-permute-start | bytes 294920 | tf_op jit(solution)/shard_map/ppermute | solution.py:25
  4.5 4.6 %collective-permute-start.15 = (bf16[2,64,384]{2,1,0:T(8,128)(2,1)S(1)}, bf16[2,64,384]{2,1,0:T(8,128)(2,1)S(1)}, u32[]{:S(2)}, u32[]{:S(2)}) collective-permute-start(bf16[2,64,384]{2,1,0:T(8,128)(2,1)S(1)} %get-tuple-element.60), channel_id=1, source_target_pairs={{0,32},{32,64},{64,96},{96,0},{1,33},{33,65},{65,97},{97,1},{2,34}... | collective-permute-start | bytes 294920 | tf_op jit(solution)/shard_map/ppermute | solution.py:25
  4.5 13.7 %collective-permute-start.8 = (bf16[2,64,384]{2,1,0:T(8,128)(2,1)S(1)}, bf16[2,64,384]{2,1,0:T(8,128)(2,1)S(1)}, u32[]{:S(2)}, u32[]{:S(2)}) collective-permute-start(bf16[2,64,384]{2,1,0:T(8,128)(2,1)S(1)} %get-tuple-element.61), channel_id=1, source_target_pairs={{0,1},{1,2},{2,3},{3,0},{4,5},{5,6},{6,7},{7,4},{8,9},{9,10},{10,1... | collective-permute-start | bytes 294920 | tf_op jit(solution)/shard_map/ppermute | solution.py:25
  9.1 9.1 %collective-permute-start.16 = (bf16[2,64,384]{2,1,0:T(8,128)(2,1)S(1)}, bf16[2,64,384]{2,1,0:T(8,128)(2,1)S(1)}, u32[]{:S(2)}, u32[]{:S(2)}) collective-permute-start(bf16[2,64,384]{2,1,0:T(8,128)(2,1)S(1)} %collective-permute-done.15), channel_id=1, source_target_pairs={{0,32},{32,64},{64,96},{96,0},{1,33},{33,65},{65,97},{97,1},{2,34}... | collective-permute-start | bytes 294920 | tf_op jit(solution)/shard_map/ppermute | solution.py:25
  9.4 12.2 %collective-permute-start.3 = (bf16[2,128,384]{2,1,0:T(8,128)(2,1)S(1)}, bf16[2,128,384]{2,1,0:T(8,128)(2,1)S(1)}, u32[]{:S(2)}, u32[]{:S(2)}) collective-permute-start(bf16[2,128,384]{2,1,0:T(8,128)(2,1)S(1)} %bitcast.334), channel_id=1, source_target_pairs={{0,4},{4,8},{8,12},{12,16},{16,20},{20,24},{24,28},{28,0},{1,5},{5... | collective-permute-start | bytes 589832 | tf_op jit(solution)/shard_map/ppermute | solution.py:25
  11.2 10.5 %collective-permute-start.7 = (bf16[2,64,384]{2,1,0:T(8,128)(2,1)S(1)}, bf16[2,64,384]{2,1,0:T(8,128)(2,1)S(1)}, u32[]{:S(2)}, u32[]{:S(2)}) collective-permute-start(bf16[2,64,384]{2,1,0:T(8,128)(2,1)S(1)} %get-tuple-element.61), channel_id=1, source_target_pairs={{0,3},{1,0},{2,1},{3,2},{4,7},{5,4},{6,5},{7,6},{8,11},{9,8},{10,9... | collective-permute-start | bytes 294920 | tf_op jit(solution)/shard_map/ppermute | solution.py:25
  14.2 13.6 %collective-permute-start = (bf16[2,128,384]{2,1,0:T(8,128)(2,1)S(1)}, bf16[2,128,384]{2,1,0:T(8,128)(2,1)S(1)}, u32[]{:S(2)}, u32[]{:S(2)}) collective-permute-start(bf16[2,128,384]{2,1,0:T(8,128)(2,1)S(1)} %bitcast.335), channel_id=1, source_target_pairs={{0,28},{4,0},{8,4},{12,8},{16,12},{20,16},{24,20},{28,24},{1,29},{... | collective-permute-start | bytes 589832 | tf_op jit(solution)/shard_map/ppermute | solution.py:25
  18.2 6.9 %collective-permute-start.9 = (bf16[2,64,384]{2,1,0:T(8,128)(2,1)S(1)}, bf16[2,64,384]{2,1,0:T(8,128)(2,1)S(1)}, u32[]{:S(2)}, u32[]{:S(2)}) collective-permute-start(bf16[2,64,384]{2,1,0:T(8,128)(2,1)S(1)} %collective-permute-done.8), channel_id=1, source_target_pairs={{0,1},{1,2},{2,3},{3,0},{4,5},{5,6},{6,7},{7,4},{8,9},{9,10},{10,1... | collective-permute-start | bytes 294920 | tf_op jit(solution)/shard_map/ppermute | solution.py:25
  18.4 17.7 %collective-permute-start.17 = (bf16[4,2,64,384]{3,2,1,0:T(8,128)(2,1)S(1)}, bf16[4,2,64,384]{3,2,1,0:T(8,128)(2,1)S(1)}, u32[]{:S(2)}, u32[]{:S(2)}) collective-permute-start(bf16[4,2,64,384]{3,2,1,0:T(8,128)(2,1)S(1)} %get-tuple-element.55), channel_id=1, source_target_pairs={{0,3},{1,0},{2,1},{3,2},{4,7},{5,4},{6,5},{7,6},{8,11},{9,8},{10,9... | collective-permute-start | bytes 1179656 | tf_op jit(solution)/shard_map/ppermute | solution.py:25
  21.7 6.9 %collective-permute-start.4 = (bf16[2,128,384]{2,1,0:T(8,128)(2,1)S(1)}, bf16[2,128,384]{2,1,0:T(8,128)(2,1)S(1)}, u32[]{:S(2)}, u32[]{:S(2)}) collective-permute-start(bf16[2,128,384]{2,1,0:T(8,128)(2,1)S(1)} %collective-permute-done.3), channel_id=1, source_target_pairs={{0,4},{4,8},{8,12},{12,16},{16,20},{20,24},{24,28},{28,0},{1,5},{5... | collective-permute-start | bytes 589832 | tf_op jit(solution)/shard_map/ppermute | solution.py:25
  21.7 17.6 %collective-permute-start.18 = (bf16[4,2,64,384]{3,2,1,0:T(8,128)(2,1)S(1)}, bf16[4,2,64,384]{3,2,1,0:T(8,128)(2,1)S(1)}, u32[]{:S(2)}, u32[]{:S(2)}) collective-permute-start(bf16[4,2,64,384]{3,2,1,0:T(8,128)(2,1)S(1)} %get-tuple-element.55), channel_id=1, source_target_pairs={{0,1},{1,2},{2,3},{3,0},{4,5},{5,6},{6,7},{7,4},{8,9},{9,10},{10,1... | collective-permute-start | bytes 1179656 | tf_op jit(solution)/shard_map/ppermute | solution.py:25
  25.2 14.2 %collective-permute-start.10 = (bf16[4,2,64,384]{3,2,1,0:T(8,128)(2,1)S(1)}, bf16[4,2,64,384]{3,2,1,0:T(8,128)(2,1)S(1)}, u32[]{:S(2)}, u32[]{:S(2)}) collective-permute-start(bf16[4,2,64,384]{3,2,1,0:T(8,128)(2,1)S(1)} %get-tuple-element.57), channel_id=1, source_target_pairs={{0,96},{32,0},{64,32},{96,64},{1,97},{33,1},{65,33},{97,65},{2,98}... | collective-permute-start | bytes 1179656 | tf_op jit(solution)/shard_map/ppermute | solution.py:25
  27.8 13.8 %collective-permute-start.11 = (bf16[4,2,64,384]{3,2,1,0:T(8,128)(2,1)S(1)}, bf16[4,2,64,384]{3,2,1,0:T(8,128)(2,1)S(1)}, u32[]{:S(2)}, u32[]{:S(2)}) collective-permute-start(bf16[4,2,64,384]{3,2,1,0:T(8,128)(2,1)S(1)} %get-tuple-element.57), channel_id=1, source_target_pairs={{0,32},{32,64},{64,96},{96,0},{1,33},{33,65},{65,97},{97,1},{2,34}... | collective-permute-start | bytes 1179656 | tf_op jit(solution)/shard_map/ppermute | solution.py:25
  28.5 7.5 %collective-permute-start.1 = (bf16[2,128,384]{2,1,0:T(8,128)(2,1)S(1)}, bf16[2,128,384]{2,1,0:T(8,128)(2,1)S(1)}, u32[]{:S(2)}, u32[]{:S(2)}) collective-permute-start(bf16[2,128,384]{2,1,0:T(8,128)(2,1)S(1)} %collective-permute-done), channel_id=1, source_target_pairs={{0,28},{4,0},{8,4},{12,8},{16,12},{20,16},{24,20},{28,24},{1,29},{... | collective-permute-start | bytes 589832 | tf_op jit(solution)/shard_map/ppermute | solution.py:25
  36.0 8.8 %collective-permute-start.5 = (bf16[2,128,384]{2,1,0:T(8,128)(2,1)S(1)}, bf16[2,128,384]{2,1,0:T(8,128)(2,1)S(1)}, u32[]{:S(2)}, u32[]{:S(2)}) collective-permute-start(bf16[2,128,384]{2,1,0:T(8,128)(2,1)S(1)} %collective-permute-done.4), channel_id=1, source_target_pairs={{0,4},{4,8},{8,12},{12,16},{16,20},{20,24},{24,28},{28,0},{1,5},{5... | collective-permute-start | bytes 589832 | tf_op jit(solution)/shard_map/ppermute | solution.py:25
  36.0 10.1 %collective-permute-start.2 = (bf16[2,128,384]{2,1,0:T(8,128)(2,1)S(1)}, bf16[2,128,384]{2,1,0:T(8,128)(2,1)S(1)}, u32[]{:S(2)}, u32[]{:S(2)}) collective-permute-start(bf16[2,128,384]{2,1,0:T(8,128)(2,1)S(1)} %collective-permute-done.1), channel_id=1, source_target_pairs={{0,28},{4,0},{8,4},{12,8},{16,12},{20,16},{24,20},{28,24},{1,29},{... | collective-permute-start | bytes 589832 | tf_op jit(solution)/shard_map/ppermute | solution.py:25
  39.3 6.8 %collective-permute-start.20 = (bf16[2,2,64,384]{3,2,1,0:T(8,128)(2,1)S(1)}, bf16[2,2,64,384]{3,2,1,0:T(8,128)(2,1)S(1)}, u32[]{:S(2)}, u32[]{:S(2)}) collective-permute-start(bf16[2,2,64,384]{3,2,1,0:T(8,128)(2,1)S(1)} %slice.351), channel_id=1, source_target_pairs={{0,3},{1,0},{2,1},{3,2},{4,7},{5,4},{6,5},{7,6},{8,11},{9,8},{10,9... | collective-permute-start | bytes 589832 | tf_op jit(solution)/shard_map/ppermute | solution.py:25
  39.5 7.0 %collective-permute-start.19 = (bf16[2,2,64,384]{3,2,1,0:T(8,128)(2,1)S(1)}, bf16[2,2,64,384]{3,2,1,0:T(8,128)(2,1)S(1)}, u32[]{:S(2)}, u32[]{:S(2)}) collective-permute-start(bf16[2,2,64,384]{3,2,1,0:T(8,128)(2,1)S(1)} %slice.350), channel_id=1, source_target_pairs={{0,1},{1,2},{2,3},{3,0},{4,5},{5,6},{6,7},{7,4},{8,9},{9,10},{10,1... | collective-permute-start | bytes 589832 | tf_op jit(solution)/shard_map/ppermute | solution.py:25
  41.6 6.4 %collective-permute-start.13 = (bf16[2,2,64,384]{3,2,1,0:T(8,128)(2,1)S(1)}, bf16[2,2,64,384]{3,2,1,0:T(8,128)(2,1)S(1)}, u32[]{:S(2)}, u32[]{:S(2)}) collective-permute-start(bf16[2,2,64,384]{3,2,1,0:T(8,128)(2,1)S(1)} %slice.348), channel_id=1, source_target_pairs={{0,96},{32,0},{64,32},{96,64},{1,97},{33,1},{65,33},{97,65},{2,98}... | collective-permute-start | bytes 589832 | tf_op jit(solution)/shard_map/ppermute | solution.py:25
  44.8 6.7 %collective-permute-start.12 = (bf16[2,2,64,384]{3,2,1,0:T(8,128)(2,1)S(1)}, bf16[2,2,64,384]{3,2,1,0:T(8,128)(2,1)S(1)}, u32[]{:S(2)}, u32[]{:S(2)}) collective-permute-start(bf16[2,2,64,384]{3,2,1,0:T(8,128)(2,1)S(1)} %slice.347), channel_id=1, source_target_pairs={{0,32},{32,64},{64,96},{96,0},{1,33},{33,65},{65,97},{97,1},{2,34}... | collective-permute-start | bytes 589832 | tf_op jit(solution)/shard_map/ppermute | solution.py:25
  46.1 6.9 %collective-permute-start.6 = (bf16[2,128,384]{2,1,0:T(8,128)(2,1)S(1)}, bf16[2,128,384]{2,1,0:T(8,128)(2,1)S(1)}, u32[]{:S(2)}, u32[]{:S(2)}) collective-permute-start(bf16[2,128,384]{2,1,0:T(8,128)(2,1)S(1)} %collective-permute-done.5), channel_id=1, source_target_pairs={{0,4},{4,8},{8,12},{12,16},{16,20},{20,24},{24,28},{28,0},{1,5},{5... | collective-permute-start | bytes 589832 | tf_op jit(solution)/shard_map/ppermute | solution.py:25
  53.1 1.2 copy-start.3
  75.6 7.3 %collective-permute-start.21 = (bf16[2,130,384]{2,1,0:T(8,128)(2,1)S(1)}, bf16[2,130,384]{2,1,0:T(8,128)(2,1)S(1)}, u32[]{:S(2)}, u32[]{:S(2)}) collective-permute-start(bf16[2,130,384]{2,1,0:T(8,128)(2,1)S(1)} %pad_maximum_fusion.4), channel_id=1, source_target_pairs={{0,4},{4,8},{8,12},{12,16},{16,20},{20,24},{24,28},{28,0},{1,5},{5... | collective-permute-start | bytes 599048 | tf_op jit(solution)/shard_map/ppermute | solution.py:25
  84.2 7.1 %collective-permute-start.22 = (bf16[2,130,384]{2,1,0:T(8,128)(2,1)S(1)}, bf16[2,130,384]{2,1,0:T(8,128)(2,1)S(1)}, u32[]{:S(2)}, u32[]{:S(2)}) collective-permute-start(bf16[2,130,384]{2,1,0:T(8,128)(2,1)S(1)} %pad_maximum_fusion.5), channel_id=1, source_target_pairs={{0,4},{4,8},{8,12},{12,16},{16,20},{20,24},{24,28},{28,0},{1,5},{5... | collective-permute-start | bytes 599048 | tf_op jit(solution)/shard_map/ppermute | solution.py:25
  91.5 6.1 %collective-permute-start.25 = (bf16[2,130,384]{2,1,0:T(8,128)(2,1)S(1)}, bf16[2,130,384]{2,1,0:T(8,128)(2,1)S(1)}, u32[]{:S(2)}, u32[]{:S(2)}) collective-permute-start(bf16[2,130,384]{2,1,0:T(8,128)(2,1)S(1)} %pad_maximum_fusion.8), channel_id=1, source_target_pairs={{0,28},{4,0},{8,4},{12,8},{16,12},{20,16},{24,20},{28,24},{1,29},{... | collective-permute-start | bytes 599048 | tf_op jit(solution)/shard_map/ppermute | solution.py:25
  99.1 17.6 %copy-start.1 = (bf16[2,1,128,384]{3,2,1,0:T(8,128)(2,1)S(1)}, bf16[2,1,128,384]{3,2,1,0:T(8,128)(2,1)}, u32[]{:S(2)}) copy-start(bf16[2,1,128,384]{3,2,1,0:T(8,128)(2,1)} %param.6) | copy-start | bytes 589828
  99.1 7.1 %collective-permute-start.23 = (bf16[2,130,384]{2,1,0:T(8,128)(2,1)S(1)}, bf16[2,130,384]{2,1,0:T(8,128)(2,1)S(1)}, u32[]{:S(2)}, u32[]{:S(2)}) collective-permute-start(bf16[2,130,384]{2,1,0:T(8,128)(2,1)S(1)} %pad_maximum_fusion.6), channel_id=1, source_target_pairs={{0,4},{4,8},{8,12},{12,16},{16,20},{20,24},{24,28},{28,0},{1,5},{5... | collective-permute-start | bytes 599048 | tf_op jit(solution)/shard_map/ppermute | solution.py:25
  99.3 7.0 %collective-permute-start.26 = (bf16[2,130,384]{2,1,0:T(8,128)(2,1)S(1)}, bf16[2,130,384]{2,1,0:T(8,128)(2,1)S(1)}, u32[]{:S(2)}, u32[]{:S(2)}) collective-permute-start(bf16[2,130,384]{2,1,0:T(8,128)(2,1)S(1)} %pad_maximum_fusion.9), channel_id=1, source_target_pairs={{0,28},{4,0},{8,4},{12,8},{16,12},{20,16},{24,20},{28,24},{1,29},{... | collective-permute-start | bytes 599048 | tf_op jit(solution)/shard_map/ppermute | solution.py:25
  107.9 7.1 %collective-permute-start.24 = (bf16[2,130,384]{2,1,0:T(8,128)(2,1)S(1)}, bf16[2,130,384]{2,1,0:T(8,128)(2,1)S(1)}, u32[]{:S(2)}, u32[]{:S(2)}) collective-permute-start(bf16[2,130,384]{2,1,0:T(8,128)(2,1)S(1)} %pad_maximum_fusion.7), channel_id=1, source_target_pairs={{0,4},{4,8},{8,12},{12,16},{16,20},{20,24},{24,28},{28,0},{1,5},{5... | collective-permute-start | bytes 599048 | tf_op jit(solution)/shard_map/ppermute | solution.py:25
  109.2 7.4 %collective-permute-start.27 = (bf16[2,130,384]{2,1,0:T(8,128)(2,1)S(1)}, bf16[2,130,384]{2,1,0:T(8,128)(2,1)S(1)}, u32[]{:S(2)}, u32[]{:S(2)}) collective-permute-start(bf16[2,130,384]{2,1,0:T(8,128)(2,1)S(1)} %pad_maximum_fusion.10), channel_id=1, source_target_pairs={{0,28},{4,0},{8,4},{12,8},{16,12},{20,16},{24,20},{28,24},{1,29},{... | collective-permute-start | bytes 599048 | tf_op jit(solution)/shard_map/ppermute | solution.py:25
  118.5 13.2 %collective-permute-start.32 = (bf16[2,1,128,384]{3,2,0,1:T(8,128)(2,1)S(1)}, bf16[2,1,128,384]{3,2,0,1:T(8,128)(2,1)S(1)}, u32[]{:S(2)}, u32[]{:S(2)}) collective-permute-start(bf16[2,1,128,384]{3,2,0,1:T(8,128)(2,1)S(1)} %multiply_convert_fusion), channel_id=1, source_target_pairs={{1,0},{2,1},{3,2},{4,3},{5,4},{6,5},{7,6},{8,7},{9,8},{10,9},{11,1... | collective-permute-start | bytes 589832 | tf_op jit(solution)/shard_map/ppermute | solution.py:113
  125.8 5.9 %collective-permute-start.31 = (bf16[2,1,128,384]{3,2,0,1:T(8,128)(2,1)S(1)}, bf16[2,1,128,384]{3,2,0,1:T(8,128)(2,1)S(1)}, u32[]{:S(2)}, u32[]{:S(2)}) collective-permute-start(bf16[2,1,128,384]{3,2,0,1:T(8,128)(2,1)S(1)} %multiply_convert_fusion), channel_id=1, source_target_pairs={{1,128},{2,129},{3,130},{4,131},{5,132},{6,133},{7,134},{8,135},{9... | collective-permute-start | bytes 589832 | tf_op jit(solution)/shard_map/ppermute | solution.py:232
  127.1 4.6 %collective-permute-start.30 = (bf16[2,1,128,384]{3,2,0,1:T(8,128)(2,1)S(1)}, bf16[2,1,128,384]{3,2,0,1:T(8,128)(2,1)S(1)}, u32[]{:S(2)}, u32[]{:S(2)}) collective-permute-start(bf16[2,1,128,384]{3,2,0,1:T(8,128)(2,1)S(1)} %multiply_convert_fusion), channel_id=1, source_target_pairs={{0,128},{1,129},{2,130},{3,131},{4,132},{5,133},{6,134},{7,135},{8... | collective-permute-start | bytes 589832 | tf_op jit(solution)/shard_map/ppermute | solution.py:230
  128.4 11.8 %collective-permute-start.29 = (bf16[2,1,128,384]{3,2,0,1:T(8,128)(2,1)S(1)}, bf16[2,1,128,384]{3,2,0,1:T(8,128)(2,1)S(1)}, u32[]{:S(2)}, u32[]{:S(2)}) collective-permute-start(bf16[2,1,128,384]{3,2,0,1:T(8,128)(2,1)S(1)} %multiply_convert_fusion), channel_id=1, source_target_pairs={{0,1},{1,2},{2,3},{3,4},{4,5},{5,6},{6,7},{7,8},{8,9},{9,10},{10,1... | collective-permute-start | bytes 589832 | tf_op jit(solution)/shard_map/ppermute | solution.py:113
  130.4 9.9 %collective-permute-start.28 = (bf16[2,1,128,384]{3,2,0,1:T(8,128)(2,1)S(1)}, bf16[2,1,128,384]{3,2,0,1:T(8,128)(2,1)S(1)}, u32[]{:S(2)}, u32[]{:S(2)}) collective-permute-start(bf16[2,1,128,384]{3,2,0,1:T(8,128)(2,1)S(1)} %multiply_convert_fusion), channel_id=1, source_target_pairs={{0,129},{1,130},{2,131},{3,132},{4,133},{5,134},{6,135},{7,136},{8... | collective-permute-start | bytes 589832 | tf_op jit(solution)/shard_map/ppermute | solution.py:231
  141.5 0.7 copy-start.4

commit v7 on v5

--- a/solution.py
+++ b/solution.py
@@ -99,7 +99,7 @@
         left = unpack(ring_shift(pack(left), axis, -1), rows)
         if s < left_hops:
             left = combine(left, parts[(n - left_hops + s) % n])
-    return combine(combine(right, left), parts[0])
+    return combine(right, combine(left, parts[0]))
 
 
 def row_shift(block, forward):

time: 150 us -> 150 us (level)
  no operation moved by 1% of the time
where the time goes in v7:
time: 150 us; the launch traced here: 149 us
  waiting for transfers between devices  56.5 us (38%)
  starting transfers between devices  48.4 us (32%)
  Pallas kernels  19.4 us (13%)
  other arithmetic  11.6 us (8%)
  matrix products  6.39 us (4%)
  local copies, waits for them, and re-layouts  5.96 us (4%)
    ppermute x28, waiting for transfers between devices, ring_shift(): return lax.ppermute(block, axis, [(i, (i + step) % n) for i in range(n)])  46.8 us
    ppermute x28, starting transfers between devices, ring_shift(): return lax.ppermute(block, axis, [(i, (i + step) % n) for i in range(n)])  36 us
    pallas_call x1, Pallas kernels, attention(): pl.pallas_call(functools.partial(attention_kernel, scale), grid=(frames,...  19.4 us
    ppermute x2, waiting for transfers between devices, row_shift(): return lax.ppermute(block, ROW_AXES, route)  9.76 us
    ppermute x2, starting transfers between devices, row_shift(): return lax.ppermute(block, ROW_AXES, route)  8.5 us
    unnamed x47, local copies, waits for them, and re-layouts  4.14 us
    convert_element_type x3, other arithmetic, pack(): return jnp.concatenate([summed.astype(jnp.bfloat16), stats], axis=1)  3.81 us
    dot_general x1, matrix products, per_device(): jnp.dot(columns, conv_weight.reshape(27 * width, width), preferred_elemen...  3.61 us
  transfers between devices with their start and end apart: 33, of which 15 were waited for; matrix products, arithmetic and copies ran while one was open for 4% of the time, Pallas kernels for 0%

profile of v7, /device:TPU:2, one launch (start us, length us, event | category | flops | bytes accessed | tf_op | source)
XLA Modules:
  0.0 149.0 jit_solution(15268598771650401298)
XLA Ops:
  0.0 1.1 fusion.21
  1.1 1.0 fusion.102
  2.2 2.3 %collective-permute-start.14 = (bf16[2,64,384]{2,1,0:T(8,128)(2,1)S(1)}, bf16[2,64,384]{2,1,0:T(8,128)(2,1)S(1)}, u32[]{:S(2)}, u32[]{:S(2)}) collective-permute-start(bf16[2,64,384]{2,1,0:T(8,128)(2,1)S(1)} %get-tuple-element.60), channel_id=1, source_target_pairs={{0,96},{32,0},{64,32},{96,64},{1,97},{33,1},{65,33},{97,65},{2,98}... | collective-permute-start | bytes 294920 | tf_op jit(solution)/shard_map/ppermute | solution.py:25
  4.5 1.4 collective-permute-start.8
  5.9 1.0 fusion.22
  6.9 2.2 %collective-permute-done.15 = bf16[2,64,384]{2,1,0:T(8,128)(2,1)S(1)} collective-permute-done((bf16[2,64,384]{2,1,0:T(8,128)(2,1)S(1)}, bf16[2,64,384]{2,1,0:T(8,128)(2,1)S(1)}, u32[]{:S(2)}, u32[]{:S(2)}) %collective-permute-start.15) | collective-permute-done | bytes 98336 | tf_op jit(solution)/shard_map/ppermute | solution.py:25
  9.1 1.2 convolution_convert_fusion
  10.4 1.8 %collective-permute-start.3 = (bf16[2,128,384]{2,1,0:T(8,128)(2,1)S(1)}, bf16[2,128,384]{2,1,0:T(8,128)(2,1)S(1)}, u32[]{:S(2)}, u32[]{:S(2)}) collective-permute-start(bf16[2,128,384]{2,1,0:T(8,128)(2,1)S(1)} %bitcast.310), channel_id=1, source_target_pairs={{0,4},{4,8},{8,12},{12,16},{16,20},{20,24},{24,28},{28,0},{1,5},{5... | collective-permute-start | bytes 589832 | tf_op jit(solution)/shard_map/ppermute | solution.py:25
  12.1 3.0 %collective-permute-start.7 = (bf16[2,64,384]{2,1,0:T(8,128)(2,1)S(1)}, bf16[2,64,384]{2,1,0:T(8,128)(2,1)S(1)}, u32[]{:S(2)}, u32[]{:S(2)}) collective-permute-start(bf16[2,64,384]{2,1,0:T(8,128)(2,1)S(1)} %get-tuple-element.61), channel_id=1, source_target_pairs={{0,3},{1,0},{2,1},{3,2},{4,7},{5,4},{6,5},{7,6},{8,11},{9,8},{10,9... | collective-permute-start | bytes 294920 | tf_op jit(solution)/shard_map/ppermute | solution.py:25
  15.2 4.0 %collective-permute-start = (bf16[2,128,384]{2,1,0:T(8,128)(2,1)S(1)}, bf16[2,128,384]{2,1,0:T(8,128)(2,1)S(1)}, u32[]{:S(2)}, u32[]{:S(2)}) collective-permute-start(bf16[2,128,384]{2,1,0:T(8,128)(2,1)S(1)} %bitcast.311), channel_id=1, source_target_pairs={{0,28},{4,0},{8,4},{12,8},{16,12},{20,16},{24,20},{28,24},{1,29},{... | collective-permute-start | bytes 589832 | tf_op jit(solution)/shard_map/ppermute | solution.py:25
  19.2 0.1 fusion.76
  19.3 3.3 %collective-permute-start.17 = (bf16[4,2,64,384]{3,2,1,0:T(8,128)(2,1)S(1)}, bf16[4,2,64,384]{3,2,1,0:T(8,128)(2,1)S(1)}, u32[]{:S(2)}, u32[]{:S(2)}) collective-permute-start(bf16[4,2,64,384]{3,2,1,0:T(8,128)(2,1)S(1)} %get-tuple-element.55), channel_id=1, source_target_pairs={{0,3},{1,0},{2,1},{3,2},{4,7},{5,4},{6,5},{7,6},{8,11},{9,8},{10,9... | collective-permute-start | bytes 1179656 | tf_op jit(solution)/shard_map/ppermute | solution.py:25
  22.6 0.1 collective-permute-start.18
  22.7 3.3 %collective-permute-done.9 = bf16[2,64,384]{2,1,0:T(8,128)(2,1)S(1)} collective-permute-done((bf16[2,64,384]{2,1,0:T(8,128)(2,1)S(1)}, bf16[2,64,384]{2,1,0:T(8,128)(2,1)S(1)}, u32[]{:S(2)}, u32[]{:S(2)}) %collective-permute-start.9) | collective-permute-done | bytes 98336 | tf_op jit(solution)/shard_map/ppermute | solution.py:25
  26.1 0.1 fusion.77
  26.2 2.6 %collective-permute-start.10 = (bf16[4,2,64,384]{3,2,1,0:T(8,128)(2,1)S(1)}, bf16[4,2,64,384]{3,2,1,0:T(8,128)(2,1)S(1)}, u32[]{:S(2)}, u32[]{:S(2)}) collective-permute-start(bf16[4,2,64,384]{3,2,1,0:T(8,128)(2,1)S(1)} %get-tuple-element.57), channel_id=1, source_target_pairs={{0,96},{32,0},{64,32},{96,64},{1,97},{33,1},{65,33},{97,65},{2,98}... | collective-permute-start | bytes 1179656 | tf_op jit(solution)/shard_map/ppermute | solution.py:25
  28.7 0.8 collective-permute-done.4
  29.5 0.7 collective-permute-start.1
  30.2 6.7 %collective-permute-done.1 = bf16[2,128,384]{2,1,0:T(8,128)(2,1)S(1)} collective-permute-done((bf16[2,128,384]{2,1,0:T(8,128)(2,1)S(1)}, bf16[2,128,384]{2,1,0:T(8,128)(2,1)S(1)}, u32[]{:S(2)}, u32[]{:S(2)}) %collective-permute-start.1) | collective-permute-done | bytes 196640 | tf_op jit(solution)/shard_map/ppermute | solution.py:25
  37.0 3.2 %collective-permute-start.2 = (bf16[2,128,384]{2,1,0:T(8,128)(2,1)S(1)}, bf16[2,128,384]{2,1,0:T(8,128)(2,1)S(1)}, u32[]{:S(2)}, u32[]{:S(2)}) collective-permute-start(bf16[2,128,384]{2,1,0:T(8,128)(2,1)S(1)} %collective-permute-done.1), channel_id=1, source_target_pairs={{0,28},{4,0},{8,4},{12,8},{16,12},{20,16},{24,20},{28,24},{1,29},{... | collective-permute-start | bytes 589832 | tf_op jit(solution)/shard_map/ppermute | solution.py:25
  40.3 0.1 collective-permute-start.20
  40.4 2.1 %collective-permute-start.19 = (bf16[2,2,64,384]{3,2,1,0:T(8,128)(2,1)S(1)}, bf16[2,2,64,384]{3,2,1,0:T(8,128)(2,1)S(1)}, u32[]{:S(2)}, u32[]{:S(2)}) collective-permute-start(bf16[2,2,64,384]{3,2,1,0:T(8,128)(2,1)S(1)} %slice.456), channel_id=1, source_target_pairs={{0,1},{1,2},{2,3},{3,0},{4,5},{5,6},{6,7},{7,4},{8,9},{9,10},{10,1... | collective-permute-start | bytes 589832 | tf_op jit(solution)/shard_map/ppermute | solution.py:25
  42.5 2.7 %collective-permute-start.13 = (bf16[2,2,64,384]{3,2,1,0:T(8,128)(2,1)S(1)}, bf16[2,2,64,384]{3,2,1,0:T(8,128)(2,1)S(1)}, u32[]{:S(2)}, u32[]{:S(2)}) collective-permute-start(bf16[2,2,64,384]{3,2,1,0:T(8,128)(2,1)S(1)} %slice.454), channel_id=1, source_target_pairs={{0,96},{32,0},{64,32},{96,64},{1,97},{33,1},{65,33},{97,65},{2,98}... | collective-permute-start | bytes 589832 | tf_op jit(solution)/shard_map/ppermute | solution.py:25
  45.3 0.4 collective-permute-done.5
  45.7 1.3 collective-permute-start.12
  47.1 0.3 collective-permute-done.19
  47.4 1.5 %pad_maximum_fusion.1 = bf16[4,4,2,64,384]{4,3,2,1,0:T(8,128)(2,1)} fusion(bf16[1,4,2,64,384]{4,3,2,1,0:T(8,128)(2,1)S(1)} %bitcast.308, bf16[1,4,2,64,384]{4,3,2,1,0:T(8,128)(2,1)S(1)} %maximum_bitcast_fusion.1, bf16[1,4,2,64,384]{4,3,2,1,0:T(8,128)(2,1)S(1)} %bitcast.306, bf16[1,4,2,64,384]{4,3,2,1,0:T(8,128)(2,1)S(1)} %get-tuple-element.54), kind=kLoop, calls=%fused_computation.6 | loop fusion | flops 2359296 | bytes 3145728 | tf_op jit(solution)/shard_map/stack | solution.py:205
  48.9 3.5 %collective-permute-done.12 = bf16[2,2,64,384]{3,2,1,0:T(8,128)(2,1)S(1)} collective-permute-done((bf16[2,2,64,384]{3,2,1,0:T(8,128)(2,1)S(1)}, bf16[2,2,64,384]{3,2,1,0:T(8,128)(2,1)S(1)}, u32[]{:S(2)}, u32[]{:S(2)}) %collective-permute-start.12) | collective-permute-done | bytes 196640 | tf_op jit(solution)/shard_map/ppermute | solution.py:25
  52.4 1.4 pad_maximum_fusion
  53.9 0.1 collective-permute-done.6
  54.1 1.2 copy-done.2
  55.3 19.4 %shard_map.64 = (f32[2,1,1024]{2,1,0:T(1,128)}, f32[2,1,1024]{2,1,0:T(1,128)}, f32[2,1024,384]{2,1,0:T(8,128)}, bf16[2,1024,384]{2,1,0:T(8,128)(2,1)}) custom-call(bf16[8,2,128,384]{3,2,1,0:T(8,128)(2,1)} %copy-done.2, bf16[16,2,64,384]{3,2,1,0:T(8,128)(2,1)} %bitcast.305, bf16[16,2,64,384]{3,2,1,0:T(8,128)(2,1)} %bitcast.304, bf16[384,384]{1,0:T(8,128)(2,1)} %key_w_ref.1, ...), custom_call_target="tpu_custom_call" | custom-call | flops 8858370048 | bytes 9437184 | tf_op jit(solution)/shard_map/pallas_call | solution.py:161
  74.6 1.1 fusion.91
  75.7 0.7 copy_bitcast_fusion
  76.6 0.1 collective-permute-start.21
  76.7 7.2 %collective-permute-done.21 = bf16[2,130,384]{2,1,0:T(8,128)(2,1)S(1)} collective-permute-done((bf16[2,130,384]{2,1,0:T(8,128)(2,1)S(1)}, bf16[2,130,384]{2,1,0:T(8,128)(2,1)S(1)}, u32[]{:S(2)}, u32[]{:S(2)}) %collective-permute-start.21) | collective-permute-done | bytes 199712 | tf_op jit(solution)/shard_map/ppermute | solution.py:25
  84.1 1.1 add_convert_fusion.4
  85.2 0.1 collective-permute-start.22
  85.3 7.0 %collective-permute-done.22 = bf16[2,130,384]{2,1,0:T(8,128)(2,1)S(1)} collective-permute-done((bf16[2,130,384]{2,1,0:T(8,128)(2,1)S(1)}, bf16[2,130,384]{2,1,0:T(8,128)(2,1)S(1)}, u32[]{:S(2)}, u32[]{:S(2)}) %collective-permute-start.22) | collective-permute-done | bytes 199712 | tf_op jit(solution)/shard_map/ppermute | solution.py:25
  92.5 0.3 collective-permute-start.25
  92.9 5.7 %collective-permute-done.25 = bf16[2,130,384]{2,1,0:T(8,128)(2,1)S(1)} collective-permute-done((bf16[2,130,384]{2,1,0:T(8,128)(2,1)S(1)}, bf16[2,130,384]{2,1,0:T(8,128)(2,1)S(1)}, u32[]{:S(2)}, u32[]{:S(2)}) %collective-permute-start.25) | collective-permute-done | bytes 199712 | tf_op jit(solution)/shard_map/ppermute | solution.py:25
  98.7 1.3 add_convert_fusion.3
  100.1 0.1 collective-permute-start.23
  100.3 3.3 %collective-permute-start.26 = (bf16[2,130,384]{2,1,0:T(8,128)(2,1)S(1)}, bf16[2,130,384]{2,1,0:T(8,128)(2,1)S(1)}, u32[]{:S(2)}, u32[]{:S(2)}) collective-permute-start(bf16[2,130,384]{2,1,0:T(8,128)(2,1)S(1)} %pad_maximum_fusion.9), channel_id=1, source_target_pairs={{0,28},{4,0},{8,4},{12,8},{16,12},{20,16},{24,20},{28,24},{1,29},{... | collective-permute-start | bytes 599048 | tf_op jit(solution)/shard_map/ppermute | solution.py:25
  103.6 3.6 %collective-permute-done.23 = bf16[2,130,384]{2,1,0:T(8,128)(2,1)S(1)} collective-permute-done((bf16[2,130,384]{2,1,0:T(8,128)(2,1)S(1)}, bf16[2,130,384]{2,1,0:T(8,128)(2,1)S(1)}, u32[]{:S(2)}, u32[]{:S(2)}) %collective-permute-start.23) | collective-permute-done | bytes 199712 | tf_op jit(solution)/shard_map/ppermute | solution.py:25
  107.5 1.3 add_convert_fusion.2
  108.8 1.2 collective-permute-start.24
  110.1 2.2 %collective-permute-start.27 = (bf16[2,130,384]{2,1,0:T(8,128)(2,1)S(1)}, bf16[2,130,384]{2,1,0:T(8,128)(2,1)S(1)}, u32[]{:S(2)}, u32[]{:S(2)}) collective-permute-start(bf16[2,130,384]{2,1,0:T(8,128)(2,1)S(1)} %pad_maximum_fusion.10), channel_id=1, source_target_pairs={{0,28},{4,0},{8,4},{12,8},{16,12},{20,16},{24,20},{28,24},{1,29},{... | collective-permute-start | bytes 599048 | tf_op jit(solution)/shard_map/ppermute | solution.py:25
  112.4 3.6 %collective-permute-done.24 = bf16[2,130,384]{2,1,0:T(8,128)(2,1)S(1)} collective-permute-done((bf16[2,130,384]{2,1,0:T(8,128)(2,1)S(1)}, bf16[2,130,384]{2,1,0:T(8,128)(2,1)S(1)}, u32[]{:S(2)}, u32[]{:S(2)}) %collective-permute-start.24) | collective-permute-done | bytes 199712 | tf_op jit(solution)/shard_map/ppermute | solution.py:25
  116.0 2.3 %collective-permute-done.27 = bf16[2,130,384]{2,1,0:T(8,128)(2,1)S(1)} collective-permute-done((bf16[2,130,384]{2,1,0:T(8,128)(2,1)S(1)}, bf16[2,130,384]{2,1,0:T(8,128)(2,1)S(1)}, u32[]{:S(2)}, u32[]{:S(2)}) %collective-permute-start.27) | collective-permute-done | bytes 199712 | tf_op jit(solution)/shard_map/ppermute | solution.py:25
  118.4 1.5 %multiply_reduce_fusion = (f32[2,128]{1,0:T(2,128)S(1)}, f32[2,1,128,384]{3,2,0,1:T(8,128)S(1)}) fusion(bf16[384,384]{1,0:T(8,128)(2,1)S(1)} %copy-done, f32[2,1024,384]{2,1,0:T(8,128)} %get-tuple-element.12, bf16[2,130,384]{2,1,0:T(8,128)(2,1)S(1)} %collective-permute-done.27, bf16[2,130,384]{2,1,0:T(8,128)(2,1)S(1)} %collective-permute-done.24, ...), kind=kOutput, calls=%fused_computation.30 | convolution fusion | flops 77070080 | bytes 1677312 | tf_op jit(solution)/shard_map/dot_general | solution.py:221
  120.0 0.2 multiply_convert_fusion
  120.2 1.3 collective-permute-start.28
  121.5 1.3 collective-permute-start.31
  122.8 6.6 %collective-permute-start.32 = (bf16[2,1,128,384]{3,2,0,1:T(8,128)(2,1)S(1)}, bf16[2,1,128,384]{3,2,0,1:T(8,128)(2,1)S(1)}, u32[]{:S(2)}, u32[]{:S(2)}) collective-permute-start(bf16[2,1,128,384]{3,2,0,1:T(8,128)(2,1)S(1)} %multiply_convert_fusion), channel_id=1, source_target_pairs={{1,0},{2,1},{3,2},{4,3},{5,4},{6,5},{7,6},{8,7},{9,8},{10,9},{11,1... | collective-permute-start | bytes 589832 | tf_op jit(solution)/shard_map/ppermute | solution.py:113
  129.4 1.3 collective-permute-start.30
  130.7 1.9 %collective-permute-start.29 = (bf16[2,1,128,384]{3,2,0,1:T(8,128)(2,1)S(1)}, bf16[2,1,128,384]{3,2,0,1:T(8,128)(2,1)S(1)}, u32[]{:S(2)}, u32[]{:S(2)}) collective-permute-start(bf16[2,1,128,384]{3,2,0,1:T(8,128)(2,1)S(1)} %multiply_convert_fusion), channel_id=1, source_target_pairs={{0,1},{1,2},{2,3},{3,4},{4,5},{5,6},{6,7},{7,8},{8,9},{9,10},{10,1... | collective-permute-start | bytes 589832 | tf_op jit(solution)/shard_map/ppermute | solution.py:113
  132.7 9.8 %collective-permute-done.29 = bf16[2,1,128,384]{3,2,0,1:T(8,128)(2,1)S(1)} collective-permute-done((bf16[2,1,128,384]{3,2,0,1:T(8,128)(2,1)S(1)}, bf16[2,1,128,384]{3,2,0,1:T(8,128)(2,1)S(1)}, u32[]{:S(2)}, u32[]{:S(2)}) %collective-permute-start.29) | collective-permute-done | bytes 196640 | tf_op jit(solution)/shard_map/ppermute | solution.py:113
  142.6 0.3 select_maximum_fusion
  143.2 0.1 slice_dynamic-update-slice_fusion.16
  143.5 0.1 slice_dynamic-update-slice_fusion.11
  144.0 0.2 constant_dynamic-update-slice_fusion.48
  144.5 0.9 slice-done.1
  145.4 3.6 %fusion.18 = bf16[2,1,128,384]{3,2,1,0:T(8,128)(2,1)} fusion(f32[2,1,128,384]{3,2,0,1:T(8,128)S(1)} %get-tuple-element.110, bf16[10368,384,1]{1,0,2:T(8,128)(2,1)S(1)} %bitcast.322, bf16[2,1,128,10368]{3,2,0,1:T(8,128)(2,1)S(1)} %slice_dynamic-update-slice_fusion), kind=kOutput, calls=%fused_computation.20 | convolution fusion | flops 2038628352 | bytes 13860864 | tf_op jit(solution)/shard_map/dot_general | solution.py:250
  (160 shorter events, 2.8 us)
Async XLA Ops:
  0.0 118.4 %copy-start = (bf16[384,384]{1,0:T(8,128)(2,1)S(1)}, bf16[384,384]{1,0:T(8,128)(2,1)}, u32[]{:S(2)}) copy-start(bf16[384,384]{1,0:T(8,128)(2,1)} %param.10) | copy-start | bytes 884740
  2.2 13.0 %collective-permute-start.14 = (bf16[2,64,384]{2,1,0:T(8,128)(2,1)S(1)}, bf16[2,64,384]{2,1,0:T(8,128)(2,1)S(1)}, u32[]{:S(2)}, u32[]{:S(2)}) collective-permute-start(bf16[2,64,384]{2,1,0:T(8,128)(2,1)S(1)} %get-tuple-element.60), channel_id=1, source_target_pairs={{0,96},{32,0},{64,32},{96,64},{1,97},{33,1},{65,33},{97,65},{2,98}... | collective-permute-start | bytes 294920 | tf_op jit(solution)/shard_map/ppermute | solution.py:25
  4.5 4.6 %collective-permute-start.15 = (bf16[2,64,384]{2,1,0:T(8,128)(2,1)S(1)}, bf16[2,64,384]{2,1,0:T(8,128)(2,1)S(1)}, u32[]{:S(2)}, u32[]{:S(2)}) collective-permute-start(bf16[2,64,384]{2,1,0:T(8,128)(2,1)S(1)} %get-tuple-element.60), channel_id=1, source_target_pairs={{0,32},{32,64},{64,96},{96,0},{1,33},{33,65},{65,97},{97,1},{2,34}... | collective-permute-start | bytes 294920 | tf_op jit(solution)/shard_map/ppermute | solution.py:25
  4.5 14.7 %collective-permute-start.8 = (bf16[2,64,384]{2,1,0:T(8,128)(2,1)S(1)}, bf16[2,64,384]{2,1,0:T(8,128)(2,1)S(1)}, u32[]{:S(2)}, u32[]{:S(2)}) collective-permute-start(bf16[2,64,384]{2,1,0:T(8,128)(2,1)S(1)} %get-tuple-element.61), channel_id=1, source_target_pairs={{0,1},{1,2},{2,3},{3,0},{4,5},{5,6},{6,7},{7,4},{8,9},{9,10},{10,1... | collective-permute-start | bytes 294920 | tf_op jit(solution)/shard_map/ppermute | solution.py:25
  9.1 10.1 %collective-permute-start.16 = (bf16[2,64,384]{2,1,0:T(8,128)(2,1)S(1)}, bf16[2,64,384]{2,1,0:T(8,128)(2,1)S(1)}, u32[]{:S(2)}, u32[]{:S(2)}) collective-permute-start(bf16[2,64,384]{2,1,0:T(8,128)(2,1)S(1)} %collective-permute-done.15), channel_id=1, source_target_pairs={{0,32},{32,64},{64,96},{96,0},{1,33},{33,65},{65,97},{97,1},{2,34}... | collective-permute-start | bytes 294920 | tf_op jit(solution)/shard_map/ppermute | solution.py:25
  10.4 12.2 %collective-permute-start.3 = (bf16[2,128,384]{2,1,0:T(8,128)(2,1)S(1)}, bf16[2,128,384]{2,1,0:T(8,128)(2,1)S(1)}, u32[]{:S(2)}, u32[]{:S(2)}) collective-permute-start(bf16[2,128,384]{2,1,0:T(8,128)(2,1)S(1)} %bitcast.310), channel_id=1, source_target_pairs={{0,4},{4,8},{8,12},{12,16},{16,20},{20,24},{24,28},{28,0},{1,5},{5... | collective-permute-start | bytes 589832 | tf_op jit(solution)/shard_map/ppermute | solution.py:25
  12.1 10.5 %collective-permute-start.7 = (bf16[2,64,384]{2,1,0:T(8,128)(2,1)S(1)}, bf16[2,64,384]{2,1,0:T(8,128)(2,1)S(1)}, u32[]{:S(2)}, u32[]{:S(2)}) collective-permute-start(bf16[2,64,384]{2,1,0:T(8,128)(2,1)S(1)} %get-tuple-element.61), channel_id=1, source_target_pairs={{0,3},{1,0},{2,1},{3,2},{4,7},{5,4},{6,5},{7,6},{8,11},{9,8},{10,9... | collective-permute-start | bytes 294920 | tf_op jit(solution)/shard_map/ppermute | solution.py:25
  15.2 13.6 %collective-permute-start = (bf16[2,128,384]{2,1,0:T(8,128)(2,1)S(1)}, bf16[2,128,384]{2,1,0:T(8,128)(2,1)S(1)}, u32[]{:S(2)}, u32[]{:S(2)}) collective-permute-start(bf16[2,128,384]{2,1,0:T(8,128)(2,1)S(1)} %bitcast.311), channel_id=1, source_target_pairs={{0,28},{4,0},{8,4},{12,8},{16,12},{20,16},{24,20},{28,24},{1,29},{... | collective-permute-start | bytes 589832 | tf_op jit(solution)/shard_map/ppermute | solution.py:25
  19.2 6.9 %collective-permute-start.9 = (bf16[2,64,384]{2,1,0:T(8,128)(2,1)S(1)}, bf16[2,64,384]{2,1,0:T(8,128)(2,1)S(1)}, u32[]{:S(2)}, u32[]{:S(2)}) collective-permute-start(bf16[2,64,384]{2,1,0:T(8,128)(2,1)S(1)} %collective-permute-done.8), channel_id=1, source_target_pairs={{0,1},{1,2},{2,3},{3,0},{4,5},{5,6},{6,7},{7,4},{8,9},{9,10},{10,1... | collective-permute-start | bytes 294920 | tf_op jit(solution)/shard_map/ppermute | solution.py:25
  19.3 17.7 %collective-permute-start.17 = (bf16[4,2,64,384]{3,2,1,0:T(8,128)(2,1)S(1)}, bf16[4,2,64,384]{3,2,1,0:T(8,128)(2,1)S(1)}, u32[]{:S(2)}, u32[]{:S(2)}) collective-permute-start(bf16[4,2,64,384]{3,2,1,0:T(8,128)(2,1)S(1)} %get-tuple-element.55), channel_id=1, source_target_pairs={{0,3},{1,0},{2,1},{3,2},{4,7},{5,4},{6,5},{7,6},{8,11},{9,8},{10,9... | collective-permute-start | bytes 1179656 | tf_op jit(solution)/shard_map/ppermute | solution.py:25
  22.6 6.9 %collective-permute-start.4 = (bf16[2,128,384]{2,1,0:T(8,128)(2,1)S(1)}, bf16[2,128,384]{2,1,0:T(8,128)(2,1)S(1)}, u32[]{:S(2)}, u32[]{:S(2)}) collective-permute-start(bf16[2,128,384]{2,1,0:T(8,128)(2,1)S(1)} %collective-permute-done.3), channel_id=1, source_target_pairs={{0,4},{4,8},{8,12},{12,16},{16,20},{20,24},{24,28},{28,0},{1,5},{5... | collective-permute-start | bytes 589832 | tf_op jit(solution)/shard_map/ppermute | solution.py:25
  22.6 17.6 %collective-permute-start.18 = (bf16[4,2,64,384]{3,2,1,0:T(8,128)(2,1)S(1)}, bf16[4,2,64,384]{3,2,1,0:T(8,128)(2,1)S(1)}, u32[]{:S(2)}, u32[]{:S(2)}) collective-permute-start(bf16[4,2,64,384]{3,2,1,0:T(8,128)(2,1)S(1)} %get-tuple-element.55), channel_id=1, source_target_pairs={{0,1},{1,2},{2,3},{3,0},{4,5},{5,6},{6,7},{7,4},{8,9},{9,10},{10,1... | collective-permute-start | bytes 1179656 | tf_op jit(solution)/shard_map/ppermute | solution.py:25
  26.2 14.2 %collective-permute-start.10 = (bf16[4,2,64,384]{3,2,1,0:T(8,128)(2,1)S(1)}, bf16[4,2,64,384]{3,2,1,0:T(8,128)(2,1)S(1)}, u32[]{:S(2)}, u32[]{:S(2)}) collective-permute-start(bf16[4,2,64,384]{3,2,1,0:T(8,128)(2,1)S(1)} %get-tuple-element.57), channel_id=1, source_target_pairs={{0,96},{32,0},{64,32},{96,64},{1,97},{33,1},{65,33},{97,65},{2,98}... | collective-permute-start | bytes 1179656 | tf_op jit(solution)/shard_map/ppermute | solution.py:25
  28.7 13.8 %collective-permute-start.11 = (bf16[4,2,64,384]{3,2,1,0:T(8,128)(2,1)S(1)}, bf16[4,2,64,384]{3,2,1,0:T(8,128)(2,1)S(1)}, u32[]{:S(2)}, u32[]{:S(2)}) collective-permute-start(bf16[4,2,64,384]{3,2,1,0:T(8,128)(2,1)S(1)} %get-tuple-element.57), channel_id=1, source_target_pairs={{0,32},{32,64},{64,96},{96,0},{1,33},{33,65},{65,97},{97,1},{2,34}... | collective-permute-start | bytes 1179656 | tf_op jit(solution)/shard_map/ppermute | solution.py:25
  29.5 7.5 %collective-permute-start.1 = (bf16[2,128,384]{2,1,0:T(8,128)(2,1)S(1)}, bf16[2,128,384]{2,1,0:T(8,128)(2,1)S(1)}, u32[]{:S(2)}, u32[]{:S(2)}) collective-permute-start(bf16[2,128,384]{2,1,0:T(8,128)(2,1)S(1)} %collective-permute-done), channel_id=1, source_target_pairs={{0,28},{4,0},{8,4},{12,8},{16,12},{20,16},{24,20},{28,24},{1,29},{... | collective-permute-start | bytes 589832 | tf_op jit(solution)/shard_map/ppermute | solution.py:25
  37.0 8.8 %collective-permute-start.5 = (bf16[2,128,384]{2,1,0:T(8,128)(2,1)S(1)}, bf16[2,128,384]{2,1,0:T(8,128)(2,1)S(1)}, u32[]{:S(2)}, u32[]{:S(2)}) collective-permute-start(bf16[2,128,384]{2,1,0:T(8,128)(2,1)S(1)} %collective-permute-done.4), channel_id=1, source_target_pairs={{0,4},{4,8},{8,12},{12,16},{16,20},{20,24},{24,28},{28,0},{1,5},{5... | collective-permute-start | bytes 589832 | tf_op jit(solution)/shard_map/ppermute | solution.py:25
  37.0 10.1 %collective-permute-start.2 = (bf16[2,128,384]{2,1,0:T(8,128)(2,1)S(1)}, bf16[2,128,384]{2,1,0:T(8,128)(2,1)S(1)}, u32[]{:S(2)}, u32[]{:S(2)}) collective-permute-start(bf16[2,128,384]{2,1,0:T(8,128)(2,1)S(1)} %collective-permute-done.1), channel_id=1, source_target_pairs={{0,28},{4,0},{8,4},{12,8},{16,12},{20,16},{24,20},{28,24},{1,29},{... | collective-permute-start | bytes 589832 | tf_op jit(solution)/shard_map/ppermute | solution.py:25
  40.3 6.8 %collective-permute-start.20 = (bf16[2,2,64,384]{3,2,1,0:T(8,128)(2,1)S(1)}, bf16[2,2,64,384]{3,2,1,0:T(8,128)(2,1)S(1)}, u32[]{:S(2)}, u32[]{:S(2)}) collective-permute-start(bf16[2,2,64,384]{3,2,1,0:T(8,128)(2,1)S(1)} %slice.457), channel_id=1, source_target_pairs={{0,3},{1,0},{2,1},{3,2},{4,7},{5,4},{6,5},{7,6},{8,11},{9,8},{10,9... | collective-permute-start | bytes 589832 | tf_op jit(solution)/shard_map/ppermute | solution.py:25
  40.4 7.0 %collective-permute-start.19 = (bf16[2,2,64,384]{3,2,1,0:T(8,128)(2,1)S(1)}, bf16[2,2,64,384]{3,2,1,0:T(8,128)(2,1)S(1)}, u32[]{:S(2)}, u32[]{:S(2)}) collective-permute-start(bf16[2,2,64,384]{3,2,1,0:T(8,128)(2,1)S(1)} %slice.456), channel_id=1, source_target_pairs={{0,1},{1,2},{2,3},{3,0},{4,5},{5,6},{6,7},{7,4},{8,9},{9,10},{10,1... | collective-permute-start | bytes 589832 | tf_op jit(solution)/shard_map/ppermute | solution.py:25
  42.5 6.4 %collective-permute-start.13 = (bf16[2,2,64,384]{3,2,1,0:T(8,128)(2,1)S(1)}, bf16[2,2,64,384]{3,2,1,0:T(8,128)(2,1)S(1)}, u32[]{:S(2)}, u32[]{:S(2)}) collective-permute-start(bf16[2,2,64,384]{3,2,1,0:T(8,128)(2,1)S(1)} %slice.454), channel_id=1, source_target_pairs={{0,96},{32,0},{64,32},{96,64},{1,97},{33,1},{65,33},{97,65},{2,98}... | collective-permute-start | bytes 589832 | tf_op jit(solution)/shard_map/ppermute | solution.py:25
  45.7 6.7 %collective-permute-start.12 = (bf16[2,2,64,384]{3,2,1,0:T(8,128)(2,1)S(1)}, bf16[2,2,64,384]{3,2,1,0:T(8,128)(2,1)S(1)}, u32[]{:S(2)}, u32[]{:S(2)}) collective-permute-start(bf16[2,2,64,384]{3,2,1,0:T(8,128)(2,1)S(1)} %slice.453), channel_id=1, source_target_pairs={{0,32},{32,64},{64,96},{96,0},{1,33},{33,65},{65,97},{97,1},{2,34}... | collective-permute-start | bytes 589832 | tf_op jit(solution)/shard_map/ppermute | solution.py:25
  47.1 6.9 %collective-permute-start.6 = (bf16[2,128,384]{2,1,0:T(8,128)(2,1)S(1)}, bf16[2,128,384]{2,1,0:T(8,128)(2,1)S(1)}, u32[]{:S(2)}, u32[]{:S(2)}) collective-permute-start(bf16[2,128,384]{2,1,0:T(8,128)(2,1)S(1)} %collective-permute-done.5), channel_id=1, source_target_pairs={{0,4},{4,8},{8,12},{12,16},{16,20},{20,24},{24,28},{28,0},{1,5},{5... | collective-permute-start | bytes 589832 | tf_op jit(solution)/shard_map/ppermute | solution.py:25
  54.1 1.2 copy-start.2
  74.6 43.8 %copy-start.1 = (bf16[2,1,128,384]{3,2,1,0:T(8,128)(2,1)S(1)}, bf16[2,1,128,384]{3,2,1,0:T(8,128)(2,1)}, u32[]{:S(2)}) copy-start(bf16[2,1,128,384]{3,2,1,0:T(8,128)(2,1)} %param.6) | copy-start | bytes 589828
  76.6 7.3 %collective-permute-start.21 = (bf16[2,130,384]{2,1,0:T(8,128)(2,1)S(1)}, bf16[2,130,384]{2,1,0:T(8,128)(2,1)S(1)}, u32[]{:S(2)}, u32[]{:S(2)}) collective-permute-start(bf16[2,130,384]{2,1,0:T(8,128)(2,1)S(1)} %pad_maximum_fusion.4), channel_id=1, source_target_pairs={{0,4},{4,8},{8,12},{12,16},{16,20},{20,24},{24,28},{28,0},{1,5},{5... | collective-permute-start | bytes 599048 | tf_op jit(solution)/shard_map/ppermute | solution.py:25
  85.2 7.1 %collective-permute-start.22 = (bf16[2,130,384]{2,1,0:T(8,128)(2,1)S(1)}, bf16[2,130,384]{2,1,0:T(8,128)(2,1)S(1)}, u32[]{:S(2)}, u32[]{:S(2)}) collective-permute-start(bf16[2,130,384]{2,1,0:T(8,128)(2,1)S(1)} %pad_maximum_fusion.5), channel_id=1, source_target_pairs={{0,4},{4,8},{8,12},{12,16},{16,20},{20,24},{24,28},{28,0},{1,5},{5... | collective-permute-start | bytes 599048 | tf_op jit(solution)/shard_map/ppermute | solution.py:25
  92.5 6.1 %collective-permute-start.25 = (bf16[2,130,384]{2,1,0:T(8,128)(2,1)S(1)}, bf16[2,130,384]{2,1,0:T(8,128)(2,1)S(1)}, u32[]{:S(2)}, u32[]{:S(2)}) collective-permute-start(bf16[2,130,384]{2,1,0:T(8,128)(2,1)S(1)} %pad_maximum_fusion.8), channel_id=1, source_target_pairs={{0,28},{4,0},{8,4},{12,8},{16,12},{20,16},{24,20},{28,24},{1,29},{... | collective-permute-start | bytes 599048 | tf_op jit(solution)/shard_map/ppermute | solution.py:25
  100.1 7.1 %collective-permute-start.23 = (bf16[2,130,384]{2,1,0:T(8,128)(2,1)S(1)}, bf16[2,130,384]{2,1,0:T(8,128)(2,1)S(1)}, u32[]{:S(2)}, u32[]{:S(2)}) collective-permute-start(bf16[2,130,384]{2,1,0:T(8,128)(2,1)S(1)} %pad_maximum_fusion.6), channel_id=1, source_target_pairs={{0,4},{4,8},{8,12},{12,16},{16,20},{20,24},{24,28},{28,0},{1,5},{5... | collective-permute-start | bytes 599048 | tf_op jit(solution)/shard_map/ppermute | solution.py:25
  100.3 7.0 %collective-permute-start.26 = (bf16[2,130,384]{2,1,0:T(8,128)(2,1)S(1)}, bf16[2,130,384]{2,1,0:T(8,128)(2,1)S(1)}, u32[]{:S(2)}, u32[]{:S(2)}) collective-permute-start(bf16[2,130,384]{2,1,0:T(8,128)(2,1)S(1)} %pad_maximum_fusion.9), channel_id=1, source_target_pairs={{0,28},{4,0},{8,4},{12,8},{16,12},{20,16},{24,20},{28,24},{1,29},{... | collective-permute-start | bytes 599048 | tf_op jit(solution)/shard_map/ppermute | solution.py:25
  108.8 7.1 %collective-permute-start.24 = (bf16[2,130,384]{2,1,0:T(8,128)(2,1)S(1)}, bf16[2,130,384]{2,1,0:T(8,128)(2,1)S(1)}, u32[]{:S(2)}, u32[]{:S(2)}) collective-permute-start(bf16[2,130,384]{2,1,0:T(8,128)(2,1)S(1)} %pad_maximum_fusion.7), channel_id=1, source_target_pairs={{0,4},{4,8},{8,12},{12,16},{16,20},{20,24},{24,28},{28,0},{1,5},{5... | collective-permute-start | bytes 599048 | tf_op jit(solution)/shard_map/ppermute | solution.py:25
  110.1 8.2 %collective-permute-start.27 = (bf16[2,130,384]{2,1,0:T(8,128)(2,1)S(1)}, bf16[2,130,384]{2,1,0:T(8,128)(2,1)S(1)}, u32[]{:S(2)}, u32[]{:S(2)}) collective-permute-start(bf16[2,130,384]{2,1,0:T(8,128)(2,1)S(1)} %pad_maximum_fusion.10), channel_id=1, source_target_pairs={{0,28},{4,0},{8,4},{12,8},{16,12},{20,16},{24,20},{28,24},{1,29},{... | collective-permute-start | bytes 599048 | tf_op jit(solution)/shard_map/ppermute | solution.py:25
  120.2 12.4 %collective-permute-start.28 = (bf16[2,1,128,384]{3,2,0,1:T(8,128)(2,1)S(1)}, bf16[2,1,128,384]{3,2,0,1:T(8,128)(2,1)S(1)}, u32[]{:S(2)}, u32[]{:S(2)}) collective-permute-start(bf16[2,1,128,384]{3,2,0,1:T(8,128)(2,1)S(1)} %multiply_convert_fusion), channel_id=1, source_target_pairs={{0,129},{1,130},{2,131},{3,132},{4,133},{5,134},{6,135},{7,136},{8... | collective-permute-start | bytes 589832 | tf_op jit(solution)/shard_map/ppermute | solution.py:231
  121.5 11.2 %collective-permute-start.31 = (bf16[2,1,128,384]{3,2,0,1:T(8,128)(2,1)S(1)}, bf16[2,1,128,384]{3,2,0,1:T(8,128)(2,1)S(1)}, u32[]{:S(2)}, u32[]{:S(2)}) collective-permute-start(bf16[2,1,128,384]{3,2,0,1:T(8,128)(2,1)S(1)} %multiply_convert_fusion), channel_id=1, source_target_pairs={{1,128},{2,129},{3,130},{4,131},{5,132},{6,133},{7,134},{8,135},{9... | collective-permute-start | bytes 589832 | tf_op jit(solution)/shard_map/ppermute | solution.py:232
  122.8 19.7 %collective-permute-start.32 = (bf16[2,1,128,384]{3,2,0,1:T(8,128)(2,1)S(1)}, bf16[2,1,128,384]{3,2,0,1:T(8,128)(2,1)S(1)}, u32[]{:S(2)}, u32[]{:S(2)}) collective-permute-start(bf16[2,1,128,384]{3,2,0,1:T(8,128)(2,1)S(1)} %multiply_convert_fusion), channel_id=1, source_target_pairs={{1,0},{2,1},{3,2},{4,3},{5,4},{6,5},{7,6},{8,7},{9,8},{10,9},{11,1... | collective-permute-start | bytes 589832 | tf_op jit(solution)/shard_map/ppermute | solution.py:113
  129.4 13.2 %collective-permute-start.30 = (bf16[2,1,128,384]{3,2,0,1:T(8,128)(2,1)S(1)}, bf16[2,1,128,384]{3,2,0,1:T(8,128)(2,1)S(1)}, u32[]{:S(2)}, u32[]{:S(2)}) collective-permute-start(bf16[2,1,128,384]{3,2,0,1:T(8,128)(2,1)S(1)} %multiply_convert_fusion), channel_id=1, source_target_pairs={{0,128},{1,129},{2,130},{3,131},{4,132},{5,133},{6,134},{7,135},{8... | collective-permute-start | bytes 589832 | tf_op jit(solution)/shard_map/ppermute | solution.py:230
  130.7 11.8 %collective-permute-start.29 = (bf16[2,1,128,384]{3,2,0,1:T(8,128)(2,1)S(1)}, bf16[2,1,128,384]{3,2,0,1:T(8,128)(2,1)S(1)}, u32[]{:S(2)}, u32[]{:S(2)}) collective-permute-start(bf16[2,1,128,384]{3,2,0,1:T(8,128)(2,1)S(1)} %multiply_convert_fusion), channel_id=1, source_target_pairs={{0,1},{1,2},{2,3},{3,4},{4,5},{5,6},{6,7},{7,8},{8,9},{9,10},{10,1... | collective-permute-start | bytes 589832 | tf_op jit(solution)/shard_map/ppermute | solution.py:113
  132.7 11.8 %slice-start = ((s8[7962624]{0:T(1024)(128)(4,1)}), s8[4194304]{0:T(1024)(128)(4,1)S(1)}, s32[]{:S(2)}) async-start(s8[7962624]{0:T(1024)(128)(4,1)} %bitcast.320), calls=%async_computation | async-start | bytes 8388608
  143.3 2.1 %slice-start.1 = ((s8[7962624]{0:T(1024)(128)(4,1)}), s8[3768320]{0:T(1024)(128)(4,1)S(1)}, s32[]{:S(2)}) async-start(s8[7962624]{0:T(1024)(128)(4,1)} %bitcast.320), calls=%async_computation.1 | async-start | bytes 7536640

commit v8 on v7

--- a/solution.py
+++ b/solution.py
@@ -196,7 +196,7 @@
     scale = 1.0 / math.sqrt(width)
 
     query = project(flat, query_weight).reshape(frames, count, width)
-    query_rel = ring_gather(query, "z")
+    query_rel = ring_gather(query, "z", halve=True)
     tokens = normed.reshape(frames, count, width)
     half = count // 2
     chains = []

time: 150 us -> 156 us (1.040)
  starting transfers between devices: 48.4 us -> 57.3 us
  waiting for transfers between devices: 56.5 us -> 54.8 us
    ppermute x28 -> x29, starting transfers between devices: 36 us -> 41.7 us  [ring_shift(): return lax.ppermute(block, axis, [(i, (i + step) % n) for i in range(n)])]
    ppermute x2, starting transfers between devices: 8.5 us -> 11.8 us  [row_shift(): return lax.ppermute(block, ROW_AXES, route)]
    ppermute x28 -> x29, waiting for transfers between devices: 46.8 us -> 45.1 us  [ring_shift(): return lax.ppermute(block, axis, [(i, (i + step) % n) for i in range(n)])]
    unnamed x47 -> x46, local copies, waits for them, and re-layouts: 4.14 us -> 2.95 us
  transfers between devices with their start and end apart: 33 -> 34, of which waited for: 15 -> 15; matrix products, arithmetic and copies ran while one was open for 4% -> 3% of each run, Pallas kernels for 0% -> 0%
where the time goes in v8:
time: 156 us; the launch traced here: 155 us
  starting transfers between devices  57.3 us (37%)
  waiting for transfers between devices  54.8 us (35%)
  Pallas kernels  19.4 us (12%)
  other arithmetic  11.6 us (7%)
  matrix products  6.39 us (4%)
  local copies, waits for them, and re-layouts  4.78 us (3%)
    ppermute x29, waiting for transfers between devices, ring_shift(): return lax.ppermute(block, axis, [(i, (i + step) % n) for i in range(n)])  45.1 us
    ppermute x29, starting transfers between devices, ring_shift(): return lax.ppermute(block, axis, [(i, (i + step) % n) for i in range(n)])  41.7 us
    pallas_call x1, Pallas kernels, attention(): pl.pallas_call(functools.partial(attention_kernel, scale), grid=(frames,...  19.4 us
    ppermute x2, starting transfers between devices, row_shift(): return lax.ppermute(block, ROW_AXES, route)  11.8 us
    ppermute x2, waiting for transfers between devices, row_shift(): return lax.ppermute(block, ROW_AXES, route)  9.76 us
    convert_element_type x3, other arithmetic, pack(): return jnp.concatenate([summed.astype(jnp.bfloat16), stats], axis=1)  3.81 us
    dot_general x1, matrix products, per_device(): jnp.dot(columns, conv_weight.reshape(27 * width, width), preferred_elemen...  3.61 us
    another operation x6, other arithmetic, per_device(): outer = jnp.stack(ring_gather(inner, second, halve=True))  3.18 us
  transfers between devices with their start and end apart: 34, of which 15 were waited for; matrix products, arithmetic and copies ran while one was open for 3% of the time, Pallas kernels for 0%

profile of v8, /device:TPU:2, one launch (start us, length us, event | category | flops | bytes accessed | tf_op | source)
XLA Modules:
  0.0 155.1 jit_solution(11531296995043639382)
XLA Ops:
  0.0 1.1 fusion.21
  1.1 1.0 fusion.103
  2.2 1.6 %collective-permute-start.16 = (bf16[2,64,384]{2,1,0:T(8,128)(2,1)S(1)}, bf16[2,64,384]{2,1,0:T(8,128)(2,1)S(1)}, u32[]{:S(2)}, u32[]{:S(2)}) collective-permute-start(bf16[2,64,384]{2,1,0:T(8,128)(2,1)S(1)} %get-tuple-element.60), channel_id=1, source_target_pairs={{0,32},{32,64},{64,96},{96,0},{1,33},{33,65},{65,97},{97,1},{2,34}... | collective-permute-start | bytes 294920 | tf_op jit(solution)/shard_map/ppermute | solution.py:25
  3.8 1.0 fusion.22
  4.8 1.2 convolution_convert_fusion
  6.0 2.0 %collective-permute-start.3 = (bf16[2,128,384]{2,1,0:T(8,128)(2,1)S(1)}, bf16[2,128,384]{2,1,0:T(8,128)(2,1)S(1)}, u32[]{:S(2)}, u32[]{:S(2)}) collective-permute-start(bf16[2,128,384]{2,1,0:T(8,128)(2,1)S(1)} %bitcast.312), channel_id=1, source_target_pairs={{0,4},{4,8},{8,12},{12,16},{16,20},{20,24},{24,28},{28,0},{1,5},{5... | collective-permute-start | bytes 589832 | tf_op jit(solution)/shard_map/ppermute | solution.py:25
  8.0 0.5 collective-permute-start.15
  8.6 3.0 %collective-permute-start.8 = (bf16[2,64,384]{2,1,0:T(8,128)(2,1)S(1)}, bf16[2,64,384]{2,1,0:T(8,128)(2,1)S(1)}, u32[]{:S(2)}, u32[]{:S(2)}) collective-permute-start(bf16[2,64,384]{2,1,0:T(8,128)(2,1)S(1)} %get-tuple-element.61), channel_id=1, source_target_pairs={{0,3},{1,0},{2,1},{3,2},{4,7},{5,4},{6,5},{7,6},{8,11},{9,8},{10,9... | collective-permute-start | bytes 294920 | tf_op jit(solution)/shard_map/ppermute | solution.py:25
  11.6 1.5 collective-permute-start.17
  13.1 4.1 %collective-permute-start = (bf16[2,128,384]{2,1,0:T(8,128)(2,1)S(1)}, bf16[2,128,384]{2,1,0:T(8,128)(2,1)S(1)}, u32[]{:S(2)}, u32[]{:S(2)}) collective-permute-start(bf16[2,128,384]{2,1,0:T(8,128)(2,1)S(1)} %bitcast.314), channel_id=1, source_target_pairs={{0,28},{4,0},{8,4},{12,8},{16,12},{20,16},{24,20},{28,24},{1,29},{... | collective-permute-start | bytes 589832 | tf_op jit(solution)/shard_map/ppermute | solution.py:25
  17.2 0.2 collective-permute-done.9
  17.4 0.8 collective-permute-start.10
  18.3 1.1 collective-permute-start.4
  19.3 0.1 fusion.77
  19.4 3.3 %collective-permute-start.18 = (bf16[4,2,64,384]{3,2,1,0:T(8,128)(2,1)S(1)}, bf16[4,2,64,384]{3,2,1,0:T(8,128)(2,1)S(1)}, u32[]{:S(2)}, u32[]{:S(2)}) collective-permute-start(bf16[4,2,64,384]{3,2,1,0:T(8,128)(2,1)S(1)} %get-tuple-element.55), channel_id=1, source_target_pairs={{0,3},{1,0},{2,1},{3,2},{4,7},{5,4},{6,5},{7,6},{8,11},{9,8},{10,9... | collective-permute-start | bytes 1179656 | tf_op jit(solution)/shard_map/ppermute | solution.py:25
  22.7 0.5 collective-permute-done.10
  23.2 0.1 fusion.78
  23.3 1.8 %collective-permute-start.11 = (bf16[4,2,64,384]{3,2,1,0:T(8,128)(2,1)S(1)}, bf16[4,2,64,384]{3,2,1,0:T(8,128)(2,1)S(1)}, u32[]{:S(2)}, u32[]{:S(2)}) collective-permute-start(bf16[4,2,64,384]{3,2,1,0:T(8,128)(2,1)S(1)} %get-tuple-element.57), channel_id=1, source_target_pairs={{0,96},{32,0},{64,32},{96,64},{1,97},{33,1},{65,33},{97,65},{2,98}... | collective-permute-start | bytes 1179656 | tf_op jit(solution)/shard_map/ppermute | solution.py:25
  25.1 5.1 %collective-permute-start.1 = (bf16[2,128,384]{2,1,0:T(8,128)(2,1)S(1)}, bf16[2,128,384]{2,1,0:T(8,128)(2,1)S(1)}, u32[]{:S(2)}, u32[]{:S(2)}) collective-permute-start(bf16[2,128,384]{2,1,0:T(8,128)(2,1)S(1)} %collective-permute-done), channel_id=1, source_target_pairs={{0,28},{4,0},{8,4},{12,8},{16,12},{20,16},{24,20},{28,24},{1,29},{... | collective-permute-start | bytes 589832 | tf_op jit(solution)/shard_map/ppermute | solution.py:25
  30.3 4.6 %collective-permute-done.1 = bf16[2,128,384]{2,1,0:T(8,128)(2,1)S(1)} collective-permute-done((bf16[2,128,384]{2,1,0:T(8,128)(2,1)S(1)}, bf16[2,128,384]{2,1,0:T(8,128)(2,1)S(1)}, u32[]{:S(2)}, u32[]{:S(2)}) %collective-permute-start.1) | collective-permute-done | bytes 196640 | tf_op jit(solution)/shard_map/ppermute | solution.py:25
  34.8 2.3 %collective-permute-done.5 = bf16[2,128,384]{2,1,0:T(8,128)(2,1)S(1)} collective-permute-done((bf16[2,128,384]{2,1,0:T(8,128)(2,1)S(1)}, bf16[2,128,384]{2,1,0:T(8,128)(2,1)S(1)}, u32[]{:S(2)}, u32[]{:S(2)}) %collective-permute-start.5) | collective-permute-done | bytes 196640 | tf_op jit(solution)/shard_map/ppermute | solution.py:25
  37.1 1.4 collective-permute-start.2
  38.6 4.2 %collective-permute-done.2 = bf16[2,128,384]{2,1,0:T(8,128)(2,1)S(1)} collective-permute-done((bf16[2,128,384]{2,1,0:T(8,128)(2,1)S(1)}, bf16[2,128,384]{2,1,0:T(8,128)(2,1)S(1)}, u32[]{:S(2)}, u32[]{:S(2)}) %collective-permute-start.2) | collective-permute-done | bytes 196640 | tf_op jit(solution)/shard_map/ppermute | solution.py:25
  42.8 3.5 %collective-permute-start.7 = (bf16[1,128,384]{2,1,0:T(8,128)(2,1)S(1)}, bf16[1,128,384]{2,1,0:T(8,128)(2,1)S(1)}, u32[]{:S(2)}, u32[]{:S(2)}) collective-permute-start(bf16[1,128,384]{2,1,0:T(8,128)(2,1)S(1)} %slice.461), channel_id=1, source_target_pairs={{0,28},{4,0},{8,4},{12,8},{16,12},{20,16},{24,20},{28,24},{1,29},{... | collective-permute-start | bytes 294920 | tf_op jit(solution)/shard_map/ppermute | solution.py:25
  46.4 0.8 collective-permute-start.21
  47.1 1.4 collective-permute-start.20
  48.6 1.9 %collective-permute-start.14 = (bf16[2,2,64,384]{3,2,1,0:T(8,128)(2,1)S(1)}, bf16[2,2,64,384]{3,2,1,0:T(8,128)(2,1)S(1)}, u32[]{:S(2)}, u32[]{:S(2)}) collective-permute-start(bf16[2,2,64,384]{3,2,1,0:T(8,128)(2,1)S(1)} %slice.464), channel_id=1, source_target_pairs={{0,96},{32,0},{64,32},{96,64},{1,97},{33,1},{65,33},{97,65},{2,98}... | collective-permute-start | bytes 589832 | tf_op jit(solution)/shard_map/ppermute | solution.py:25
  50.6 0.3 collective-permute-start.13
  51.0 1.1 collective-permute-done.21
  52.1 2.0 %collective-permute-done.20 = bf16[2,2,64,384]{3,2,1,0:T(8,128)(2,1)S(1)} collective-permute-done((bf16[2,2,64,384]{3,2,1,0:T(8,128)(2,1)S(1)}, bf16[2,2,64,384]{3,2,1,0:T(8,128)(2,1)S(1)}, u32[]{:S(2)}, u32[]{:S(2)}) %collective-permute-start.20) | collective-permute-done | bytes 196640 | tf_op jit(solution)/shard_map/ppermute | solution.py:25
  54.2 1.5 pad_maximum_fusion.1
  55.6 0.8 collective-permute-done.13
  56.5 1.4 pad_maximum_fusion
  57.9 19.4 %shard_map.64 = (f32[2,1,1024]{2,1,0:T(1,128)}, f32[2,1,1024]{2,1,0:T(1,128)}, f32[2,1024,384]{2,1,0:T(8,128)}, bf16[2,1024,384]{2,1,0:T(8,128)(2,1)}) custom-call(bf16[8,2,128,384]{3,2,1,0:T(8,128)(2,1)} %copy-done.2, bf16[16,2,64,384]{3,2,1,0:T(8,128)(2,1)} %bitcast.307, bf16[16,2,64,384]{3,2,1,0:T(8,128)(2,1)} %bitcast.306, bf16[384,384]{1,0:T(8,128)(2,1)} %key_w_ref.1, ...), custom_call_target="tpu_custom_call" | custom-call | flops 8858370048 | bytes 9437184 | tf_op jit(solution)/shard_map/pallas_call | solution.py:161
  77.3 1.1 fusion.92
  78.4 0.7 copy_bitcast_fusion
  79.3 0.3 collective-permute-start.22
  79.6 6.8 %collective-permute-done.22 = bf16[2,130,384]{2,1,0:T(8,128)(2,1)S(1)} collective-permute-done((bf16[2,130,384]{2,1,0:T(8,128)(2,1)S(1)}, bf16[2,130,384]{2,1,0:T(8,128)(2,1)S(1)}, u32[]{:S(2)}, u32[]{:S(2)}) %collective-permute-start.22) | collective-permute-done | bytes 199712 | tf_op jit(solution)/shard_map/ppermute | solution.py:25
  86.5 1.1 add_convert_fusion.4
  87.7 0.3 collective-permute-start.23
  88.0 8.4 %collective-permute-done.23 = bf16[2,130,384]{2,1,0:T(8,128)(2,1)S(1)} collective-permute-done((bf16[2,130,384]{2,1,0:T(8,128)(2,1)S(1)}, bf16[2,130,384]{2,1,0:T(8,128)(2,1)S(1)}, u32[]{:S(2)}, u32[]{:S(2)}) %collective-permute-start.23) | collective-permute-done | bytes 199712 | tf_op jit(solution)/shard_map/ppermute | solution.py:25
  96.6 0.1 collective-permute-start.26
  96.7 5.8 %collective-permute-done.26 = bf16[2,130,384]{2,1,0:T(8,128)(2,1)S(1)} collective-permute-done((bf16[2,130,384]{2,1,0:T(8,128)(2,1)S(1)}, bf16[2,130,384]{2,1,0:T(8,128)(2,1)S(1)}, u32[]{:S(2)}, u32[]{:S(2)}) %collective-permute-start.26) | collective-permute-done | bytes 199712 | tf_op jit(solution)/shard_map/ppermute | solution.py:25
  102.6 1.3 add_convert_fusion.3
  104.0 0.1 collective-permute-start.24
  104.2 3.3 %collective-permute-start.27 = (bf16[2,130,384]{2,1,0:T(8,128)(2,1)S(1)}, bf16[2,130,384]{2,1,0:T(8,128)(2,1)S(1)}, u32[]{:S(2)}, u32[]{:S(2)}) collective-permute-start(bf16[2,130,384]{2,1,0:T(8,128)(2,1)S(1)} %pad_maximum_fusion.9), channel_id=1, source_target_pairs={{0,28},{4,0},{8,4},{12,8},{16,12},{20,16},{24,20},{28,24},{1,29},{... | collective-permute-start | bytes 599048 | tf_op jit(solution)/shard_map/ppermute | solution.py:25
  107.5 3.6 %collective-permute-done.24 = bf16[2,130,384]{2,1,0:T(8,128)(2,1)S(1)} collective-permute-done((bf16[2,130,384]{2,1,0:T(8,128)(2,1)S(1)}, bf16[2,130,384]{2,1,0:T(8,128)(2,1)S(1)}, u32[]{:S(2)}, u32[]{:S(2)}) %collective-permute-start.24) | collective-permute-done | bytes 199712 | tf_op jit(solution)/shard_map/ppermute | solution.py:25
  111.4 1.3 add_convert_fusion.2
  112.8 0.1 collective-permute-start.25
  112.9 3.4 %collective-permute-start.28 = (bf16[2,130,384]{2,1,0:T(8,128)(2,1)S(1)}, bf16[2,130,384]{2,1,0:T(8,128)(2,1)S(1)}, u32[]{:S(2)}, u32[]{:S(2)}) collective-permute-start(bf16[2,130,384]{2,1,0:T(8,128)(2,1)S(1)} %pad_maximum_fusion.10), channel_id=1, source_target_pairs={{0,28},{4,0},{8,4},{12,8},{16,12},{20,16},{24,20},{28,24},{1,29},{... | collective-permute-start | bytes 599048 | tf_op jit(solution)/shard_map/ppermute | solution.py:25
  116.3 3.6 %collective-permute-done.25 = bf16[2,130,384]{2,1,0:T(8,128)(2,1)S(1)} collective-permute-done((bf16[2,130,384]{2,1,0:T(8,128)(2,1)S(1)}, bf16[2,130,384]{2,1,0:T(8,128)(2,1)S(1)}, u32[]{:S(2)}, u32[]{:S(2)}) %collective-permute-start.25) | collective-permute-done | bytes 199712 | tf_op jit(solution)/shard_map/ppermute | solution.py:25
  119.9 1.3 collective-permute-done.28
  121.3 1.5 multiply_reduce_fusion
  122.9 0.2 multiply_convert_fusion
  123.1 1.3 collective-permute-start.29
  124.4 1.3 collective-permute-start.32
  125.7 9.8 %collective-permute-start.33 = (bf16[2,1,128,384]{3,2,0,1:T(8,128)(2,1)S(1)}, bf16[2,1,128,384]{3,2,0,1:T(8,128)(2,1)S(1)}, u32[]{:S(2)}, u32[]{:S(2)}) collective-permute-start(bf16[2,1,128,384]{3,2,0,1:T(8,128)(2,1)S(1)} %multiply_convert_fusion), channel_id=1, source_target_pairs={{1,0},{2,1},{3,2},{4,3},{5,4},{6,5},{7,6},{8,7},{9,8},{10,9},{11,1... | collective-permute-start | bytes 589832 | tf_op jit(solution)/shard_map/ppermute | solution.py:113
  135.5 1.3 collective-permute-start.31
  136.8 1.9 %collective-permute-start.30 = (bf16[2,1,128,384]{3,2,0,1:T(8,128)(2,1)S(1)}, bf16[2,1,128,384]{3,2,0,1:T(8,128)(2,1)S(1)}, u32[]{:S(2)}, u32[]{:S(2)}) collective-permute-start(bf16[2,1,128,384]{3,2,0,1:T(8,128)(2,1)S(1)} %multiply_convert_fusion), channel_id=1, source_target_pairs={{0,1},{1,2},{2,3},{3,4},{4,5},{5,6},{6,7},{7,8},{8,9},{9,10},{10,1... | collective-permute-start | bytes 589832 | tf_op jit(solution)/shard_map/ppermute | solution.py:113
  138.9 9.8 %collective-permute-done.30 = bf16[2,1,128,384]{3,2,0,1:T(8,128)(2,1)S(1)} collective-permute-done((bf16[2,1,128,384]{3,2,0,1:T(8,128)(2,1)S(1)}, bf16[2,1,128,384]{3,2,0,1:T(8,128)(2,1)S(1)}, u32[]{:S(2)}, u32[]{:S(2)}) %collective-permute-start.30) | collective-permute-done | bytes 196640 | tf_op jit(solution)/shard_map/ppermute | solution.py:113
  148.7 0.3 select_maximum_fusion
  150.2 0.2 constant_dynamic-update-slice_fusion.48
  150.6 0.9 slice-done.1
  151.5 3.6 %fusion.18 = bf16[2,1,128,384]{3,2,1,0:T(8,128)(2,1)} fusion(f32[2,1,128,384]{3,2,0,1:T(8,128)S(1)} %get-tuple-element.110, bf16[10368,384,1]{1,0,2:T(8,128)(2,1)S(1)} %bitcast.324, bf16[2,1,128,10368]{3,2,0,1:T(8,128)(2,1)S(1)} %slice_dynamic-update-slice_fusion), kind=kOutput, calls=%fused_computation.20 | convolution fusion | flops 2038628352 | bytes 13860864 | tf_op jit(solution)/shard_map/dot_general | solution.py:250
  (164 shorter events, 3.0 us)
Async XLA Ops:
  0.0 121.3 %copy-start = (bf16[384,384]{1,0:T(8,128)(2,1)S(1)}, bf16[384,384]{1,0:T(8,128)(2,1)}, u32[]{:S(2)}) copy-start(bf16[384,384]{1,0:T(8,128)(2,1)} %param.10) | copy-start | bytes 884740
  2.2 9.4 %collective-permute-start.16 = (bf16[2,64,384]{2,1,0:T(8,128)(2,1)S(1)}, bf16[2,64,384]{2,1,0:T(8,128)(2,1)S(1)}, u32[]{:S(2)}, u32[]{:S(2)}) collective-permute-start(bf16[2,64,384]{2,1,0:T(8,128)(2,1)S(1)} %get-tuple-element.60), channel_id=1, source_target_pairs={{0,32},{32,64},{64,96},{96,0},{1,33},{33,65},{65,97},{97,1},{2,34}... | collective-permute-start | bytes 294920 | tf_op jit(solution)/shard_map/ppermute | solution.py:25
  6.0 12.2 %collective-permute-start.3 = (bf16[2,128,384]{2,1,0:T(8,128)(2,1)S(1)}, bf16[2,128,384]{2,1,0:T(8,128)(2,1)S(1)}, u32[]{:S(2)}, u32[]{:S(2)}) collective-permute-start(bf16[2,128,384]{2,1,0:T(8,128)(2,1)S(1)} %bitcast.312), channel_id=1, source_target_pairs={{0,4},{4,8},{8,12},{12,16},{16,20},{20,24},{24,28},{28,0},{1,5},{5... | collective-permute-start | bytes 589832 | tf_op jit(solution)/shard_map/ppermute | solution.py:25
  8.0 5.1 %collective-permute-start.15 = (bf16[2,64,384]{2,1,0:T(8,128)(2,1)S(1)}, bf16[2,64,384]{2,1,0:T(8,128)(2,1)S(1)}, u32[]{:S(2)}, u32[]{:S(2)}) collective-permute-start(bf16[2,64,384]{2,1,0:T(8,128)(2,1)S(1)} %get-tuple-element.60), channel_id=1, source_target_pairs={{0,96},{32,0},{64,32},{96,64},{1,97},{33,1},{65,33},{97,65},{2,98}... | collective-permute-start | bytes 294920 | tf_op jit(solution)/shard_map/ppermute | solution.py:25
  8.6 14.2 %collective-permute-start.8 = (bf16[2,64,384]{2,1,0:T(8,128)(2,1)S(1)}, bf16[2,64,384]{2,1,0:T(8,128)(2,1)S(1)}, u32[]{:S(2)}, u32[]{:S(2)}) collective-permute-start(bf16[2,64,384]{2,1,0:T(8,128)(2,1)S(1)} %get-tuple-element.61), channel_id=1, source_target_pairs={{0,3},{1,0},{2,1},{3,2},{4,7},{5,4},{6,5},{7,6},{8,11},{9,8},{10,9... | collective-permute-start | bytes 294920 | tf_op jit(solution)/shard_map/ppermute | solution.py:25
  11.6 5.8 %collective-permute-start.9 = (bf16[2,64,384]{2,1,0:T(8,128)(2,1)S(1)}, bf16[2,64,384]{2,1,0:T(8,128)(2,1)S(1)}, u32[]{:S(2)}, u32[]{:S(2)}) collective-permute-start(bf16[2,64,384]{2,1,0:T(8,128)(2,1)S(1)} %get-tuple-element.61), channel_id=1, source_target_pairs={{0,1},{1,2},{2,3},{3,0},{4,5},{5,6},{6,7},{7,4},{8,9},{9,10},{10,1... | collective-permute-start | bytes 294920 | tf_op jit(solution)/shard_map/ppermute | solution.py:25
  11.6 7.8 %collective-permute-start.17 = (bf16[2,64,384]{2,1,0:T(8,128)(2,1)S(1)}, bf16[2,64,384]{2,1,0:T(8,128)(2,1)S(1)}, u32[]{:S(2)}, u32[]{:S(2)}) collective-permute-start(bf16[2,64,384]{2,1,0:T(8,128)(2,1)S(1)} %collective-permute-done.16), channel_id=1, source_target_pairs={{0,32},{32,64},{64,96},{96,0},{1,33},{33,65},{65,97},{97,1},{2,34}... | collective-permute-start | bytes 294920 | tf_op jit(solution)/shard_map/ppermute | solution.py:25
  13.1 12.0 %collective-permute-start = (bf16[2,128,384]{2,1,0:T(8,128)(2,1)S(1)}, bf16[2,128,384]{2,1,0:T(8,128)(2,1)S(1)}, u32[]{:S(2)}, u32[]{:S(2)}) collective-permute-start(bf16[2,128,384]{2,1,0:T(8,128)(2,1)S(1)} %bitcast.314), channel_id=1, source_target_pairs={{0,28},{4,0},{8,4},{12,8},{16,12},{20,16},{24,20},{28,24},{1,29},{... | collective-permute-start | bytes 589832 | tf_op jit(solution)/shard_map/ppermute | solution.py:25
  17.4 5.8 %collective-permute-start.10 = (bf16[2,64,384]{2,1,0:T(8,128)(2,1)S(1)}, bf16[2,64,384]{2,1,0:T(8,128)(2,1)S(1)}, u32[]{:S(2)}, u32[]{:S(2)}) collective-permute-start(bf16[2,64,384]{2,1,0:T(8,128)(2,1)S(1)} %collective-permute-done.9), channel_id=1, source_target_pairs={{0,1},{1,2},{2,3},{3,0},{4,5},{5,6},{6,7},{7,4},{8,9},{9,10},{10,1... | collective-permute-start | bytes 294920 | tf_op jit(solution)/shard_map/ppermute | solution.py:25
  18.3 12.0 %collective-permute-start.4 = (bf16[2,128,384]{2,1,0:T(8,128)(2,1)S(1)}, bf16[2,128,384]{2,1,0:T(8,128)(2,1)S(1)}, u32[]{:S(2)}, u32[]{:S(2)}) collective-permute-start(bf16[2,128,384]{2,1,0:T(8,128)(2,1)S(1)} %collective-permute-done.3), channel_id=1, source_target_pairs={{0,4},{4,8},{8,12},{12,16},{16,20},{20,24},{24,28},{28,0},{1,5},{5... | collective-permute-start | bytes 589832 | tf_op jit(solution)/shard_map/ppermute | solution.py:25
  19.4 23.4 %collective-permute-start.18 = (bf16[4,2,64,384]{3,2,1,0:T(8,128)(2,1)S(1)}, bf16[4,2,64,384]{3,2,1,0:T(8,128)(2,1)S(1)}, u32[]{:S(2)}, u32[]{:S(2)}) collective-permute-start(bf16[4,2,64,384]{3,2,1,0:T(8,128)(2,1)S(1)} %get-tuple-element.55), channel_id=1, source_target_pairs={{0,3},{1,0},{2,1},{3,2},{4,7},{5,4},{6,5},{7,6},{8,11},{9,8},{10,9... | collective-permute-start | bytes 1179656 | tf_op jit(solution)/shard_map/ppermute | solution.py:25
  22.7 23.6 %collective-permute-start.19 = (bf16[4,2,64,384]{3,2,1,0:T(8,128)(2,1)S(1)}, bf16[4,2,64,384]{3,2,1,0:T(8,128)(2,1)S(1)}, u32[]{:S(2)}, u32[]{:S(2)}) collective-permute-start(bf16[4,2,64,384]{3,2,1,0:T(8,128)(2,1)S(1)} %get-tuple-element.55), channel_id=1, source_target_pairs={{0,1},{1,2},{2,3},{3,0},{4,5},{5,6},{6,7},{7,4},{8,9},{9,10},{10,1... | collective-permute-start | bytes 1179656 | tf_op jit(solution)/shard_map/ppermute | solution.py:25
  23.3 23.8 %collective-permute-start.11 = (bf16[4,2,64,384]{3,2,1,0:T(8,128)(2,1)S(1)}, bf16[4,2,64,384]{3,2,1,0:T(8,128)(2,1)S(1)}, u32[]{:S(2)}, u32[]{:S(2)}) collective-permute-start(bf16[4,2,64,384]{3,2,1,0:T(8,128)(2,1)S(1)} %get-tuple-element.57), channel_id=1, source_target_pairs={{0,96},{32,0},{64,32},{96,64},{1,97},{33,1},{65,33},{97,65},{2,98}... | collective-permute-start | bytes 1179656 | tf_op jit(solution)/shard_map/ppermute | solution.py:25
  25.1 9.7 %collective-permute-start.1 = (bf16[2,128,384]{2,1,0:T(8,128)(2,1)S(1)}, bf16[2,128,384]{2,1,0:T(8,128)(2,1)S(1)}, u32[]{:S(2)}, u32[]{:S(2)}) collective-permute-start(bf16[2,128,384]{2,1,0:T(8,128)(2,1)S(1)} %collective-permute-done), channel_id=1, source_target_pairs={{0,28},{4,0},{8,4},{12,8},{16,12},{20,16},{24,20},{28,24},{1,29},{... | collective-permute-start | bytes 589832 | tf_op jit(solution)/shard_map/ppermute | solution.py:25
  30.2 6.9 %collective-permute-start.5 = (bf16[2,128,384]{2,1,0:T(8,128)(2,1)S(1)}, bf16[2,128,384]{2,1,0:T(8,128)(2,1)S(1)}, u32[]{:S(2)}, u32[]{:S(2)}) collective-permute-start(bf16[2,128,384]{2,1,0:T(8,128)(2,1)S(1)} %collective-permute-done.4), channel_id=1, source_target_pairs={{0,4},{4,8},{8,12},{12,16},{16,20},{20,24},{24,28},{28,0},{1,5},{5... | collective-permute-start | bytes 589832 | tf_op jit(solution)/shard_map/ppermute | solution.py:25
  34.8 13.8 %collective-permute-start.12 = (bf16[4,2,64,384]{3,2,1,0:T(8,128)(2,1)S(1)}, bf16[4,2,64,384]{3,2,1,0:T(8,128)(2,1)S(1)}, u32[]{:S(2)}, u32[]{:S(2)}) collective-permute-start(bf16[4,2,64,384]{3,2,1,0:T(8,128)(2,1)S(1)} %get-tuple-element.57), channel_id=1, source_target_pairs={{0,32},{32,64},{64,96},{96,0},{1,33},{33,65},{65,97},{97,1},{2,34}... | collective-permute-start | bytes 1179656 | tf_op jit(solution)/shard_map/ppermute | solution.py:25
  37.1 5.7 %collective-permute-start.2 = (bf16[2,128,384]{2,1,0:T(8,128)(2,1)S(1)}, bf16[2,128,384]{2,1,0:T(8,128)(2,1)S(1)}, u32[]{:S(2)}, u32[]{:S(2)}) collective-permute-start(bf16[2,128,384]{2,1,0:T(8,128)(2,1)S(1)} %collective-permute-done.1), channel_id=1, source_target_pairs={{0,28},{4,0},{8,4},{12,8},{16,12},{20,16},{24,20},{28,24},{1,29},{... | collective-permute-start | bytes 589832 | tf_op jit(solution)/shard_map/ppermute | solution.py:25
  42.8 7.8 %collective-permute-start.6 = (bf16[1,128,384]{2,1,0:T(8,128)(2,1)S(1)}, bf16[1,128,384]{2,1,0:T(8,128)(2,1)S(1)}, u32[]{:S(2)}, u32[]{:S(2)}) collective-permute-start(bf16[1,128,384]{2,1,0:T(8,128)(2,1)S(1)} %slice.460), channel_id=1, source_target_pairs={{0,4},{4,8},{8,12},{12,16},{16,20},{20,24},{24,28},{28,0},{1,5},{5... | collective-permute-start | bytes 294920 | tf_op jit(solution)/shard_map/ppermute | solution.py:25
  42.8 8.0 %collective-permute-start.7 = (bf16[1,128,384]{2,1,0:T(8,128)(2,1)S(1)}, bf16[1,128,384]{2,1,0:T(8,128)(2,1)S(1)}, u32[]{:S(2)}, u32[]{:S(2)}) collective-permute-start(bf16[1,128,384]{2,1,0:T(8,128)(2,1)S(1)} %slice.461), channel_id=1, source_target_pairs={{0,28},{4,0},{8,4},{12,8},{16,12},{20,16},{24,20},{28,24},{1,29},{... | collective-permute-start | bytes 294920 | tf_op jit(solution)/shard_map/ppermute | solution.py:25
  46.4 5.7 %collective-permute-start.21 = (bf16[2,2,64,384]{3,2,1,0:T(8,128)(2,1)S(1)}, bf16[2,2,64,384]{3,2,1,0:T(8,128)(2,1)S(1)}, u32[]{:S(2)}, u32[]{:S(2)}) collective-permute-start(bf16[2,2,64,384]{3,2,1,0:T(8,128)(2,1)S(1)} %slice.467), channel_id=1, source_target_pairs={{0,3},{1,0},{2,1},{3,2},{4,7},{5,4},{6,5},{7,6},{8,11},{9,8},{10,9... | collective-permute-start | bytes 589832 | tf_op jit(solution)/shard_map/ppermute | solution.py:25
  47.1 7.0 %collective-permute-start.20 = (bf16[2,2,64,384]{3,2,1,0:T(8,128)(2,1)S(1)}, bf16[2,2,64,384]{3,2,1,0:T(8,128)(2,1)S(1)}, u32[]{:S(2)}, u32[]{:S(2)}) collective-permute-start(bf16[2,2,64,384]{3,2,1,0:T(8,128)(2,1)S(1)} %slice.466), channel_id=1, source_target_pairs={{0,1},{1,2},{2,3},{3,0},{4,5},{5,6},{6,7},{7,4},{8,9},{9,10},{10,1... | collective-permute-start | bytes 589832 | tf_op jit(solution)/shard_map/ppermute | solution.py:25
  48.6 7.0 %collective-permute-start.14 = (bf16[2,2,64,384]{3,2,1,0:T(8,128)(2,1)S(1)}, bf16[2,2,64,384]{3,2,1,0:T(8,128)(2,1)S(1)}, u32[]{:S(2)}, u32[]{:S(2)}) collective-permute-start(bf16[2,2,64,384]{3,2,1,0:T(8,128)(2,1)S(1)} %slice.464), channel_id=1, source_target_pairs={{0,96},{32,0},{64,32},{96,64},{1,97},{33,1},{65,33},{97,65},{2,98}... | collective-permute-start | bytes 589832 | tf_op jit(solution)/shard_map/ppermute | solution.py:25
  50.6 5.9 %collective-permute-start.13 = (bf16[2,2,64,384]{3,2,1,0:T(8,128)(2,1)S(1)}, bf16[2,2,64,384]{3,2,1,0:T(8,128)(2,1)S(1)}, u32[]{:S(2)}, u32[]{:S(2)}) collective-permute-start(bf16[2,2,64,384]{3,2,1,0:T(8,128)(2,1)S(1)} %slice.463), channel_id=1, source_target_pairs={{0,32},{32,64},{64,96},{96,0},{1,33},{33,65},{65,97},{97,1},{2,34}... | collective-permute-start | bytes 589832 | tf_op jit(solution)/shard_map/ppermute | solution.py:25
  51.0 6.9 %copy-start.2 = (bf16[8,2,128,384]{3,2,1,0:T(8,128)(2,1)}, bf16[8,2,128,384]{3,2,1,0:T(8,128)(2,1)S(1)}, u32[]{:S(2)}) copy-start(bf16[8,2,128,384]{3,2,1,0:T(8,128)(2,1)S(1)} %bitcast_dynamic-update-slice_fusion.query_ref) | copy-start | bytes 4718596
  77.3 44.0 %copy-start.1 = (bf16[2,1,128,384]{3,2,1,0:T(8,128)(2,1)S(1)}, bf16[2,1,128,384]{3,2,1,0:T(8,128)(2,1)}, u32[]{:S(2)}) copy-start(bf16[2,1,128,384]{3,2,1,0:T(8,128)(2,1)} %param.6) | copy-start | bytes 589828
  79.3 7.1 %collective-permute-start.22 = (bf16[2,130,384]{2,1,0:T(8,128)(2,1)S(1)}, bf16[2,130,384]{2,1,0:T(8,128)(2,1)S(1)}, u32[]{:S(2)}, u32[]{:S(2)}) collective-permute-start(bf16[2,130,384]{2,1,0:T(8,128)(2,1)S(1)} %pad_maximum_fusion.4), channel_id=1, source_target_pairs={{0,4},{4,8},{8,12},{12,16},{16,20},{20,24},{24,28},{28,0},{1,5},{5... | collective-permute-start | bytes 599048 | tf_op jit(solution)/shard_map/ppermute | solution.py:25
  87.7 8.7 %collective-permute-start.23 = (bf16[2,130,384]{2,1,0:T(8,128)(2,1)S(1)}, bf16[2,130,384]{2,1,0:T(8,128)(2,1)S(1)}, u32[]{:S(2)}, u32[]{:S(2)}) collective-permute-start(bf16[2,130,384]{2,1,0:T(8,128)(2,1)S(1)} %pad_maximum_fusion.5), channel_id=1, source_target_pairs={{0,4},{4,8},{8,12},{12,16},{16,20},{20,24},{24,28},{28,0},{1,5},{5... | collective-permute-start | bytes 599048 | tf_op jit(solution)/shard_map/ppermute | solution.py:25
  96.6 6.0 %collective-permute-start.26 = (bf16[2,130,384]{2,1,0:T(8,128)(2,1)S(1)}, bf16[2,130,384]{2,1,0:T(8,128)(2,1)S(1)}, u32[]{:S(2)}, u32[]{:S(2)}) collective-permute-start(bf16[2,130,384]{2,1,0:T(8,128)(2,1)S(1)} %pad_maximum_fusion.8), channel_id=1, source_target_pairs={{0,28},{4,0},{8,4},{12,8},{16,12},{20,16},{24,20},{28,24},{1,29},{... | collective-permute-start | bytes 599048 | tf_op jit(solution)/shard_map/ppermute | solution.py:25
  104.0 7.1 %collective-permute-start.24 = (bf16[2,130,384]{2,1,0:T(8,128)(2,1)S(1)}, bf16[2,130,384]{2,1,0:T(8,128)(2,1)S(1)}, u32[]{:S(2)}, u32[]{:S(2)}) collective-permute-start(bf16[2,130,384]{2,1,0:T(8,128)(2,1)S(1)} %pad_maximum_fusion.6), channel_id=1, source_target_pairs={{0,4},{4,8},{8,12},{12,16},{16,20},{20,24},{24,28},{28,0},{1,5},{5... | collective-permute-start | bytes 599048 | tf_op jit(solution)/shard_map/ppermute | solution.py:25
  104.2 7.0 %collective-permute-start.27 = (bf16[2,130,384]{2,1,0:T(8,128)(2,1)S(1)}, bf16[2,130,384]{2,1,0:T(8,128)(2,1)S(1)}, u32[]{:S(2)}, u32[]{:S(2)}) collective-permute-start(bf16[2,130,384]{2,1,0:T(8,128)(2,1)S(1)} %pad_maximum_fusion.9), channel_id=1, source_target_pairs={{0,28},{4,0},{8,4},{12,8},{16,12},{20,16},{24,20},{28,24},{1,29},{... | collective-permute-start | bytes 599048 | tf_op jit(solution)/shard_map/ppermute | solution.py:25
  112.8 7.1 %collective-permute-start.25 = (bf16[2,130,384]{2,1,0:T(8,128)(2,1)S(1)}, bf16[2,130,384]{2,1,0:T(8,128)(2,1)S(1)}, u32[]{:S(2)}, u32[]{:S(2)}) collective-permute-start(bf16[2,130,384]{2,1,0:T(8,128)(2,1)S(1)} %pad_maximum_fusion.7), channel_id=1, source_target_pairs={{0,4},{4,8},{8,12},{12,16},{16,20},{20,24},{24,28},{28,0},{1,5},{5... | collective-permute-start | bytes 599048 | tf_op jit(solution)/shard_map/ppermute | solution.py:25
  112.9 8.3 %collective-permute-start.28 = (bf16[2,130,384]{2,1,0:T(8,128)(2,1)S(1)}, bf16[2,130,384]{2,1,0:T(8,128)(2,1)S(1)}, u32[]{:S(2)}, u32[]{:S(2)}) collective-permute-start(bf16[2,130,384]{2,1,0:T(8,128)(2,1)S(1)} %pad_maximum_fusion.10), channel_id=1, source_target_pairs={{0,28},{4,0},{8,4},{12,8},{16,12},{20,16},{24,20},{28,24},{1,29},{... | collective-permute-start | bytes 599048 | tf_op jit(solution)/shard_map/ppermute | solution.py:25
  123.1 15.7 %collective-permute-start.29 = (bf16[2,1,128,384]{3,2,0,1:T(8,128)(2,1)S(1)}, bf16[2,1,128,384]{3,2,0,1:T(8,128)(2,1)S(1)}, u32[]{:S(2)}, u32[]{:S(2)}) collective-permute-start(bf16[2,1,128,384]{3,2,0,1:T(8,128)(2,1)S(1)} %multiply_convert_fusion), channel_id=1, source_target_pairs={{0,129},{1,130},{2,131},{3,132},{4,133},{5,134},{6,135},{7,136},{8... | collective-permute-start | bytes 589832 | tf_op jit(solution)/shard_map/ppermute | solution.py:231
  124.4 14.5 %collective-permute-start.32 = (bf16[2,1,128,384]{3,2,0,1:T(8,128)(2,1)S(1)}, bf16[2,1,128,384]{3,2,0,1:T(8,128)(2,1)S(1)}, u32[]{:S(2)}, u32[]{:S(2)}) collective-permute-start(bf16[2,1,128,384]{3,2,0,1:T(8,128)(2,1)S(1)} %multiply_convert_fusion), channel_id=1, source_target_pairs={{1,128},{2,129},{3,130},{4,131},{5,132},{6,133},{7,134},{8,135},{9... | collective-permute-start | bytes 589832 | tf_op jit(solution)/shard_map/ppermute | solution.py:232
  125.7 23.0 %collective-permute-start.33 = (bf16[2,1,128,384]{3,2,0,1:T(8,128)(2,1)S(1)}, bf16[2,1,128,384]{3,2,0,1:T(8,128)(2,1)S(1)}, u32[]{:S(2)}, u32[]{:S(2)}) collective-permute-start(bf16[2,1,128,384]{3,2,0,1:T(8,128)(2,1)S(1)} %multiply_convert_fusion), channel_id=1, source_target_pairs={{1,0},{2,1},{3,2},{4,3},{5,4},{6,5},{7,6},{8,7},{9,8},{10,9},{11,1... | collective-permute-start | bytes 589832 | tf_op jit(solution)/shard_map/ppermute | solution.py:113
  135.5 13.2 %collective-permute-start.31 = (bf16[2,1,128,384]{3,2,0,1:T(8,128)(2,1)S(1)}, bf16[2,1,128,384]{3,2,0,1:T(8,128)(2,1)S(1)}, u32[]{:S(2)}, u32[]{:S(2)}) collective-permute-start(bf16[2,1,128,384]{3,2,0,1:T(8,128)(2,1)S(1)} %multiply_convert_fusion), channel_id=1, source_target_pairs={{0,128},{1,129},{2,130},{3,131},{4,132},{5,133},{6,134},{7,135},{8... | collective-permute-start | bytes 589832 | tf_op jit(solution)/shard_map/ppermute | solution.py:230
  136.8 11.8 %collective-permute-start.30 = (bf16[2,1,128,384]{3,2,0,1:T(8,128)(2,1)S(1)}, bf16[2,1,128,384]{3,2,0,1:T(8,128)(2,1)S(1)}, u32[]{:S(2)}, u32[]{:S(2)}) collective-permute-start(bf16[2,1,128,384]{3,2,0,1:T(8,128)(2,1)S(1)} %multiply_convert_fusion), channel_id=1, source_target_pairs={{0,1},{1,2},{2,3},{3,4},{4,5},{5,6},{6,7},{7,8},{8,9},{9,10},{10,1... | collective-permute-start | bytes 589832 | tf_op jit(solution)/shard_map/ppermute | solution.py:113
  138.8 11.8 %slice-start = ((s8[7962624]{0:T(1024)(128)(4,1)}), s8[4194304]{0:T(1024)(128)(4,1)S(1)}, s32[]{:S(2)}) async-start(s8[7962624]{0:T(1024)(128)(4,1)} %bitcast.322), calls=%async_computation | async-start | bytes 8388608
  149.4 2.1 %slice-start.1 = ((s8[7962624]{0:T(1024)(128)(4,1)}), s8[3768320]{0:T(1024)(128)(4,1)S(1)}, s32[]{:S(2)}) async-start(s8[7962624]{0:T(1024)(128)(4,1)} %bitcast.322), calls=%async_computation.1 | async-start | bytes 7536640
